TPU v7x, 32 devices: a whole 2x2x4 slice. The times are simulated.
32 devices in a mesh: tm: 16 (over z, y, x), rows: 2 (over core).
Axes of the slice: x: 2, y: 2, z: 4, core: 2. Of those that a mesh axis runs over, the one named last changes fastest.
Arguments:
- frames: bfloat16 [64, 16, 128, 128], P('tm', 'rows'), may hold values from -6 to 6
- conv_in: bfloat16 [3, 3, 128, 128], replicated, may hold values from -0.09375 to 0.09375
- decay: float32 [64, 128], P('tm'), may hold values from 0.35 to 1, as said below
- conv_out: bfloat16 [3, 3, 128, 128], replicated, may hold values from -0.0234375 to 0.0234375
- skip: float32 [128], replicated, may hold values from -4 to 4
Outputs:
- mixed: bfloat16 [64, 16, 128, 128], P('tm', 'rows')
Inputs may be any that keep to these rules, and one draw needn't show every extreme that they name: `decay`: every entry lies strictly between 0 and 1.
All inputs are finite; a program needn't handle non-finite values.
Results may differ from a plain program's by a relative error of at most 0.0045.
Values may be sent and summed in bfloat16 or wider, within the bound.
No kernel may reach another device: no remote copies, remote signals or barrier semaphores. Data moves between devices by JAX's collectives and lax.ppermute only.
A program may use at most 192 MiB of HBM per device.

v0:
```python
import jax
import jax.numpy as jnp
from jax import lax
from jax.sharding import PartitionSpec as P


def extended(x, sides, width):
    for axis, dim in sides:
        size, length = (lax.axis_size(axis), x.shape[dim])
        up = [(i, (i + 1) % size) for i in range(size - 1)]
        down = [(j, i) for i, j in up]
        last = lax.slice_in_dim(x, length - width, length, axis=dim)
        first = lax.slice_in_dim(x, 0, width, axis=dim)
        before = lax.ppermute(last, axis, up)
        after = lax.ppermute(first, axis, down)
        x = jnp.concatenate([before, x, after], axis=dim)
    return x


def entering(x, axis, combine, identity):
    length, position = (lax.axis_size(axis), lax.axis_index(axis))
    everything = jax.tree.map(
        lambda part, kind: lax.all_gather(part.astype(kind), axis), x, (jnp.bfloat16, jnp.bfloat16)
    )
    start = jax.tree.map(
        lambda part, zero: jnp.broadcast_to(jnp.asarray(zero, part.dtype), part.shape), x, identity
    )

    def step(k, before):
        reached = k < position
        new = combine(
            before, jax.tree.map(lambda part, own: part[k].astype(own.dtype), everything, x)
        )
        return jax.tree.map(lambda a, b: jnp.where(reached, a, b), new, before)

    return lax.fori_loop(0, length, step, start)


def conv_bands(padded, weight, rows):
    width = padded.shape[1]
    channels = padded.shape[2]
    columns = jnp.pad(padded, ((0, 0), (1, 1), (0, 0)))
    total = jnp.zeros((rows * width, weight.shape[3]), jnp.float32)
    for down in range(3):
        for across in range(3):
            window = columns[down : down + rows, across : across + width, :].reshape(
                rows * width, channels
            )
            total = total + jnp.dot(
                window, weight[down, across], preferred_element_type=jnp.float32
            )
    return total.reshape(rows, width, weight.shape[3])


def combine(earlier, later):
    return (earlier[0] * later[0], later[0] * earlier[1] + later[1])


def shards(frames, conv_in, decay, conv_out, skip):
    count, band, width, channels = frames.shape
    state_width = conv_in.shape[3]
    margin = 1
    padded_in = extended(frames, (("rows", 1),), margin)
    out_rows = band + 2 * margin - 2
    state = jnp.zeros((out_rows, width, state_width), jnp.float32)
    power = jnp.ones((state_width,), jnp.float32)
    local_states = []
    products = []
    for frame_index in range(count):
        drive = conv_bands(padded_in[frame_index], conv_in, out_rows)
        state = decay[frame_index] * state + drive
        power = power * decay[frame_index]
        local_states.append(state)
        products.append(power)
    stacked = jnp.stack(local_states)
    cumulative = jnp.stack(products)[:, None, None, :]
    identity = (
        jnp.ones((state_width,), jnp.float32),
        jnp.zeros((out_rows, width, state_width), jnp.float32),
    )
    _, incoming = entering((power, state), "tm", combine, identity)
    inner = (stacked + cumulative * incoming[None]).astype(jnp.bfloat16)
    rounded = extended(inner, (("rows", 1),), 1)
    results = []
    for frame_index in range(count):
        value = conv_bands(rounded[frame_index], conv_out, band) + skip * frames[
            frame_index
        ].astype(jnp.float32)
        results.append(value.astype(jnp.bfloat16))
    return jnp.stack(results)


def solution(mesh):
    return jax.shard_map(
        shards,
        mesh=mesh,
        in_specs=(P("tm", "rows", None, None), P(), P("tm", None), P(), P()),
        out_specs=P("tm", "rows", None, None),
        check_vma=False,
    )
```

profile of v0, /device:TPU:0, one launch (start us, length us, event | category | flops | bytes accessed | tf_op | source)
XLA Modules:
  0.0 150.4 jit_solution(4802805536995535079)
XLA Ops:
  6.5 1.0 fusion.175
  7.6 2.5 %collective-permute-start = (bf16[4,1,128,128]{3,2,1,0:T(8,128)(2,1)S(1)}, bf16[4,1,128,128]{3,2,1,0:T(8,128)(2,1)S(1)}, u32[]{:S(2)}, u32[]{:S(2)}) collective-permute-start(bf16[4,1,128,128]{3,2,1,0:T(8,128)(2,1)S(1)} %get-tuple-element.182), channel_id=1, source_target_pairs={{0,1},{2,3},{4,5},{6,7},{8,9},{10,11},{12,13},{14,15},{16,17},{18,... | collective-permute-start | bytes 393224 | tf_op jit(solution)/shard_map/ppermute | solution.py:14
  10.1 1.3 collective-permute-start.1
  11.4 1.3 fusion.174
  12.7 0.7 constant_dynamic-update-slice_fusion.6
  13.8 0.9 pad_slice_fusion.37
  15.7 0.9 pad_slice_fusion.25
  18.1 0.2 convolution_add_fusion.52
  18.8 0.2 convolution_add_fusion.48
  19.2 0.2 convolution_add_fusion.46
  19.4 0.2 convolution_add_fusion.45
  19.9 0.2 convolution_add_fusion.43
  20.1 0.2 convolution_add_fusion.41
  20.5 0.2 convolution_add_fusion.39
  21.2 0.2 convolution_add_fusion.36
  21.6 0.2 convolution_add_fusion.33
  21.8 0.2 convolution_add_fusion.32
  22.3 0.2 convolution_add_fusion.30
  23.1 0.2 fusion.4
  23.6 1.2 fusion.170
  24.8 41.6 %all-gather = bf16[16,1,128]{2,1,0:T(2,128)(2,1)S(1)} all-gather(bf16[1,1,128]{2,1,0:T(2,128)(2,1)S(1)} %get-tuple-element.237), channel_id=1, replica_groups=mesh['tm'=16,'rows'=2] {'tm'}, dimensions={0}, use_global_device_ids=true | all-gather | bytes 4352 | tf_op jit(solution)/shard_map/all_gather | solution.py:23
  66.4 37.5 %all-gather.3.cloned.1.call-done = bf16[16,8,128,128]{3,2,1,0:T(8,128)(2,1)} async-done(((bf16[1,8,128,128]{3,2,1,0:T(8,128)(2,1)}), bf16[16,8,128,128]{3,2,1,0:T(8,128)(2,1)}) %all-gather.3.cloned.1.call-update) | async-done | bytes 4194320 | tf_op jit(solution)/shard_map/all_gather | solution.py:23
  103.9 20.8 %while.14 = (s32[]{:T(128)}, f32[8,128,128]{2,1,0:T(8,128)S(1)}, s32[]{:T(128)}, bf16[16,128]{1,0:T(8,128)(2,1)S(1)}, bf16[16,8,128,128]{3,2,1,0:T(8,128)(2,1)}, /*index=5*/s32[]{:T(128)}, s32[]{:T(128)}) while((s32[]{:T(128)}, f32[8,128,128]{2,1,0:T(8,128)S(1)}, s32[]{:T(128)}, bf16[16,128]{1,0:T(8,128)(2,1)S(1)}, ...), condition=%wide.region_1.2_spmd.clone, body=%wide.region_0.1_spmd.clone.sunk | while | flops 655492 | bytes 1312105 | solution.py:36
  103.9 1.3 fusion.250
  105.2 1.3 fusion.250
  106.5 1.3 fusion.250
  107.8 1.3 fusion.250
  109.1 1.3 fusion.250
  110.4 1.3 fusion.250
  111.7 1.3 fusion.250
  113.0 1.3 fusion.250
  114.3 1.3 fusion.250
  115.6 1.3 fusion.250
  116.9 1.3 fusion.250
  118.2 1.3 fusion.250
  119.5 1.3 fusion.250
  120.8 1.3 fusion.250
  122.1 1.3 fusion.250
  123.4 1.3 fusion.250
  124.7 1.4 fusion.1
  126.1 1.3 collective-permute-start.2
  127.4 1.5 collective-permute-start.3
  128.9 1.8 %collective-permute-done.3 = bf16[4,1,128,128]{3,2,1,0:T(8,128)(2,1)S(1)} collective-permute-done((bf16[4,1,128,128]{3,2,1,0:T(8,128)(2,1)S(1)}, bf16[4,1,128,128]{3,2,1,0:T(8,128)(2,1)S(1)}, u32[]{:S(2)}, u32[]{:S(2)}) %collective-permute-start.3) | collective-permute-done | bytes 131104 | tf_op jit(solution)/shard_map/ppermute | solution.py:15
  131.0 0.4 pad_slice_fusion.1
  131.3 0.6 copy-done.3
  132.3 0.4 pad_slice_fusion.7
  133.1 0.4 pad_slice_fusion.13
  133.9 0.3 pad_slice_fusion.19
  134.7 0.3 pad_maximum_fusion.8
  135.2 0.2 convolution_add_fusion.5
  135.4 0.2 convolution_add_fusion.4
  135.8 0.2 convolution_add_fusion.2
  136.5 0.2 convolution_add_fusion.12
  136.9 0.2 convolution_add_fusion.10
  137.1 0.2 convolution_add_fusion.9
  137.6 0.2 convolution_add_fusion.20
  138.2 0.2 convolution_add_fusion.17
  139.5 0.5 slice-done
  140.7 0.2 fusion.9
  140.9 0.2 fusion.8
  141.2 0.2 fusion.7
  141.6 0.4 copy-done.5
  142.0 0.4 add_convert_fusion.3
  142.4 1.1 pad_maximum_fusion.1
  (93 shorter events, 11.3 us)
Async XLA Ops:
  6.5 6.1 %copy-start.4 = (f32[4,128]{1,0:T(4,128)S(1)}, f32[4,128]{1,0:T(4,128)}, u32[]{:S(2)}) copy-start(f32[4,128]{1,0:T(4,128)} %param.9) | copy-start | bytes 6148
  6.5 97.4 %all-gather.3.cloned.1.call-start = ((), (), s32[]{:S(2)}) async-start(), calls=%async_computation | async-start | bytes 4456448 | tf_op jit(solution)/shard_map/all_gather | solution.py:23
  7.5 5.2 %copy-start.1 = (bf16[4,8,128,128]{3,2,1,0:T(8,128)(2,1)S(1)}, bf16[4,8,128,128]{3,2,1,0:T(8,128)(2,1)}, u32[]{:S(2)}) copy-start(bf16[4,8,128,128]{3,2,1,0:T(8,128)(2,1)} %param.7) | copy-start | bytes 3145732
  7.6 5.1 %collective-permute-start = (bf16[4,1,128,128]{3,2,1,0:T(8,128)(2,1)S(1)}, bf16[4,1,128,128]{3,2,1,0:T(8,128)(2,1)S(1)}, u32[]{:S(2)}, u32[]{:S(2)}) collective-permute-start(bf16[4,1,128,128]{3,2,1,0:T(8,128)(2,1)S(1)} %get-tuple-element.182), channel_id=1, source_target_pairs={{0,1},{2,3},{4,5},{6,7},{8,9},{10,11},{12,13},{14,15},{16,17},{18,... | collective-permute-start | bytes 393224 | tf_op jit(solution)/shard_map/ppermute | solution.py:14
  10.1 3.4 %collective-permute-start.1 = (bf16[4,1,128,128]{3,2,1,0:T(8,128)(2,1)S(1)}, bf16[4,1,128,128]{3,2,1,0:T(8,128)(2,1)S(1)}, u32[]{:S(2)}, u32[]{:S(2)}) collective-permute-start(bf16[4,1,128,128]{3,2,1,0:T(8,128)(2,1)S(1)} %get-tuple-element.181), channel_id=1, source_target_pairs={{1,0},{3,2},{5,4},{7,6},{9,8},{11,10},{13,12},{15,14},{17,16},{19,... | collective-permute-start | bytes 393224 | tf_op jit(solution)/shard_map/ppermute | solution.py:15
  13.8 1.0 copy-start.2
  126.1 8.6 %copy-start = (bf16[4,8,128,128]{3,2,1,0:T(8,128)(2,1)}, bf16[4,8,128,128]{3,2,1,0:T(8,128)(2,1)S(1)}, u32[]{:S(2)}) copy-start(bf16[4,8,128,128]{3,2,1,0:T(8,128)(2,1)S(1)} %fusion.1) | copy-start | bytes 3145732
  126.1 2.8 %collective-permute-start.2 = (bf16[4,1,128,128]{3,2,1,0:T(8,128)(2,1)S(1)}, bf16[4,1,128,128]{3,2,1,0:T(8,128)(2,1)S(1)}, u32[]{:S(2)}, u32[]{:S(2)}) collective-permute-start(bf16[4,1,128,128]{3,2,1,0:T(8,128)(2,1)S(1)} %get-tuple-element.172), channel_id=1, source_target_pairs={{0,1},{2,3},{4,5},{6,7},{8,9},{10,11},{12,13},{14,15},{16,17},{18,... | collective-permute-start | bytes 393224 | tf_op jit(solution)/shard_map/ppermute | solution.py:14
  127.4 3.2 %collective-permute-start.3 = (bf16[4,1,128,128]{3,2,1,0:T(8,128)(2,1)S(1)}, bf16[4,1,128,128]{3,2,1,0:T(8,128)(2,1)S(1)}, u32[]{:S(2)}, u32[]{:S(2)}) collective-permute-start(bf16[4,1,128,128]{3,2,1,0:T(8,128)(2,1)S(1)} %get-tuple-element.173), channel_id=1, source_target_pairs={{1,0},{3,2},{5,4},{7,6},{9,8},{11,10},{13,12},{15,14},{17,16},{19,... | collective-permute-start | bytes 393224 | tf_op jit(solution)/shard_map/ppermute | solution.py:15
  131.0 1.0 copy-start.3
  139.1 1.0 slice-start
  141.4 0.7 copy-start.5
Sparse Core Ops, SparseCore 0:
  24.9 78.9 all-gather.2
where the time goes:
time: 151 us; the launch traced here: 150 us
  blocking collectives  41.6 us (28%)
  waiting for transfers between devices  39.3 us (26%)
  other arithmetic  24.7 us (16%)
  matrix products  15.2 us (10%)
  between operations  14.1 us (9%)
  local copies, waits for them, and re-layouts  8.37 us (6%)
  starting transfers between devices  6.56 us (4%)
    all_gather x1, blocking collectives, entering(): lax.all_gather(part.astype(kind), axis)  41.6 us
    all_gather x1, waiting for transfers between devices, entering(): lax.all_gather(part.astype(kind), axis)  37.5 us
    select_n x16, other arithmetic, step(): return jax.tree.map(lambda a, b: jnp.where(reached, a, b), new, before)  20.1 us
    dot_general x72, matrix products, conv_bands(): jnp.dot(window, weight[down, across], preferred_element_type=jnp.float32)  15.2 us
    slice x11, local copies, waits for them, and re-layouts, conv_bands(): columns[down:down + rows, across:across + width, :]  5.2 us
    ppermute x2, starting transfers between devices, extended(): before = lax.ppermute(last, axis, up)  3.79 us
  transfers between devices with their start and end apart: 5, of which 2 were waited for; matrix products, arithmetic and copies ran while one was open for 1% of the time, Pallas kernels for 0%

commit v1 on v0

v1 whole, which is shorter than its diff:
```python
import jax
import jax.numpy as jnp
from jax import lax
from jax.sharding import PartitionSpec as P


def extended(x, sides, width):
    for axis, dim in sides:
        size, length = (lax.axis_size(axis), x.shape[dim])
        up = [(i, (i + 1) % size) for i in range(size - 1)]
        down = [(j, i) for i, j in up]
        last = lax.slice_in_dim(x, length - width, length, axis=dim)
        first = lax.slice_in_dim(x, 0, width, axis=dim)
        before = lax.ppermute(last, axis, up)
        after = lax.ppermute(first, axis, down)
        x = jnp.concatenate([before, x, after], axis=dim)
    return x


def conv_rows(padded, weight):
    return lax.conv_general_dilated(
        padded,
        weight,
        window_strides=(1, 1),
        padding=((0, 0), (1, 1)),
        dimension_numbers=("NHWC", "HWIO", "NHWC"),
        preferred_element_type=jnp.float32,
    )


def split3(p):
    hi = lax.reduce_precision(p, exponent_bits=8, mantissa_bits=7)
    rest = p - hi
    mid = lax.reduce_precision(rest, exponent_bits=8, mantissa_bits=7)
    low = rest - mid
    return jnp.stack([hi, mid, low]).astype(jnp.bfloat16)


def incoming_state(power, state, axis):
    n = lax.axis_size(axis)
    rows, width, channels = state.shape
    win_p, win_s = power, state
    acc_p, acc_s = None, None
    shift = 1
    while shift < n:
        pairs = [(i, i + shift) for i in range(n - shift)]
        payload = jnp.concatenate(
            [win_s.astype(jnp.bfloat16).reshape(rows * width, channels), split3(win_p)], axis=0
        )
        got = lax.ppermute(payload, axis, pairs)
        got_s = got[: rows * width].astype(jnp.float32).reshape(rows, width, channels)
        got_p = jnp.sum(got[rows * width :].astype(jnp.float32), axis=0)
        if acc_s is None:
            acc_p, acc_s = got_p, got_s
        else:
            acc_s = acc_p * got_s + acc_s
            acc_p = got_p * acc_p
        if 2 * shift < n:
            win_s = win_p * got_s + win_s
            win_p = got_p * win_p
        shift *= 2
    if acc_s is None:
        return jnp.zeros_like(state)
    return acc_s


def shards(frames, conv_in, decay, conv_out, skip):
    count = frames.shape[0]
    with jax.named_scope("input_conv"):
        padded_in = extended(frames, (("rows", 1),), 1)
        drive = conv_rows(padded_in, conv_in)
    with jax.named_scope("local_recurrence"):
        state = jnp.zeros(drive.shape[1:], jnp.float32)
        power = jnp.ones(decay.shape[1:], jnp.float32)
        local_states = []
        products = []
        for frame_index in range(count):
            state = decay[frame_index] * state + drive[frame_index]
            power = power * decay[frame_index]
            local_states.append(state)
            products.append(power)
        stacked = jnp.stack(local_states)
        cumulative = jnp.stack(products)[:, None, None, :]
    with jax.named_scope("carry_across_blocks"):
        incoming = incoming_state(power, state, "tm")
    with jax.named_scope("output_conv"):
        inner = (stacked + cumulative * incoming[None]).astype(jnp.bfloat16)
        rounded = extended(inner, (("rows", 1),), 1)
        value = conv_rows(rounded, conv_out) + skip * frames.astype(jnp.float32)
    return value.astype(jnp.bfloat16)


def solution(mesh):
    return jax.shard_map(
        shards,
        mesh=mesh,
        in_specs=(P("tm", "rows", None, None), P(), P("tm", None), P(), P()),
        out_specs=P("tm", "rows", None, None),
        check_vma=False,
    )
```

time: 151 us -> 89 us (0.59)
  the two profiles are of different devices: /device:TPU:0 before, /device:TPU:25 now
where the time goes in v1:
time: 89 us; the launch traced here: 88.5 us
  waiting for transfers between devices  38.2 us (43%)
  starting transfers between devices  16.8 us (19%)
  local copies, waits for them, and re-layouts  15.5 us (17%)
  other arithmetic  11.9 us (13%)
  matrix products  5.7 us (6%)
    ppermute x4, waiting for transfers between devices, incoming_state(): got = lax.ppermute(payload, axis, pairs)  37.2 us
    ppermute x4, starting transfers between devices, incoming_state(): got = lax.ppermute(payload, axis, pairs)  7.9 us
    ppermute x2, starting transfers between devices, extended(): after = lax.ppermute(first, axis, down)  6.28 us
    concatenate x4, local copies, waits for them, and re-layouts, incoming_state(): jnp.concatenate([win_s.astype(jnp.bfloat16).reshape(rows * width, channel...  6.05 us
    conv_general_dilated x2, matrix products, conv_rows(): lax.conv_general_dilated(padded, weight, window_strides=(1, 1), padding=(...  5.7 us
    conv_general_dilated x5, local copies, waits for them, and re-layouts, conv_rows(): lax.conv_general_dilated(padded, weight, window_strides=(1, 1), padding=(...  2.83 us
    concatenate x2, other arithmetic, extended(): x = jnp.concatenate([before, x, after], axis=dim)  2.71 us
    convert_element_type x3, other arithmetic, incoming_state(): got[:rows * width].astype(jnp.float32).reshape(rows, width, channels)  2.66 us
  transfers between devices with their start and end apart: 8, of which 5 were waited for; matrix products, arithmetic and copies ran while one was open for 5% of the time, Pallas kernels for 0%

profile of v1, /device:TPU:25, one launch (start us, length us, event | category | flops | bytes accessed | tf_op | source)
XLA Modules:
  0.0 88.5 jit_solution(2810097941399805331)
XLA Ops:
  0.0 0.0 copy-start
  0.0 1.0 %fusion.35 = (bf16[4,1,128,128]{3,2,1,0:T(8,128)(2,1)S(1)}, bf16[4,1,128,128]{3,2,1,0:T(8,128)(2,1)S(1)}) fusion(bf16[4,8,128,128]{3,2,1,0:T(8,128)(2,1)} %param.5), kind=kLoop, calls=%fused_computation.83 | loop fusion | bytes 524288 | tf_op jit(solution)/shard_map/input_conv/slice | solution.py:12
  1.0 1.3 %collective-permute-start = (bf16[4,1,128,128]{3,2,1,0:T(8,128)(2,1)S(1)}, bf16[4,1,128,128]{3,2,1,0:T(8,128)(2,1)S(1)}, u32[]{:S(2)}, u32[]{:S(2)}) collective-permute-start(bf16[4,1,128,128]{3,2,1,0:T(8,128)(2,1)S(1)} %get-tuple-element.29), channel_id=1, source_target_pairs={{0,1},{2,3},{4,5},{6,7},{8,9},{10,11},{12,13},{14,15},{16,17},{18,... | collective-permute-start | bytes 393224 | tf_op jit(solution)/shard_map/input_conv/ppermute | solution.py:14
  2.3 3.0 %collective-permute-start.1 = (bf16[4,1,128,128]{3,2,1,0:T(8,128)(2,1)S(1)}, bf16[4,1,128,128]{3,2,1,0:T(8,128)(2,1)S(1)}, u32[]{:S(2)}, u32[]{:S(2)}) collective-permute-start(bf16[4,1,128,128]{3,2,1,0:T(8,128)(2,1)S(1)} %get-tuple-element.30), channel_id=1, source_target_pairs={{1,0},{3,2},{5,4},{7,6},{9,8},{11,10},{13,12},{15,14},{17,16},{19,... | collective-permute-start | bytes 393224 | tf_op jit(solution)/shard_map/input_conv/ppermute | solution.py:15
  5.4 0.8 fusion.25
  6.2 0.8 fusion.30
  7.1 0.0 collective-permute-done
  7.1 0.0 collective-permute-done.1
  7.1 1.4 %maximum_bitcast_fusion.1 = bf16[10,4,128,128]{3,2,0,1:T(8,128)(2,1)S(1)} fusion(bf16[4,1,128,128]{3,2,1,0:T(8,128)(2,1)S(1)} %collective-permute-done.1, bf16[4,8,128,128]{3,2,1,0:T(8,128)(2,1)} %param.5, bf16[4,1,128,128]{3,2,1,0:T(8,128)(2,1)S(1)} %collective-permute-done), kind=kLoop, calls=%fused_computation.20 | loop fusion | flops 1310720 | bytes 2621440 | tf_op jit(solution)/shard_map/input_conv/concatenate | solution.py:16
  8.5 1.0 %copy.29 = bf16[10,4,128,128]{3,1,2,0:T(4,128)(2,1)S(1)} copy(bf16[10,4,128,128]{3,2,0,1:T(8,128)(2,1)S(1)} %maximum_bitcast_fusion.1) | data formatting | bytes 2621440
  9.5 0.5 pad.clone
  10.0 0.0 copy-start.7
  10.1 0.1 slice.84
  10.1 0.7 fusion.5
  10.8 0.0 copy-done
  10.8 0.0 copy-done.7
  10.8 2.8 %fusion.13 = f32[8,32,17,128]{3,1,2,0:T(8,128)S(1)} fusion(bf16[3,3,128,128]{3,2,1,0:T(8,128)(2,1)S(1)} %copy-done, bf16[10,4,8,19,128]{4,1,3,2,0:T(4,128)(2,1)S(1)} %fusion.5, pred[32,17]{0,1:T(8,128)(4,1)S(1)} %copy-done.7), kind=kOutput, calls=%fused_computation.18 | convolution fusion | flops 1284014080 | bytes 4080160 | tf_op jit(solution)/shard_map/input_conv/conv_general_dilated | solution.py:21
  13.7 1.3 %copy.18 = f32[8,32,17,128]{3,0,2,1:T(8,128)S(1)} copy(f32[8,32,17,128]{3,1,2,0:T(8,128)S(1)} %fusion.13) | data formatting | bytes 4456448 | tf_op jit(solution)/shard_map/input_conv/conv_general_dilated | solution.py:21
  15.0 0.1 slice_bitcast_fusion.1
  15.1 0.3 multiply_add_fusion.2
  15.4 0.1 copy.19
  15.6 0.1 copy.20
  15.7 0.1 copy.21
  15.8 0.1 copy.22
  15.9 0.2 fusion.33
  16.1 0.1 concatenate.23
  16.2 3.1 %collective-permute-start.2 = (bf16[1027,128]{1,0:T(8,128)(2,1)S(1)}, bf16[1027,128]{1,0:T(8,128)(2,1)S(1)}, u32[]{:S(2)}, u32[]{:S(2)}) collective-permute-start(bf16[1027,128]{1,0:T(8,128)(2,1)S(1)} %concatenate.23), channel_id=1, source_target_pairs={{0,2},{2,4},{4,6},{6,8},{8,10},{10,12},{12,14},{14,16},{16,18},{18... | collective-permute-start | bytes 788744 | tf_op jit(solution)/shard_map/carry_across_blocks/ppermute | solution.py:50
  19.3 8.9 %collective-permute-done.2 = bf16[1027,128]{1,0:T(8,128)(2,1)S(1)} collective-permute-done((bf16[1027,128]{1,0:T(8,128)(2,1)S(1)}, bf16[1027,128]{1,0:T(8,128)(2,1)S(1)}, u32[]{:S(2)}, u32[]{:S(2)}) %collective-permute-start.2) | collective-permute-done | bytes 262944 | tf_op jit(solution)/shard_map/carry_across_blocks/ppermute | solution.py:50
  28.2 0.1 fusion.23
  28.3 1.4 %concatenate.24 = bf16[1027,128]{1,0:T(8,128)(2,1)} concatenate(bf16[1024,128]{1,0:T(8,128)(2,1)S(1)} %fusion.23, bf16[1,128]{1,0:T(2,128)(2,1)S(1)} %get-tuple-element.43, bf16[1,128]{1,0:T(2,128)(2,1)S(1)} %get-tuple-element.42, bf16[1,128]{1,0:T(2,128)(2,1)S(1)} %get-tuple-element.11), dimensions={0} | concatenate | bytes 525824 | tf_op jit(solution)/shard_map/carry_across_blocks/concatenate | solution.py:47
  29.6 2.2 %collective-permute-start.3 = (bf16[1027,128]{1,0:T(8,128)(2,1)}, bf16[1027,128]{1,0:T(8,128)(2,1)S(1)}, u32[]{:S(2)}, u32[]{:S(2)}) collective-permute-start(bf16[1027,128]{1,0:T(8,128)(2,1)} %concatenate.24), channel_id=1, source_target_pairs={{0,4},{2,6},{4,8},{6,10},{8,12},{10,14},{12,16},{14,18},{16,20},{1... | collective-permute-start | bytes 788744 | tf_op jit(solution)/shard_map/carry_across_blocks/ppermute | solution.py:50
  31.9 8.2 %collective-permute-done.3 = bf16[1027,128]{1,0:T(8,128)(2,1)S(1)} collective-permute-done((bf16[1027,128]{1,0:T(8,128)(2,1)}, bf16[1027,128]{1,0:T(8,128)(2,1)S(1)}, u32[]{:S(2)}, u32[]{:S(2)}) %collective-permute-start.3) | collective-permute-done | bytes 262944 | tf_op jit(solution)/shard_map/carry_across_blocks/ppermute | solution.py:50
  40.1 0.8 fusion.24
  41.0 2.2 %concatenate.25 = bf16[1027,128]{1,0:T(8,128)(2,1)} concatenate(bf16[1024,128]{1,0:T(8,128)(2,1)} %fusion.24, bf16[1,128]{1,0:T(2,128)(2,1)S(1)} %get-tuple-element.41, bf16[1,128]{1,0:T(2,128)(2,1)S(1)} %get-tuple-element.40, bf16[1,128]{1,0:T(2,128)(2,1)S(1)} %get-tuple-element.7), dimensions={0} | concatenate | bytes 525824 | tf_op jit(solution)/shard_map/carry_across_blocks/concatenate | solution.py:47
  43.2 1.3 %collective-permute-start.4 = (bf16[1027,128]{1,0:T(8,128)(2,1)}, bf16[1027,128]{1,0:T(8,128)(2,1)S(1)}, u32[]{:S(2)}, u32[]{:S(2)}) collective-permute-start(bf16[1027,128]{1,0:T(8,128)(2,1)} %concatenate.25), channel_id=1, source_target_pairs={{0,8},{2,10},{4,12},{6,14},{8,16},{10,18},{12,20},{14,22},{16,24},... | collective-permute-start | bytes 788744 | tf_op jit(solution)/shard_map/carry_across_blocks/ppermute | solution.py:50
  44.5 0.8 slice_convert_fusion.2
  45.3 0.8 slice_convert_fusion.1
  46.2 5.7 %collective-permute-done.4 = bf16[1027,128]{1,0:T(8,128)(2,1)S(1)} collective-permute-done((bf16[1027,128]{1,0:T(8,128)(2,1)}, bf16[1027,128]{1,0:T(8,128)(2,1)S(1)}, u32[]{:S(2)}, u32[]{:S(2)}) %collective-permute-start.4) | collective-permute-done | bytes 262944 | tf_op jit(solution)/shard_map/carry_across_blocks/ppermute | solution.py:50
  51.9 0.9 add_convert_fusion
  52.7 2.3 %concatenate.26 = bf16[1027,128]{1,0:T(8,128)(2,1)} concatenate(bf16[1024,128]{1,0:T(8,128)(2,1)} %add_convert_fusion, bf16[1,128]{1,0:T(2,128)(2,1)S(1)} %get-tuple-element.39, bf16[1,128]{1,0:T(2,128)(2,1)S(1)} %get-tuple-element.38, bf16[1,128]{1,0:T(2,128)(2,1)S(1)} %get-tuple-element.37), dimensions={0} | concatenate | bytes 525824 | tf_op jit(solution)/shard_map/carry_across_blocks/concatenate | solution.py:47
  55.1 1.3 %collective-permute-start.5 = (bf16[1027,128]{1,0:T(8,128)(2,1)}, bf16[1027,128]{1,0:T(8,128)(2,1)S(1)}, u32[]{:S(2)}, u32[]{:S(2)}) collective-permute-start(bf16[1027,128]{1,0:T(8,128)(2,1)} %concatenate.26), channel_id=1, source_target_pairs={{0,16},{2,18},{4,20},{6,22},{8,24},{10,26},{12,28},{14,30},{1,17},... | collective-permute-start | bytes 788744 | tf_op jit(solution)/shard_map/carry_across_blocks/ppermute | solution.py:50
  56.4 1.0 %slice_convert_fusion = f32[1024,128]{1,0:T(8,128)S(1)} fusion(bf16[1027,128]{1,0:T(8,128)(2,1)} %copy-done.4), kind=kLoop, calls=%fused_computation.36 | loop fusion | flops 131072 | bytes 786432 | tf_op jit(solution)/shard_map/carry_across_blocks/convert_element_type | solution.py:51
  57.4 14.5 %collective-permute-done.5 = bf16[1027,128]{1,0:T(8,128)(2,1)S(1)} collective-permute-done((bf16[1027,128]{1,0:T(8,128)(2,1)}, bf16[1027,128]{1,0:T(8,128)(2,1)S(1)}, u32[]{:S(2)}, u32[]{:S(2)}) %collective-permute-start.5) | collective-permute-done | bytes 262944 | tf_op jit(solution)/shard_map/carry_across_blocks/ppermute | solution.py:50
  71.9 0.1 fusion.19
  72.1 0.3 copy.23
  72.4 0.2 fusion.4
  72.6 0.3 fusion.34
  73.0 1.3 %collective-permute-start.6 = (bf16[4,1,128,128]{3,1,2,0:T(2,128)(2,1)S(1)}, bf16[4,1,128,128]{3,1,2,0:T(2,128)(2,1)S(1)}, u32[]{:S(2)}, u32[]{:S(2)}) collective-permute-start(bf16[4,1,128,128]{3,1,2,0:T(2,128)(2,1)S(1)} %get-tuple-element.27), channel_id=1, source_target_pairs={{0,1},{2,3},{4,5},{6,7},{8,9},{10,11},{12,13},{14,15},{16,17},{18,... | collective-permute-start | bytes 393224 | tf_op jit(solution)/shard_map/output_conv/ppermute | solution.py:14
  74.3 3.2 %collective-permute-start.7 = (bf16[4,1,128,128]{3,1,2,0:T(2,128)(2,1)S(1)}, bf16[4,1,128,128]{3,1,2,0:T(2,128)(2,1)S(1)}, u32[]{:S(2)}, u32[]{:S(2)}) collective-permute-start(bf16[4,1,128,128]{3,1,2,0:T(2,128)(2,1)S(1)} %get-tuple-element.28), channel_id=1, source_target_pairs={{1,0},{3,2},{5,4},{7,6},{9,8},{11,10},{13,12},{15,14},{17,16},{19,... | collective-permute-start | bytes 393224 | tf_op jit(solution)/shard_map/output_conv/ppermute | solution.py:15
  77.5 0.0 collective-permute-done.6
  77.5 0.9 %collective-permute-done.7 = bf16[4,1,128,128]{3,1,2,0:T(2,128)(2,1)S(1)} collective-permute-done((bf16[4,1,128,128]{3,1,2,0:T(2,128)(2,1)S(1)}, bf16[4,1,128,128]{3,1,2,0:T(2,128)(2,1)S(1)}, u32[]{:S(2)}, u32[]{:S(2)}) %collective-permute-start.7) | collective-permute-done | bytes 131104 | tf_op jit(solution)/shard_map/output_conv/ppermute | solution.py:15
  78.5 1.3 %maximum_bitcast_fusion = bf16[10,4,128,128]{3,0,2,1:T(8,128)(2,1)S(1)} fusion(bf16[4,1,128,128]{3,1,2,0:T(2,128)(2,1)S(1)} %collective-permute-done.7, bf16[4,8,128,128]{3,1,2,0:T(8,128)(2,1)S(1)} %fusion.4, bf16[4,1,128,128]{3,1,2,0:T(2,128)(2,1)S(1)} %collective-permute-done.6), kind=kLoop, calls=%fused_computation.9 | loop fusion | flops 3932160 | bytes 2621440 | tf_op jit(solution)/shard_map/output_conv/concatenate | solution.py:16
  79.8 1.0 %copy.30 = bf16[10,4,128,128]{3,1,2,0:T(4,128)(2,1)S(1)} copy(bf16[10,4,128,128]{3,0,2,1:T(8,128)(2,1)S(1)} %maximum_bitcast_fusion) | data formatting | bytes 2621440
  80.8 0.5 pad.2.clone
  81.3 0.0 copy-start.6
  81.3 0.1 slice.99
  81.4 0.7 fusion.6
  82.1 0.2 copy-done.6
  82.3 2.9 %fusion.16 = f32[8,32,17,128]{3,1,2,0:T(8,128)S(1)} fusion(bf16[3,3,128,128]{3,2,1,0:T(8,128)(2,1)S(1)} %copy-done.6, bf16[10,4,8,19,128]{4,1,3,2,0:T(4,128)(2,1)S(1)} %fusion.6, pred[32,17]{0,1:T(8,128)(4,1)S(1)} %copy-done.7), kind=kOutput, calls=%fused_computation.19 | convolution fusion | flops 1284014080 | bytes 4080160 | tf_op jit(solution)/shard_map/output_conv/conv_general_dilated | solution.py:21
  85.2 0.0 copy-start.1
  85.2 0.0 copy-start.5
  85.2 1.3 %copy.26 = f32[8,32,17,128]{3,0,2,1:T(8,128)S(1)} copy(f32[8,32,17,128]{3,1,2,0:T(8,128)S(1)} %fusion.16) | data formatting | bytes 4456448 | tf_op jit(solution)/shard_map/output_conv/conv_general_dilated | solution.py:21
  86.5 0.8 fusion.3
  87.3 1.2 %copy.28 = bf16[4,8,128,128]{3,2,1,0:T(8,128)(2,1)} copy(bf16[4,8,128,128]{3,1,2,0:T(8,128)(2,1)S(1)} %fusion.3) | data formatting | bytes 2097152 | tf_op jit(solution)/shard_map/convert_element_type | solution.py:90
  (21 shorter events, 0.2 us)
Async XLA Ops:
  0.0 10.8 %copy-start = (bf16[3,3,128,128]{3,2,1,0:T(8,128)(2,1)S(1)}, bf16[3,3,128,128]{3,2,1,0:T(8,128)(2,1)}, u32[]{:S(2)}) copy-start(bf16[3,3,128,128]{3,2,1,0:T(8,128)(2,1)} %param.6) | copy-start | bytes 884740
  1.0 6.0 %collective-permute-start = (bf16[4,1,128,128]{3,2,1,0:T(8,128)(2,1)S(1)}, bf16[4,1,128,128]{3,2,1,0:T(8,128)(2,1)S(1)}, u32[]{:S(2)}, u32[]{:S(2)}) collective-permute-start(bf16[4,1,128,128]{3,2,1,0:T(8,128)(2,1)S(1)} %get-tuple-element.29), channel_id=1, source_target_pairs={{0,1},{2,3},{4,5},{6,7},{8,9},{10,11},{12,13},{14,15},{16,17},{18,... | collective-permute-start | bytes 393224 | tf_op jit(solution)/shard_map/input_conv/ppermute | solution.py:14
  2.3 4.7 %collective-permute-start.1 = (bf16[4,1,128,128]{3,2,1,0:T(8,128)(2,1)S(1)}, bf16[4,1,128,128]{3,2,1,0:T(8,128)(2,1)S(1)}, u32[]{:S(2)}, u32[]{:S(2)}) collective-permute-start(bf16[4,1,128,128]{3,2,1,0:T(8,128)(2,1)S(1)} %get-tuple-element.30), channel_id=1, source_target_pairs={{1,0},{3,2},{5,4},{7,6},{9,8},{11,10},{13,12},{15,14},{17,16},{19,... | collective-permute-start | bytes 393224 | tf_op jit(solution)/shard_map/input_conv/ppermute | solution.py:15
  10.0 0.8 copy-start.7
  16.2 12.0 %collective-permute-start.2 = (bf16[1027,128]{1,0:T(8,128)(2,1)S(1)}, bf16[1027,128]{1,0:T(8,128)(2,1)S(1)}, u32[]{:S(2)}, u32[]{:S(2)}) collective-permute-start(bf16[1027,128]{1,0:T(8,128)(2,1)S(1)} %concatenate.23), channel_id=1, source_target_pairs={{0,2},{2,4},{4,6},{6,8},{8,10},{10,12},{12,14},{14,16},{16,18},{18... | collective-permute-start | bytes 788744 | tf_op jit(solution)/shard_map/carry_across_blocks/ppermute | solution.py:50
  29.6 10.4 %collective-permute-start.3 = (bf16[1027,128]{1,0:T(8,128)(2,1)}, bf16[1027,128]{1,0:T(8,128)(2,1)S(1)}, u32[]{:S(2)}, u32[]{:S(2)}) collective-permute-start(bf16[1027,128]{1,0:T(8,128)(2,1)} %concatenate.24), channel_id=1, source_target_pairs={{0,4},{2,6},{4,8},{6,10},{8,12},{10,14},{12,16},{14,18},{16,20},{1... | collective-permute-start | bytes 788744 | tf_op jit(solution)/shard_map/carry_across_blocks/ppermute | solution.py:50
  43.2 8.6 %collective-permute-start.4 = (bf16[1027,128]{1,0:T(8,128)(2,1)}, bf16[1027,128]{1,0:T(8,128)(2,1)S(1)}, u32[]{:S(2)}, u32[]{:S(2)}) collective-permute-start(bf16[1027,128]{1,0:T(8,128)(2,1)} %concatenate.25), channel_id=1, source_target_pairs={{0,8},{2,10},{4,12},{6,14},{8,16},{10,18},{12,20},{14,22},{16,24},... | collective-permute-start | bytes 788744 | tf_op jit(solution)/shard_map/carry_across_blocks/ppermute | solution.py:50
  51.8 0.9 %copy-start.4 = (bf16[1027,128]{1,0:T(8,128)(2,1)}, bf16[1027,128]{1,0:T(8,128)(2,1)S(1)}, u32[]{:S(2)}) copy-start(bf16[1027,128]{1,0:T(8,128)(2,1)S(1)} %collective-permute-done.4) | copy-start | bytes 788740
  52.7 19.2 %copy-start.2 = (f32[1024,128]{1,0:T(8,128)S(1)}, f32[1024,128]{1,0:T(8,128)}, u32[]{:S(2)}) copy-start(f32[1024,128]{1,0:T(8,128)} %slice_convert_fusion.2) | copy-start | bytes 1572868
  52.7 19.2 %copy-start.3 = (f32[1024,128]{1,0:T(8,128)S(1)}, f32[1024,128]{1,0:T(8,128)}, u32[]{:S(2)}) copy-start(f32[1024,128]{1,0:T(8,128)} %slice_convert_fusion.1) | copy-start | bytes 1572868
  55.1 16.8 %collective-permute-start.5 = (bf16[1027,128]{1,0:T(8,128)(2,1)}, bf16[1027,128]{1,0:T(8,128)(2,1)S(1)}, u32[]{:S(2)}, u32[]{:S(2)}) collective-permute-start(bf16[1027,128]{1,0:T(8,128)(2,1)} %concatenate.26), channel_id=1, source_target_pairs={{0,16},{2,18},{4,20},{6,22},{8,24},{10,26},{12,28},{14,30},{1,17},... | collective-permute-start | bytes 788744 | tf_op jit(solution)/shard_map/carry_across_blocks/ppermute | solution.py:50
  73.0 4.5 %collective-permute-start.6 = (bf16[4,1,128,128]{3,1,2,0:T(2,128)(2,1)S(1)}, bf16[4,1,128,128]{3,1,2,0:T(2,128)(2,1)S(1)}, u32[]{:S(2)}, u32[]{:S(2)}) collective-permute-start(bf16[4,1,128,128]{3,1,2,0:T(2,128)(2,1)S(1)} %get-tuple-element.27), channel_id=1, source_target_pairs={{0,1},{2,3},{4,5},{6,7},{8,9},{10,11},{12,13},{14,15},{16,17},{18,... | collective-permute-start | bytes 393224 | tf_op jit(solution)/shard_map/output_conv/ppermute | solution.py:14
  74.3 4.2 %collective-permute-start.7 = (bf16[4,1,128,128]{3,1,2,0:T(2,128)(2,1)S(1)}, bf16[4,1,128,128]{3,1,2,0:T(2,128)(2,1)S(1)}, u32[]{:S(2)}, u32[]{:S(2)}) collective-permute-start(bf16[4,1,128,128]{3,1,2,0:T(2,128)(2,1)S(1)} %get-tuple-element.28), channel_id=1, source_target_pairs={{1,0},{3,2},{5,4},{7,6},{9,8},{11,10},{13,12},{15,14},{17,16},{19,... | collective-permute-start | bytes 393224 | tf_op jit(solution)/shard_map/output_conv/ppermute | solution.py:15
  81.3 1.0 %copy-start.6 = (bf16[3,3,128,128]{3,2,1,0:T(8,128)(2,1)S(1)}, bf16[3,3,128,128]{3,2,1,0:T(8,128)(2,1)}, u32[]{:S(2)}) copy-start(bf16[3,3,128,128]{3,2,1,0:T(8,128)(2,1)} %param.8) | copy-start | bytes 884740
  85.2 1.3 %copy-start.1 = (bf16[4,8,128,128]{3,2,1,0:T(8,128)(2,1)S(1)}, bf16[4,8,128,128]{3,2,1,0:T(8,128)(2,1)}, u32[]{:S(2)}) copy-start(bf16[4,8,128,128]{3,2,1,0:T(8,128)(2,1)} %param.5) | copy-start | bytes 3145732
  85.2 1.3 %copy-start.5 = (f32[128]{0:T(128)S(1)}, f32[128]{0:T(128)}, u32[]{:S(2)}) copy-start(f32[128]{0:T(128)} %param.9) | copy-start | bytes 1540

commit v2 on v1

v2 whole, which is shorter than its diff:
```python
import jax
import jax.numpy as jnp
from jax import lax
from jax.experimental import pallas as pl
from jax.experimental.pallas import tpu as pltpu
from jax.sharding import PartitionSpec as P


def halo_rows(x, axis, dim):
    size, length = (lax.axis_size(axis), x.shape[dim])
    up = [(i, (i + 1) % size) for i in range(size - 1)]
    down = [(j, i) for i, j in up]
    last = lax.slice_in_dim(x, length - 1, length, axis=dim)
    first = lax.slice_in_dim(x, 0, 1, axis=dim)
    before = lax.ppermute(last, axis, up)
    after = lax.ppermute(first, axis, down)
    return before, after


def grouped_taps(weight):
    down, across, k, m = weight.shape
    return jnp.transpose(weight, (0, 2, 1, 3)).reshape(down, k, across * m)


def conv_taps(x, w_ref):
    rows = x.shape[0] - 2
    width, k = x.shape[1], x.shape[2]
    m = w_ref.shape[2] // 3
    n = rows * width
    acc = None
    for a in range(3):
        lhs = x[a : a + rows].reshape(n, k)
        part = jnp.dot(lhs, w_ref[a], preferred_element_type=jnp.float32)
        acc = part if acc is None else acc + part
    column = lax.broadcasted_iota(jnp.int32, (n, m), 0) % width
    from_left = pltpu.roll(acc[:, :m], 1, 0)
    from_right = pltpu.roll(acc[:, 2 * m :], n - 1, 0)
    total = acc[:, m : 2 * m]
    total = total + jnp.where(column == 0, 0.0, from_left)
    total = total + jnp.where(column == width - 1, 0.0, from_right)
    return total


def input_kernel(decay_ref, top_ref, frame_ref, bottom_ref, w_ref, out_ref, state_ref):
    f = pl.program_id(0)
    band, width, m = out_ref.shape[1:]

    @pl.when(f == 0)
    def _():
        state_ref[...] = jnp.zeros_like(state_ref)

    x = jnp.concatenate([top_ref[0], frame_ref[0], bottom_ref[0]], axis=0)
    drive = conv_taps(x, w_ref)
    state = decay_ref[pl.ds(f, 1), :] * state_ref[...] + drive
    state_ref[...] = state
    out_ref[0] = state.reshape(band, width, m)


def output_kernel(
    cum_ref, skip_ref, incoming_ref, top_ref, local_ref, bottom_ref, frame_ref, w_ref, out_ref
):
    f = pl.program_id(0)
    band, width, m = out_ref.shape[1:]
    inner = (local_ref[0] + cum_ref[pl.ds(f, 1), :] * incoming_ref[...]).astype(jnp.bfloat16)
    x = jnp.concatenate([top_ref[0], inner, bottom_ref[0]], axis=0)
    total = conv_taps(x, w_ref)
    frame = frame_ref[0].reshape(band * width, m).astype(jnp.float32)
    total = total + skip_ref[...] * frame
    out_ref[0] = total.astype(jnp.bfloat16).reshape(band, width, m)


def input_stage(frames, conv_in, decay):
    count, band, width, channels = frames.shape
    state_width = conv_in.shape[3]
    top, bottom = halo_rows(frames, "rows", 1)
    halo = pl.BlockSpec((1, 1, width, channels), lambda f: (f, 0, 0, 0))
    return pl.pallas_call(
        input_kernel,
        grid=(count,),
        in_specs=[
            pl.BlockSpec((count, state_width), lambda f: (0, 0)),
            halo,
            pl.BlockSpec((1, band, width, channels), lambda f: (f, 0, 0, 0)),
            halo,
            pl.BlockSpec((3, channels, 3 * state_width), lambda f: (0, 0, 0)),
        ],
        out_specs=pl.BlockSpec((1, band, width, state_width), lambda f: (f, 0, 0, 0)),
        out_shape=jax.ShapeDtypeStruct((count, band, width, state_width), jnp.float32),
        scratch_shapes=[pltpu.VMEM((band * width, state_width), jnp.float32)],
        compiler_params=pltpu.CompilerParams(dimension_semantics=("arbitrary",)),
    )(decay, top, frames, bottom, grouped_taps(conv_in))


def output_stage(local, cumulative, incoming, frames, conv_out, skip):
    count, band, width, state_width = local.shape
    channels = conv_out.shape[3]
    edges = jnp.concatenate([local[:, :1], local[:, -1:]], axis=1)
    edges = edges + cumulative[:, None, None, :] * jnp.concatenate(
        [incoming[None, :1], incoming[None, -1:]], axis=1
    )
    top, bottom = halo_rows(edges.astype(jnp.bfloat16), "rows", 1)
    halo = pl.BlockSpec((1, 1, width, state_width), lambda f: (f, 0, 0, 0))
    return pl.pallas_call(
        output_kernel,
        grid=(count,),
        in_specs=[
            pl.BlockSpec((count, state_width), lambda f: (0, 0)),
            pl.BlockSpec((1, channels), lambda f: (0, 0)),
            pl.BlockSpec((band, width, state_width), lambda f: (0, 0, 0)),
            halo,
            pl.BlockSpec((1, band, width, state_width), lambda f: (f, 0, 0, 0)),
            halo,
            pl.BlockSpec((1, band, width, channels), lambda f: (f, 0, 0, 0)),
            pl.BlockSpec((3, state_width, 3 * channels), lambda f: (0, 0, 0)),
        ],
        out_specs=pl.BlockSpec((1, band, width, channels), lambda f: (f, 0, 0, 0)),
        out_shape=jax.ShapeDtypeStruct((count, band, width, channels), jnp.bfloat16),
        compiler_params=pltpu.CompilerParams(dimension_semantics=("arbitrary",)),
    )(cumulative, skip.reshape(1, channels), incoming, top, local, bottom, frames, grouped_taps(conv_out))


def incoming_state(products, state, axis):
    n = lax.axis_size(axis)
    me = lax.axis_index(axis)
    block = lax.broadcasted_iota(jnp.int32, (n, 1), 0)

    def span(lo, hi):
        inside = (block >= lo) & (block <= hi)
        return jnp.prod(jnp.where(inside, products, 1.0), axis=0)

    win_s = state
    acc_s = None
    shift = 1
    while shift < n:
        pairs = [(i, i + shift) for i in range(n - shift)]
        got = lax.ppermute(win_s.astype(jnp.bfloat16), axis, pairs).astype(jnp.float32)
        if acc_s is None:
            acc_s = got
        else:
            acc_s = span(me - shift + 1, me - 1) * got + acc_s
        if 2 * shift < n:
            win_s = span(me - shift + 1, me) * got + win_s
        shift *= 2
    if acc_s is None:
        return jnp.zeros_like(state)
    return acc_s


def shards(frames, conv_in, decay, conv_out, skip):
    with jax.named_scope("block_decay_products"):
        cumulative = jnp.cumprod(decay, axis=0)
        products = lax.all_gather(cumulative[-1], "tm")
    with jax.named_scope("input_conv_and_recurrence"):
        local = input_stage(frames, conv_in, decay)
    with jax.named_scope("carry_across_blocks"):
        incoming = incoming_state(products, local[-1], "tm")
    with jax.named_scope("output_conv"):
        return output_stage(local, cumulative, incoming, frames, conv_out, skip)


def solution(mesh):
    return jax.shard_map(
        shards,
        mesh=mesh,
        in_specs=(P("tm", "rows", None, None), P(), P("tm", None), P(), P()),
        out_specs=P("tm", "rows", None, None),
        check_vma=False,
    )
```

time: 89 us -> 98.5 us (1.11)
  the two profiles are of different devices: /device:TPU:25 before, /device:TPU:0 now
where the time goes in v2:
time: 98.5 us; the launch traced here: 97.9 us
  blocking collectives  39.1 us (40%)
  starting transfers between devices  24.6 us (25%)
  waiting for transfers between devices  11.5 us (12%)
  Pallas kernels  11.5 us (12%)
  local copies, waits for them, and re-layouts  7.46 us (8%)
  other arithmetic  3.55 us (4%)
    all_gather x1, blocking collectives, shards(): products = lax.all_gather(cumulative[-1], 'tm')  39.1 us
    ppermute x4, starting transfers between devices, incoming_state(): lax.ppermute(win_s.astype(jnp.bfloat16), axis, pairs).astype(jnp.float32)  15.9 us
    ppermute x4, waiting for transfers between devices, incoming_state(): lax.ppermute(win_s.astype(jnp.bfloat16), axis, pairs).astype(jnp.float32)  11.5 us
    ppermute x2, starting transfers between devices, halo_rows(): before = lax.ppermute(last, axis, up)  6.08 us
    pallas_call x1, Pallas kernels, output_stage(): pl.pallas_call(output_kernel, grid=(count,), in_specs=[pl.BlockSpec((coun...  5.95 us
    pallas_call x1, Pallas kernels, input_stage(): pl.pallas_call(input_kernel, grid=(count,), in_specs=[pl.BlockSpec((count...  5.51 us
    unnamed x19, local copies, waits for them, and re-layouts  3.37 us
    ppermute x2, starting transfers between devices, halo_rows(): after = lax.ppermute(first, axis, down)  2.58 us
  transfers between devices with their start and end apart: 8, of which 3 were waited for; matrix products, arithmetic and copies ran while one was open for 4% of the time, Pallas kernels for 0%

profile of v2, /device:TPU:0, one launch (start us, length us, event | category | flops | bytes accessed | tf_op | source)
XLA Modules:
  0.0 97.9 jit_solution(5052539688439483621)
XLA Ops:
  0.0 1.0 %fusion.11 = (bf16[4,1,128,128]{3,2,1,0:T(8,128)(2,1)S(1)}, bf16[4,1,128,128]{3,2,1,0:T(8,128)(2,1)S(1)}) fusion(bf16[4,8,128,128]{3,2,1,0:T(8,128)(2,1)} %frame_ref.3), kind=kLoop, calls=%fused_computation.37 | loop fusion | bytes 524288 | tf_op jit(solution)/shard_map/input_conv_and_recurrence/slice | solution.py:14
  1.0 1.3 %collective-permute-start.1 = (bf16[4,1,128,128]{3,2,1,0:T(8,128)(2,1)S(1)}, bf16[4,1,128,128]{3,2,1,0:T(8,128)(2,1)S(1)}, u32[]{:S(2)}, u32[]{:S(2)}) collective-permute-start(bf16[4,1,128,128]{3,2,1,0:T(8,128)(2,1)S(1)} %get-tuple-element.13), channel_id=1, source_target_pairs={{1,0},{3,2},{5,4},{7,6},{9,8},{11,10},{13,12},{15,14},{17,16},{19,... | collective-permute-start | bytes 393224 | tf_op jit(solution)/shard_map/input_conv_and_recurrence/ppermute | solution.py:16
  2.3 3.0 %collective-permute-start = (bf16[4,1,128,128]{3,2,1,0:T(8,128)(2,1)S(1)}, bf16[4,1,128,128]{3,2,1,0:T(8,128)(2,1)S(1)}, u32[]{:S(2)}, u32[]{:S(2)}) collective-permute-start(bf16[4,1,128,128]{3,2,1,0:T(8,128)(2,1)S(1)} %get-tuple-element.14), channel_id=1, source_target_pairs={{0,1},{2,3},{4,5},{6,7},{8,9},{10,11},{12,13},{14,15},{16,17},{18,... | collective-permute-start | bytes 393224 | tf_op jit(solution)/shard_map/input_conv_and_recurrence/ppermute | solution.py:15
  5.3 0.7 reduce_window.9.cum_ref
  6.1 0.0 copy-start.7
  6.1 1.2 %copy.12 = bf16[3,3,128,128]{2,3,1,0:T(8,128)(2,1)S(1)} copy(bf16[3,3,128,128]{3,2,1,0:T(8,128)(2,1)} %param.6) | data formatting | bytes 589824 | tf_op args[1]
  7.2 0.9 copy.13.w_ref
  8.1 0.0 collective-permute-done.1.bottom_ref
  8.2 0.0 copy-start.3
  8.2 0.0 collective-permute-done.top_ref
  8.2 0.6 copy-done.3
  8.8 0.0 copy-start.4
  8.8 0.6 copy-done.4
  9.4 5.5 %input_conv_and_recurrence.1.local_ref = f32[4,8,128,128]{3,2,1,0:T(8,128)} custom-call(f32[4,128]{1,0:T(4,128)} %decay_ref.1, bf16[4,1,128,128]{3,2,1,0:T(8,128)(2,1)} %copy-done.4, bf16[4,8,128,128]{3,2,1,0:T(8,128)(2,1)} %frame_ref.3, bf16[4,1,128,128]{3,2,1,0:T(8,128)(2,1)} %copy-done.3, bf16[3,128,384]{2,1,0:T(8,128)(2,1)} %copy.13.w_ref), custom_call_target="tpu_custom_call" | custom-call | tf_op jit(solution)/shard_map/input_conv_and_recurrence/pallas_call | solution.py:77
  15.0 0.0 copy-start
  15.0 1.2 %fusion.7 = bf16[8,128,128]{2,1,0:T(8,128)(2,1)S(1)} fusion(f32[4,8,128,128]{3,2,1,0:T(8,128)} %input_conv_and_recurrence.1.local_ref), kind=kLoop, calls=%fused_computation.15 | loop fusion | bytes 524288 | tf_op jit(solution)/shard_map/carry_across_blocks/convert_element_type | solution.py:136
  16.2 4.9 %collective-permute-start.2 = (bf16[8,128,128]{2,1,0:T(8,128)(2,1)S(1)}, bf16[8,128,128]{2,1,0:T(8,128)(2,1)S(1)}, u32[]{:S(2)}, u32[]{:S(2)}) collective-permute-start(bf16[8,128,128]{2,1,0:T(8,128)(2,1)S(1)} %fusion.7), channel_id=1, source_target_pairs={{0,2},{2,4},{4,6},{6,8},{8,10},{10,12},{12,14},{14,16},{16,18},{18... | collective-permute-start | bytes 786440 | tf_op jit(solution)/shard_map/carry_across_blocks/ppermute | solution.py:136
  21.1 39.1 %all-gather = f32[16,1,128]{2,1,0:T(1,128)S(1)} all-gather(f32[1,1,128]{2,1,0:T(1,128)S(1)} %slice_bitcast_fusion.3), channel_id=1, replica_groups=mesh['tm'=16,'rows'=2] {'tm'}, dimensions={0}, use_global_device_ids=true | all-gather | bytes 8704 | tf_op jit(solution)/shard_map/block_decay_products/all_gather | solution.py:152
  60.2 0.1 select_reduce_fusion.5
  60.3 0.0 collective-permute-done.2
  60.3 1.1 %fusion.9 = bf16[8,128,128]{2,1,0:T(8,128)(2,1)S(1)} fusion(f32[4,8,128,128]{3,2,1,0:T(8,128)} %input_conv_and_recurrence.1.local_ref, bf16[8,128,128]{2,1,0:T(8,128)(2,1)S(1)} %collective-permute-done.2, f32[128]{0:T(128)S(1)} %get-tuple-element.8), kind=kLoop, calls=%fused_computation.18 | loop fusion | flops 524288 | bytes 1049088 | tf_op jit(solution)/shard_map/carry_across_blocks/convert_element_type | solution.py:136
  61.4 1.3 %collective-permute-start.3 = (bf16[8,128,128]{2,1,0:T(8,128)(2,1)S(1)}, bf16[8,128,128]{2,1,0:T(8,128)(2,1)S(1)}, u32[]{:S(2)}, u32[]{:S(2)}) collective-permute-start(bf16[8,128,128]{2,1,0:T(8,128)(2,1)S(1)} %fusion.9), channel_id=1, source_target_pairs={{0,4},{2,6},{4,8},{6,10},{8,12},{10,14},{12,16},{14,18},{16,20},{1... | collective-permute-start | bytes 786440 | tf_op jit(solution)/shard_map/carry_across_blocks/ppermute | solution.py:136
  62.7 3.9 %collective-permute-done.3 = bf16[8,128,128]{2,1,0:T(8,128)(2,1)S(1)} collective-permute-done((bf16[8,128,128]{2,1,0:T(8,128)(2,1)S(1)}, bf16[8,128,128]{2,1,0:T(8,128)(2,1)S(1)}, u32[]{:S(2)}, u32[]{:S(2)}) %collective-permute-start.3) | collective-permute-done | bytes 262176 | tf_op jit(solution)/shard_map/carry_across_blocks/ppermute | solution.py:136
  66.6 1.2 %fusion.8 = bf16[8,128,128]{2,1,0:T(8,128)(2,1)S(1)} fusion(bf16[8,128,128]{2,1,0:T(8,128)(2,1)S(1)} %collective-permute-done.3, f32[128]{0:T(128)S(1)} %get-tuple-element.9, f32[4,8,128,128]{3,2,1,0:T(8,128)} %input_conv_and_recurrence.1.local_ref, bf16[8,128,128]{2,1,0:T(8,128)(2,1)S(1)} %collective-permute-done.2, f32[128]{0:T(128)S(1)} %get-tuple-element.8), kind=kLoop, calls=%fused_computation.16 | loop fusion | flops 917504 | bytes 1311744 | tf_op jit(solution)/shard_map/carry_across_blocks/convert_element_type | solution.py:136
  67.7 4.1 %collective-permute-start.4 = (bf16[8,128,128]{2,1,0:T(8,128)(2,1)S(1)}, bf16[8,128,128]{2,1,0:T(8,128)(2,1)S(1)}, u32[]{:S(2)}, u32[]{:S(2)}) collective-permute-start(bf16[8,128,128]{2,1,0:T(8,128)(2,1)S(1)} %fusion.8), channel_id=1, source_target_pairs={{0,8},{2,10},{4,12},{6,14},{8,16},{10,18},{12,20},{14,22},{16,24},... | collective-permute-start | bytes 786440 | tf_op jit(solution)/shard_map/carry_across_blocks/ppermute | solution.py:136
  71.8 3.9 %collective-permute-done.4 = bf16[8,128,128]{2,1,0:T(8,128)(2,1)S(1)} collective-permute-done((bf16[8,128,128]{2,1,0:T(8,128)(2,1)S(1)}, bf16[8,128,128]{2,1,0:T(8,128)(2,1)S(1)}, u32[]{:S(2)}, u32[]{:S(2)}) %collective-permute-start.4) | collective-permute-done | bytes 262176 | tf_op jit(solution)/shard_map/carry_across_blocks/ppermute | solution.py:136
  75.7 0.0 copy-done
  75.7 0.2 fusion.5
  75.9 0.0 copy-start.2
  75.9 5.7 %collective-permute-start.5 = (bf16[8,128,128]{2,1,0:T(8,128)(2,1)S(1)}, bf16[8,128,128]{2,1,0:T(8,128)(2,1)S(1)}, u32[]{:S(2)}, u32[]{:S(2)}) collective-permute-start(bf16[8,128,128]{2,1,0:T(8,128)(2,1)S(1)} %fusion.5), channel_id=1, source_target_pairs={{0,16},{2,18},{4,20},{6,22},{8,24},{10,26},{12,28},{14,30},{1,17},... | collective-permute-start | bytes 786440 | tf_op jit(solution)/shard_map/carry_across_blocks/ppermute | solution.py:136
  81.6 3.8 %collective-permute-done.5 = bf16[8,128,128]{2,1,0:T(8,128)(2,1)S(1)} collective-permute-done((bf16[8,128,128]{2,1,0:T(8,128)(2,1)S(1)}, bf16[8,128,128]{2,1,0:T(8,128)(2,1)S(1)}, u32[]{:S(2)}, u32[]{:S(2)}) %collective-permute-start.5) | collective-permute-done | bytes 262176 | tf_op jit(solution)/shard_map/carry_across_blocks/ppermute | solution.py:136
  85.4 0.2 fusion.2.incoming_ref
  85.6 0.0 copy-start.1
  85.7 0.0 copy-done.7
  85.7 0.1 fusion.6
  85.8 1.3 %collective-permute-start.7 = (bf16[4,1,128,128]{3,2,1,0:T(8,128)(2,1)S(1)}, bf16[4,1,128,128]{3,2,1,0:T(8,128)(2,1)S(1)}, u32[]{:S(2)}, u32[]{:S(2)}) collective-permute-start(bf16[4,1,128,128]{3,2,1,0:T(8,128)(2,1)S(1)} %get-tuple-element.17), channel_id=1, source_target_pairs={{1,0},{3,2},{5,4},{7,6},{9,8},{11,10},{13,12},{15,14},{17,16},{19,... | collective-permute-start | bytes 393224 | tf_op jit(solution)/shard_map/output_conv/ppermute | solution.py:16
  87.1 3.0 %collective-permute-start.6 = (bf16[4,1,128,128]{3,2,1,0:T(8,128)(2,1)S(1)}, bf16[4,1,128,128]{3,2,1,0:T(8,128)(2,1)S(1)}, u32[]{:S(2)}, u32[]{:S(2)}) collective-permute-start(bf16[4,1,128,128]{3,2,1,0:T(8,128)(2,1)S(1)} %get-tuple-element.18), channel_id=1, source_target_pairs={{0,1},{2,3},{4,5},{6,7},{8,9},{10,11},{12,13},{14,15},{16,17},{18,... | collective-permute-start | bytes 393224 | tf_op jit(solution)/shard_map/output_conv/ppermute | solution.py:15
  90.1 0.0 copy-done.2
  90.1 0.2 copy.14
  90.3 0.9 copy.15.w_ref
  91.2 0.0 collective-permute-done.7.bottom_ref
  91.2 0.0 copy-start.5
  91.3 0.0 collective-permute-done.6.top_ref
  91.3 0.0 copy-start.6
  91.3 0.0 copy-done.1
  91.3 0.6 copy-done.5
  91.9 0.1 copy-done.6
  92.0 6.0 %output_conv.1 = bf16[4,8,128,128]{3,2,1,0:T(8,128)(2,1)} custom-call(f32[4,128]{1,0:T(4,128)} %copy-done.7, f32[1,128]{1,0:T(1,128)} %bitcast.31, f32[8,128,128]{2,1,0:T(8,128)} %copy-done.1, bf16[4,1,128,128]{3,2,1,0:T(8,128)(2,1)} %copy-done.6, f32[4,8,128,128]{3,2,1,0:T(8,128)} %input_conv_and_recurrence.1.local_ref, bf16[4,1,128,128]{3,2,1,0:T(8,128)(2,1)} %copy-done.5, ...), custom_call_target="tpu_custom_call" | custom-call | tf_op jit(solution)/shard_map/output_conv/pallas_call | solution.py:103
  (8 shorter events, 0.1 us)
Async XLA Ops:
  1.0 7.2 %collective-permute-start.1 = (bf16[4,1,128,128]{3,2,1,0:T(8,128)(2,1)S(1)}, bf16[4,1,128,128]{3,2,1,0:T(8,128)(2,1)S(1)}, u32[]{:S(2)}, u32[]{:S(2)}) collective-permute-start(bf16[4,1,128,128]{3,2,1,0:T(8,128)(2,1)S(1)} %get-tuple-element.13), channel_id=1, source_target_pairs={{1,0},{3,2},{5,4},{7,6},{9,8},{11,10},{13,12},{15,14},{17,16},{19,... | collective-permute-start | bytes 393224 | tf_op jit(solution)/shard_map/input_conv_and_recurrence/ppermute | solution.py:16
  2.3 5.9 %collective-permute-start = (bf16[4,1,128,128]{3,2,1,0:T(8,128)(2,1)S(1)}, bf16[4,1,128,128]{3,2,1,0:T(8,128)(2,1)S(1)}, u32[]{:S(2)}, u32[]{:S(2)}) collective-permute-start(bf16[4,1,128,128]{3,2,1,0:T(8,128)(2,1)S(1)} %get-tuple-element.14), channel_id=1, source_target_pairs={{0,1},{2,3},{4,5},{6,7},{8,9},{10,11},{12,13},{14,15},{16,17},{18,... | collective-permute-start | bytes 393224 | tf_op jit(solution)/shard_map/input_conv_and_recurrence/ppermute | solution.py:15
  6.1 79.6 %copy-start.7 = (f32[4,128]{1,0:T(4,128)}, f32[4,128]{1,0:T(4,128)S(1)}, u32[]{:S(2)}) copy-start(f32[4,128]{1,0:T(4,128)S(1)} %reduce_window.9.cum_ref) | copy-start | bytes 6148
  8.2 0.7 copy-start.3
  8.8 0.6 copy-start.4
  15.0 60.7 %copy-start = (f32[4,8,128,128]{3,2,1,0:T(8,128)S(1)}, f32[4,8,128,128]{3,2,1,0:T(8,128)}, u32[]{:S(2)}) copy-start(f32[4,8,128,128]{3,2,1,0:T(8,128)} %input_conv_and_recurrence.1.local_ref) | copy-start | bytes 6291460
  16.2 44.1 %collective-permute-start.2 = (bf16[8,128,128]{2,1,0:T(8,128)(2,1)S(1)}, bf16[8,128,128]{2,1,0:T(8,128)(2,1)S(1)}, u32[]{:S(2)}, u32[]{:S(2)}) collective-permute-start(bf16[8,128,128]{2,1,0:T(8,128)(2,1)S(1)} %fusion.7), channel_id=1, source_target_pairs={{0,2},{2,4},{4,6},{6,8},{8,10},{10,12},{12,14},{14,16},{16,18},{18... | collective-permute-start | bytes 786440 | tf_op jit(solution)/shard_map/carry_across_blocks/ppermute | solution.py:136
  61.4 5.2 %collective-permute-start.3 = (bf16[8,128,128]{2,1,0:T(8,128)(2,1)S(1)}, bf16[8,128,128]{2,1,0:T(8,128)(2,1)S(1)}, u32[]{:S(2)}, u32[]{:S(2)}) collective-permute-start(bf16[8,128,128]{2,1,0:T(8,128)(2,1)S(1)} %fusion.9), channel_id=1, source_target_pairs={{0,4},{2,6},{4,8},{6,10},{8,12},{10,14},{12,16},{14,18},{16,20},{1... | collective-permute-start | bytes 786440 | tf_op jit(solution)/shard_map/carry_across_blocks/ppermute | solution.py:136
  67.7 7.9 %collective-permute-start.4 = (bf16[8,128,128]{2,1,0:T(8,128)(2,1)S(1)}, bf16[8,128,128]{2,1,0:T(8,128)(2,1)S(1)}, u32[]{:S(2)}, u32[]{:S(2)}) collective-permute-start(bf16[8,128,128]{2,1,0:T(8,128)(2,1)S(1)} %fusion.8), channel_id=1, source_target_pairs={{0,8},{2,10},{4,12},{6,14},{8,16},{10,18},{12,20},{14,22},{16,24},... | collective-permute-start | bytes 786440 | tf_op jit(solution)/shard_map/carry_across_blocks/ppermute | solution.py:136
  75.9 14.3 %copy-start.2 = (bf16[3,3,128,128]{3,2,1,0:T(8,128)(2,1)S(1)}, bf16[3,3,128,128]{3,2,1,0:T(8,128)(2,1)}, u32[]{:S(2)}) copy-start(bf16[3,3,128,128]{3,2,1,0:T(8,128)(2,1)} %param.8) | copy-start | bytes 884740
  75.9 9.6 %collective-permute-start.5 = (bf16[8,128,128]{2,1,0:T(8,128)(2,1)S(1)}, bf16[8,128,128]{2,1,0:T(8,128)(2,1)S(1)}, u32[]{:S(2)}, u32[]{:S(2)}) collective-permute-start(bf16[8,128,128]{2,1,0:T(8,128)(2,1)S(1)} %fusion.5), channel_id=1, source_target_pairs={{0,16},{2,18},{4,20},{6,22},{8,24},{10,26},{12,28},{14,30},{1,17},... | collective-permute-start | bytes 786440 | tf_op jit(solution)/shard_map/carry_across_blocks/ppermute | solution.py:136
  85.6 5.7 %copy-start.1 = (f32[8,128,128]{2,1,0:T(8,128)}, f32[8,128,128]{2,1,0:T(8,128)S(1)}, u32[]{:S(2)}) copy-start(f32[8,128,128]{2,1,0:T(8,128)S(1)} %fusion.2.incoming_ref) | copy-start | bytes 1572868
  85.8 5.5 %collective-permute-start.7 = (bf16[4,1,128,128]{3,2,1,0:T(8,128)(2,1)S(1)}, bf16[4,1,128,128]{3,2,1,0:T(8,128)(2,1)S(1)}, u32[]{:S(2)}, u32[]{:S(2)}) collective-permute-start(bf16[4,1,128,128]{3,2,1,0:T(8,128)(2,1)S(1)} %get-tuple-element.17), channel_id=1, source_target_pairs={{1,0},{3,2},{5,4},{7,6},{9,8},{11,10},{13,12},{15,14},{17,16},{19,... | collective-permute-start | bytes 393224 | tf_op jit(solution)/shard_map/output_conv/ppermute | solution.py:16
  87.1 4.2 %collective-permute-start.6 = (bf16[4,1,128,128]{3,2,1,0:T(8,128)(2,1)S(1)}, bf16[4,1,128,128]{3,2,1,0:T(8,128)(2,1)S(1)}, u32[]{:S(2)}, u32[]{:S(2)}) collective-permute-start(bf16[4,1,128,128]{3,2,1,0:T(8,128)(2,1)S(1)} %get-tuple-element.18), channel_id=1, source_target_pairs={{0,1},{2,3},{4,5},{6,7},{8,9},{10,11},{12,13},{14,15},{16,17},{18,... | collective-permute-start | bytes 393224 | tf_op jit(solution)/shard_map/output_conv/ppermute | solution.py:15
  91.2 0.6 copy-start.5
  91.3 0.7 copy-start.6

commit v3 on v2

--- a/solution.py
+++ b/solution.py
@@ -17,21 +17,16 @@
     return before, after
 
 
-def grouped_taps(weight):
-    down, across, k, m = weight.shape
-    return jnp.transpose(weight, (0, 2, 1, 3)).reshape(down, k, across * m)
-
-
 def conv_taps(x, w_ref):
     rows = x.shape[0] - 2
     width, k = x.shape[1], x.shape[2]
-    m = w_ref.shape[2] // 3
+    m = w_ref.shape[3]
     n = rows * width
-    acc = None
-    for a in range(3):
-        lhs = x[a : a + rows].reshape(n, k)
-        part = jnp.dot(lhs, w_ref[a], preferred_element_type=jnp.float32)
-        acc = part if acc is None else acc + part
+    lhs = jnp.concatenate([x[a : a + rows].reshape(n, k) for a in range(3)], axis=1)
+    weight = jnp.concatenate(
+        [jnp.concatenate([w_ref[a, b] for b in range(3)], axis=1) for a in range(3)], axis=0
+    )
+    acc = jnp.dot(lhs, weight, preferred_element_type=jnp.float32)
     column = lax.broadcasted_iota(jnp.int32, (n, m), 0) % width
     from_left = pltpu.roll(acc[:, :m], 1, 0)
     from_right = pltpu.roll(acc[:, 2 * m :], n - 1, 0)
@@ -82,13 +77,13 @@
             halo,
             pl.BlockSpec((1, band, width, channels), lambda f: (f, 0, 0, 0)),
             halo,
-            pl.BlockSpec((3, channels, 3 * state_width), lambda f: (0, 0, 0)),
+            pl.BlockSpec((3, 3, channels, state_width), lambda f: (0, 0, 0, 0)),
         ],
         out_specs=pl.BlockSpec((1, band, width, state_width), lambda f: (f, 0, 0, 0)),
         out_shape=jax.ShapeDtypeStruct((count, band, width, state_width), jnp.float32),
         scratch_shapes=[pltpu.VMEM((band * width, state_width), jnp.float32)],
         compiler_params=pltpu.CompilerParams(dimension_semantics=("arbitrary",)),
-    )(decay, top, frames, bottom, grouped_taps(conv_in))
+    )(decay, top, frames, bottom, conv_in)
 
 
 def output_stage(local, cumulative, incoming, frames, conv_out, skip):
@@ -111,35 +106,46 @@
             pl.BlockSpec((1, band, width, state_width), lambda f: (f, 0, 0, 0)),
             halo,
             pl.BlockSpec((1, band, width, channels), lambda f: (f, 0, 0, 0)),
-            pl.BlockSpec((3, state_width, 3 * channels), lambda f: (0, 0, 0)),
+            pl.BlockSpec((3, 3, state_width, channels), lambda f: (0, 0, 0, 0)),
         ],
         out_specs=pl.BlockSpec((1, band, width, channels), lambda f: (f, 0, 0, 0)),
         out_shape=jax.ShapeDtypeStruct((count, band, width, channels), jnp.bfloat16),
         compiler_params=pltpu.CompilerParams(dimension_semantics=("arbitrary",)),
-    )(cumulative, skip.reshape(1, channels), incoming, top, local, bottom, frames, grouped_taps(conv_out))
+    )(cumulative, skip.reshape(1, channels), incoming, top, local, bottom, frames, conv_out)
 
 
-def incoming_state(products, state, axis):
+def split3(p, rows):
+    hi = lax.reduce_precision(p, exponent_bits=8, mantissa_bits=7)
+    rest = p - hi
+    mid = lax.reduce_precision(rest, exponent_bits=8, mantissa_bits=7)
+    low = rest - mid
+    parts = jnp.stack([hi, mid, low]).astype(jnp.bfloat16)
+    return jnp.pad(parts, ((0, rows - 3), (0, 0)))
+
+
+def incoming_state(power, state, axis):
     n = lax.axis_size(axis)
-    me = lax.axis_index(axis)
-    block = lax.broadcasted_iota(jnp.int32, (n, 1), 0)
-
-    def span(lo, hi):
-        inside = (block >= lo) & (block <= hi)
-        return jnp.prod(jnp.where(inside, products, 1.0), axis=0)
-
-    win_s = state
-    acc_s = None
+    rows, width, channels = state.shape
+    cells = rows * width
+    win_p, win_s = power, state
+    acc_p, acc_s = None, None
     shift = 1
     while shift < n:
         pairs = [(i, i + shift) for i in range(n - shift)]
-        got = lax.ppermute(win_s.astype(jnp.bfloat16), axis, pairs).astype(jnp.float32)
+        payload = jnp.concatenate(
+            [win_s.astype(jnp.bfloat16).reshape(cells, channels), split3(win_p, 16)], axis=0
+        )
+        got = lax.ppermute(payload, axis, pairs)
+        got_s = got[:cells].astype(jnp.float32).reshape(rows, width, channels)
+        got_p = jnp.sum(got[cells : cells + 3].astype(jnp.float32), axis=0)
         if acc_s is None:
-            acc_s = got
+            acc_p, acc_s = got_p, got_s
         else:
-            acc_s = span(me - shift + 1, me - 1) * got + acc_s
+            acc_s = acc_p * got_s + acc_s
+            acc_p = got_p * acc_p
         if 2 * shift < n:
-            win_s = span(me - shift + 1, me) * got + win_s
+            win_s = win_p * got_s + win_s
+            win_p = got_p * win_p
         shift *= 2
     if acc_s is None:
         return jnp.zeros_like(state)
@@ -148,12 +154,14 @@
 
 def shards(frames, conv_in, decay, conv_out, skip):
     with jax.named_scope("block_decay_products"):
-        cumulative = jnp.cumprod(decay, axis=0)
-        products = lax.all_gather(cumulative[-1], "tm")
+        running = [decay[0]]
+        for frame_index in range(1, decay.shape[0]):
+            running.append(running[-1] * decay[frame_index])
+        cumulative = jnp.stack(running)
     with jax.named_scope("input_conv_and_recurrence"):
         local = input_stage(frames, conv_in, decay)
     with jax.named_scope("carry_across_blocks"):
-        incoming = incoming_state(products, local[-1], "tm")
+        incoming = incoming_state(cumulative[-1], local[-1], "tm")
     with jax.named_scope("output_conv"):
         return output_stage(local, cumulative, incoming, frames, conv_out, skip)
 

time: 98.5 us -> 71 us (0.72)
  the two profiles are of different devices: /device:TPU:0 before, /device:TPU:25 now
where the time goes in v3:
time: 71 us; the launch traced here: 70.5 us
  waiting for transfers between devices  36.3 us (51%)
  starting transfers between devices  16.9 us (24%)
  Pallas kernels  10.7 us (15%)
  local copies, waits for them, and re-layouts  4.5 us (6%)
  other arithmetic  1.87 us (3%)
    ppermute x4, waiting for transfers between devices, incoming_state(): got = lax.ppermute(payload, axis, pairs)  33.3 us
    ppermute x4, starting transfers between devices, incoming_state(): got = lax.ppermute(payload, axis, pairs)  7.95 us
    ppermute x2, starting transfers between devices, halo_rows(): after = lax.ppermute(first, axis, down)  6.33 us
    pallas_call x1, Pallas kernels, output_stage(): pl.pallas_call(output_kernel, grid=(count,), in_specs=[pl.BlockSpec((coun...  5.57 us
    pallas_call x1, Pallas kernels, input_stage(): pl.pallas_call(input_kernel, grid=(count,), in_specs=[pl.BlockSpec((count...  5.13 us
    ppermute x2, waiting for transfers between devices, halo_rows(): before = lax.ppermute(last, axis, up)  2.98 us
    ppermute x2, starting transfers between devices, halo_rows(): before = lax.ppermute(last, axis, up)  2.58 us
  transfers between devices with their start and end apart: 8, of which 6 were waited for; matrix products, arithmetic and copies ran while one was open for 3% of the time, Pallas kernels for 0%

profile of v3, /device:TPU:25, one launch (start us, length us, event | category | flops | bytes accessed | tf_op | source)
XLA Modules:
  0.0 70.5 jit_solution(1997465754610914731)
XLA Ops:
  0.0 1.0 %fusion.31 = (bf16[4,1,128,128]{3,2,1,0:T(8,128)(2,1)S(1)}, bf16[4,1,128,128]{3,2,1,0:T(8,128)(2,1)S(1)}) fusion(bf16[4,8,128,128]{3,2,1,0:T(8,128)(2,1)} %frame_ref.3), kind=kLoop, calls=%fused_computation.75 | loop fusion | bytes 524288 | tf_op jit(solution)/shard_map/input_conv_and_recurrence/slice | solution.py:14
  1.0 2.6 %collective-permute-start.1 = (bf16[4,1,128,128]{3,2,1,0:T(8,128)(2,1)S(1)}, bf16[4,1,128,128]{3,2,1,0:T(8,128)(2,1)S(1)}, u32[]{:S(2)}, u32[]{:S(2)}) collective-permute-start(bf16[4,1,128,128]{3,2,1,0:T(8,128)(2,1)S(1)} %get-tuple-element.19), channel_id=1, source_target_pairs={{1,0},{3,2},{5,4},{7,6},{9,8},{11,10},{13,12},{15,14},{17,16},{19,... | collective-permute-start | bytes 393224 | tf_op jit(solution)/shard_map/input_conv_and_recurrence/ppermute | solution.py:16
  3.6 1.3 %collective-permute-start = (bf16[4,1,128,128]{3,2,1,0:T(8,128)(2,1)S(1)}, bf16[4,1,128,128]{3,2,1,0:T(8,128)(2,1)S(1)}, u32[]{:S(2)}, u32[]{:S(2)}) collective-permute-start(bf16[4,1,128,128]{3,2,1,0:T(8,128)(2,1)S(1)} %get-tuple-element.20), channel_id=1, source_target_pairs={{0,1},{2,3},{4,5},{6,7},{8,9},{10,11},{12,13},{14,15},{16,17},{18,... | collective-permute-start | bytes 393224 | tf_op jit(solution)/shard_map/input_conv_and_recurrence/ppermute | solution.py:15
  4.9 0.8 %reduce-precision_convert_fusion.7 = (bf16[1,128]{1,0:T(2,128)(2,1)S(1)}, f32[1,128]{1,0:T(1,128)S(1)}, f32[1,128]{1,0:T(1,128)S(1)}, f32[1,128]{1,0:T(1,128)S(1)}, f32[1,128]{1,0:T(1,128)S(1)}) fusion(f32[4,128]{1,0:T(4,128)} %decay_ref.1), kind=kLoop, calls=%fused_computation.60 | loop fusion | flops 640 | bytes 4352 | tf_op jit(solution)/shard_map/convert.10
  5.7 0.0 collective-permute-done.1.bottom_ref
  5.8 0.0 copy-start.1
  5.8 1.1 %collective-permute-done.top_ref = bf16[4,1,128,128]{3,2,1,0:T(8,128)(2,1)S(1)} collective-permute-done((bf16[4,1,128,128]{3,2,1,0:T(8,128)(2,1)S(1)}, bf16[4,1,128,128]{3,2,1,0:T(8,128)(2,1)S(1)}, u32[]{:S(2)}, u32[]{:S(2)}) %collective-permute-start) | collective-permute-done | bytes 131104 | tf_op jit(solution)/shard_map/input_conv_and_recurrence/ppermute | solution.py:15
  6.8 0.0 copy-done.1
  6.8 0.0 copy-start.2
  6.8 0.7 copy-done.2
  7.5 5.1 %input_conv_and_recurrence.1.local_ref = f32[4,8,128,128]{3,2,1,0:T(8,128)} custom-call(f32[4,128]{1,0:T(4,128)} %decay_ref.1, bf16[4,1,128,128]{3,2,1,0:T(8,128)(2,1)} %copy-done.2, bf16[4,8,128,128]{3,2,1,0:T(8,128)(2,1)} %frame_ref.3, bf16[4,1,128,128]{3,2,1,0:T(8,128)(2,1)} %copy-done.1, bf16[3,3,128,128]{3,2,1,0:T(8,128)(2,1)} %w_ref.2), custom_call_target="tpu_custom_call" | custom-call | tf_op jit(solution)/shard_map/input_conv_and_recurrence/pallas_call | solution.py:72
  12.6 1.1 %slice.80 = f32[1,8,128,128]{3,2,1,0:T(8,128)S(1)} slice(f32[4,8,128,128]{3,2,1,0:T(8,128)} %input_conv_and_recurrence.1.local_ref), slice={[3:4], [0:8], [0:128], [0:128]} | slice | bytes 1048576 | tf_op jit(solution)/shard_map/carry_across_blocks/slice | solution.py:164
  13.8 3.1 %collective-permute-start.2 = (bf16[1040,128]{1,0:T(8,128)(2,1)S(1)}, bf16[1040,128]{1,0:T(8,128)(2,1)S(1)}, u32[]{:S(2)}, u32[]{:S(2)}) collective-permute-start(bf16[1040,128]{1,0:T(8,128)(2,1)S(1)} %pad_maximum_fusion), channel_id=1, source_target_pairs={{0,2},{2,4},{4,6},{6,8},{8,10},{10,12},{12,14},{14,16},{16,18},{18... | collective-permute-start | bytes 798728 | tf_op jit(solution)/shard_map/carry_across_blocks/ppermute | solution.py:138
  16.9 7.8 %collective-permute-done.2 = bf16[1040,128]{1,0:T(8,128)(2,1)S(1)} collective-permute-done((bf16[1040,128]{1,0:T(8,128)(2,1)S(1)}, bf16[1040,128]{1,0:T(8,128)(2,1)S(1)}, u32[]{:S(2)}, u32[]{:S(2)}) %collective-permute-start.2) | collective-permute-done | bytes 266272 | tf_op jit(solution)/shard_map/carry_across_blocks/ppermute | solution.py:138
  24.7 0.1 fusion.3
  24.8 2.2 %collective-permute-start.3 = (bf16[1040,128]{1,0:T(8,128)(2,1)S(1)}, bf16[1040,128]{1,0:T(8,128)(2,1)S(1)}, u32[]{:S(2)}, u32[]{:S(2)}) collective-permute-start(bf16[1040,128]{1,0:T(8,128)(2,1)S(1)} %pad_maximum_fusion.1), channel_id=1, source_target_pairs={{0,4},{2,6},{4,8},{6,10},{8,12},{10,14},{12,16},{14,18},{16,20},{1... | collective-permute-start | bytes 798728 | tf_op jit(solution)/shard_map/carry_across_blocks/ppermute | solution.py:138
  27.1 0.0 copy-start.5
  27.1 1.1 %fusion.30 = (f32[4,1,128,128]{3,2,1,0:T(8,128)S(1)}, f32[4,1,128,128]{3,2,1,0:T(8,128)S(1)}) fusion(f32[4,8,128,128]{3,2,1,0:T(8,128)} %input_conv_and_recurrence.1.local_ref), kind=kLoop, calls=%fused_computation.74 | loop fusion | bytes 1048576 | tf_op jit(solution)/shard_map/output_conv/slice | solution.py:92
  28.2 5.7 %collective-permute-done.3 = bf16[1040,128]{1,0:T(8,128)(2,1)S(1)} collective-permute-done((bf16[1040,128]{1,0:T(8,128)(2,1)S(1)}, bf16[1040,128]{1,0:T(8,128)(2,1)S(1)}, u32[]{:S(2)}, u32[]{:S(2)}) %collective-permute-start.3) | collective-permute-done | bytes 266272 | tf_op jit(solution)/shard_map/carry_across_blocks/ppermute | solution.py:138
  34.0 0.1 fusion.2
  34.2 1.3 %collective-permute-start.4 = (bf16[1040,128]{1,0:T(8,128)(2,1)S(1)}, bf16[1040,128]{1,0:T(8,128)(2,1)S(1)}, u32[]{:S(2)}, u32[]{:S(2)}) collective-permute-start(bf16[1040,128]{1,0:T(8,128)(2,1)S(1)} %pad_maximum_fusion.2), channel_id=1, source_target_pairs={{0,8},{2,10},{4,12},{6,14},{8,16},{10,18},{12,20},{14,22},{16,24},... | collective-permute-start | bytes 798728 | tf_op jit(solution)/shard_map/carry_across_blocks/ppermute | solution.py:138
  35.5 5.8 %collective-permute-done.4 = bf16[1040,128]{1,0:T(8,128)(2,1)S(1)} collective-permute-done((bf16[1040,128]{1,0:T(8,128)(2,1)S(1)}, bf16[1040,128]{1,0:T(8,128)(2,1)S(1)}, u32[]{:S(2)}, u32[]{:S(2)}) %collective-permute-start.4) | collective-permute-done | bytes 266272 | tf_op jit(solution)/shard_map/carry_across_blocks/ppermute | solution.py:138
  41.4 0.2 add_convert_fusion
  41.6 1.3 %collective-permute-start.5 = (bf16[1040,128]{1,0:T(8,128)(2,1)S(1)}, bf16[1040,128]{1,0:T(8,128)(2,1)S(1)}, u32[]{:S(2)}, u32[]{:S(2)}) collective-permute-start(bf16[1040,128]{1,0:T(8,128)(2,1)S(1)} %pad_maximum_fusion.3), channel_id=1, source_target_pairs={{0,16},{2,18},{4,20},{6,22},{8,24},{10,26},{12,28},{14,30},{1,17},... | collective-permute-start | bytes 798728 | tf_op jit(solution)/shard_map/carry_across_blocks/ppermute | solution.py:138
  42.9 14.0 %collective-permute-done.5 = bf16[1040,128]{1,0:T(8,128)(2,1)S(1)} collective-permute-done((bf16[1040,128]{1,0:T(8,128)(2,1)S(1)}, bf16[1040,128]{1,0:T(8,128)(2,1)S(1)}, u32[]{:S(2)}, u32[]{:S(2)}) %collective-permute-start.5) | collective-permute-done | bytes 266272 | tf_op jit(solution)/shard_map/carry_across_blocks/ppermute | solution.py:138
  57.0 0.1 fusion.1.incoming_ref
  57.1 0.0 copy-start
  57.2 0.0 copy-done.5
  57.2 0.1 fusion
  57.3 3.7 %collective-permute-start.7 = (bf16[4,1,128,128]{3,2,1,0:T(8,128)(2,1)S(1)}, bf16[4,1,128,128]{3,2,1,0:T(8,128)(2,1)S(1)}, u32[]{:S(2)}, u32[]{:S(2)}) collective-permute-start(bf16[4,1,128,128]{3,2,1,0:T(8,128)(2,1)S(1)} %get-tuple-element.23), channel_id=1, source_target_pairs={{1,0},{3,2},{5,4},{7,6},{9,8},{11,10},{13,12},{15,14},{17,16},{19,... | collective-permute-start | bytes 393224 | tf_op jit(solution)/shard_map/output_conv/ppermute | solution.py:16
  61.0 1.3 %collective-permute-start.6 = (bf16[4,1,128,128]{3,2,1,0:T(8,128)(2,1)S(1)}, bf16[4,1,128,128]{3,2,1,0:T(8,128)(2,1)S(1)}, u32[]{:S(2)}, u32[]{:S(2)}) collective-permute-start(bf16[4,1,128,128]{3,2,1,0:T(8,128)(2,1)S(1)} %get-tuple-element.24), channel_id=1, source_target_pairs={{0,1},{2,3},{4,5},{6,7},{8,9},{10,11},{12,13},{14,15},{16,17},{18,... | collective-permute-start | bytes 393224 | tf_op jit(solution)/shard_map/output_conv/ppermute | solution.py:15
  62.3 0.0 collective-permute-done.7.bottom_ref
  62.3 0.0 copy-start.3
  62.4 1.9 %collective-permute-done.6.top_ref = bf16[4,1,128,128]{3,2,1,0:T(8,128)(2,1)S(1)} collective-permute-done((bf16[4,1,128,128]{3,2,1,0:T(8,128)(2,1)S(1)}, bf16[4,1,128,128]{3,2,1,0:T(8,128)(2,1)S(1)}, u32[]{:S(2)}, u32[]{:S(2)}) %collective-permute-start.6) | collective-permute-done | bytes 131104 | tf_op jit(solution)/shard_map/output_conv/ppermute | solution.py:15
  64.3 0.0 copy-start.4
  64.3 0.0 copy-done
  64.3 0.0 copy-done.3
  64.3 0.6 copy-done.4
  64.9 5.6 %output_conv.1 = bf16[4,8,128,128]{3,2,1,0:T(8,128)(2,1)} custom-call(f32[4,128]{1,0:T(4,128)} %copy-done.5, f32[1,128]{1,0:T(1,128)} %bitcast.45, f32[8,128,128]{2,1,0:T(8,128)} %copy-done, bf16[4,1,128,128]{3,2,1,0:T(8,128)(2,1)} %copy-done.4, f32[4,8,128,128]{3,2,1,0:T(8,128)} %input_conv_and_recurrence.1.local_ref, bf16[4,1,128,128]{3,2,1,0:T(8,128)(2,1)} %copy-done.3, ...), custom_call_target="tpu_custom_call" | custom-call | tf_op jit(solution)/shard_map/output_conv/pallas_call | solution.py:98
  (28 shorter events, 0.5 us)
Async XLA Ops:
  1.0 4.8 %collective-permute-start.1 = (bf16[4,1,128,128]{3,2,1,0:T(8,128)(2,1)S(1)}, bf16[4,1,128,128]{3,2,1,0:T(8,128)(2,1)S(1)}, u32[]{:S(2)}, u32[]{:S(2)}) collective-permute-start(bf16[4,1,128,128]{3,2,1,0:T(8,128)(2,1)S(1)} %get-tuple-element.19), channel_id=1, source_target_pairs={{1,0},{3,2},{5,4},{7,6},{9,8},{11,10},{13,12},{15,14},{17,16},{19,... | collective-permute-start | bytes 393224 | tf_op jit(solution)/shard_map/input_conv_and_recurrence/ppermute | solution.py:16
  3.6 3.2 %collective-permute-start = (bf16[4,1,128,128]{3,2,1,0:T(8,128)(2,1)S(1)}, bf16[4,1,128,128]{3,2,1,0:T(8,128)(2,1)S(1)}, u32[]{:S(2)}, u32[]{:S(2)}) collective-permute-start(bf16[4,1,128,128]{3,2,1,0:T(8,128)(2,1)S(1)} %get-tuple-element.20), channel_id=1, source_target_pairs={{0,1},{2,3},{4,5},{6,7},{8,9},{10,11},{12,13},{14,15},{16,17},{18,... | collective-permute-start | bytes 393224 | tf_op jit(solution)/shard_map/input_conv_and_recurrence/ppermute | solution.py:15
  5.8 1.1 %copy-start.1 = (bf16[4,1,128,128]{3,2,1,0:T(8,128)(2,1)}, bf16[4,1,128,128]{3,2,1,0:T(8,128)(2,1)S(1)}, u32[]{:S(2)}) copy-start(bf16[4,1,128,128]{3,2,1,0:T(8,128)(2,1)S(1)} %collective-permute-done.1.bottom_ref) | copy-start | bytes 393220
  6.8 0.7 copy-start.2
  13.8 10.9 %collective-permute-start.2 = (bf16[1040,128]{1,0:T(8,128)(2,1)S(1)}, bf16[1040,128]{1,0:T(8,128)(2,1)S(1)}, u32[]{:S(2)}, u32[]{:S(2)}) collective-permute-start(bf16[1040,128]{1,0:T(8,128)(2,1)S(1)} %pad_maximum_fusion), channel_id=1, source_target_pairs={{0,2},{2,4},{4,6},{6,8},{8,10},{10,12},{12,14},{14,16},{16,18},{18... | collective-permute-start | bytes 798728 | tf_op jit(solution)/shard_map/carry_across_blocks/ppermute | solution.py:138
  24.8 9.1 %collective-permute-start.3 = (bf16[1040,128]{1,0:T(8,128)(2,1)S(1)}, bf16[1040,128]{1,0:T(8,128)(2,1)S(1)}, u32[]{:S(2)}, u32[]{:S(2)}) collective-permute-start(bf16[1040,128]{1,0:T(8,128)(2,1)S(1)} %pad_maximum_fusion.1), channel_id=1, source_target_pairs={{0,4},{2,6},{4,8},{6,10},{8,12},{10,14},{12,16},{14,18},{16,20},{1... | collective-permute-start | bytes 798728 | tf_op jit(solution)/shard_map/carry_across_blocks/ppermute | solution.py:138
  27.1 30.1 %copy-start.5 = (f32[4,128]{1,0:T(4,128)}, f32[4,128]{1,0:T(4,128)S(1)}, u32[]{:S(2)}) copy-start(f32[4,128]{1,0:T(4,128)S(1)} %pad_maximum_fusion.4.cum_ref) | copy-start | bytes 6148
  34.2 7.2 %collective-permute-start.4 = (bf16[1040,128]{1,0:T(8,128)(2,1)S(1)}, bf16[1040,128]{1,0:T(8,128)(2,1)S(1)}, u32[]{:S(2)}, u32[]{:S(2)}) collective-permute-start(bf16[1040,128]{1,0:T(8,128)(2,1)S(1)} %pad_maximum_fusion.2), channel_id=1, source_target_pairs={{0,8},{2,10},{4,12},{6,14},{8,16},{10,18},{12,20},{14,22},{16,24},... | collective-permute-start | bytes 798728 | tf_op jit(solution)/shard_map/carry_across_blocks/ppermute | solution.py:138
  41.6 15.4 %collective-permute-start.5 = (bf16[1040,128]{1,0:T(8,128)(2,1)S(1)}, bf16[1040,128]{1,0:T(8,128)(2,1)S(1)}, u32[]{:S(2)}, u32[]{:S(2)}) collective-permute-start(bf16[1040,128]{1,0:T(8,128)(2,1)S(1)} %pad_maximum_fusion.3), channel_id=1, source_target_pairs={{0,16},{2,18},{4,20},{6,22},{8,24},{10,26},{12,28},{14,30},{1,17},... | collective-permute-start | bytes 798728 | tf_op jit(solution)/shard_map/carry_across_blocks/ppermute | solution.py:138
  57.1 7.2 %copy-start = (f32[8,128,128]{2,1,0:T(8,128)}, f32[8,128,128]{2,1,0:T(8,128)S(1)}, u32[]{:S(2)}) copy-start(f32[8,128,128]{2,1,0:T(8,128)S(1)} %fusion.1.incoming_ref) | copy-start | bytes 1572868
  57.3 5.1 %collective-permute-start.7 = (bf16[4,1,128,128]{3,2,1,0:T(8,128)(2,1)S(1)}, bf16[4,1,128,128]{3,2,1,0:T(8,128)(2,1)S(1)}, u32[]{:S(2)}, u32[]{:S(2)}) collective-permute-start(bf16[4,1,128,128]{3,2,1,0:T(8,128)(2,1)S(1)} %get-tuple-element.23), channel_id=1, source_target_pairs={{1,0},{3,2},{5,4},{7,6},{9,8},{11,10},{13,12},{15,14},{17,16},{19,... | collective-permute-start | bytes 393224 | tf_op jit(solution)/shard_map/output_conv/ppermute | solution.py:16
  61.0 3.2 %collective-permute-start.6 = (bf16[4,1,128,128]{3,2,1,0:T(8,128)(2,1)S(1)}, bf16[4,1,128,128]{3,2,1,0:T(8,128)(2,1)S(1)}, u32[]{:S(2)}, u32[]{:S(2)}) collective-permute-start(bf16[4,1,128,128]{3,2,1,0:T(8,128)(2,1)S(1)} %get-tuple-element.24), channel_id=1, source_target_pairs={{0,1},{2,3},{4,5},{6,7},{8,9},{10,11},{12,13},{14,15},{16,17},{18,... | collective-permute-start | bytes 393224 | tf_op jit(solution)/shard_map/output_conv/ppermute | solution.py:15
  62.3 1.9 %copy-start.3 = (bf16[4,1,128,128]{3,2,1,0:T(8,128)(2,1)}, bf16[4,1,128,128]{3,2,1,0:T(8,128)(2,1)S(1)}, u32[]{:S(2)}) copy-start(bf16[4,1,128,128]{3,2,1,0:T(8,128)(2,1)S(1)} %collective-permute-done.7.bottom_ref) | copy-start | bytes 393220
  64.3 0.7 copy-start.4

commit v4 on v3

--- a/solution.py
+++ b/solution.py
@@ -17,16 +17,8 @@
     return before, after
 
 
-def conv_taps(x, w_ref):
-    rows = x.shape[0] - 2
-    width, k = x.shape[1], x.shape[2]
-    m = w_ref.shape[3]
-    n = rows * width
-    lhs = jnp.concatenate([x[a : a + rows].reshape(n, k) for a in range(3)], axis=1)
-    weight = jnp.concatenate(
-        [jnp.concatenate([w_ref[a, b] for b in range(3)], axis=1) for a in range(3)], axis=0
-    )
-    acc = jnp.dot(lhs, weight, preferred_element_type=jnp.float32)
+def shifted_sum(acc, width, m):
+    n = acc.shape[0]
     column = lax.broadcasted_iota(jnp.int32, (n, m), 0) % width
     from_left = pltpu.roll(acc[:, :m], 1, 0)
     from_right = pltpu.roll(acc[:, 2 * m :], n - 1, 0)
@@ -36,7 +28,30 @@
     return total
 
 
-def input_kernel(decay_ref, top_ref, frame_ref, bottom_ref, w_ref, out_ref, state_ref):
+def tap_row(w_ref, a):
+    return jnp.concatenate([w_ref[a, b] for b in range(3)], axis=1)
+
+
+def conv_band(band_rows, w_ref):
+    rows, width, k = band_rows.shape
+    m = w_ref.shape[3]
+    n = rows * width
+    zero = jnp.zeros((1, width, k), band_rows.dtype)
+    x = jnp.concatenate([zero, band_rows, zero], axis=0)
+    lhs = jnp.concatenate([x[a : a + rows].reshape(n, k) for a in range(3)], axis=1)
+    weight = jnp.concatenate([tap_row(w_ref, a) for a in range(3)], axis=0)
+    acc = jnp.dot(lhs, weight, preferred_element_type=jnp.float32)
+    return shifted_sum(acc, width, m)
+
+
+def halo_effect(row, w_ref, a):
+    width = row.shape[0]
+    m = w_ref.shape[3]
+    acc = jnp.dot(row, tap_row(w_ref, a), preferred_element_type=jnp.float32)
+    return shifted_sum(acc, width, m)
+
+
+def input_kernel(decay_ref, frame_ref, w_ref, out_ref, state_ref):
     f = pl.program_id(0)
     band, width, m = out_ref.shape[1:]
 
@@ -44,74 +59,124 @@
     def _():
         state_ref[...] = jnp.zeros_like(state_ref)
 
-    x = jnp.concatenate([top_ref[0], frame_ref[0], bottom_ref[0]], axis=0)
-    drive = conv_taps(x, w_ref)
+    drive = conv_band(frame_ref[0], w_ref)
     state = decay_ref[pl.ds(f, 1), :] * state_ref[...] + drive
     state_ref[...] = state
     out_ref[0] = state.reshape(band, width, m)
 
 
+def input_edge_kernel(decay_ref, top_ref, bottom_ref, w_ref, out_ref):
+    count, _, width, m = out_ref.shape
+    upper = jnp.zeros((width, m), jnp.float32)
+    lower = jnp.zeros((width, m), jnp.float32)
+    for f in range(count):
+        rate = decay_ref[f : f + 1, :]
+        upper = rate * upper + halo_effect(top_ref[f, 0], w_ref, 0)
+        lower = rate * lower + halo_effect(bottom_ref[f, 0], w_ref, 2)
+        out_ref[f, 0] = upper
+        out_ref[f, 1] = lower
+
+
+def with_edges(local, edges):
+    return jnp.concatenate([local[:1] + edges[:1], local[1:-1], local[-1:] + edges[1:]], axis=0)
+
+
 def output_kernel(
-    cum_ref, skip_ref, incoming_ref, top_ref, local_ref, bottom_ref, frame_ref, w_ref, out_ref
+    cum_ref, skip_ref, incoming_ref, edge_ref, local_ref, frame_ref, w_ref, out_ref, rim_ref
 ):
     f = pl.program_id(0)
     band, width, m = out_ref.shape[1:]
-    inner = (local_ref[0] + cum_ref[pl.ds(f, 1), :] * incoming_ref[...]).astype(jnp.bfloat16)
-    x = jnp.concatenate([top_ref[0], inner, bottom_ref[0]], axis=0)
-    total = conv_taps(x, w_ref)
+    state = with_edges(local_ref[0], edge_ref[0])
+    inner = (state + cum_ref[pl.ds(f, 1), :] * incoming_ref[...]).astype(jnp.bfloat16)
+    total = conv_band(inner, w_ref)
     frame = frame_ref[0].reshape(band * width, m).astype(jnp.float32)
     total = total + skip_ref[...] * frame
     out_ref[0] = total.astype(jnp.bfloat16).reshape(band, width, m)
+    rim_ref[0, 0] = total[:width]
+    rim_ref[0, 1] = total[(band - 1) * width :]
+
+
+def output_edge_kernel(rim_ref, top_ref, bottom_ref, w_ref, out_ref):
+    count = rim_ref.shape[0]
+    for f in range(count):
+        out_ref[f, 0] = (rim_ref[f, 0] + halo_effect(top_ref[f, 0], w_ref, 0)).astype(jnp.bfloat16)
+        out_ref[f, 1] = (rim_ref[f, 1] + halo_effect(bottom_ref[f, 0], w_ref, 2)).astype(
+            jnp.bfloat16
+        )
+
+
+def whole(shape):
+    return pl.BlockSpec(shape, lambda: (0,) * len(shape))
 
 
 def input_stage(frames, conv_in, decay):
     count, band, width, channels = frames.shape
     state_width = conv_in.shape[3]
     top, bottom = halo_rows(frames, "rows", 1)
-    halo = pl.BlockSpec((1, 1, width, channels), lambda f: (f, 0, 0, 0))
-    return pl.pallas_call(
+    local = pl.pallas_call(
         input_kernel,
         grid=(count,),
         in_specs=[
             pl.BlockSpec((count, state_width), lambda f: (0, 0)),
-            halo,
             pl.BlockSpec((1, band, width, channels), lambda f: (f, 0, 0, 0)),
-            halo,
             pl.BlockSpec((3, 3, channels, state_width), lambda f: (0, 0, 0, 0)),
         ],
         out_specs=pl.BlockSpec((1, band, width, state_width), lambda f: (f, 0, 0, 0)),
         out_shape=jax.ShapeDtypeStruct((count, band, width, state_width), jnp.float32),
         scratch_shapes=[pltpu.VMEM((band * width, state_width), jnp.float32)],
         compiler_params=pltpu.CompilerParams(dimension_semantics=("arbitrary",)),
-    )(decay, top, frames, bottom, conv_in)
-
-
-def output_stage(local, cumulative, incoming, frames, conv_out, skip):
+    )(decay, frames, conv_in)
+    edges = pl.pallas_call(
+        input_edge_kernel,
+        in_specs=[
+            whole(decay.shape),
+            whole(top.shape),
+            whole(bottom.shape),
+            whole(conv_in.shape),
+        ],
+        out_specs=whole((count, 2, width, state_width)),
+        out_shape=jax.ShapeDtypeStruct((count, 2, width, state_width), jnp.float32),
+    )(decay, top, bottom, conv_in)
+    return local, edges
+
+
+def output_stage(local, edges, cumulative, incoming, frames, conv_out, skip):
     count, band, width, state_width = local.shape
     channels = conv_out.shape[3]
-    edges = jnp.concatenate([local[:, :1], local[:, -1:]], axis=1)
-    edges = edges + cumulative[:, None, None, :] * jnp.concatenate(
+    rims = jnp.concatenate([local[:, :1], local[:, -1:]], axis=1) + edges
+    rims = rims + cumulative[:, None, None, :] * jnp.concatenate(
         [incoming[None, :1], incoming[None, -1:]], axis=1
     )
-    top, bottom = halo_rows(edges.astype(jnp.bfloat16), "rows", 1)
-    halo = pl.BlockSpec((1, 1, width, state_width), lambda f: (f, 0, 0, 0))
-    return pl.pallas_call(
+    top, bottom = halo_rows(rims.astype(jnp.bfloat16), "rows", 1)
+    body, rim = pl.pallas_call(
         output_kernel,
         grid=(count,),
         in_specs=[
             pl.BlockSpec((count, state_width), lambda f: (0, 0)),
             pl.BlockSpec((1, channels), lambda f: (0, 0)),
             pl.BlockSpec((band, width, state_width), lambda f: (0, 0, 0)),
-            halo,
+            pl.BlockSpec((1, 2, width, state_width), lambda f: (f, 0, 0, 0)),
             pl.BlockSpec((1, band, width, state_width), lambda f: (f, 0, 0, 0)),
-            halo,
             pl.BlockSpec((1, band, width, channels), lambda f: (f, 0, 0, 0)),
             pl.BlockSpec((3, 3, state_width, channels), lambda f: (0, 0, 0, 0)),
         ],
-        out_specs=pl.BlockSpec((1, band, width, channels), lambda f: (f, 0, 0, 0)),
-        out_shape=jax.ShapeDtypeStruct((count, band, width, channels), jnp.bfloat16),
+        out_specs=[
+            pl.BlockSpec((1, band, width, channels), lambda f: (f, 0, 0, 0)),
+            pl.BlockSpec((1, 2, width, channels), lambda f: (f, 0, 0, 0)),
+        ],
+        out_shape=[
+            jax.ShapeDtypeStruct((count, band, width, channels), jnp.bfloat16),
+            jax.ShapeDtypeStruct((count, 2, width, channels), jnp.float32),
+        ],
         compiler_params=pltpu.CompilerParams(dimension_semantics=("arbitrary",)),
-    )(cumulative, skip.reshape(1, channels), incoming, top, local, bottom, frames, conv_out)
+    )(cumulative, skip.reshape(1, channels), incoming, edges, local, frames, conv_out)
+    fixed = pl.pallas_call(
+        output_edge_kernel,
+        in_specs=[whole(rim.shape), whole(top.shape), whole(bottom.shape), whole(conv_out.shape)],
+        out_specs=whole((count, 2, width, channels)),
+        out_shape=jax.ShapeDtypeStruct((count, 2, width, channels), jnp.bfloat16),
+    )(rim, top, bottom, conv_out)
+    return body.at[:, :1].set(fixed[:, :1]).at[:, -1:].set(fixed[:, 1:])
 
 
 def split3(p, rows):
@@ -159,11 +224,11 @@
             running.append(running[-1] * decay[frame_index])
         cumulative = jnp.stack(running)
     with jax.named_scope("input_conv_and_recurrence"):
-        local = input_stage(frames, conv_in, decay)
+        local, edges = input_stage(frames, conv_in, decay)
     with jax.named_scope("carry_across_blocks"):
-        incoming = incoming_state(cumulative[-1], local[-1], "tm")
+        incoming = incoming_state(cumulative[-1], with_edges(local[-1], edges[-1]), "tm")
     with jax.named_scope("output_conv"):
-        return output_stage(local, cumulative, incoming, frames, conv_out, skip)
+        return output_stage(local, edges, cumulative, incoming, frames, conv_out, skip)
 
 
 def solution(mesh):

time: 71 us -> 82.2 us (1.16)
  Pallas kernels: 10.7 us -> 15.3 us
  local copies, waits for them, and re-layouts: 4.5 us -> 8.25 us
  waiting for transfers between devices: 36.3 us -> 38.2 us
  other arithmetic: 1.87 us -> 2.86 us
    ppermute x4, waiting for transfers between devices: 33.3 us -> 38.2 us  [incoming_state(): got = lax.ppermute(payload, axis, pairs)]
    pallas_call x0 -> x2, Pallas kernels: none -> 4.58 us  [the longest x1 2.29 us: output_stage(): pl.pallas_call(output_edge_kernel, in_specs=[whole(rim.shape), whole(top....]
    scatter x0 -> x2, local copies, waits for them, and re-layouts: none -> 3.17 us  [output_stage(): return body.at[:, :1].set(fixed[:, :1]).at[:, -1:].set(fixed[:, 1:])]
    ppermute x2, waiting for transfers between devices: 2.98 us -> 0.01 us  [halo_rows(): before = lax.ppermute(last, axis, up)]
    add x0 -> x1, other arithmetic: none -> 0.95 us  [with_edges(): local[:1] + edges[:1]]
    unnamed x12 -> x14, local copies, waits for them, and re-layouts: 1.32 us -> 1.96 us
  transfers between devices with their start and end apart: 8 -> 8, of which waited for: 6 -> 4; matrix products, arithmetic and copies ran while one was open for 3% -> 4% of each run, Pallas kernels for 0% -> 13%
where the time goes in v4:
time: 82.2 us; the launch traced here: 81.6 us
  waiting for transfers between devices  38.2 us (46%)
  starting transfers between devices  16.6 us (20%)
  Pallas kernels  15.3 us (19%)
  local copies, waits for them, and re-layouts  8.25 us (10%)
  other arithmetic  2.86 us (3%)
    ppermute x4, waiting for transfers between devices, incoming_state(): got = lax.ppermute(payload, axis, pairs)  38.2 us
    ppermute x4, starting transfers between devices, incoming_state(): got = lax.ppermute(payload, axis, pairs)  7.95 us
    ppermute x2, starting transfers between devices, halo_rows(): after = lax.ppermute(first, axis, down)  6.08 us
    pallas_call x1, Pallas kernels, output_stage(): pl.pallas_call(output_kernel, grid=(count,), in_specs=[pl.BlockSpec((coun...  5.72 us
    pallas_call x1, Pallas kernels, input_stage(): pl.pallas_call(input_kernel, grid=(count,), in_specs=[pl.BlockSpec((count...  5.03 us
    scatter x2, local copies, waits for them, and re-layouts, output_stage(): return body.at[:, :1].set(fixed[:, :1]).at[:, -1:].set(fixed[:, 1:])  3.17 us
    ppermute x2, starting transfers between devices, halo_rows(): before = lax.ppermute(last, axis, up)  2.58 us
    pallas_call x1, Pallas kernels, output_stage(): pl.pallas_call(output_edge_kernel, in_specs=[whole(rim.shape), whole(top....  2.29 us
  transfers between devices with their start and end apart: 8, of which 4 were waited for; matrix products, arithmetic and copies ran while one was open for 4% of the time, Pallas kernels for 13%

profile of v4, /device:TPU:25, one launch (start us, length us, event | category | flops | bytes accessed | tf_op | source)
XLA Modules:
  0.0 81.6 jit_solution(11780489912177134142)
XLA Ops:
  0.0 1.0 %fusion.34 = (bf16[4,1,128,128]{3,2,1,0:T(8,128)(2,1)S(1)}, bf16[4,1,128,128]{3,2,1,0:T(8,128)(2,1)S(1)}) fusion(bf16[4,8,128,128]{3,2,1,0:T(8,128)(2,1)} %frame_ref.3), kind=kLoop, calls=%fused_computation.84 | loop fusion | bytes 524288 | tf_op jit(solution)/shard_map/input_conv_and_recurrence/slice | solution.py:14
  1.0 1.3 %collective-permute-start = (bf16[4,1,128,128]{3,2,1,0:T(8,128)(2,1)S(1)}, bf16[4,1,128,128]{3,2,1,0:T(8,128)(2,1)S(1)}, u32[]{:S(2)}, u32[]{:S(2)}) collective-permute-start(bf16[4,1,128,128]{3,2,1,0:T(8,128)(2,1)S(1)} %get-tuple-element.50), channel_id=1, source_target_pairs={{0,1},{2,3},{4,5},{6,7},{8,9},{10,11},{12,13},{14,15},{16,17},{18,... | collective-permute-start | bytes 393224 | tf_op jit(solution)/shard_map/input_conv_and_recurrence/ppermute | solution.py:15
  2.3 3.0 %collective-permute-start.1 = (bf16[4,1,128,128]{3,2,1,0:T(8,128)(2,1)S(1)}, bf16[4,1,128,128]{3,2,1,0:T(8,128)(2,1)S(1)}, u32[]{:S(2)}, u32[]{:S(2)}) collective-permute-start(bf16[4,1,128,128]{3,2,1,0:T(8,128)(2,1)S(1)} %get-tuple-element.49), channel_id=1, source_target_pairs={{1,0},{3,2},{5,4},{7,6},{9,8},{11,10},{13,12},{15,14},{17,16},{19,... | collective-permute-start | bytes 393224 | tf_op jit(solution)/shard_map/input_conv_and_recurrence/ppermute | solution.py:16
  5.3 0.8 %reduce-precision_convert_fusion.7 = (bf16[1,128]{1,0:T(2,128)(2,1)S(1)}, f32[1,128]{1,0:T(1,128)S(1)}, f32[1,128]{1,0:T(1,128)S(1)}, f32[1,128]{1,0:T(1,128)S(1)}, f32[1,128]{1,0:T(1,128)S(1)}) fusion(f32[4,128]{1,0:T(4,128)} %decay_ref.3), kind=kLoop, calls=%fused_computation.69 | loop fusion | flops 640 | bytes 4352 | tf_op jit(solution)/shard_map/convert.10
  6.2 5.0 %input_conv_and_recurrence.2.local_ref = f32[4,8,128,128]{3,2,1,0:T(8,128)} custom-call(f32[4,128]{1,0:T(4,128)} %decay_ref.3, bf16[4,8,128,128]{3,2,1,0:T(8,128)(2,1)} %frame_ref.3, bf16[3,3,128,128]{3,2,1,0:T(8,128)(2,1)} %w_ref.5), custom_call_target="tpu_custom_call" | custom-call | tf_op jit(solution)/shard_map/input_conv_and_recurrence/pallas_call | solution.py:116
  11.2 1.0 %slice_bitcast_fusion = f32[6,128,128]{2,1,0:T(8,128)S(1)} fusion(f32[4,8,128,128]{3,2,1,0:T(8,128)} %input_conv_and_recurrence.2.local_ref), kind=kLoop, calls=%fused_computation.10 | loop fusion | bytes 786432 | tf_op jit(solution)/shard_map/carry_across_blocks/slice | solution.py:81
  12.3 0.0 collective-permute-done.top_ref
  12.3 0.0 copy-start.2
  12.3 0.0 collective-permute-done.1.bottom_ref
  12.3 0.6 copy-done.2
  12.9 0.0 copy-start.3
  12.9 0.6 copy-done.3
  13.6 2.3 %input_conv_and_recurrence.3.edge_ref = f32[4,2,128,128]{3,2,1,0:T(8,128)} custom-call(f32[4,128]{1,0:T(4,128)} %decay_ref.3, bf16[4,1,128,128]{3,2,1,0:T(8,128)(2,1)} %copy-done.2, bf16[4,1,128,128]{3,2,1,0:T(8,128)(2,1)} %copy-done.3, bf16[3,3,128,128]{3,2,1,0:T(8,128)(2,1)} %w_ref.5), custom_call_target="tpu_custom_call" | custom-call | tf_op jit(solution)/shard_map/input_conv_and_recurrence/pallas_call | solution.py:129
  15.9 0.9 %fusion.6 = (f32[1,128,128]{2,1,0:T(8,128)S(1)}, f32[1,128,128]{2,1,0:T(8,128)S(1)}) fusion(f32[4,2,128,128]{3,2,1,0:T(8,128)} %input_conv_and_recurrence.3.edge_ref, f32[4,8,128,128]{3,2,1,0:T(8,128)} %input_conv_and_recurrence.2.local_ref), kind=kLoop, calls=%fused_computation.28 | loop fusion | flops 32768 | bytes 393216 | tf_op jit(solution)/shard_map/carry_across_blocks/add | solution.py:81
  16.9 3.1 %collective-permute-start.2 = (bf16[1040,128]{1,0:T(8,128)(2,1)S(1)}, bf16[1040,128]{1,0:T(8,128)(2,1)S(1)}, u32[]{:S(2)}, u32[]{:S(2)}) collective-permute-start(bf16[1040,128]{1,0:T(8,128)(2,1)S(1)} %pad_maximum_fusion.1), channel_id=1, source_target_pairs={{0,2},{2,4},{4,6},{6,8},{8,10},{10,12},{12,14},{14,16},{16,18},{18... | collective-permute-start | bytes 798728 | tf_op jit(solution)/shard_map/carry_across_blocks/ppermute | solution.py:203
  20.0 8.7 %collective-permute-done.2 = bf16[1040,128]{1,0:T(8,128)(2,1)S(1)} collective-permute-done((bf16[1040,128]{1,0:T(8,128)(2,1)S(1)}, bf16[1040,128]{1,0:T(8,128)(2,1)S(1)}, u32[]{:S(2)}, u32[]{:S(2)}) %collective-permute-start.2) | collective-permute-done | bytes 266272 | tf_op jit(solution)/shard_map/carry_across_blocks/ppermute | solution.py:203
  28.8 0.1 fusion.4
  28.9 2.2 %collective-permute-start.3 = (bf16[1040,128]{1,0:T(8,128)(2,1)S(1)}, bf16[1040,128]{1,0:T(8,128)(2,1)S(1)}, u32[]{:S(2)}, u32[]{:S(2)}) collective-permute-start(bf16[1040,128]{1,0:T(8,128)(2,1)S(1)} %pad_maximum_fusion.2), channel_id=1, source_target_pairs={{0,4},{2,6},{4,8},{6,10},{8,12},{10,14},{12,16},{14,18},{16,20},{1... | collective-permute-start | bytes 798728 | tf_op jit(solution)/shard_map/carry_across_blocks/ppermute | solution.py:203
  31.1 0.0 copy-start.6
  31.1 1.1 %fusion.33 = (f32[4,1,128,128]{3,2,1,0:T(8,128)S(1)}, f32[4,1,128,128]{3,2,1,0:T(8,128)S(1)}) fusion(f32[4,8,128,128]{3,2,1,0:T(8,128)} %input_conv_and_recurrence.2.local_ref), kind=kLoop, calls=%fused_computation.83 | loop fusion | bytes 1048576 | tf_op jit(solution)/shard_map/output_conv/slice | solution.py:146
  32.2 7.0 %collective-permute-done.3 = bf16[1040,128]{1,0:T(8,128)(2,1)S(1)} collective-permute-done((bf16[1040,128]{1,0:T(8,128)(2,1)S(1)}, bf16[1040,128]{1,0:T(8,128)(2,1)S(1)}, u32[]{:S(2)}, u32[]{:S(2)}) %collective-permute-start.3) | collective-permute-done | bytes 266272 | tf_op jit(solution)/shard_map/carry_across_blocks/ppermute | solution.py:203
  39.3 0.1 fusion.3
  39.5 1.3 %collective-permute-start.4 = (bf16[1040,128]{1,0:T(8,128)(2,1)S(1)}, bf16[1040,128]{1,0:T(8,128)(2,1)S(1)}, u32[]{:S(2)}, u32[]{:S(2)}) collective-permute-start(bf16[1040,128]{1,0:T(8,128)(2,1)S(1)} %pad_maximum_fusion.3), channel_id=1, source_target_pairs={{0,8},{2,10},{4,12},{6,14},{8,16},{10,18},{12,20},{14,22},{16,24},... | collective-permute-start | bytes 798728 | tf_op jit(solution)/shard_map/carry_across_blocks/ppermute | solution.py:203
  40.9 7.2 %collective-permute-done.4 = bf16[1040,128]{1,0:T(8,128)(2,1)S(1)} collective-permute-done((bf16[1040,128]{1,0:T(8,128)(2,1)S(1)}, bf16[1040,128]{1,0:T(8,128)(2,1)S(1)}, u32[]{:S(2)}, u32[]{:S(2)}) %collective-permute-start.4) | collective-permute-done | bytes 266272 | tf_op jit(solution)/shard_map/carry_across_blocks/ppermute | solution.py:203
  48.1 0.2 add_convert_fusion
  48.3 1.3 %collective-permute-start.5 = (bf16[1040,128]{1,0:T(8,128)(2,1)S(1)}, bf16[1040,128]{1,0:T(8,128)(2,1)S(1)}, u32[]{:S(2)}, u32[]{:S(2)}) collective-permute-start(bf16[1040,128]{1,0:T(8,128)(2,1)S(1)} %pad_maximum_fusion.4), channel_id=1, source_target_pairs={{0,16},{2,18},{4,20},{6,22},{8,24},{10,26},{12,28},{14,30},{1,17},... | collective-permute-start | bytes 798728 | tf_op jit(solution)/shard_map/carry_across_blocks/ppermute | solution.py:203
  49.6 0.0 copy-start
  49.7 15.3 %collective-permute-done.5 = bf16[1040,128]{1,0:T(8,128)(2,1)S(1)} collective-permute-done((bf16[1040,128]{1,0:T(8,128)(2,1)S(1)}, bf16[1040,128]{1,0:T(8,128)(2,1)S(1)}, u32[]{:S(2)}, u32[]{:S(2)}) %collective-permute-start.5) | collective-permute-done | bytes 266272 | tf_op jit(solution)/shard_map/carry_across_blocks/ppermute | solution.py:203
  65.0 0.1 fusion.2.incoming_ref
  65.2 0.0 copy-start.1
  65.2 0.0 copy-done.6
  65.2 0.0 copy-done
  65.2 0.1 fusion.1
  65.3 1.3 %collective-permute-start.6 = (bf16[4,1,128,128]{3,2,1,0:T(8,128)(2,1)S(1)}, bf16[4,1,128,128]{3,2,1,0:T(8,128)(2,1)S(1)}, u32[]{:S(2)}, u32[]{:S(2)}) collective-permute-start(bf16[4,1,128,128]{3,2,1,0:T(8,128)(2,1)S(1)} %get-tuple-element.54), channel_id=1, source_target_pairs={{0,1},{2,3},{4,5},{6,7},{8,9},{10,11},{12,13},{14,15},{16,17},{18,... | collective-permute-start | bytes 393224 | tf_op jit(solution)/shard_map/output_conv/ppermute | solution.py:15
  66.6 3.0 %collective-permute-start.7 = (bf16[4,1,128,128]{3,2,1,0:T(8,128)(2,1)S(1)}, bf16[4,1,128,128]{3,2,1,0:T(8,128)(2,1)S(1)}, u32[]{:S(2)}, u32[]{:S(2)}) collective-permute-start(bf16[4,1,128,128]{3,2,1,0:T(8,128)(2,1)S(1)} %get-tuple-element.53), channel_id=1, source_target_pairs={{1,0},{3,2},{5,4},{7,6},{9,8},{11,10},{13,12},{15,14},{17,16},{19,... | collective-permute-start | bytes 393224 | tf_op jit(solution)/shard_map/output_conv/ppermute | solution.py:16
  69.7 0.0 copy-done.1
  69.7 5.7 %output_conv.2 = (bf16[4,8,128,128]{3,2,1,0:T(8,128)(2,1)}, f32[4,2,128,128]{3,2,1,0:T(8,128)}) custom-call(f32[4,128]{1,0:T(4,128)} %copy-done.6, f32[1,128]{1,0:T(1,128)} %bitcast.51, f32[8,128,128]{2,1,0:T(8,128)} %copy-done.1, f32[4,2,128,128]{3,2,1,0:T(8,128)} %input_conv_and_recurrence.3.edge_ref, ...), custom_call_target="tpu_custom_call" | custom-call | tf_op jit(solution)/shard_map/output_conv/pallas_call | solution.py:151
  75.4 0.0 collective-permute-done.6.top_ref
  75.4 0.0 copy-start.4
  75.4 0.0 collective-permute-done.7.bottom_ref
  75.4 0.0 copy-start.5
  75.5 0.6 copy-done.4
  76.1 0.0 copy-done.5
  76.1 2.3 %output_conv.3 = bf16[4,2,128,128]{3,2,1,0:T(8,128)(2,1)} custom-call(f32[4,2,128,128]{3,2,1,0:T(8,128)} %get-tuple-element.32.rim_ref, bf16[4,1,128,128]{3,2,1,0:T(8,128)(2,1)} %copy-done.4, bf16[4,1,128,128]{3,2,1,0:T(8,128)(2,1)} %copy-done.5, bf16[3,3,128,128]{3,2,1,0:T(8,128)(2,1)} %w_ref.7), custom_call_target="tpu_custom_call" | custom-call | tf_op jit(solution)/shard_map/output_conv/pallas_call | solution.py:173
  78.4 1.6 %slice_dynamic-update-slice_fusion.1 = bf16[4,8,128,128]{3,2,1,0:T(8,128)(2,1)} fusion(bf16[4,8,128,128]{3,2,1,0:T(8,128)(2,1)} %get-tuple-element.31, bf16[4,2,128,128]{3,2,1,0:T(8,128)(2,1)} %output_conv.3), kind=kLoop, calls=%fused_computation.20 | loop fusion | bytes 262144 | tf_op jit(solution)/shard_map/output_conv/scatter | solution.py:179
  80.0 1.6 %slice_dynamic-update-slice_fusion = bf16[4,8,128,128]{3,2,1,0:T(8,128)(2,1)} fusion(bf16[4,8,128,128]{3,2,1,0:T(8,128)(2,1)} %slice_dynamic-update-slice_fusion.1, bf16[4,2,128,128]{3,2,1,0:T(8,128)(2,1)} %output_conv.3), kind=kLoop, calls=%fused_computation.19 | loop fusion | bytes 262144 | tf_op jit(solution)/shard_map/output_conv/scatter | solution.py:179
  (29 shorter events, 0.5 us)
Async XLA Ops:
  1.0 11.3 %collective-permute-start = (bf16[4,1,128,128]{3,2,1,0:T(8,128)(2,1)S(1)}, bf16[4,1,128,128]{3,2,1,0:T(8,128)(2,1)S(1)}, u32[]{:S(2)}, u32[]{:S(2)}) collective-permute-start(bf16[4,1,128,128]{3,2,1,0:T(8,128)(2,1)S(1)} %get-tuple-element.50), channel_id=1, source_target_pairs={{0,1},{2,3},{4,5},{6,7},{8,9},{10,11},{12,13},{14,15},{16,17},{18,... | collective-permute-start | bytes 393224 | tf_op jit(solution)/shard_map/input_conv_and_recurrence/ppermute | solution.py:15
  2.3 10.0 %collective-permute-start.1 = (bf16[4,1,128,128]{3,2,1,0:T(8,128)(2,1)S(1)}, bf16[4,1,128,128]{3,2,1,0:T(8,128)(2,1)S(1)}, u32[]{:S(2)}, u32[]{:S(2)}) collective-permute-start(bf16[4,1,128,128]{3,2,1,0:T(8,128)(2,1)S(1)} %get-tuple-element.49), channel_id=1, source_target_pairs={{1,0},{3,2},{5,4},{7,6},{9,8},{11,10},{13,12},{15,14},{17,16},{19,... | collective-permute-start | bytes 393224 | tf_op jit(solution)/shard_map/input_conv_and_recurrence/ppermute | solution.py:16
  12.3 0.7 copy-start.2
  12.9 0.6 copy-start.3
  16.9 11.8 %collective-permute-start.2 = (bf16[1040,128]{1,0:T(8,128)(2,1)S(1)}, bf16[1040,128]{1,0:T(8,128)(2,1)S(1)}, u32[]{:S(2)}, u32[]{:S(2)}) collective-permute-start(bf16[1040,128]{1,0:T(8,128)(2,1)S(1)} %pad_maximum_fusion.1), channel_id=1, source_target_pairs={{0,2},{2,4},{4,6},{6,8},{8,10},{10,12},{12,14},{14,16},{16,18},{18... | collective-permute-start | bytes 798728 | tf_op jit(solution)/shard_map/carry_across_blocks/ppermute | solution.py:203
  28.9 10.4 %collective-permute-start.3 = (bf16[1040,128]{1,0:T(8,128)(2,1)S(1)}, bf16[1040,128]{1,0:T(8,128)(2,1)S(1)}, u32[]{:S(2)}, u32[]{:S(2)}) collective-permute-start(bf16[1040,128]{1,0:T(8,128)(2,1)S(1)} %pad_maximum_fusion.2), channel_id=1, source_target_pairs={{0,4},{2,6},{4,8},{6,10},{8,12},{10,14},{12,16},{14,18},{16,20},{1... | collective-permute-start | bytes 798728 | tf_op jit(solution)/shard_map/carry_across_blocks/ppermute | solution.py:203
  31.1 34.1 %copy-start.6 = (f32[4,128]{1,0:T(4,128)}, f32[4,128]{1,0:T(4,128)S(1)}, u32[]{:S(2)}) copy-start(f32[4,128]{1,0:T(4,128)S(1)} %pad_maximum_fusion.5.cum_ref) | copy-start | bytes 6148
  39.5 8.6 %collective-permute-start.4 = (bf16[1040,128]{1,0:T(8,128)(2,1)S(1)}, bf16[1040,128]{1,0:T(8,128)(2,1)S(1)}, u32[]{:S(2)}, u32[]{:S(2)}) collective-permute-start(bf16[1040,128]{1,0:T(8,128)(2,1)S(1)} %pad_maximum_fusion.3), channel_id=1, source_target_pairs={{0,8},{2,10},{4,12},{6,14},{8,16},{10,18},{12,20},{14,22},{16,24},... | collective-permute-start | bytes 798728 | tf_op jit(solution)/shard_map/carry_across_blocks/ppermute | solution.py:203
  48.3 16.7 %collective-permute-start.5 = (bf16[1040,128]{1,0:T(8,128)(2,1)S(1)}, bf16[1040,128]{1,0:T(8,128)(2,1)S(1)}, u32[]{:S(2)}, u32[]{:S(2)}) collective-permute-start(bf16[1040,128]{1,0:T(8,128)(2,1)S(1)} %pad_maximum_fusion.4), channel_id=1, source_target_pairs={{0,16},{2,18},{4,20},{6,22},{8,24},{10,26},{12,28},{14,30},{1,17},... | collective-permute-start | bytes 798728 | tf_op jit(solution)/shard_map/carry_across_blocks/ppermute | solution.py:203
  49.6 15.6 %copy-start = (f32[4,2,128,128]{3,2,1,0:T(8,128)S(1)}, f32[4,2,128,128]{3,2,1,0:T(8,128)}, u32[]{:S(2)}) copy-start(f32[4,2,128,128]{3,2,1,0:T(8,128)} %input_conv_and_recurrence.3.edge_ref) | copy-start | bytes 1572868
  65.2 4.5 %copy-start.1 = (f32[8,128,128]{2,1,0:T(8,128)}, f32[8,128,128]{2,1,0:T(8,128)S(1)}, u32[]{:S(2)}) copy-start(f32[8,128,128]{2,1,0:T(8,128)S(1)} %fusion.2.incoming_ref) | copy-start | bytes 1572868
  65.3 10.1 %collective-permute-start.6 = (bf16[4,1,128,128]{3,2,1,0:T(8,128)(2,1)S(1)}, bf16[4,1,128,128]{3,2,1,0:T(8,128)(2,1)S(1)}, u32[]{:S(2)}, u32[]{:S(2)}) collective-permute-start(bf16[4,1,128,128]{3,2,1,0:T(8,128)(2,1)S(1)} %get-tuple-element.54), channel_id=1, source_target_pairs={{0,1},{2,3},{4,5},{6,7},{8,9},{10,11},{12,13},{14,15},{16,17},{18,... | collective-permute-start | bytes 393224 | tf_op jit(solution)/shard_map/output_conv/ppermute | solution.py:15
  66.6 8.8 %collective-permute-start.7 = (bf16[4,1,128,128]{3,2,1,0:T(8,128)(2,1)S(1)}, bf16[4,1,128,128]{3,2,1,0:T(8,128)(2,1)S(1)}, u32[]{:S(2)}, u32[]{:S(2)}) collective-permute-start(bf16[4,1,128,128]{3,2,1,0:T(8,128)(2,1)S(1)} %get-tuple-element.53), channel_id=1, source_target_pairs={{1,0},{3,2},{5,4},{7,6},{9,8},{11,10},{13,12},{15,14},{17,16},{19,... | collective-permute-start | bytes 393224 | tf_op jit(solution)/shard_map/output_conv/ppermute | solution.py:16
  75.4 0.6 copy-start.4
  75.4 0.7 copy-start.5

commit v5 on v3

--- a/solution.py
+++ b/solution.py
@@ -8,6 +8,13 @@
 
 def halo_rows(x, axis, dim):
     size, length = (lax.axis_size(axis), x.shape[dim])
+    if size == 2:
+        upper = lax.axis_index(axis) == 0
+        last = lax.slice_in_dim(x, length - 1, length, axis=dim)
+        first = lax.slice_in_dim(x, 0, 1, axis=dim)
+        got = lax.ppermute(jnp.where(upper, last, first), axis, [(0, 1), (1, 0)])
+        zero = jnp.zeros_like(got)
+        return jnp.where(upper, zero, got), jnp.where(upper, got, zero)
     up = [(i, (i + 1) % size) for i in range(size - 1)]
     down = [(j, i) for i, j in up]
     last = lax.slice_in_dim(x, length - 1, length, axis=dim)
@@ -36,19 +43,38 @@
     return total
 
 
-def input_kernel(decay_ref, top_ref, frame_ref, bottom_ref, w_ref, out_ref, state_ref):
+def input_kernel(
+    decay_ref, top_ref, frame_ref, bottom_ref, w_ref, out_ref, cum_ref, send_ref, state_ref, power_ref
+):
     f = pl.program_id(0)
     band, width, m = out_ref.shape[1:]
+    cells = band * width
 
     @pl.when(f == 0)
     def _():
         state_ref[...] = jnp.zeros_like(state_ref)
+        power_ref[...] = jnp.ones_like(power_ref)
 
     x = jnp.concatenate([top_ref[0], frame_ref[0], bottom_ref[0]], axis=0)
     drive = conv_taps(x, w_ref)
-    state = decay_ref[pl.ds(f, 1), :] * state_ref[...] + drive
+    rate = decay_ref[pl.ds(f, 1), :]
+    state = rate * state_ref[...] + drive
+    power = rate * power_ref[...]
     state_ref[...] = state
+    power_ref[...] = power
     out_ref[0] = state.reshape(band, width, m)
+    cum_ref[pl.ds(f, 1), :] = power
+
+    @pl.when(f == pl.num_programs(0) - 1)
+    def _():
+        hi = power.astype(jnp.bfloat16)
+        rest = power - hi.astype(jnp.float32)
+        mid = rest.astype(jnp.bfloat16)
+        low = (rest - mid.astype(jnp.float32)).astype(jnp.bfloat16)
+        pad = send_ref.shape[0] - cells - 3
+        send_ref[...] = jnp.concatenate(
+            [state.astype(jnp.bfloat16), hi, mid, low, jnp.zeros((pad, m), jnp.bfloat16)], axis=0
+        )
 
 
 def output_kernel(
@@ -69,6 +95,7 @@
     state_width = conv_in.shape[3]
     top, bottom = halo_rows(frames, "rows", 1)
     halo = pl.BlockSpec((1, 1, width, channels), lambda f: (f, 0, 0, 0))
+    payload_rows = band * width + 16
     return pl.pallas_call(
         input_kernel,
         grid=(count,),
@@ -79,9 +106,20 @@
             halo,
             pl.BlockSpec((3, 3, channels, state_width), lambda f: (0, 0, 0, 0)),
         ],
-        out_specs=pl.BlockSpec((1, band, width, state_width), lambda f: (f, 0, 0, 0)),
-        out_shape=jax.ShapeDtypeStruct((count, band, width, state_width), jnp.float32),
-        scratch_shapes=[pltpu.VMEM((band * width, state_width), jnp.float32)],
+        out_specs=[
+            pl.BlockSpec((1, band, width, state_width), lambda f: (f, 0, 0, 0)),
+            pl.BlockSpec((count, state_width), lambda f: (0, 0)),
+            pl.BlockSpec((payload_rows, state_width), lambda f: (0, 0)),
+        ],
+        out_shape=[
+            jax.ShapeDtypeStruct((count, band, width, state_width), jnp.float32),
+            jax.ShapeDtypeStruct((count, state_width), jnp.float32),
+            jax.ShapeDtypeStruct((payload_rows, state_width), jnp.bfloat16),
+        ],
+        scratch_shapes=[
+            pltpu.VMEM((band * width, state_width), jnp.float32),
+            pltpu.VMEM((1, state_width), jnp.float32),
+        ],
         compiler_params=pltpu.CompilerParams(dimension_semantics=("arbitrary",)),
     )(decay, top, frames, bottom, conv_in)
 
@@ -123,19 +161,22 @@
     return jnp.pad(parts, ((0, rows - 3), (0, 0)))
 
 
-def incoming_state(power, state, axis):
+def incoming_state(power, state, first_payload, axis):
     n = lax.axis_size(axis)
     rows, width, channels = state.shape
     cells = rows * width
     win_p, win_s = power, state
     acc_p, acc_s = None, None
+    payload = first_payload
     shift = 1
     while shift < n:
         pairs = [(i, i + shift) for i in range(n - shift)]
-        payload = jnp.concatenate(
-            [win_s.astype(jnp.bfloat16).reshape(cells, channels), split3(win_p, 16)], axis=0
-        )
+        if payload is None:
+            payload = jnp.concatenate(
+                [win_s.astype(jnp.bfloat16).reshape(cells, channels), split3(win_p, 16)], axis=0
+            )
         got = lax.ppermute(payload, axis, pairs)
+        payload = None
         got_s = got[:cells].astype(jnp.float32).reshape(rows, width, channels)
         got_p = jnp.sum(got[cells : cells + 3].astype(jnp.float32), axis=0)
         if acc_s is None:
@@ -153,15 +194,10 @@
 
 
 def shards(frames, conv_in, decay, conv_out, skip):
-    with jax.named_scope("block_decay_products"):
-        running = [decay[0]]
-        for frame_index in range(1, decay.shape[0]):
-            running.append(running[-1] * decay[frame_index])
-        cumulative = jnp.stack(running)
     with jax.named_scope("input_conv_and_recurrence"):
-        local = input_stage(frames, conv_in, decay)
+        local, cumulative, first_payload = input_stage(frames, conv_in, decay)
     with jax.named_scope("carry_across_blocks"):
-        incoming = incoming_state(cumulative[-1], local[-1], "tm")
+        incoming = incoming_state(cumulative[-1], local[-1], first_payload, "tm")
     with jax.named_scope("output_conv"):
         return output_stage(local, cumulative, incoming, frames, conv_out, skip)
 

time: 71 us -> 64 us (0.901)
  starting transfers between devices: 16.9 us -> 9.96 us
  local copies, waits for them, and re-layouts: 4.5 us -> 2.19 us
  other arithmetic: 1.87 us -> 4.06 us
    ppermute x4 -> x2, starting transfers between devices: 8.91 us -> 2.01 us  [halo_rows(): got = lax.ppermute(jnp.where(upper, last, first), axis, [(0, 1), (1, 0)])]
    select_n x0 -> x4, other arithmetic: none -> 2.45 us  [the longest x2 1.45 us: halo_rows(): return (jnp.where(upper, zero, got), jnp.where(upper, got, zero))]
    unnamed x12 -> x4, local copies, waits for them, and re-layouts: 1.32 us -> 0.01 us
    ppermute x4, waiting for transfers between devices: 33.3 us -> 34.4 us  [incoming_state(): got = lax.ppermute(payload, axis, pairs)]
    ppermute x4 -> x2, waiting for transfers between devices: 2.99 us -> 1.97 us  [halo_rows(): got = lax.ppermute(jnp.where(upper, last, first), axis, [(0, 1), (1, 0)])]
    slice x3 -> x1, local copies, waits for them, and re-layouts: 2.08 us -> 1.08 us  [shards(): incoming = incoming_state(cumulative[-1], local[-1], first_payload, 'tm')]
  transfers between devices with their start and end apart: 8 -> 6, of which waited for: 6 -> 6; matrix products, arithmetic and copies ran while one was open for 3% -> 4% of each run, Pallas kernels for 0% -> 0%
where the time goes in v5:
time: 64 us; the launch traced here: 63.6 us
  waiting for transfers between devices  36.4 us (57%)
  Pallas kernels  10.8 us (17%)
  starting transfers between devices  9.96 us (16%)
  other arithmetic  4.06 us (6%)
  local copies, waits for them, and re-layouts  2.19 us (3%)
    ppermute x4, waiting for transfers between devices, incoming_state(): got = lax.ppermute(payload, axis, pairs)  34.4 us
    ppermute x4, starting transfers between devices, incoming_state(): got = lax.ppermute(payload, axis, pairs)  7.95 us
    pallas_call x1, Pallas kernels, output_stage(): pl.pallas_call(output_kernel, grid=(count,), in_specs=[pl.BlockSpec((coun...  5.58 us
    pallas_call x1, Pallas kernels, input_stage(): pl.pallas_call(input_kernel, grid=(count,), in_specs=[pl.BlockSpec((count...  5.25 us
    ppermute x2, starting transfers between devices, halo_rows(): got = lax.ppermute(jnp.where(upper, last, first), axis, [(0, 1), (1, 0)])  2.01 us
    ppermute x2, waiting for transfers between devices, halo_rows(): got = lax.ppermute(jnp.where(upper, last, first), axis, [(0, 1), (1, 0)])  1.97 us
    select_n x2, other arithmetic, halo_rows(): return (jnp.where(upper, zero, got), jnp.where(upper, got, zero))  1.45 us
  transfers between devices with their start and end apart: 6, of which 6 were waited for; matrix products, arithmetic and copies ran while one was open for 4% of the time, Pallas kernels for 0%

profile of v5, /device:TPU:25, one launch (start us, length us, event | category | flops | bytes accessed | tf_op | source)
XLA Modules:
  0.0 63.6 jit_solution(11522474557403435319)
XLA Ops:
  0.0 1.0 %slice_select_fusion.1 = bf16[4,1,128,128]{3,2,1,0:T(8,128)(2,1)S(1)} fusion(bf16[4,8,128,128]{3,2,1,0:T(8,128)(2,1)} %frame_ref.3, pred[]{:T(512)S(6)} %eq.4), kind=kLoop, calls=%fused_computation.16 | loop fusion | flops 65536 | bytes 393217 | tf_op jit(solution)/shard_map/input_conv_and_recurrence/jit(_where)/select_n | solution.py:15
  1.0 0.7 %collective-permute-start = (bf16[4,1,128,128]{3,2,1,0:T(8,128)(2,1)S(1)}, bf16[4,1,128,128]{3,2,1,0:T(8,128)(2,1)S(1)}, u32[]{:S(2)}, u32[]{:S(2)}) collective-permute-start(bf16[4,1,128,128]{3,2,1,0:T(8,128)(2,1)S(1)} %slice_select_fusion.1), channel_id=1, source_target_pairs={{0,1},{1,0},{2,3},{3,2},{4,5},{5,4},{6,7},{7,6},{8,9},{9,8},{10,11... | collective-permute-start | bytes 393224 | tf_op jit(solution)/shard_map/input_conv_and_recurrence/ppermute | solution.py:15
  1.7 1.0 %collective-permute-done = bf16[4,1,128,128]{3,2,1,0:T(8,128)(2,1)S(1)} collective-permute-done((bf16[4,1,128,128]{3,2,1,0:T(8,128)(2,1)S(1)}, bf16[4,1,128,128]{3,2,1,0:T(8,128)(2,1)S(1)}, u32[]{:S(2)}, u32[]{:S(2)}) %collective-permute-start) | collective-permute-done | bytes 131104 | tf_op jit(solution)/shard_map/input_conv_and_recurrence/ppermute | solution.py:15
  2.7 0.7 %broadcast_select_fusion.2 = (bf16[4,1,128,128]{3,2,1,0:T(8,128)(2,1)}, bf16[4,1,128,128]{3,2,1,0:T(8,128)(2,1)}) fusion(bf16[4,1,128,128]{3,2,1,0:T(8,128)(2,1)S(1)} %collective-permute-done, pred[]{:T(512)S(6)} %eq.4), kind=kLoop, calls=%fused_computation.19 | loop fusion | flops 131072 | bytes 393217 | tf_op jit(solution)/shard_map/input_conv_and_recurrence/jit(_where)/select_n | solution.py:17
  3.4 5.3 %input_conv_and_recurrence.1 = (f32[4,8,128,128]{3,2,1,0:T(8,128)}, f32[4,128]{1,0:T(4,128)}, bf16[1040,128]{1,0:T(8,128)(2,1)}) custom-call(f32[4,128]{1,0:T(4,128)} %decay_ref.1, bf16[4,1,128,128]{3,2,1,0:T(8,128)(2,1)} %get-tuple-element.26.top_ref, bf16[4,8,128,128]{3,2,1,0:T(8,128)(2,1)} %frame_ref.3, ...), custom_call_target="tpu_custom_call" | custom-call | tf_op jit(solution)/shard_map/input_conv_and_recurrence/pallas_call | solution.py:99
  8.7 0.0 copy-start.1
  8.7 3.1 %collective-permute-start.1 = (bf16[1040,128]{1,0:T(8,128)(2,1)}, bf16[1040,128]{1,0:T(8,128)(2,1)S(1)}, u32[]{:S(2)}, u32[]{:S(2)}) collective-permute-start(bf16[1040,128]{1,0:T(8,128)(2,1)} %get-tuple-element.9), channel_id=1, source_target_pairs={{0,2},{2,4},{4,6},{6,8},{8,10},{10,12},{12,14},{14,16},{16,18},{18... | collective-permute-start | bytes 798728 | tf_op jit(solution)/shard_map/carry_across_blocks/ppermute | solution.py:178
  11.8 1.1 %slice.56 = f32[1,8,128,128]{3,2,1,0:T(8,128)S(1)} slice(f32[4,8,128,128]{3,2,1,0:T(8,128)} %get-tuple-element.10.local_ref), slice={[3:4], [0:8], [0:128], [0:128]} | slice | bytes 1048576 | tf_op jit(solution)/shard_map/carry_across_blocks/slice | solution.py:200
  12.9 7.3 %collective-permute-done.1 = bf16[1040,128]{1,0:T(8,128)(2,1)S(1)} collective-permute-done((bf16[1040,128]{1,0:T(8,128)(2,1)}, bf16[1040,128]{1,0:T(8,128)(2,1)S(1)}, u32[]{:S(2)}, u32[]{:S(2)}) %collective-permute-start.1) | collective-permute-done | bytes 266272 | tf_op jit(solution)/shard_map/carry_across_blocks/ppermute | solution.py:178
  20.2 0.7 %reduce-precision_convert_fusion.5 = (bf16[1,128]{1,0:T(2,128)(2,1)S(1)}, f32[1,128]{1,0:T(1,128)S(1)}, f32[128]{0:T(128)S(1)}) fusion(f32[4,128]{1,0:T(4,128)} %get-tuple-element.8.cum_ref, f32[128]{0:T(128)S(1)} %convert_reduce_fusion.2), kind=kLoop, calls=%fused_computation.54 | loop fusion | flops 384 | bytes 2304 | tf_op jit(solution)/shard_map/convert.7
  20.9 0.1 fusion.3
  21.0 2.2 %collective-permute-start.2 = (bf16[1040,128]{1,0:T(8,128)(2,1)S(1)}, bf16[1040,128]{1,0:T(8,128)(2,1)S(1)}, u32[]{:S(2)}, u32[]{:S(2)}) collective-permute-start(bf16[1040,128]{1,0:T(8,128)(2,1)S(1)} %pad_maximum_fusion), channel_id=1, source_target_pairs={{0,4},{2,6},{4,8},{6,10},{8,12},{10,14},{12,16},{14,18},{16,20},{1... | collective-permute-start | bytes 798728 | tf_op jit(solution)/shard_map/carry_across_blocks/ppermute | solution.py:178
  23.3 1.1 %fusion.26 = (f32[4,1,128,128]{3,2,1,0:T(8,128)S(1)}, f32[4,1,128,128]{3,2,1,0:T(8,128)S(1)}) fusion(f32[4,8,128,128]{3,2,1,0:T(8,128)} %get-tuple-element.10.local_ref), kind=kLoop, calls=%fused_computation.65 | loop fusion | bytes 1048576 | tf_op jit(solution)/shard_map/output_conv/slice | solution.py:130
  24.4 6.2 %collective-permute-done.2 = bf16[1040,128]{1,0:T(8,128)(2,1)S(1)} collective-permute-done((bf16[1040,128]{1,0:T(8,128)(2,1)S(1)}, bf16[1040,128]{1,0:T(8,128)(2,1)S(1)}, u32[]{:S(2)}, u32[]{:S(2)}) %collective-permute-start.2) | collective-permute-done | bytes 266272 | tf_op jit(solution)/shard_map/carry_across_blocks/ppermute | solution.py:178
  30.6 0.0 copy-done.1
  30.6 0.1 fusion.2
  30.8 1.3 %collective-permute-start.3 = (bf16[1040,128]{1,0:T(8,128)(2,1)S(1)}, bf16[1040,128]{1,0:T(8,128)(2,1)S(1)}, u32[]{:S(2)}, u32[]{:S(2)}) collective-permute-start(bf16[1040,128]{1,0:T(8,128)(2,1)S(1)} %pad_maximum_fusion.1), channel_id=1, source_target_pairs={{0,8},{2,10},{4,12},{6,14},{8,16},{10,18},{12,20},{14,22},{16,24},... | collective-permute-start | bytes 798728 | tf_op jit(solution)/shard_map/carry_across_blocks/ppermute | solution.py:178
  32.2 6.3 %collective-permute-done.3 = bf16[1040,128]{1,0:T(8,128)(2,1)S(1)} collective-permute-done((bf16[1040,128]{1,0:T(8,128)(2,1)S(1)}, bf16[1040,128]{1,0:T(8,128)(2,1)S(1)}, u32[]{:S(2)}, u32[]{:S(2)}) %collective-permute-start.3) | collective-permute-done | bytes 266272 | tf_op jit(solution)/shard_map/carry_across_blocks/ppermute | solution.py:178
  38.5 0.2 add_convert_fusion
  38.7 1.3 %collective-permute-start.4 = (bf16[1040,128]{1,0:T(8,128)(2,1)S(1)}, bf16[1040,128]{1,0:T(8,128)(2,1)S(1)}, u32[]{:S(2)}, u32[]{:S(2)}) collective-permute-start(bf16[1040,128]{1,0:T(8,128)(2,1)S(1)} %pad_maximum_fusion.2), channel_id=1, source_target_pairs={{0,16},{2,18},{4,20},{6,22},{8,24},{10,26},{12,28},{14,30},{1,17},... | collective-permute-start | bytes 798728 | tf_op jit(solution)/shard_map/carry_across_blocks/ppermute | solution.py:178
  40.1 14.6 %collective-permute-done.4 = bf16[1040,128]{1,0:T(8,128)(2,1)S(1)} collective-permute-done((bf16[1040,128]{1,0:T(8,128)(2,1)S(1)}, bf16[1040,128]{1,0:T(8,128)(2,1)S(1)}, u32[]{:S(2)}, u32[]{:S(2)}) %collective-permute-start.4) | collective-permute-done | bytes 266272 | tf_op jit(solution)/shard_map/carry_across_blocks/ppermute | solution.py:178
  54.7 0.1 fusion.1.incoming_ref
  54.9 0.0 copy-start
  54.9 0.1 fusion
  55.0 1.3 %collective-permute-start.5 = (bf16[4,1,128,128]{3,2,1,0:T(8,128)(2,1)S(1)}, bf16[4,1,128,128]{3,2,1,0:T(8,128)(2,1)S(1)}, u32[]{:S(2)}, u32[]{:S(2)}) collective-permute-start(bf16[4,1,128,128]{3,2,1,0:T(8,128)(2,1)S(1)} %slice_select_fusion), channel_id=1, source_target_pairs={{0,1},{1,0},{2,3},{3,2},{4,5},{5,4},{6,7},{7,6},{8,9},{9,8},{10,11... | collective-permute-start | bytes 393224 | tf_op jit(solution)/shard_map/output_conv/ppermute | solution.py:15
  56.3 1.0 %collective-permute-done.5 = bf16[4,1,128,128]{3,2,1,0:T(8,128)(2,1)S(1)} collective-permute-done((bf16[4,1,128,128]{3,2,1,0:T(8,128)(2,1)S(1)}, bf16[4,1,128,128]{3,2,1,0:T(8,128)(2,1)S(1)}, u32[]{:S(2)}, u32[]{:S(2)}) %collective-permute-start.5) | collective-permute-done | bytes 131104 | tf_op jit(solution)/shard_map/output_conv/ppermute | solution.py:15
  57.3 0.7 %broadcast_select_fusion = (bf16[4,1,128,128]{3,2,1,0:T(8,128)(2,1)}, bf16[4,1,128,128]{3,2,1,0:T(8,128)(2,1)}) fusion(bf16[4,1,128,128]{3,2,1,0:T(8,128)(2,1)S(1)} %collective-permute-done.5, pred[]{:T(512)S(6)} %eq.4), kind=kLoop, calls=%fused_computation.17 | loop fusion | flops 131072 | bytes 393217 | tf_op jit(solution)/shard_map/output_conv/jit(_where)/select_n | solution.py:17
  58.0 0.0 copy-done
  58.0 5.6 %output_conv.1 = bf16[4,8,128,128]{3,2,1,0:T(8,128)(2,1)} custom-call(f32[4,128]{1,0:T(4,128)} %get-tuple-element.8.cum_ref, f32[1,128]{1,0:T(1,128)} %bitcast.43, f32[8,128,128]{2,1,0:T(8,128)} %copy-done, bf16[4,1,128,128]{3,2,1,0:T(8,128)(2,1)} %get-tuple-element.24.top_ref, f32[4,8,128,128]{3,2,1,0:T(8,128)} %get-tuple-element.10.local_ref, ...), custom_call_target="tpu_custom_call" | custom-call | tf_op jit(solution)/shard_map/output_conv/pallas_call | solution.py:136
  (22 shorter events, 0.4 us)
Async XLA Ops:
  1.0 1.7 %collective-permute-start = (bf16[4,1,128,128]{3,2,1,0:T(8,128)(2,1)S(1)}, bf16[4,1,128,128]{3,2,1,0:T(8,128)(2,1)S(1)}, u32[]{:S(2)}, u32[]{:S(2)}) collective-permute-start(bf16[4,1,128,128]{3,2,1,0:T(8,128)(2,1)S(1)} %slice_select_fusion.1), channel_id=1, source_target_pairs={{0,1},{1,0},{2,3},{3,2},{4,5},{5,4},{6,7},{7,6},{8,9},{9,8},{10,11... | collective-permute-start | bytes 393224 | tf_op jit(solution)/shard_map/input_conv_and_recurrence/ppermute | solution.py:15
  8.7 21.9 %copy-start.1 = (f32[4,128]{1,0:T(4,128)S(1)}, f32[4,128]{1,0:T(4,128)}, u32[]{:S(2)}) copy-start(f32[4,128]{1,0:T(4,128)} %get-tuple-element.8.cum_ref) | copy-start | bytes 6148
  8.7 11.5 %collective-permute-start.1 = (bf16[1040,128]{1,0:T(8,128)(2,1)}, bf16[1040,128]{1,0:T(8,128)(2,1)S(1)}, u32[]{:S(2)}, u32[]{:S(2)}) collective-permute-start(bf16[1040,128]{1,0:T(8,128)(2,1)} %get-tuple-element.9), channel_id=1, source_target_pairs={{0,2},{2,4},{4,6},{6,8},{8,10},{10,12},{12,14},{14,16},{16,18},{18... | collective-permute-start | bytes 798728 | tf_op jit(solution)/shard_map/carry_across_blocks/ppermute | solution.py:178
  21.0 9.5 %collective-permute-start.2 = (bf16[1040,128]{1,0:T(8,128)(2,1)S(1)}, bf16[1040,128]{1,0:T(8,128)(2,1)S(1)}, u32[]{:S(2)}, u32[]{:S(2)}) collective-permute-start(bf16[1040,128]{1,0:T(8,128)(2,1)S(1)} %pad_maximum_fusion), channel_id=1, source_target_pairs={{0,4},{2,6},{4,8},{6,10},{8,12},{10,14},{12,16},{14,18},{16,20},{1... | collective-permute-start | bytes 798728 | tf_op jit(solution)/shard_map/carry_across_blocks/ppermute | solution.py:178
  30.8 7.7 %collective-permute-start.3 = (bf16[1040,128]{1,0:T(8,128)(2,1)S(1)}, bf16[1040,128]{1,0:T(8,128)(2,1)S(1)}, u32[]{:S(2)}, u32[]{:S(2)}) collective-permute-start(bf16[1040,128]{1,0:T(8,128)(2,1)S(1)} %pad_maximum_fusion.1), channel_id=1, source_target_pairs={{0,8},{2,10},{4,12},{6,14},{8,16},{10,18},{12,20},{14,22},{16,24},... | collective-permute-start | bytes 798728 | tf_op jit(solution)/shard_map/carry_across_blocks/ppermute | solution.py:178
  38.7 16.0 %collective-permute-start.4 = (bf16[1040,128]{1,0:T(8,128)(2,1)S(1)}, bf16[1040,128]{1,0:T(8,128)(2,1)S(1)}, u32[]{:S(2)}, u32[]{:S(2)}) collective-permute-start(bf16[1040,128]{1,0:T(8,128)(2,1)S(1)} %pad_maximum_fusion.2), channel_id=1, source_target_pairs={{0,16},{2,18},{4,20},{6,22},{8,24},{10,26},{12,28},{14,30},{1,17},... | collective-permute-start | bytes 798728 | tf_op jit(solution)/shard_map/carry_across_blocks/ppermute | solution.py:178
  54.9 3.1 %copy-start = (f32[8,128,128]{2,1,0:T(8,128)}, f32[8,128,128]{2,1,0:T(8,128)S(1)}, u32[]{:S(2)}) copy-start(f32[8,128,128]{2,1,0:T(8,128)S(1)} %fusion.1.incoming_ref) | copy-start | bytes 1572868
  55.0 2.3 %collective-permute-start.5 = (bf16[4,1,128,128]{3,2,1,0:T(8,128)(2,1)S(1)}, bf16[4,1,128,128]{3,2,1,0:T(8,128)(2,1)S(1)}, u32[]{:S(2)}, u32[]{:S(2)}) collective-permute-start(bf16[4,1,128,128]{3,2,1,0:T(8,128)(2,1)S(1)} %slice_select_fusion), channel_id=1, source_target_pairs={{0,1},{1,0},{2,3},{3,2},{4,5},{5,4},{6,7},{7,6},{8,9},{9,8},{10,11... | collective-permute-start | bytes 393224 | tf_op jit(solution)/shard_map/output_conv/ppermute | solution.py:15

commit v6 on v5

--- a/solution.py
+++ b/solution.py
@@ -4,6 +4,8 @@
 from jax.experimental import pallas as pl
 from jax.experimental.pallas import tpu as pltpu
 from jax.sharding import PartitionSpec as P
+
+CHUNKS = 2
 
 
 def halo_rows(x, axis, dim):
@@ -71,10 +73,12 @@
         rest = power - hi.astype(jnp.float32)
         mid = rest.astype(jnp.bfloat16)
         low = (rest - mid.astype(jnp.float32)).astype(jnp.bfloat16)
-        pad = send_ref.shape[0] - cells - 3
-        send_ref[...] = jnp.concatenate(
-            [state.astype(jnp.bfloat16), hi, mid, low, jnp.zeros((pad, m), jnp.bfloat16)], axis=0
-        )
+        chunks, chunk_rows = send_ref.shape[0], send_ref.shape[1]
+        part = cells // chunks
+        pad = jnp.zeros((chunk_rows - part - 3, m), jnp.bfloat16)
+        for c in range(chunks):
+            piece = state[c * part : (c + 1) * part].astype(jnp.bfloat16)
+            send_ref[c] = jnp.concatenate([piece, hi, mid, low, pad], axis=0)
 
 
 def output_kernel(
@@ -95,7 +99,7 @@
     state_width = conv_in.shape[3]
     top, bottom = halo_rows(frames, "rows", 1)
     halo = pl.BlockSpec((1, 1, width, channels), lambda f: (f, 0, 0, 0))
-    payload_rows = band * width + 16
+    payload_shape = (CHUNKS, band * width // CHUNKS + 16, state_width)
     return pl.pallas_call(
         input_kernel,
         grid=(count,),
@@ -109,12 +113,12 @@
         out_specs=[
             pl.BlockSpec((1, band, width, state_width), lambda f: (f, 0, 0, 0)),
             pl.BlockSpec((count, state_width), lambda f: (0, 0)),
-            pl.BlockSpec((payload_rows, state_width), lambda f: (0, 0)),
+            pl.BlockSpec(payload_shape, lambda f: (0, 0, 0)),
         ],
         out_shape=[
             jax.ShapeDtypeStruct((count, band, width, state_width), jnp.float32),
             jax.ShapeDtypeStruct((count, state_width), jnp.float32),
-            jax.ShapeDtypeStruct((payload_rows, state_width), jnp.bfloat16),
+            jax.ShapeDtypeStruct(payload_shape, jnp.bfloat16),
         ],
         scratch_shapes=[
             pltpu.VMEM((band * width, state_width), jnp.float32),
@@ -163,8 +167,7 @@
 
 def incoming_state(power, state, first_payload, axis):
     n = lax.axis_size(axis)
-    rows, width, channels = state.shape
-    cells = rows * width
+    cells, channels = state.shape
     win_p, win_s = power, state
     acc_p, acc_s = None, None
     payload = first_payload
@@ -173,11 +176,11 @@
         pairs = [(i, i + shift) for i in range(n - shift)]
         if payload is None:
             payload = jnp.concatenate(
-                [win_s.astype(jnp.bfloat16).reshape(cells, channels), split3(win_p, 16)], axis=0
+                [win_s.astype(jnp.bfloat16), split3(win_p, 16)], axis=0
             )
         got = lax.ppermute(payload, axis, pairs)
         payload = None
-        got_s = got[:cells].astype(jnp.float32).reshape(rows, width, channels)
+        got_s = got[:cells].astype(jnp.float32)
         got_p = jnp.sum(got[cells : cells + 3].astype(jnp.float32), axis=0)
         if acc_s is None:
             acc_p, acc_s = got_p, got_s
@@ -197,7 +200,14 @@
     with jax.named_scope("input_conv_and_recurrence"):
         local, cumulative, first_payload = input_stage(frames, conv_in, decay)
     with jax.named_scope("carry_across_blocks"):
-        incoming = incoming_state(cumulative[-1], local[-1], first_payload, "tm")
+        count, band, width, state_width = local.shape
+        end = local[-1].reshape(band * width, state_width)
+        part = band * width // CHUNKS
+        pieces = [
+            incoming_state(cumulative[-1], end[c * part : (c + 1) * part], first_payload[c], "tm")
+            for c in range(CHUNKS)
+        ]
+        incoming = jnp.concatenate(pieces, axis=0).reshape(band, width, state_width)
     with jax.named_scope("output_conv"):
         return output_stage(local, cumulative, incoming, frames, conv_out, skip)
 

time: 64 us -> 68.9 us (1.077)
  starting transfers between devices: 9.96 us -> 24.1 us
  waiting for transfers between devices: 36.4 us -> 25.5 us
  local copies, waits for them, and re-layouts: 2.19 us -> 3.15 us
    ppermute x4 -> x8, waiting for transfers between devices: 34.4 us -> 24.4 us  [incoming_state(): got = lax.ppermute(payload, axis, pairs)]
    ppermute x4 -> x8, starting transfers between devices: 7.95 us -> 15.6 us  [incoming_state(): got = lax.ppermute(payload, axis, pairs)]
    ppermute x2, starting transfers between devices: 2.01 us -> 8.51 us  [halo_rows(): got = lax.ppermute(jnp.where(upper, last, first), axis, [(0, 1), (1, 0)])]
    squeeze x0 -> x1, local copies, waits for them, and re-layouts: none -> 0.99 us  [shards(): first_payload[c]]
    concatenate x3 -> x7, other arithmetic: 0.06 us -> 0.91 us  [the longest x1 0.84 us: shards(): incoming = jnp.concatenate(pieces, axis=0).reshape(band, width, state_width)]
    ppermute x2, waiting for transfers between devices: 1.97 us -> 1.13 us  [halo_rows(): got = lax.ppermute(jnp.where(upper, last, first), axis, [(0, 1), (1, 0)])]
  transfers between devices with their start and end apart: 6 -> 10, of which waited for: 6 -> 9; matrix products, arithmetic and copies ran while one was open for 4% -> 5% of each run, Pallas kernels for 0% -> 0%
where the time goes in v6:
time: 68.9 us; the launch traced here: 68.2 us
  waiting for transfers between devices  25.5 us (37%)
  starting transfers between devices  24.1 us (35%)
  Pallas kernels  10.8 us (16%)
  other arithmetic  4.29 us (6%)
  local copies, waits for them, and re-layouts  3.15 us (5%)
    ppermute x8, waiting for transfers between devices, incoming_state(): got = lax.ppermute(payload, axis, pairs)  24.4 us
    ppermute x8, starting transfers between devices, incoming_state(): got = lax.ppermute(payload, axis, pairs)  15.6 us
    ppermute x2, starting transfers between devices, halo_rows(): got = lax.ppermute(jnp.where(upper, last, first), axis, [(0, 1), (1, 0)])  8.51 us
    pallas_call x1, Pallas kernels, output_stage(): pl.pallas_call(output_kernel, grid=(count,), in_specs=[pl.BlockSpec((coun...  5.57 us
    pallas_call x1, Pallas kernels, input_stage(): pl.pallas_call(input_kernel, grid=(count,), in_specs=[pl.BlockSpec((count...  5.24 us
    select_n x2, other arithmetic, halo_rows(): return (jnp.where(upper, zero, got), jnp.where(upper, got, zero))  1.44 us
  transfers between devices with their start and end apart: 10, of which 9 were waited for; matrix products, arithmetic and copies ran while one was open for 5% of the time, Pallas kernels for 0%

profile of v6, /device:TPU:25, one launch (start us, length us, event | category | flops | bytes accessed | tf_op | source)
XLA Modules:
  0.0 68.2 jit_solution(9280913802337331306)
XLA Ops:
  0.0 1.0 %slice_select_fusion.1 = bf16[4,1,128,128]{3,2,1,0:T(8,128)(2,1)S(1)} fusion(bf16[4,8,128,128]{3,2,1,0:T(8,128)(2,1)} %frame_ref.3, pred[]{:T(512)S(6)} %eq.4), kind=kLoop, calls=%fused_computation.39 | loop fusion | flops 65536 | bytes 393217 | tf_op jit(solution)/shard_map/input_conv_and_recurrence/jit(_where)/select_n | solution.py:17
  1.0 0.7 %collective-permute-start = (bf16[4,1,128,128]{3,2,1,0:T(8,128)(2,1)S(1)}, bf16[4,1,128,128]{3,2,1,0:T(8,128)(2,1)S(1)}, u32[]{:S(2)}, u32[]{:S(2)}) collective-permute-start(bf16[4,1,128,128]{3,2,1,0:T(8,128)(2,1)S(1)} %slice_select_fusion.1), channel_id=1, source_target_pairs={{0,1},{1,0},{2,3},{3,2},{4,5},{5,4},{6,7},{7,6},{8,9},{9,8},{10,11... | collective-permute-start | bytes 393224 | tf_op jit(solution)/shard_map/input_conv_and_recurrence/ppermute | solution.py:17
  1.7 1.0 %collective-permute-done = bf16[4,1,128,128]{3,2,1,0:T(8,128)(2,1)S(1)} collective-permute-done((bf16[4,1,128,128]{3,2,1,0:T(8,128)(2,1)S(1)}, bf16[4,1,128,128]{3,2,1,0:T(8,128)(2,1)S(1)}, u32[]{:S(2)}, u32[]{:S(2)}) %collective-permute-start) | collective-permute-done | bytes 131104 | tf_op jit(solution)/shard_map/input_conv_and_recurrence/ppermute | solution.py:17
  2.7 0.7 %broadcast_select_fusion.2 = (bf16[4,1,128,128]{3,2,1,0:T(8,128)(2,1)}, bf16[4,1,128,128]{3,2,1,0:T(8,128)(2,1)}) fusion(bf16[4,1,128,128]{3,2,1,0:T(8,128)(2,1)S(1)} %collective-permute-done, pred[]{:T(512)S(6)} %eq.4), kind=kLoop, calls=%fused_computation.42 | loop fusion | flops 131072 | bytes 393217 | tf_op jit(solution)/shard_map/input_conv_and_recurrence/jit(_where)/select_n | solution.py:19
  3.4 5.2 %input_conv_and_recurrence.1 = (f32[4,8,128,128]{3,2,1,0:T(8,128)}, f32[4,128]{1,0:T(4,128)}, bf16[2,528,128]{2,1,0:T(8,128)(2,1)}) custom-call(f32[4,128]{1,0:T(4,128)} %decay_ref.1, bf16[4,1,128,128]{3,2,1,0:T(8,128)(2,1)} %get-tuple-element.32.top_ref, bf16[4,8,128,128]{3,2,1,0:T(8,128)(2,1)} %frame_ref.3, ...), custom_call_target="tpu_custom_call" | custom-call | tf_op jit(solution)/shard_map/input_conv_and_recurrence/pallas_call | solution.py:103
  8.7 0.0 copy-start
  8.7 1.0 %slice_bitcast_fusion.1 = (bf16[528,128]{1,0:T(8,128)(2,1)S(1)}, bf16[528,128]{1,0:T(8,128)(2,1)S(1)}) fusion(bf16[2,528,128]{2,1,0:T(8,128)(2,1)} %get-tuple-element.9), kind=kLoop, calls=%fused_computation.36 | loop fusion | bytes 540672 | tf_op jit(solution)/shard_map/carry_across_blocks/squeeze | solution.py:207
  9.7 3.1 %collective-permute-start.5 = (bf16[528,128]{1,0:T(8,128)(2,1)S(1)}, bf16[528,128]{1,0:T(8,128)(2,1)S(1)}, u32[]{:S(2)}, u32[]{:S(2)}) collective-permute-start(bf16[528,128]{1,0:T(8,128)(2,1)S(1)} %get-tuple-element.28), channel_id=1, source_target_pairs={{0,2},{2,4},{4,6},{6,8},{8,10},{10,12},{12,14},{14,16},{16,18},{18... | collective-permute-start | bytes 405512 | tf_op jit(solution)/shard_map/carry_across_blocks/ppermute | solution.py:181
  12.8 3.1 %collective-permute-start.1 = (bf16[528,128]{1,0:T(8,128)(2,1)S(1)}, bf16[528,128]{1,0:T(8,128)(2,1)S(1)}, u32[]{:S(2)}, u32[]{:S(2)}) collective-permute-start(bf16[528,128]{1,0:T(8,128)(2,1)S(1)} %get-tuple-element.27), channel_id=1, source_target_pairs={{0,2},{2,4},{4,6},{6,8},{8,10},{10,12},{12,14},{14,16},{16,18},{18... | collective-permute-start | bytes 405512 | tf_op jit(solution)/shard_map/carry_across_blocks/ppermute | solution.py:181
  15.9 1.1 %fusion.56 = (f32[1,4,128,128]{3,2,1,0:T(8,128)S(1)}, f32[1,4,128,128]{3,2,1,0:T(8,128)S(1)}) fusion(f32[4,8,128,128]{3,2,1,0:T(8,128)} %get-tuple-element.10.local_ref), kind=kLoop, calls=%fused_computation.125 | loop fusion | bytes 1048576 | tf_op jit(solution)/shard_map/carry_across_blocks/slice | solution.py:207
  17.0 1.1 %fusion.55 = (f32[4,1,128,128]{3,2,1,0:T(8,128)S(1)}, f32[4,1,128,128]{3,2,1,0:T(8,128)S(1)}) fusion(f32[4,8,128,128]{3,2,1,0:T(8,128)} %get-tuple-element.10.local_ref), kind=kLoop, calls=%fused_computation.124 | loop fusion | bytes 1048576 | tf_op jit(solution)/shard_map/output_conv/slice | solution.py:134
  18.1 0.1 collective-permute-done.5
  18.2 2.8 %collective-permute-done.1 = bf16[528,128]{1,0:T(8,128)(2,1)S(1)} collective-permute-done((bf16[528,128]{1,0:T(8,128)(2,1)S(1)}, bf16[528,128]{1,0:T(8,128)(2,1)S(1)}, u32[]{:S(2)}, u32[]{:S(2)}) %collective-permute-start.1) | collective-permute-done | bytes 135200 | tf_op jit(solution)/shard_map/carry_across_blocks/ppermute | solution.py:181
  21.0 0.0 copy-done
  21.1 2.2 %collective-permute-start.2 = (bf16[528,128]{1,0:T(8,128)(2,1)S(1)}, bf16[528,128]{1,0:T(8,128)(2,1)S(1)}, u32[]{:S(2)}, u32[]{:S(2)}) collective-permute-start(bf16[528,128]{1,0:T(8,128)(2,1)S(1)} %pad_maximum_fusion.1), channel_id=1, source_target_pairs={{0,4},{2,6},{4,8},{6,10},{8,12},{10,14},{12,16},{14,18},{16,20},{1... | collective-permute-start | bytes 405512 | tf_op jit(solution)/shard_map/carry_across_blocks/ppermute | solution.py:181
  23.4 4.4 %collective-permute-done.2 = bf16[528,128]{1,0:T(8,128)(2,1)S(1)} collective-permute-done((bf16[528,128]{1,0:T(8,128)(2,1)S(1)}, bf16[528,128]{1,0:T(8,128)(2,1)S(1)}, u32[]{:S(2)}, u32[]{:S(2)}) %collective-permute-start.2) | collective-permute-done | bytes 135200 | tf_op jit(solution)/shard_map/carry_across_blocks/ppermute | solution.py:181
  27.8 0.1 fusion.14
  27.9 1.3 %collective-permute-start.3 = (bf16[528,128]{1,0:T(8,128)(2,1)S(1)}, bf16[528,128]{1,0:T(8,128)(2,1)S(1)}, u32[]{:S(2)}, u32[]{:S(2)}) collective-permute-start(bf16[528,128]{1,0:T(8,128)(2,1)S(1)} %pad_maximum_fusion.2), channel_id=1, source_target_pairs={{0,8},{2,10},{4,12},{6,14},{8,16},{10,18},{12,20},{14,22},{16,24},... | collective-permute-start | bytes 405512 | tf_op jit(solution)/shard_map/carry_across_blocks/ppermute | solution.py:181
  29.3 1.9 %collective-permute-start.6 = (bf16[528,128]{1,0:T(8,128)(2,1)S(1)}, bf16[528,128]{1,0:T(8,128)(2,1)S(1)}, u32[]{:S(2)}, u32[]{:S(2)}) collective-permute-start(bf16[528,128]{1,0:T(8,128)(2,1)S(1)} %pad_maximum_fusion.4), channel_id=1, source_target_pairs={{0,4},{2,6},{4,8},{6,10},{8,12},{10,14},{12,16},{14,18},{16,20},{1... | collective-permute-start | bytes 405512 | tf_op jit(solution)/shard_map/carry_across_blocks/ppermute | solution.py:181
  31.2 2.5 %collective-permute-done.3 = bf16[528,128]{1,0:T(8,128)(2,1)S(1)} collective-permute-done((bf16[528,128]{1,0:T(8,128)(2,1)S(1)}, bf16[528,128]{1,0:T(8,128)(2,1)S(1)}, u32[]{:S(2)}, u32[]{:S(2)}) %collective-permute-start.3) | collective-permute-done | bytes 135200 | tf_op jit(solution)/shard_map/carry_across_blocks/ppermute | solution.py:181
  33.8 3.6 %collective-permute-done.6 = bf16[528,128]{1,0:T(8,128)(2,1)S(1)} collective-permute-done((bf16[528,128]{1,0:T(8,128)(2,1)S(1)}, bf16[528,128]{1,0:T(8,128)(2,1)S(1)}, u32[]{:S(2)}, u32[]{:S(2)}) %collective-permute-start.6) | collective-permute-done | bytes 135200 | tf_op jit(solution)/shard_map/carry_across_blocks/ppermute | solution.py:181
  37.3 0.2 fusion.6
  37.5 1.3 %collective-permute-start.4 = (bf16[528,128]{1,0:T(8,128)(2,1)S(1)}, bf16[528,128]{1,0:T(8,128)(2,1)S(1)}, u32[]{:S(2)}, u32[]{:S(2)}) collective-permute-start(bf16[528,128]{1,0:T(8,128)(2,1)S(1)} %pad_maximum_fusion.3), channel_id=1, source_target_pairs={{0,16},{2,18},{4,20},{6,22},{8,24},{10,26},{12,28},{14,30},{1,17},... | collective-permute-start | bytes 405512 | tf_op jit(solution)/shard_map/carry_across_blocks/ppermute | solution.py:181
  38.9 1.3 %collective-permute-start.7 = (bf16[528,128]{1,0:T(8,128)(2,1)S(1)}, bf16[528,128]{1,0:T(8,128)(2,1)S(1)}, u32[]{:S(2)}, u32[]{:S(2)}) collective-permute-start(bf16[528,128]{1,0:T(8,128)(2,1)S(1)} %pad_maximum_fusion.5), channel_id=1, source_target_pairs={{0,8},{2,10},{4,12},{6,14},{8,16},{10,18},{12,20},{14,22},{16,24},... | collective-permute-start | bytes 405512 | tf_op jit(solution)/shard_map/carry_across_blocks/ppermute | solution.py:181
  40.2 5.4 %collective-permute-done.4 = bf16[528,128]{1,0:T(8,128)(2,1)S(1)} collective-permute-done((bf16[528,128]{1,0:T(8,128)(2,1)S(1)}, bf16[528,128]{1,0:T(8,128)(2,1)S(1)}, u32[]{:S(2)}, u32[]{:S(2)}) %collective-permute-start.4) | collective-permute-done | bytes 135200 | tf_op jit(solution)/shard_map/carry_across_blocks/ppermute | solution.py:181
  45.6 0.1 fusion.3
  45.8 0.0 collective-permute-done.7
  45.8 0.1 fusion.12
  45.9 1.3 %collective-permute-start.8 = (bf16[528,128]{1,0:T(8,128)(2,1)S(1)}, bf16[528,128]{1,0:T(8,128)(2,1)S(1)}, u32[]{:S(2)}, u32[]{:S(2)}) collective-permute-start(bf16[528,128]{1,0:T(8,128)(2,1)S(1)} %pad_maximum_fusion.6), channel_id=1, source_target_pairs={{0,16},{2,18},{4,20},{6,22},{8,24},{10,26},{12,28},{14,30},{1,17},... | collective-permute-start | bytes 405512 | tf_op jit(solution)/shard_map/carry_across_blocks/ppermute | solution.py:181
  47.2 5.6 %collective-permute-done.8 = bf16[528,128]{1,0:T(8,128)(2,1)S(1)} collective-permute-done((bf16[528,128]{1,0:T(8,128)(2,1)S(1)}, bf16[528,128]{1,0:T(8,128)(2,1)S(1)}, u32[]{:S(2)}, u32[]{:S(2)}) %collective-permute-start.8) | collective-permute-done | bytes 135200 | tf_op jit(solution)/shard_map/carry_across_blocks/ppermute | solution.py:181
  52.9 0.1 fusion.9
  53.0 0.1 fusion
  53.1 7.8 %collective-permute-start.9 = (bf16[4,1,128,128]{3,2,1,0:T(8,128)(2,1)S(1)}, bf16[4,1,128,128]{3,2,1,0:T(8,128)(2,1)S(1)}, u32[]{:S(2)}, u32[]{:S(2)}) collective-permute-start(bf16[4,1,128,128]{3,2,1,0:T(8,128)(2,1)S(1)} %slice_select_fusion), channel_id=1, source_target_pairs={{0,1},{1,0},{2,3},{3,2},{4,5},{5,4},{6,7},{7,6},{8,9},{9,8},{10,11... | collective-permute-start | bytes 393224 | tf_op jit(solution)/shard_map/output_conv/ppermute | solution.py:17
  60.9 0.8 %pad_maximum_fusion = f32[1024,128]{1,0:T(8,128)} fusion(f32[512,128]{1,0:T(8,128)S(1)} %fusion.9, f32[512,128]{1,0:T(8,128)S(1)} %fusion.3), kind=kLoop, calls=%fused_computation | loop fusion | flops 131072 | bytes 1048576 | tf_op jit(solution)/shard_map/carry_across_blocks/concatenate | solution.py:210
  61.7 0.1 collective-permute-done.9
  61.9 0.7 %broadcast_select_fusion = (bf16[4,1,128,128]{3,2,1,0:T(8,128)(2,1)}, bf16[4,1,128,128]{3,2,1,0:T(8,128)(2,1)}) fusion(bf16[4,1,128,128]{3,2,1,0:T(8,128)(2,1)S(1)} %collective-permute-done.9, pred[]{:T(512)S(6)} %eq.4), kind=kLoop, calls=%fused_computation.40 | loop fusion | flops 131072 | bytes 393217 | tf_op jit(solution)/shard_map/output_conv/jit(_where)/select_n | solution.py:19
  62.6 5.6 %output_conv.1 = bf16[4,8,128,128]{3,2,1,0:T(8,128)(2,1)} custom-call(f32[4,128]{1,0:T(4,128)} %get-tuple-element.8.cum_ref, f32[1,128]{1,0:T(1,128)} %bitcast.69, f32[8,128,128]{2,1,0:T(8,128)} %bitcast.62, bf16[4,1,128,128]{3,2,1,0:T(8,128)(2,1)} %get-tuple-element.30.top_ref, f32[4,8,128,128]{3,2,1,0:T(8,128)} %get-tuple-element.10.local_ref, ...), custom_call_target="tpu_custom_call" | custom-call | tf_op jit(solution)/shard_map/output_conv/pallas_call | solution.py:140
  (34 shorter events, 0.4 us)
Async XLA Ops:
  1.0 1.7 %collective-permute-start = (bf16[4,1,128,128]{3,2,1,0:T(8,128)(2,1)S(1)}, bf16[4,1,128,128]{3,2,1,0:T(8,128)(2,1)S(1)}, u32[]{:S(2)}, u32[]{:S(2)}) collective-permute-start(bf16[4,1,128,128]{3,2,1,0:T(8,128)(2,1)S(1)} %slice_select_fusion.1), channel_id=1, source_target_pairs={{0,1},{1,0},{2,3},{3,2},{4,5},{5,4},{6,7},{7,6},{8,9},{9,8},{10,11... | collective-permute-start | bytes 393224 | tf_op jit(solution)/shard_map/input_conv_and_recurrence/ppermute | solution.py:17
  8.7 12.3 %copy-start = (f32[4,128]{1,0:T(4,128)S(1)}, f32[4,128]{1,0:T(4,128)}, u32[]{:S(2)}) copy-start(f32[4,128]{1,0:T(4,128)} %get-tuple-element.8.cum_ref) | copy-start | bytes 6148
  9.7 8.5 %collective-permute-start.5 = (bf16[528,128]{1,0:T(8,128)(2,1)S(1)}, bf16[528,128]{1,0:T(8,128)(2,1)S(1)}, u32[]{:S(2)}, u32[]{:S(2)}) collective-permute-start(bf16[528,128]{1,0:T(8,128)(2,1)S(1)} %get-tuple-element.28), channel_id=1, source_target_pairs={{0,2},{2,4},{4,6},{6,8},{8,10},{10,12},{12,14},{14,16},{16,18},{18... | collective-permute-start | bytes 405512 | tf_op jit(solution)/shard_map/carry_across_blocks/ppermute | solution.py:181
  12.8 8.2 %collective-permute-start.1 = (bf16[528,128]{1,0:T(8,128)(2,1)S(1)}, bf16[528,128]{1,0:T(8,128)(2,1)S(1)}, u32[]{:S(2)}, u32[]{:S(2)}) collective-permute-start(bf16[528,128]{1,0:T(8,128)(2,1)S(1)} %get-tuple-element.27), channel_id=1, source_target_pairs={{0,2},{2,4},{4,6},{6,8},{8,10},{10,12},{12,14},{14,16},{16,18},{18... | collective-permute-start | bytes 405512 | tf_op jit(solution)/shard_map/carry_across_blocks/ppermute | solution.py:181
  21.1 6.7 %collective-permute-start.2 = (bf16[528,128]{1,0:T(8,128)(2,1)S(1)}, bf16[528,128]{1,0:T(8,128)(2,1)S(1)}, u32[]{:S(2)}, u32[]{:S(2)}) collective-permute-start(bf16[528,128]{1,0:T(8,128)(2,1)S(1)} %pad_maximum_fusion.1), channel_id=1, source_target_pairs={{0,4},{2,6},{4,8},{6,10},{8,12},{10,14},{12,16},{14,18},{16,20},{1... | collective-permute-start | bytes 405512 | tf_op jit(solution)/shard_map/carry_across_blocks/ppermute | solution.py:181
  27.9 5.8 %collective-permute-start.3 = (bf16[528,128]{1,0:T(8,128)(2,1)S(1)}, bf16[528,128]{1,0:T(8,128)(2,1)S(1)}, u32[]{:S(2)}, u32[]{:S(2)}) collective-permute-start(bf16[528,128]{1,0:T(8,128)(2,1)S(1)} %pad_maximum_fusion.2), channel_id=1, source_target_pairs={{0,8},{2,10},{4,12},{6,14},{8,16},{10,18},{12,20},{14,22},{16,24},... | collective-permute-start | bytes 405512 | tf_op jit(solution)/shard_map/carry_across_blocks/ppermute | solution.py:181
  29.3 8.1 %collective-permute-start.6 = (bf16[528,128]{1,0:T(8,128)(2,1)S(1)}, bf16[528,128]{1,0:T(8,128)(2,1)S(1)}, u32[]{:S(2)}, u32[]{:S(2)}) collective-permute-start(bf16[528,128]{1,0:T(8,128)(2,1)S(1)} %pad_maximum_fusion.4), channel_id=1, source_target_pairs={{0,4},{2,6},{4,8},{6,10},{8,12},{10,14},{12,16},{14,18},{16,20},{1... | collective-permute-start | bytes 405512 | tf_op jit(solution)/shard_map/carry_across_blocks/ppermute | solution.py:181
  37.5 8.1 %collective-permute-start.4 = (bf16[528,128]{1,0:T(8,128)(2,1)S(1)}, bf16[528,128]{1,0:T(8,128)(2,1)S(1)}, u32[]{:S(2)}, u32[]{:S(2)}) collective-permute-start(bf16[528,128]{1,0:T(8,128)(2,1)S(1)} %pad_maximum_fusion.3), channel_id=1, source_target_pairs={{0,16},{2,18},{4,20},{6,22},{8,24},{10,26},{12,28},{14,30},{1,17},... | collective-permute-start | bytes 405512 | tf_op jit(solution)/shard_map/carry_across_blocks/ppermute | solution.py:181
  38.9 6.8 %collective-permute-start.7 = (bf16[528,128]{1,0:T(8,128)(2,1)S(1)}, bf16[528,128]{1,0:T(8,128)(2,1)S(1)}, u32[]{:S(2)}, u32[]{:S(2)}) collective-permute-start(bf16[528,128]{1,0:T(8,128)(2,1)S(1)} %pad_maximum_fusion.5), channel_id=1, source_target_pairs={{0,8},{2,10},{4,12},{6,14},{8,16},{10,18},{12,20},{14,22},{16,24},... | collective-permute-start | bytes 405512 | tf_op jit(solution)/shard_map/carry_across_blocks/ppermute | solution.py:181
  45.9 6.9 %collective-permute-start.8 = (bf16[528,128]{1,0:T(8,128)(2,1)S(1)}, bf16[528,128]{1,0:T(8,128)(2,1)S(1)}, u32[]{:S(2)}, u32[]{:S(2)}) collective-permute-start(bf16[528,128]{1,0:T(8,128)(2,1)S(1)} %pad_maximum_fusion.6), channel_id=1, source_target_pairs={{0,16},{2,18},{4,20},{6,22},{8,24},{10,26},{12,28},{14,30},{1,17},... | collective-permute-start | bytes 405512 | tf_op jit(solution)/shard_map/carry_across_blocks/ppermute | solution.py:181
  53.1 8.8 %collective-permute-start.9 = (bf16[4,1,128,128]{3,2,1,0:T(8,128)(2,1)S(1)}, bf16[4,1,128,128]{3,2,1,0:T(8,128)(2,1)S(1)}, u32[]{:S(2)}, u32[]{:S(2)}) collective-permute-start(bf16[4,1,128,128]{3,2,1,0:T(8,128)(2,1)S(1)} %slice_select_fusion), channel_id=1, source_target_pairs={{0,1},{1,0},{2,3},{3,2},{4,5},{5,4},{6,7},{7,6},{8,9},{9,8},{10,11... | collective-permute-start | bytes 393224 | tf_op jit(solution)/shard_map/output_conv/ppermute | solution.py:17

commit v7 on v5

--- a/solution.py
+++ b/solution.py
@@ -8,20 +8,26 @@
 
 def halo_rows(x, axis, dim):
     size, length = (lax.axis_size(axis), x.shape[dim])
+    position = lax.axis_index(axis)
     if size == 2:
-        upper = lax.axis_index(axis) == 0
-        last = lax.slice_in_dim(x, length - 1, length, axis=dim)
-        first = lax.slice_in_dim(x, 0, 1, axis=dim)
-        got = lax.ppermute(jnp.where(upper, last, first), axis, [(0, 1), (1, 0)])
-        zero = jnp.zeros_like(got)
-        return jnp.where(upper, zero, got), jnp.where(upper, got, zero)
+        row = (1 - position) * (length - 1)
+        got = lax.ppermute(lax.dynamic_slice_in_dim(x, row, 1, axis=dim), axis, [(0, 1), (1, 0)])
+        flags = jnp.stack([position == 1, position == 0]).astype(jnp.int32)
+        return got, got, flags
     up = [(i, (i + 1) % size) for i in range(size - 1)]
     down = [(j, i) for i, j in up]
     last = lax.slice_in_dim(x, length - 1, length, axis=dim)
     first = lax.slice_in_dim(x, 0, 1, axis=dim)
     before = lax.ppermute(last, axis, up)
     after = lax.ppermute(first, axis, down)
-    return before, after
+    return before, after, jnp.ones((2,), jnp.int32)
+
+
+def padded_band(flags_ref, above, band_rows, below):
+    zero = jnp.zeros_like(above)
+    top = jnp.where(flags_ref[0] == 1, above, zero)
+    bottom = jnp.where(flags_ref[1] == 1, below, zero)
+    return jnp.concatenate([top, band_rows, bottom], axis=0)
 
 
 def conv_taps(x, w_ref):
@@ -44,7 +50,17 @@
 
 
 def input_kernel(
-    decay_ref, top_ref, frame_ref, bottom_ref, w_ref, out_ref, cum_ref, send_ref, state_ref, power_ref
+    flags_ref,
+    decay_ref,
+    top_ref,
+    frame_ref,
+    bottom_ref,
+    w_ref,
+    out_ref,
+    cum_ref,
+    send_ref,
+    state_ref,
+    power_ref,
 ):
     f = pl.program_id(0)
     band, width, m = out_ref.shape[1:]
@@ -55,7 +71,7 @@
         state_ref[...] = jnp.zeros_like(state_ref)
         power_ref[...] = jnp.ones_like(power_ref)
 
-    x = jnp.concatenate([top_ref[0], frame_ref[0], bottom_ref[0]], axis=0)
+    x = padded_band(flags_ref, top_ref[0], frame_ref[0], bottom_ref[0])
     drive = conv_taps(x, w_ref)
     rate = decay_ref[pl.ds(f, 1), :]
     state = rate * state_ref[...] + drive
@@ -78,12 +94,12 @@
 
 
 def output_kernel(
-    cum_ref, skip_ref, incoming_ref, top_ref, local_ref, bottom_ref, frame_ref, w_ref, out_ref
+    flags_ref, cum_ref, skip_ref, incoming_ref, top_ref, local_ref, bottom_ref, frame_ref, w_ref, out_ref
 ):
     f = pl.program_id(0)
     band, width, m = out_ref.shape[1:]
     inner = (local_ref[0] + cum_ref[pl.ds(f, 1), :] * incoming_ref[...]).astype(jnp.bfloat16)
-    x = jnp.concatenate([top_ref[0], inner, bottom_ref[0]], axis=0)
+    x = padded_band(flags_ref, top_ref[0], inner, bottom_ref[0])
     total = conv_taps(x, w_ref)
     frame = frame_ref[0].reshape(band * width, m).astype(jnp.float32)
     total = total + skip_ref[...] * frame
@@ -93,13 +109,14 @@
 def input_stage(frames, conv_in, decay):
     count, band, width, channels = frames.shape
     state_width = conv_in.shape[3]
-    top, bottom = halo_rows(frames, "rows", 1)
+    top, bottom, flags = halo_rows(frames, "rows", 1)
     halo = pl.BlockSpec((1, 1, width, channels), lambda f: (f, 0, 0, 0))
     payload_rows = band * width + 16
     return pl.pallas_call(
         input_kernel,
         grid=(count,),
         in_specs=[
+            pl.BlockSpec(memory_space=pltpu.SMEM),
             pl.BlockSpec((count, state_width), lambda f: (0, 0)),
             halo,
             pl.BlockSpec((1, band, width, channels), lambda f: (f, 0, 0, 0)),
@@ -121,7 +138,7 @@
             pltpu.VMEM((1, state_width), jnp.float32),
         ],
         compiler_params=pltpu.CompilerParams(dimension_semantics=("arbitrary",)),
-    )(decay, top, frames, bottom, conv_in)
+    )(flags, decay, top, frames, bottom, conv_in)
 
 
 def output_stage(local, cumulative, incoming, frames, conv_out, skip):
@@ -131,12 +148,13 @@
     edges = edges + cumulative[:, None, None, :] * jnp.concatenate(
         [incoming[None, :1], incoming[None, -1:]], axis=1
     )
-    top, bottom = halo_rows(edges.astype(jnp.bfloat16), "rows", 1)
+    top, bottom, flags = halo_rows(edges.astype(jnp.bfloat16), "rows", 1)
     halo = pl.BlockSpec((1, 1, width, state_width), lambda f: (f, 0, 0, 0))
     return pl.pallas_call(
         output_kernel,
         grid=(count,),
         in_specs=[
+            pl.BlockSpec(memory_space=pltpu.SMEM),
             pl.BlockSpec((count, state_width), lambda f: (0, 0)),
             pl.BlockSpec((1, channels), lambda f: (0, 0)),
             pl.BlockSpec((band, width, state_width), lambda f: (0, 0, 0)),
@@ -149,7 +167,7 @@
         out_specs=pl.BlockSpec((1, band, width, channels), lambda f: (f, 0, 0, 0)),
         out_shape=jax.ShapeDtypeStruct((count, band, width, channels), jnp.bfloat16),
         compiler_params=pltpu.CompilerParams(dimension_semantics=("arbitrary",)),
-    )(cumulative, skip.reshape(1, channels), incoming, top, local, bottom, frames, conv_out)
+    )(flags, cumulative, skip.reshape(1, channels), incoming, top, local, bottom, frames, conv_out)
 
 
 def split3(p, rows):

time: 64 us -> 63.8 us (level)
  local copies, waits for them, and re-layouts: 2.19 us -> 4.41 us
  other arithmetic: 4.06 us -> 2.16 us
  waiting for transfers between devices: 36.4 us -> 35.7 us
    select_n x4 -> x0, other arithmetic: 2.45 us -> none  [the longest x2 1.45 us: halo_rows(): return (jnp.where(upper, zero, got), jnp.where(upper, got, zero))]
    unnamed x4 -> x8, local copies, waits for them, and re-layouts: 0.01 us -> 1.31 us
    dynamic_slice x0 -> x2, local copies, waits for them, and re-layouts: none -> 0.93 us  [halo_rows(): lax.dynamic_slice_in_dim(x, row, 1, axis=dim)]
  transfers between devices with their start and end apart: 6 -> 6, of which waited for: 6 -> 6; matrix products, arithmetic and copies ran while one was open for 4% -> 5% of each run, Pallas kernels for 0% -> 0%
where the time goes in v7:
time: 63.8 us; the launch traced here: 63.4 us
  waiting for transfers between devices  35.7 us (56%)
  Pallas kernels  10.9 us (17%)
  starting transfers between devices  9.96 us (16%)
  local copies, waits for them, and re-layouts  4.41 us (7%)
  other arithmetic  2.16 us (3%)
    ppermute x4, waiting for transfers between devices, incoming_state(): got = lax.ppermute(payload, axis, pairs)  34.4 us
    ppermute x4, starting transfers between devices, incoming_state(): got = lax.ppermute(payload, axis, pairs)  7.95 us
    pallas_call x1, Pallas kernels, output_stage(): pl.pallas_call(output_kernel, grid=(count,), in_specs=[pl.BlockSpec(memor...  5.61 us
    pallas_call x1, Pallas kernels, input_stage(): pl.pallas_call(input_kernel, grid=(count,), in_specs=[pl.BlockSpec(memory...  5.29 us
    ppermute x2, starting transfers between devices, halo_rows(): lax.ppermute(lax.dynamic_slice_in_dim(x, row, 1, axis=dim), axis, [(0, 1)...  2.01 us
    ppermute x2, waiting for transfers between devices, halo_rows(): lax.ppermute(lax.dynamic_slice_in_dim(x, row, 1, axis=dim), axis, [(0, 1)...  1.36 us
    unnamed x8, local copies, waits for them, and re-layouts  1.31 us
  transfers between devices with their start and end apart: 6, of which 6 were waited for; matrix products, arithmetic and copies ran while one was open for 5% of the time, Pallas kernels for 0%

profile of v7, /device:TPU:25, one launch (start us, length us, event | category | flops | bytes accessed | tf_op | source)
XLA Modules:
  0.0 63.4 jit_solution(2387540480539707447)
XLA Ops:
  0.0 0.9 %constant_dynamic-slice_fusion.1 = bf16[4,1,128,128]{3,2,1,0:T(8,128)(2,1)S(1)} fusion(bf16[4,8,128,128]{3,2,1,0:T(8,128)(2,1)} %frame_ref.3, s32[]{:T(128)S(6)} %select_n.6), kind=kLoop, calls=%fused_computation.42 | loop fusion | bytes 262148 | tf_op jit(solution)/shard_map/input_conv_and_recurrence/dynamic_slice | solution.py:14
  0.9 0.7 %collective-permute-start = (bf16[4,1,128,128]{3,2,1,0:T(8,128)(2,1)S(1)}, bf16[4,1,128,128]{3,2,1,0:T(8,128)(2,1)S(1)}, u32[]{:S(2)}, u32[]{:S(2)}) collective-permute-start(bf16[4,1,128,128]{3,2,1,0:T(8,128)(2,1)S(1)} %constant_dynamic-slice_fusion.1), channel_id=1, source_target_pairs={{0,1},{1,0},{2,3},{3,2},{4,5},{5,4},{6,7},{7,6},{8,9},{9,8},{10,11... | collective-permute-start | bytes 393224 | tf_op jit(solution)/shard_map/input_conv_and_recurrence/ppermute | solution.py:14
  1.7 0.6 add_convert_fusion.1.flags_ref
  2.3 0.4 collective-permute-done.top_ref.bottom_ref
  2.6 0.0 copy-start.1
  2.6 0.6 %copy-done.1 = bf16[4,1,128,128]{3,2,1,0:T(8,128)(2,1)} copy-done((bf16[4,1,128,128]{3,2,1,0:T(8,128)(2,1)}, bf16[4,1,128,128]{3,2,1,0:T(8,128)(2,1)S(1)}, u32[]{:S(2)}) %copy-start.1) | copy-done | bytes 131096
  3.3 5.3 %input_conv_and_recurrence.1 = (f32[4,8,128,128]{3,2,1,0:T(8,128)}, f32[4,128]{1,0:T(4,128)}, bf16[1040,128]{1,0:T(8,128)(2,1)}) custom-call(s32[2]{0:T(128)} %add_convert_fusion.1.flags_ref, f32[4,128]{1,0:T(4,128)} %decay_ref.1, bf16[4,1,128,128]{3,2,1,0:T(8,128)(2,1)} %copy-done.1, bf16[4,8,128,128]{3,2,1,0:T(8,128)(2,1)} %frame_ref.3, ...), custom_call_target="tpu_custom_call" | custom-call | tf_op jit(solution)/shard_map/input_conv_and_recurrence/pallas_call | solution.py:115
  8.6 0.0 copy-start.3
  8.6 3.1 %collective-permute-start.1 = (bf16[1040,128]{1,0:T(8,128)(2,1)}, bf16[1040,128]{1,0:T(8,128)(2,1)S(1)}, u32[]{:S(2)}, u32[]{:S(2)}) collective-permute-start(bf16[1040,128]{1,0:T(8,128)(2,1)} %get-tuple-element.9), channel_id=1, source_target_pairs={{0,2},{2,4},{4,6},{6,8},{8,10},{10,12},{12,14},{14,16},{16,18},{18... | collective-permute-start | bytes 798728 | tf_op jit(solution)/shard_map/carry_across_blocks/ppermute | solution.py:196
  11.7 1.1 %slice.42 = f32[1,8,128,128]{3,2,1,0:T(8,128)S(1)} slice(f32[4,8,128,128]{3,2,1,0:T(8,128)} %get-tuple-element.10.local_ref), slice={[3:4], [0:8], [0:128], [0:128]} | slice | bytes 1048576 | tf_op jit(solution)/shard_map/carry_across_blocks/slice | solution.py:218
  12.8 7.3 %collective-permute-done.1 = bf16[1040,128]{1,0:T(8,128)(2,1)S(1)} collective-permute-done((bf16[1040,128]{1,0:T(8,128)(2,1)}, bf16[1040,128]{1,0:T(8,128)(2,1)S(1)}, u32[]{:S(2)}, u32[]{:S(2)}) %collective-permute-start.1) | collective-permute-done | bytes 266272 | tf_op jit(solution)/shard_map/carry_across_blocks/ppermute | solution.py:196
  20.1 0.6 %reduce-precision_convert_fusion.5 = (bf16[1,128]{1,0:T(2,128)(2,1)S(1)}, f32[1,128]{1,0:T(1,128)S(1)}, f32[128]{0:T(128)S(1)}) fusion(f32[4,128]{1,0:T(4,128)} %get-tuple-element.8.cum_ref, f32[128]{0:T(128)S(1)} %convert_reduce_fusion.2), kind=kLoop, calls=%fused_computation.54 | loop fusion | flops 384 | bytes 2304 | tf_op jit(solution)/shard_map/convert.7
  20.8 0.1 fusion.5
  20.9 2.2 %collective-permute-start.2 = (bf16[1040,128]{1,0:T(8,128)(2,1)S(1)}, bf16[1040,128]{1,0:T(8,128)(2,1)S(1)}, u32[]{:S(2)}, u32[]{:S(2)}) collective-permute-start(bf16[1040,128]{1,0:T(8,128)(2,1)S(1)} %pad_maximum_fusion), channel_id=1, source_target_pairs={{0,4},{2,6},{4,8},{6,10},{8,12},{10,14},{12,16},{14,18},{16,20},{1... | collective-permute-start | bytes 798728 | tf_op jit(solution)/shard_map/carry_across_blocks/ppermute | solution.py:196
  23.2 1.1 %fusion.28 = (f32[4,1,128,128]{3,2,1,0:T(8,128)S(1)}, f32[4,1,128,128]{3,2,1,0:T(8,128)S(1)}) fusion(f32[4,8,128,128]{3,2,1,0:T(8,128)} %get-tuple-element.10.local_ref), kind=kLoop, calls=%fused_computation.65 | loop fusion | bytes 1048576 | tf_op jit(solution)/shard_map/output_conv/slice | solution.py:147
  24.2 6.2 %collective-permute-done.2 = bf16[1040,128]{1,0:T(8,128)(2,1)S(1)} collective-permute-done((bf16[1040,128]{1,0:T(8,128)(2,1)S(1)}, bf16[1040,128]{1,0:T(8,128)(2,1)S(1)}, u32[]{:S(2)}, u32[]{:S(2)}) %collective-permute-start.2) | collective-permute-done | bytes 266272 | tf_op jit(solution)/shard_map/carry_across_blocks/ppermute | solution.py:196
  30.4 0.0 copy-done.3
  30.5 0.1 fusion.4
  30.6 1.3 %collective-permute-start.3 = (bf16[1040,128]{1,0:T(8,128)(2,1)S(1)}, bf16[1040,128]{1,0:T(8,128)(2,1)S(1)}, u32[]{:S(2)}, u32[]{:S(2)}) collective-permute-start(bf16[1040,128]{1,0:T(8,128)(2,1)S(1)} %pad_maximum_fusion.1), channel_id=1, source_target_pairs={{0,8},{2,10},{4,12},{6,14},{8,16},{10,18},{12,20},{14,22},{16,24},... | collective-permute-start | bytes 798728 | tf_op jit(solution)/shard_map/carry_across_blocks/ppermute | solution.py:196
  32.0 6.3 %collective-permute-done.3 = bf16[1040,128]{1,0:T(8,128)(2,1)S(1)} collective-permute-done((bf16[1040,128]{1,0:T(8,128)(2,1)S(1)}, bf16[1040,128]{1,0:T(8,128)(2,1)S(1)}, u32[]{:S(2)}, u32[]{:S(2)}) %collective-permute-start.3) | collective-permute-done | bytes 266272 | tf_op jit(solution)/shard_map/carry_across_blocks/ppermute | solution.py:196
  38.3 0.2 add_convert_fusion
  38.6 1.3 %collective-permute-start.4 = (bf16[1040,128]{1,0:T(8,128)(2,1)S(1)}, bf16[1040,128]{1,0:T(8,128)(2,1)S(1)}, u32[]{:S(2)}, u32[]{:S(2)}) collective-permute-start(bf16[1040,128]{1,0:T(8,128)(2,1)S(1)} %pad_maximum_fusion.2), channel_id=1, source_target_pairs={{0,16},{2,18},{4,20},{6,22},{8,24},{10,26},{12,28},{14,30},{1,17},... | collective-permute-start | bytes 798728 | tf_op jit(solution)/shard_map/carry_across_blocks/ppermute | solution.py:196
  39.9 14.6 %collective-permute-done.4 = bf16[1040,128]{1,0:T(8,128)(2,1)S(1)} collective-permute-done((bf16[1040,128]{1,0:T(8,128)(2,1)S(1)}, bf16[1040,128]{1,0:T(8,128)(2,1)S(1)}, u32[]{:S(2)}, u32[]{:S(2)}) %collective-permute-start.4) | collective-permute-done | bytes 266272 | tf_op jit(solution)/shard_map/carry_across_blocks/ppermute | solution.py:196
  54.6 0.1 fusion.incoming_ref
  54.7 0.0 copy-start
  54.8 0.1 fusion.3
  54.9 1.3 %collective-permute-start.5 = (bf16[4,1,128,128]{3,2,1,0:T(8,128)(2,1)S(1)}, bf16[4,1,128,128]{3,2,1,0:T(8,128)(2,1)S(1)}, u32[]{:S(2)}, u32[]{:S(2)}) collective-permute-start(bf16[4,1,128,128]{3,2,1,0:T(8,128)(2,1)S(1)} %fusion.3), channel_id=1, source_target_pairs={{0,1},{1,0},{2,3},{3,2},{4,5},{5,4},{6,7},{7,6},{8,9},{9,8},{10,11... | collective-permute-start | bytes 393224 | tf_op jit(solution)/shard_map/output_conv/ppermute | solution.py:14
  56.1 1.0 %collective-permute-done.5.top_ref.bottom_ref = bf16[4,1,128,128]{3,2,1,0:T(8,128)(2,1)S(1)} collective-permute-done((bf16[4,1,128,128]{3,2,1,0:T(8,128)(2,1)S(1)}, bf16[4,1,128,128]{3,2,1,0:T(8,128)(2,1)S(1)}, u32[]{:S(2)}, u32[]{:S(2)}) %collective-permute-start.5) | collective-permute-done | bytes 131104 | tf_op jit(solution)/shard_map/output_conv/ppermute | solution.py:14
  57.1 0.0 copy-start.2
  57.1 0.0 copy-done
  57.1 0.6 %copy-done.2 = bf16[4,1,128,128]{3,2,1,0:T(8,128)(2,1)} copy-done((bf16[4,1,128,128]{3,2,1,0:T(8,128)(2,1)}, bf16[4,1,128,128]{3,2,1,0:T(8,128)(2,1)S(1)}, u32[]{:S(2)}) %copy-start.2) | copy-done | bytes 131096
  57.8 5.6 %output_conv.1 = bf16[4,8,128,128]{3,2,1,0:T(8,128)(2,1)} custom-call(s32[2]{0:T(128)} %add_convert_fusion.1.flags_ref, f32[4,128]{1,0:T(4,128)} %get-tuple-element.8.cum_ref, f32[1,128]{1,0:T(1,128)} %bitcast.45, f32[8,128,128]{2,1,0:T(8,128)} %copy-done, bf16[4,1,128,128]{3,2,1,0:T(8,128)(2,1)} %copy-done.2, ...), custom_call_target="tpu_custom_call" | custom-call | tf_op jit(solution)/shard_map/output_conv/pallas_call | solution.py:153
  (22 shorter events, 0.4 us)
Async XLA Ops:
  0.9 1.7 %collective-permute-start = (bf16[4,1,128,128]{3,2,1,0:T(8,128)(2,1)S(1)}, bf16[4,1,128,128]{3,2,1,0:T(8,128)(2,1)S(1)}, u32[]{:S(2)}, u32[]{:S(2)}) collective-permute-start(bf16[4,1,128,128]{3,2,1,0:T(8,128)(2,1)S(1)} %constant_dynamic-slice_fusion.1), channel_id=1, source_target_pairs={{0,1},{1,0},{2,3},{3,2},{4,5},{5,4},{6,7},{7,6},{8,9},{9,8},{10,11... | collective-permute-start | bytes 393224 | tf_op jit(solution)/shard_map/input_conv_and_recurrence/ppermute | solution.py:14
  2.6 0.7 %copy-start.1 = (bf16[4,1,128,128]{3,2,1,0:T(8,128)(2,1)}, bf16[4,1,128,128]{3,2,1,0:T(8,128)(2,1)S(1)}, u32[]{:S(2)}) copy-start(bf16[4,1,128,128]{3,2,1,0:T(8,128)(2,1)S(1)} %collective-permute-done.top_ref.bottom_ref) | copy-start | bytes 393220
  8.6 21.8 %copy-start.3 = (f32[4,128]{1,0:T(4,128)S(1)}, f32[4,128]{1,0:T(4,128)}, u32[]{:S(2)}) copy-start(f32[4,128]{1,0:T(4,128)} %get-tuple-element.8.cum_ref) | copy-start | bytes 6148
  8.6 11.5 %collective-permute-start.1 = (bf16[1040,128]{1,0:T(8,128)(2,1)}, bf16[1040,128]{1,0:T(8,128)(2,1)S(1)}, u32[]{:S(2)}, u32[]{:S(2)}) collective-permute-start(bf16[1040,128]{1,0:T(8,128)(2,1)} %get-tuple-element.9), channel_id=1, source_target_pairs={{0,2},{2,4},{4,6},{6,8},{8,10},{10,12},{12,14},{14,16},{16,18},{18... | collective-permute-start | bytes 798728 | tf_op jit(solution)/shard_map/carry_across_blocks/ppermute | solution.py:196
  20.9 9.5 %collective-permute-start.2 = (bf16[1040,128]{1,0:T(8,128)(2,1)S(1)}, bf16[1040,128]{1,0:T(8,128)(2,1)S(1)}, u32[]{:S(2)}, u32[]{:S(2)}) collective-permute-start(bf16[1040,128]{1,0:T(8,128)(2,1)S(1)} %pad_maximum_fusion), channel_id=1, source_target_pairs={{0,4},{2,6},{4,8},{6,10},{8,12},{10,14},{12,16},{14,18},{16,20},{1... | collective-permute-start | bytes 798728 | tf_op jit(solution)/shard_map/carry_across_blocks/ppermute | solution.py:196
  30.6 7.7 %collective-permute-start.3 = (bf16[1040,128]{1,0:T(8,128)(2,1)S(1)}, bf16[1040,128]{1,0:T(8,128)(2,1)S(1)}, u32[]{:S(2)}, u32[]{:S(2)}) collective-permute-start(bf16[1040,128]{1,0:T(8,128)(2,1)S(1)} %pad_maximum_fusion.1), channel_id=1, source_target_pairs={{0,8},{2,10},{4,12},{6,14},{8,16},{10,18},{12,20},{14,22},{16,24},... | collective-permute-start | bytes 798728 | tf_op jit(solution)/shard_map/carry_across_blocks/ppermute | solution.py:196
  38.6 16.0 %collective-permute-start.4 = (bf16[1040,128]{1,0:T(8,128)(2,1)S(1)}, bf16[1040,128]{1,0:T(8,128)(2,1)S(1)}, u32[]{:S(2)}, u32[]{:S(2)}) collective-permute-start(bf16[1040,128]{1,0:T(8,128)(2,1)S(1)} %pad_maximum_fusion.2), channel_id=1, source_target_pairs={{0,16},{2,18},{4,20},{6,22},{8,24},{10,26},{12,28},{14,30},{1,17},... | collective-permute-start | bytes 798728 | tf_op jit(solution)/shard_map/carry_across_blocks/ppermute | solution.py:196
  54.7 2.4 %copy-start = (f32[8,128,128]{2,1,0:T(8,128)}, f32[8,128,128]{2,1,0:T(8,128)S(1)}, u32[]{:S(2)}) copy-start(f32[8,128,128]{2,1,0:T(8,128)S(1)} %fusion.incoming_ref) | copy-start | bytes 1572868
  54.9 2.3 %collective-permute-start.5 = (bf16[4,1,128,128]{3,2,1,0:T(8,128)(2,1)S(1)}, bf16[4,1,128,128]{3,2,1,0:T(8,128)(2,1)S(1)}, u32[]{:S(2)}, u32[]{:S(2)}) collective-permute-start(bf16[4,1,128,128]{3,2,1,0:T(8,128)(2,1)S(1)} %fusion.3), channel_id=1, source_target_pairs={{0,1},{1,0},{2,3},{3,2},{4,5},{5,4},{6,7},{7,6},{8,9},{9,8},{10,11... | collective-permute-start | bytes 393224 | tf_op jit(solution)/shard_map/output_conv/ppermute | solution.py:14
  57.1 0.7 %copy-start.2 = (bf16[4,1,128,128]{3,2,1,0:T(8,128)(2,1)}, bf16[4,1,128,128]{3,2,1,0:T(8,128)(2,1)S(1)}, u32[]{:S(2)}) copy-start(bf16[4,1,128,128]{3,2,1,0:T(8,128)(2,1)S(1)} %collective-permute-done.5.top_ref.bottom_ref) | copy-start | bytes 393220

commit v8 on v5

--- a/solution.py
+++ b/solution.py
@@ -9,12 +9,9 @@
 def halo_rows(x, axis, dim):
     size, length = (lax.axis_size(axis), x.shape[dim])
     if size == 2:
-        upper = lax.axis_index(axis) == 0
-        last = lax.slice_in_dim(x, length - 1, length, axis=dim)
-        first = lax.slice_in_dim(x, 0, 1, axis=dim)
-        got = lax.ppermute(jnp.where(upper, last, first), axis, [(0, 1), (1, 0)])
-        zero = jnp.zeros_like(got)
-        return jnp.where(upper, zero, got), jnp.where(upper, got, zero)
+        row = (1 - lax.axis_index(axis)) * (length - 1)
+        got = lax.ppermute(lax.dynamic_slice_in_dim(x, row, 1, axis=dim), axis, [(0, 1), (1, 0)])
+        return got, got
     up = [(i, (i + 1) % size) for i in range(size - 1)]
     down = [(j, i) for i, j in up]
     last = lax.slice_in_dim(x, length - 1, length, axis=dim)
@@ -22,6 +19,15 @@
     before = lax.ppermute(last, axis, up)
     after = lax.ppermute(first, axis, down)
     return before, after
+
+
+def padded_band(above, band_rows, below, axis):
+    if lax.axis_size(axis) == 2:
+        position = lax.axis_index(axis)
+        zero = jnp.zeros_like(above)
+        above = jnp.where(position == 1, above, zero)
+        below = jnp.where(position == 0, below, zero)
+    return jnp.concatenate([above, band_rows, below], axis=0)
 
 
 def conv_taps(x, w_ref):
@@ -44,7 +50,16 @@
 
 
 def input_kernel(
-    decay_ref, top_ref, frame_ref, bottom_ref, w_ref, out_ref, cum_ref, send_ref, state_ref, power_ref
+    decay_ref,
+    top_ref,
+    frame_ref,
+    bottom_ref,
+    w_ref,
+    out_ref,
+    cum_ref,
+    send_ref,
+    state_ref,
+    power_ref,
 ):
     f = pl.program_id(0)
     band, width, m = out_ref.shape[1:]
@@ -55,7 +70,7 @@
         state_ref[...] = jnp.zeros_like(state_ref)
         power_ref[...] = jnp.ones_like(power_ref)
 
-    x = jnp.concatenate([top_ref[0], frame_ref[0], bottom_ref[0]], axis=0)
+    x = padded_band(top_ref[f], frame_ref[0], bottom_ref[f], "rows")
     drive = conv_taps(x, w_ref)
     rate = decay_ref[pl.ds(f, 1), :]
     state = rate * state_ref[...] + drive
@@ -83,7 +98,7 @@
     f = pl.program_id(0)
     band, width, m = out_ref.shape[1:]
     inner = (local_ref[0] + cum_ref[pl.ds(f, 1), :] * incoming_ref[...]).astype(jnp.bfloat16)
-    x = jnp.concatenate([top_ref[0], inner, bottom_ref[0]], axis=0)
+    x = padded_band(top_ref[f], inner, bottom_ref[f], "rows")
     total = conv_taps(x, w_ref)
     frame = frame_ref[0].reshape(band * width, m).astype(jnp.float32)
     total = total + skip_ref[...] * frame
@@ -94,7 +109,7 @@
     count, band, width, channels = frames.shape
     state_width = conv_in.shape[3]
     top, bottom = halo_rows(frames, "rows", 1)
-    halo = pl.BlockSpec((1, 1, width, channels), lambda f: (f, 0, 0, 0))
+    halo = pl.BlockSpec(memory_space=pltpu.VMEM)
     payload_rows = band * width + 16
     return pl.pallas_call(
         input_kernel,
@@ -132,7 +147,7 @@
         [incoming[None, :1], incoming[None, -1:]], axis=1
     )
     top, bottom = halo_rows(edges.astype(jnp.bfloat16), "rows", 1)
-    halo = pl.BlockSpec((1, 1, width, state_width), lambda f: (f, 0, 0, 0))
+    halo = pl.BlockSpec(memory_space=pltpu.VMEM)
     return pl.pallas_call(
         output_kernel,
         grid=(count,),

time: 64 us -> 63.6 us (level)
  other arithmetic: 4.06 us -> 1.55 us
  local copies, waits for them, and re-layouts: 2.19 us -> 4.41 us
    select_n x4 -> x0, other arithmetic: 2.45 us -> none  [the longest x2 1.45 us: halo_rows(): return (jnp.where(upper, zero, got), jnp.where(upper, got, zero))]
    unnamed x4 -> x8, local copies, waits for them, and re-layouts: 0.01 us -> 1.31 us
    dynamic_slice x0 -> x2, local copies, waits for them, and re-layouts: none -> 0.93 us  [halo_rows(): lax.dynamic_slice_in_dim(x, row, 1, axis=dim)]
where the time goes in v8:
time: 63.6 us; the launch traced here: 63.2 us
  waiting for transfers between devices  36.4 us (57%)
  Pallas kernels  10.7 us (17%)
  starting transfers between devices  9.96 us (16%)
  local copies, waits for them, and re-layouts  4.41 us (7%)
  other arithmetic  1.55 us (2%)
    ppermute x4, waiting for transfers between devices, incoming_state(): got = lax.ppermute(payload, axis, pairs)  34.4 us
    ppermute x4, starting transfers between devices, incoming_state(): got = lax.ppermute(payload, axis, pairs)  7.95 us
    pallas_call x1, Pallas kernels, output_stage(): pl.pallas_call(output_kernel, grid=(count,), in_specs=[pl.BlockSpec((coun...  5.48 us
    pallas_call x1, Pallas kernels, input_stage(): pl.pallas_call(input_kernel, grid=(count,), in_specs=[pl.BlockSpec((count...  5.21 us
    ppermute x2, starting transfers between devices, halo_rows(): lax.ppermute(lax.dynamic_slice_in_dim(x, row, 1, axis=dim), axis, [(0, 1)...  2.01 us
    ppermute x2, waiting for transfers between devices, halo_rows(): lax.ppermute(lax.dynamic_slice_in_dim(x, row, 1, axis=dim), axis, [(0, 1)...  1.97 us
    unnamed x8, local copies, waits for them, and re-layouts  1.31 us
  transfers between devices with their start and end apart: 6, of which 6 were waited for; matrix products, arithmetic and copies ran while one was open for 4% of the time, Pallas kernels for 0%

profile of v8, /device:TPU:25, one launch (start us, length us, event | category | flops | bytes accessed | tf_op | source)
XLA Modules:
  0.0 63.2 jit_solution(2337244401661387049)
XLA Ops:
  0.0 0.9 %constant_dynamic-slice_fusion.1 = bf16[4,1,128,128]{3,2,1,0:T(8,128)(2,1)S(1)} fusion(bf16[4,8,128,128]{3,2,1,0:T(8,128)(2,1)} %frame_ref.3, s32[]{:T(128)S(6)} %select_n.6), kind=kLoop, calls=%fused_computation.41 | loop fusion | bytes 262148 | tf_op jit(solution)/shard_map/input_conv_and_recurrence/dynamic_slice | solution.py:13
  0.9 0.7 %collective-permute-start = (bf16[4,1,128,128]{3,2,1,0:T(8,128)(2,1)S(1)}, bf16[4,1,128,128]{3,2,1,0:T(8,128)(2,1)S(1)}, u32[]{:S(2)}, u32[]{:S(2)}) collective-permute-start(bf16[4,1,128,128]{3,2,1,0:T(8,128)(2,1)S(1)} %constant_dynamic-slice_fusion.1), channel_id=1, source_target_pairs={{0,1},{1,0},{2,3},{3,2},{4,5},{5,4},{6,7},{7,6},{8,9},{9,8},{10,11... | collective-permute-start | bytes 393224 | tf_op jit(solution)/shard_map/input_conv_and_recurrence/ppermute | solution.py:13
  1.7 1.0 %collective-permute-done.top_ref.bottom_ref = bf16[4,1,128,128]{3,2,1,0:T(8,128)(2,1)S(1)} collective-permute-done((bf16[4,1,128,128]{3,2,1,0:T(8,128)(2,1)S(1)}, bf16[4,1,128,128]{3,2,1,0:T(8,128)(2,1)S(1)}, u32[]{:S(2)}, u32[]{:S(2)}) %collective-permute-start) | collective-permute-done | bytes 131104 | tf_op jit(solution)/shard_map/input_conv_and_recurrence/ppermute | solution.py:13
  2.6 0.0 copy-start.1
  2.6 0.6 %copy-done.1 = bf16[4,1,128,128]{3,2,1,0:T(8,128)(2,1)} copy-done((bf16[4,1,128,128]{3,2,1,0:T(8,128)(2,1)}, bf16[4,1,128,128]{3,2,1,0:T(8,128)(2,1)S(1)}, u32[]{:S(2)}) %copy-start.1) | copy-done | bytes 131096
  3.3 5.2 %input_conv_and_recurrence.1 = (f32[4,8,128,128]{3,2,1,0:T(8,128)}, f32[4,128]{1,0:T(4,128)}, bf16[1040,128]{1,0:T(8,128)(2,1)}) custom-call(f32[4,128]{1,0:T(4,128)} %decay_ref.1, bf16[4,1,128,128]{3,2,1,0:T(8,128)(2,1)} %copy-done.1, bf16[4,8,128,128]{3,2,1,0:T(8,128)(2,1)} %frame_ref.3, bf16[4,1,128,128]{3,2,1,0:T(8,128)(2,1)} %copy-done.1, ...), custom_call_target="tpu_custom_call" | custom-call | tf_op jit(solution)/shard_map/input_conv_and_recurrence/pallas_call | solution.py:114
  8.5 0.0 copy-start.3
  8.5 3.1 %collective-permute-start.1 = (bf16[1040,128]{1,0:T(8,128)(2,1)}, bf16[1040,128]{1,0:T(8,128)(2,1)S(1)}, u32[]{:S(2)}, u32[]{:S(2)}) collective-permute-start(bf16[1040,128]{1,0:T(8,128)(2,1)} %get-tuple-element.9), channel_id=1, source_target_pairs={{0,2},{2,4},{4,6},{6,8},{8,10},{10,12},{12,14},{14,16},{16,18},{18... | collective-permute-start | bytes 798728 | tf_op jit(solution)/shard_map/carry_across_blocks/ppermute | solution.py:193
  11.6 1.1 %slice.42 = f32[1,8,128,128]{3,2,1,0:T(8,128)S(1)} slice(f32[4,8,128,128]{3,2,1,0:T(8,128)} %get-tuple-element.10.local_ref), slice={[3:4], [0:8], [0:128], [0:128]} | slice | bytes 1048576 | tf_op jit(solution)/shard_map/carry_across_blocks/slice | solution.py:215
  12.7 7.3 %collective-permute-done.1 = bf16[1040,128]{1,0:T(8,128)(2,1)S(1)} collective-permute-done((bf16[1040,128]{1,0:T(8,128)(2,1)}, bf16[1040,128]{1,0:T(8,128)(2,1)S(1)}, u32[]{:S(2)}, u32[]{:S(2)}) %collective-permute-start.1) | collective-permute-done | bytes 266272 | tf_op jit(solution)/shard_map/carry_across_blocks/ppermute | solution.py:193
  20.0 0.6 %reduce-precision_convert_fusion.5 = (bf16[1,128]{1,0:T(2,128)(2,1)S(1)}, f32[1,128]{1,0:T(1,128)S(1)}, f32[128]{0:T(128)S(1)}) fusion(f32[4,128]{1,0:T(4,128)} %get-tuple-element.8.cum_ref, f32[128]{0:T(128)S(1)} %convert_reduce_fusion.2), kind=kLoop, calls=%fused_computation.53 | loop fusion | flops 384 | bytes 2304 | tf_op jit(solution)/shard_map/convert.7
  20.7 0.1 fusion.5
  20.8 2.2 %collective-permute-start.2 = (bf16[1040,128]{1,0:T(8,128)(2,1)S(1)}, bf16[1040,128]{1,0:T(8,128)(2,1)S(1)}, u32[]{:S(2)}, u32[]{:S(2)}) collective-permute-start(bf16[1040,128]{1,0:T(8,128)(2,1)S(1)} %pad_maximum_fusion), channel_id=1, source_target_pairs={{0,4},{2,6},{4,8},{6,10},{8,12},{10,14},{12,16},{14,18},{16,20},{1... | collective-permute-start | bytes 798728 | tf_op jit(solution)/shard_map/carry_across_blocks/ppermute | solution.py:193
  23.1 1.1 %fusion.28 = (f32[4,1,128,128]{3,2,1,0:T(8,128)S(1)}, f32[4,1,128,128]{3,2,1,0:T(8,128)S(1)}) fusion(f32[4,8,128,128]{3,2,1,0:T(8,128)} %get-tuple-element.10.local_ref), kind=kLoop, calls=%fused_computation.64 | loop fusion | bytes 1048576 | tf_op jit(solution)/shard_map/output_conv/slice | solution.py:145
  24.2 6.2 %collective-permute-done.2 = bf16[1040,128]{1,0:T(8,128)(2,1)S(1)} collective-permute-done((bf16[1040,128]{1,0:T(8,128)(2,1)S(1)}, bf16[1040,128]{1,0:T(8,128)(2,1)S(1)}, u32[]{:S(2)}, u32[]{:S(2)}) %collective-permute-start.2) | collective-permute-done | bytes 266272 | tf_op jit(solution)/shard_map/carry_across_blocks/ppermute | solution.py:193
  30.3 0.0 copy-done.3
  30.4 0.1 fusion.4
  30.5 1.3 %collective-permute-start.3 = (bf16[1040,128]{1,0:T(8,128)(2,1)S(1)}, bf16[1040,128]{1,0:T(8,128)(2,1)S(1)}, u32[]{:S(2)}, u32[]{:S(2)}) collective-permute-start(bf16[1040,128]{1,0:T(8,128)(2,1)S(1)} %pad_maximum_fusion.1), channel_id=1, source_target_pairs={{0,8},{2,10},{4,12},{6,14},{8,16},{10,18},{12,20},{14,22},{16,24},... | collective-permute-start | bytes 798728 | tf_op jit(solution)/shard_map/carry_across_blocks/ppermute | solution.py:193
  31.9 6.3 %collective-permute-done.3 = bf16[1040,128]{1,0:T(8,128)(2,1)S(1)} collective-permute-done((bf16[1040,128]{1,0:T(8,128)(2,1)S(1)}, bf16[1040,128]{1,0:T(8,128)(2,1)S(1)}, u32[]{:S(2)}, u32[]{:S(2)}) %collective-permute-start.3) | collective-permute-done | bytes 266272 | tf_op jit(solution)/shard_map/carry_across_blocks/ppermute | solution.py:193
  38.3 0.2 add_convert_fusion
  38.5 1.3 %collective-permute-start.4 = (bf16[1040,128]{1,0:T(8,128)(2,1)S(1)}, bf16[1040,128]{1,0:T(8,128)(2,1)S(1)}, u32[]{:S(2)}, u32[]{:S(2)}) collective-permute-start(bf16[1040,128]{1,0:T(8,128)(2,1)S(1)} %pad_maximum_fusion.2), channel_id=1, source_target_pairs={{0,16},{2,18},{4,20},{6,22},{8,24},{10,26},{12,28},{14,30},{1,17},... | collective-permute-start | bytes 798728 | tf_op jit(solution)/shard_map/carry_across_blocks/ppermute | solution.py:193
  39.8 14.6 %collective-permute-done.4 = bf16[1040,128]{1,0:T(8,128)(2,1)S(1)} collective-permute-done((bf16[1040,128]{1,0:T(8,128)(2,1)S(1)}, bf16[1040,128]{1,0:T(8,128)(2,1)S(1)}, u32[]{:S(2)}, u32[]{:S(2)}) %collective-permute-start.4) | collective-permute-done | bytes 266272 | tf_op jit(solution)/shard_map/carry_across_blocks/ppermute | solution.py:193
  54.5 0.1 fusion.incoming_ref
  54.6 0.0 copy-start
  54.7 0.1 fusion.3
  54.8 1.3 %collective-permute-start.5 = (bf16[4,1,128,128]{3,2,1,0:T(8,128)(2,1)S(1)}, bf16[4,1,128,128]{3,2,1,0:T(8,128)(2,1)S(1)}, u32[]{:S(2)}, u32[]{:S(2)}) collective-permute-start(bf16[4,1,128,128]{3,2,1,0:T(8,128)(2,1)S(1)} %fusion.3), channel_id=1, source_target_pairs={{0,1},{1,0},{2,3},{3,2},{4,5},{5,4},{6,7},{7,6},{8,9},{9,8},{10,11... | collective-permute-start | bytes 393224 | tf_op jit(solution)/shard_map/output_conv/ppermute | solution.py:13
  56.0 1.0 %collective-permute-done.5.top_ref.bottom_ref = bf16[4,1,128,128]{3,2,1,0:T(8,128)(2,1)S(1)} collective-permute-done((bf16[4,1,128,128]{3,2,1,0:T(8,128)(2,1)S(1)}, bf16[4,1,128,128]{3,2,1,0:T(8,128)(2,1)S(1)}, u32[]{:S(2)}, u32[]{:S(2)}) %collective-permute-start.5) | collective-permute-done | bytes 131104 | tf_op jit(solution)/shard_map/output_conv/ppermute | solution.py:13
  57.0 0.0 copy-start.2
  57.0 0.0 copy-done
  57.0 0.6 %copy-done.2 = bf16[4,1,128,128]{3,2,1,0:T(8,128)(2,1)} copy-done((bf16[4,1,128,128]{3,2,1,0:T(8,128)(2,1)}, bf16[4,1,128,128]{3,2,1,0:T(8,128)(2,1)S(1)}, u32[]{:S(2)}) %copy-start.2) | copy-done | bytes 131096
  57.7 5.5 %output_conv.1 = bf16[4,8,128,128]{3,2,1,0:T(8,128)(2,1)} custom-call(f32[4,128]{1,0:T(4,128)} %get-tuple-element.8.cum_ref, f32[1,128]{1,0:T(1,128)} %bitcast.43, f32[8,128,128]{2,1,0:T(8,128)} %copy-done, bf16[4,1,128,128]{3,2,1,0:T(8,128)(2,1)} %copy-done.2, f32[4,8,128,128]{3,2,1,0:T(8,128)} %get-tuple-element.10.local_ref, ...), custom_call_target="tpu_custom_call" | custom-call | tf_op jit(solution)/shard_map/output_conv/pallas_call | solution.py:151
  (22 shorter events, 0.4 us)
Async XLA Ops:
  0.9 1.7 %collective-permute-start = (bf16[4,1,128,128]{3,2,1,0:T(8,128)(2,1)S(1)}, bf16[4,1,128,128]{3,2,1,0:T(8,128)(2,1)S(1)}, u32[]{:S(2)}, u32[]{:S(2)}) collective-permute-start(bf16[4,1,128,128]{3,2,1,0:T(8,128)(2,1)S(1)} %constant_dynamic-slice_fusion.1), channel_id=1, source_target_pairs={{0,1},{1,0},{2,3},{3,2},{4,5},{5,4},{6,7},{7,6},{8,9},{9,8},{10,11... | collective-permute-start | bytes 393224 | tf_op jit(solution)/shard_map/input_conv_and_recurrence/ppermute | solution.py:13
  2.6 0.7 %copy-start.1 = (bf16[4,1,128,128]{3,2,1,0:T(8,128)(2,1)}, bf16[4,1,128,128]{3,2,1,0:T(8,128)(2,1)S(1)}, u32[]{:S(2)}) copy-start(bf16[4,1,128,128]{3,2,1,0:T(8,128)(2,1)S(1)} %collective-permute-done.top_ref.bottom_ref) | copy-start | bytes 393220
  8.5 21.8 %copy-start.3 = (f32[4,128]{1,0:T(4,128)S(1)}, f32[4,128]{1,0:T(4,128)}, u32[]{:S(2)}) copy-start(f32[4,128]{1,0:T(4,128)} %get-tuple-element.8.cum_ref) | copy-start | bytes 6148
  8.5 11.5 %collective-permute-start.1 = (bf16[1040,128]{1,0:T(8,128)(2,1)}, bf16[1040,128]{1,0:T(8,128)(2,1)S(1)}, u32[]{:S(2)}, u32[]{:S(2)}) collective-permute-start(bf16[1040,128]{1,0:T(8,128)(2,1)} %get-tuple-element.9), channel_id=1, source_target_pairs={{0,2},{2,4},{4,6},{6,8},{8,10},{10,12},{12,14},{14,16},{16,18},{18... | collective-permute-start | bytes 798728 | tf_op jit(solution)/shard_map/carry_across_blocks/ppermute | solution.py:193
  20.8 9.5 %collective-permute-start.2 = (bf16[1040,128]{1,0:T(8,128)(2,1)S(1)}, bf16[1040,128]{1,0:T(8,128)(2,1)S(1)}, u32[]{:S(2)}, u32[]{:S(2)}) collective-permute-start(bf16[1040,128]{1,0:T(8,128)(2,1)S(1)} %pad_maximum_fusion), channel_id=1, source_target_pairs={{0,4},{2,6},{4,8},{6,10},{8,12},{10,14},{12,16},{14,18},{16,20},{1... | collective-permute-start | bytes 798728 | tf_op jit(solution)/shard_map/carry_across_blocks/ppermute | solution.py:193
  30.5 7.7 %collective-permute-start.3 = (bf16[1040,128]{1,0:T(8,128)(2,1)S(1)}, bf16[1040,128]{1,0:T(8,128)(2,1)S(1)}, u32[]{:S(2)}, u32[]{:S(2)}) collective-permute-start(bf16[1040,128]{1,0:T(8,128)(2,1)S(1)} %pad_maximum_fusion.1), channel_id=1, source_target_pairs={{0,8},{2,10},{4,12},{6,14},{8,16},{10,18},{12,20},{14,22},{16,24},... | collective-permute-start | bytes 798728 | tf_op jit(solution)/shard_map/carry_across_blocks/ppermute | solution.py:193
  38.5 16.0 %collective-permute-start.4 = (bf16[1040,128]{1,0:T(8,128)(2,1)S(1)}, bf16[1040,128]{1,0:T(8,128)(2,1)S(1)}, u32[]{:S(2)}, u32[]{:S(2)}) collective-permute-start(bf16[1040,128]{1,0:T(8,128)(2,1)S(1)} %pad_maximum_fusion.2), channel_id=1, source_target_pairs={{0,16},{2,18},{4,20},{6,22},{8,24},{10,26},{12,28},{14,30},{1,17},... | collective-permute-start | bytes 798728 | tf_op jit(solution)/shard_map/carry_across_blocks/ppermute | solution.py:193
  54.6 2.4 %copy-start = (f32[8,128,128]{2,1,0:T(8,128)}, f32[8,128,128]{2,1,0:T(8,128)S(1)}, u32[]{:S(2)}) copy-start(f32[8,128,128]{2,1,0:T(8,128)S(1)} %fusion.incoming_ref) | copy-start | bytes 1572868
  54.8 2.3 %collective-permute-start.5 = (bf16[4,1,128,128]{3,2,1,0:T(8,128)(2,1)S(1)}, bf16[4,1,128,128]{3,2,1,0:T(8,128)(2,1)S(1)}, u32[]{:S(2)}, u32[]{:S(2)}) collective-permute-start(bf16[4,1,128,128]{3,2,1,0:T(8,128)(2,1)S(1)} %fusion.3), channel_id=1, source_target_pairs={{0,1},{1,0},{2,3},{3,2},{4,5},{5,4},{6,7},{7,6},{8,9},{9,8},{10,11... | collective-permute-start | bytes 393224 | tf_op jit(solution)/shard_map/output_conv/ppermute | solution.py:13
  57.0 0.7 %copy-start.2 = (bf16[4,1,128,128]{3,2,1,0:T(8,128)(2,1)}, bf16[4,1,128,128]{3,2,1,0:T(8,128)(2,1)S(1)}, u32[]{:S(2)}) copy-start(bf16[4,1,128,128]{3,2,1,0:T(8,128)(2,1)S(1)} %collective-permute-done.5.top_ref.bottom_ref) | copy-start | bytes 393220

commit v9 on v8

--- a/solution.py
+++ b/solution.py
@@ -58,6 +58,7 @@
     out_ref,
     cum_ref,
     send_ref,
+    block_ref,
     state_ref,
     power_ref,
 ):
@@ -86,6 +87,7 @@
         rest = power - hi.astype(jnp.float32)
         mid = rest.astype(jnp.bfloat16)
         low = (rest - mid.astype(jnp.float32)).astype(jnp.bfloat16)
+        block_ref[...] = power
         pad = send_ref.shape[0] - cells - 3
         send_ref[...] = jnp.concatenate(
             [state.astype(jnp.bfloat16), hi, mid, low, jnp.zeros((pad, m), jnp.bfloat16)], axis=0
@@ -125,11 +127,13 @@
             pl.BlockSpec((1, band, width, state_width), lambda f: (f, 0, 0, 0)),
             pl.BlockSpec((count, state_width), lambda f: (0, 0)),
             pl.BlockSpec((payload_rows, state_width), lambda f: (0, 0)),
+            pl.BlockSpec((1, state_width), lambda f: (0, 0)),
         ],
         out_shape=[
             jax.ShapeDtypeStruct((count, band, width, state_width), jnp.float32),
             jax.ShapeDtypeStruct((count, state_width), jnp.float32),
             jax.ShapeDtypeStruct((payload_rows, state_width), jnp.bfloat16),
+            jax.ShapeDtypeStruct((1, state_width), jnp.float32),
         ],
         scratch_shapes=[
             pltpu.VMEM((band * width, state_width), jnp.float32),
@@ -210,9 +214,9 @@
 
 def shards(frames, conv_in, decay, conv_out, skip):
     with jax.named_scope("input_conv_and_recurrence"):
-        local, cumulative, first_payload = input_stage(frames, conv_in, decay)
+        local, cumulative, first_payload, block = input_stage(frames, conv_in, decay)
     with jax.named_scope("carry_across_blocks"):
-        incoming = incoming_state(cumulative[-1], local[-1], first_payload, "tm")
+        incoming = incoming_state(block[0], local[-1], first_payload, "tm")
     with jax.named_scope("output_conv"):
         return output_stage(local, cumulative, incoming, frames, conv_out, skip)
 

time: 63.6 us -> 64.3 us (1.011)
    unnamed x8 -> x10, local copies, waits for them, and re-layouts: 1.31 us -> 1.3 us
where the time goes in v9:
time: 64.3 us; the launch traced here: 63.9 us
  waiting for transfers between devices  36.3 us (56%)
  Pallas kernels  10.8 us (17%)
  starting transfers between devices  10.1 us (16%)
  local copies, waits for them, and re-layouts  4.4 us (7%)
  other arithmetic  2.09 us (3%)
    ppermute x4, waiting for transfers between devices, incoming_state(): got = lax.ppermute(payload, axis, pairs)  34.4 us
    ppermute x4, starting transfers between devices, incoming_state(): got = lax.ppermute(payload, axis, pairs)  8.07 us
    pallas_call x1, Pallas kernels, output_stage(): pl.pallas_call(output_kernel, grid=(count,), in_specs=[pl.BlockSpec((coun...  5.48 us
    pallas_call x1, Pallas kernels, input_stage(): pl.pallas_call(input_kernel, grid=(count,), in_specs=[pl.BlockSpec((count...  5.28 us
    ppermute x2, starting transfers between devices, halo_rows(): lax.ppermute(lax.dynamic_slice_in_dim(x, row, 1, axis=dim), axis, [(0, 1)...  2.01 us
    ppermute x2, waiting for transfers between devices, halo_rows(): lax.ppermute(lax.dynamic_slice_in_dim(x, row, 1, axis=dim), axis, [(0, 1)...  1.97 us
    unnamed x10, local copies, waits for them, and re-layouts  1.3 us
  transfers between devices with their start and end apart: 6, of which 6 were waited for; matrix products, arithmetic and copies ran while one was open for 4% of the time, Pallas kernels for 0%

profile of v9, /device:TPU:25, one launch (start us, length us, event | category | flops | bytes accessed | tf_op | source)
XLA Modules:
  0.0 63.9 jit_solution(6938705484146160293)
XLA Ops:
  0.0 0.9 %constant_dynamic-slice_fusion.1 = bf16[4,1,128,128]{3,2,1,0:T(8,128)(2,1)S(1)} fusion(bf16[4,8,128,128]{3,2,1,0:T(8,128)(2,1)} %frame_ref.3, s32[]{:T(128)S(6)} %select_n.6), kind=kLoop, calls=%fused_computation.41 | loop fusion | bytes 262148 | tf_op jit(solution)/shard_map/input_conv_and_recurrence/dynamic_slice | solution.py:13
  0.9 0.7 %collective-permute-start = (bf16[4,1,128,128]{3,2,1,0:T(8,128)(2,1)S(1)}, bf16[4,1,128,128]{3,2,1,0:T(8,128)(2,1)S(1)}, u32[]{:S(2)}, u32[]{:S(2)}) collective-permute-start(bf16[4,1,128,128]{3,2,1,0:T(8,128)(2,1)S(1)} %constant_dynamic-slice_fusion.1), channel_id=1, source_target_pairs={{0,1},{1,0},{2,3},{3,2},{4,5},{5,4},{6,7},{7,6},{8,9},{9,8},{10,11... | collective-permute-start | bytes 393224 | tf_op jit(solution)/shard_map/input_conv_and_recurrence/ppermute | solution.py:13
  1.7 1.0 %collective-permute-done.top_ref.bottom_ref = bf16[4,1,128,128]{3,2,1,0:T(8,128)(2,1)S(1)} collective-permute-done((bf16[4,1,128,128]{3,2,1,0:T(8,128)(2,1)S(1)}, bf16[4,1,128,128]{3,2,1,0:T(8,128)(2,1)S(1)}, u32[]{:S(2)}, u32[]{:S(2)}) %collective-permute-start) | collective-permute-done | bytes 131104 | tf_op jit(solution)/shard_map/input_conv_and_recurrence/ppermute | solution.py:13
  2.6 0.0 copy-start.1
  2.6 0.6 %copy-done.1 = bf16[4,1,128,128]{3,2,1,0:T(8,128)(2,1)} copy-done((bf16[4,1,128,128]{3,2,1,0:T(8,128)(2,1)}, bf16[4,1,128,128]{3,2,1,0:T(8,128)(2,1)S(1)}, u32[]{:S(2)}) %copy-start.1) | copy-done | bytes 131096
  3.3 5.3 %input_conv_and_recurrence.1 = (f32[4,8,128,128]{3,2,1,0:T(8,128)}, f32[4,128]{1,0:T(4,128)}, bf16[1040,128]{1,0:T(8,128)(2,1)}, f32[1,128]{1,0:T(1,128)}) custom-call(f32[4,128]{1,0:T(4,128)} %decay_ref.1, bf16[4,1,128,128]{3,2,1,0:T(8,128)(2,1)} %copy-done.1, bf16[4,8,128,128]{3,2,1,0:T(8,128)(2,1)} %frame_ref.3, bf16[4,1,128,128]{3,2,1,0:T(8,128)(2,1)} %copy-done.1, ...), custom_call_target="tpu_custom_call" | custom-call | tf_op jit(solution)/shard_map/input_conv_and_recurrence/pallas_call | solution.py:116
  8.6 0.0 copy-start.3
  8.6 3.2 %collective-permute-start.1 = (bf16[1040,128]{1,0:T(8,128)(2,1)}, bf16[1040,128]{1,0:T(8,128)(2,1)S(1)}, u32[]{:S(2)}, u32[]{:S(2)}) collective-permute-start(bf16[1040,128]{1,0:T(8,128)(2,1)} %get-tuple-element.10), channel_id=1, source_target_pairs={{0,2},{2,4},{4,6},{6,8},{8,10},{10,12},{12,14},{14,16},{16,18},{18... | collective-permute-start | bytes 798728 | tf_op jit(solution)/shard_map/carry_across_blocks/ppermute | solution.py:197
  11.8 1.1 %slice.38 = f32[1,8,128,128]{3,2,1,0:T(8,128)S(1)} slice(f32[4,8,128,128]{3,2,1,0:T(8,128)} %get-tuple-element.12.local_ref), slice={[3:4], [0:8], [0:128], [0:128]} | slice | bytes 1048576 | tf_op jit(solution)/shard_map/carry_across_blocks/slice | solution.py:219
  12.9 7.3 %collective-permute-done.1 = bf16[1040,128]{1,0:T(8,128)(2,1)S(1)} collective-permute-done((bf16[1040,128]{1,0:T(8,128)(2,1)}, bf16[1040,128]{1,0:T(8,128)(2,1)S(1)}, u32[]{:S(2)}, u32[]{:S(2)}) %collective-permute-start.1) | collective-permute-done | bytes 266272 | tf_op jit(solution)/shard_map/carry_across_blocks/ppermute | solution.py:197
  20.2 0.6 reduce-precision_convert_fusion.5
  20.8 0.7 %fusion.5 = bf16[1024,128]{1,0:T(8,128)(2,1)S(1)} fusion(f32[1,8,128,128]{3,2,1,0:T(8,128)S(1)} %slice.38, bf16[1040,128]{1,0:T(8,128)(2,1)S(1)} %collective-permute-done.1, f32[128]{0:T(128)} %bitcast.41), kind=kLoop, calls=%fused_computation.18 | loop fusion | flops 524288 | bytes 1049088 | tf_op jit(solution)/shard_map/carry_across_blocks/convert_element_type | solution.py:195
  21.5 2.2 %collective-permute-start.2 = (bf16[1040,128]{1,0:T(8,128)(2,1)S(1)}, bf16[1040,128]{1,0:T(8,128)(2,1)S(1)}, u32[]{:S(2)}, u32[]{:S(2)}) collective-permute-start(bf16[1040,128]{1,0:T(8,128)(2,1)S(1)} %pad_maximum_fusion), channel_id=1, source_target_pairs={{0,4},{2,6},{4,8},{6,10},{8,12},{10,14},{12,16},{14,18},{16,20},{1... | collective-permute-start | bytes 798728 | tf_op jit(solution)/shard_map/carry_across_blocks/ppermute | solution.py:197
  23.8 1.1 %fusion.26 = (f32[4,1,128,128]{3,2,1,0:T(8,128)S(1)}, f32[4,1,128,128]{3,2,1,0:T(8,128)S(1)}) fusion(f32[4,8,128,128]{3,2,1,0:T(8,128)} %get-tuple-element.12.local_ref), kind=kLoop, calls=%fused_computation.63 | loop fusion | bytes 1048576 | tf_op jit(solution)/shard_map/output_conv/slice | solution.py:149
  24.9 6.2 %collective-permute-done.2 = bf16[1040,128]{1,0:T(8,128)(2,1)S(1)} collective-permute-done((bf16[1040,128]{1,0:T(8,128)(2,1)S(1)}, bf16[1040,128]{1,0:T(8,128)(2,1)S(1)}, u32[]{:S(2)}, u32[]{:S(2)}) %collective-permute-start.2) | collective-permute-done | bytes 266272 | tf_op jit(solution)/shard_map/carry_across_blocks/ppermute | solution.py:197
  31.1 0.0 copy-done.3
  31.1 0.1 fusion.4
  31.3 1.3 %collective-permute-start.3 = (bf16[1040,128]{1,0:T(8,128)(2,1)S(1)}, bf16[1040,128]{1,0:T(8,128)(2,1)S(1)}, u32[]{:S(2)}, u32[]{:S(2)}) collective-permute-start(bf16[1040,128]{1,0:T(8,128)(2,1)S(1)} %pad_maximum_fusion.1), channel_id=1, source_target_pairs={{0,8},{2,10},{4,12},{6,14},{8,16},{10,18},{12,20},{14,22},{16,24},... | collective-permute-start | bytes 798728 | tf_op jit(solution)/shard_map/carry_across_blocks/ppermute | solution.py:197
  32.7 6.3 %collective-permute-done.3 = bf16[1040,128]{1,0:T(8,128)(2,1)S(1)} collective-permute-done((bf16[1040,128]{1,0:T(8,128)(2,1)S(1)}, bf16[1040,128]{1,0:T(8,128)(2,1)S(1)}, u32[]{:S(2)}, u32[]{:S(2)}) %collective-permute-start.3) | collective-permute-done | bytes 266272 | tf_op jit(solution)/shard_map/carry_across_blocks/ppermute | solution.py:197
  39.0 0.2 add_convert_fusion
  39.2 1.3 %collective-permute-start.4 = (bf16[1040,128]{1,0:T(8,128)(2,1)S(1)}, bf16[1040,128]{1,0:T(8,128)(2,1)S(1)}, u32[]{:S(2)}, u32[]{:S(2)}) collective-permute-start(bf16[1040,128]{1,0:T(8,128)(2,1)S(1)} %pad_maximum_fusion.2), channel_id=1, source_target_pairs={{0,16},{2,18},{4,20},{6,22},{8,24},{10,26},{12,28},{14,30},{1,17},... | collective-permute-start | bytes 798728 | tf_op jit(solution)/shard_map/carry_across_blocks/ppermute | solution.py:197
  40.5 0.0 copy-start.4
  40.6 14.6 %collective-permute-done.4 = bf16[1040,128]{1,0:T(8,128)(2,1)S(1)} collective-permute-done((bf16[1040,128]{1,0:T(8,128)(2,1)S(1)}, bf16[1040,128]{1,0:T(8,128)(2,1)S(1)}, u32[]{:S(2)}, u32[]{:S(2)}) %collective-permute-start.4) | collective-permute-done | bytes 266272 | tf_op jit(solution)/shard_map/carry_across_blocks/ppermute | solution.py:197
  55.2 0.1 fusion.incoming_ref
  55.3 0.0 copy-start
  55.4 0.0 copy-done.4
  55.4 0.1 fusion.3
  55.5 1.3 %collective-permute-start.5 = (bf16[4,1,128,128]{3,2,1,0:T(8,128)(2,1)S(1)}, bf16[4,1,128,128]{3,2,1,0:T(8,128)(2,1)S(1)}, u32[]{:S(2)}, u32[]{:S(2)}) collective-permute-start(bf16[4,1,128,128]{3,2,1,0:T(8,128)(2,1)S(1)} %fusion.3), channel_id=1, source_target_pairs={{0,1},{1,0},{2,3},{3,2},{4,5},{5,4},{6,7},{7,6},{8,9},{9,8},{10,11... | collective-permute-start | bytes 393224 | tf_op jit(solution)/shard_map/output_conv/ppermute | solution.py:13
  56.8 1.0 %collective-permute-done.5.top_ref.bottom_ref = bf16[4,1,128,128]{3,2,1,0:T(8,128)(2,1)S(1)} collective-permute-done((bf16[4,1,128,128]{3,2,1,0:T(8,128)(2,1)S(1)}, bf16[4,1,128,128]{3,2,1,0:T(8,128)(2,1)S(1)}, u32[]{:S(2)}, u32[]{:S(2)}) %collective-permute-start.5) | collective-permute-done | bytes 131104 | tf_op jit(solution)/shard_map/output_conv/ppermute | solution.py:13
  57.8 0.0 copy-start.2
  57.8 0.0 copy-done
  57.8 0.6 %copy-done.2 = bf16[4,1,128,128]{3,2,1,0:T(8,128)(2,1)} copy-done((bf16[4,1,128,128]{3,2,1,0:T(8,128)(2,1)}, bf16[4,1,128,128]{3,2,1,0:T(8,128)(2,1)S(1)}, u32[]{:S(2)}) %copy-start.2) | copy-done | bytes 131096
  58.4 5.5 %output_conv.1 = bf16[4,8,128,128]{3,2,1,0:T(8,128)(2,1)} custom-call(f32[4,128]{1,0:T(4,128)} %get-tuple-element.9.cum_ref, f32[1,128]{1,0:T(1,128)} %bitcast.44, f32[8,128,128]{2,1,0:T(8,128)} %copy-done, bf16[4,1,128,128]{3,2,1,0:T(8,128)(2,1)} %copy-done.2, f32[4,8,128,128]{3,2,1,0:T(8,128)} %get-tuple-element.12.local_ref, ...), custom_call_target="tpu_custom_call" | custom-call | tf_op jit(solution)/shard_map/output_conv/pallas_call | solution.py:155
  (22 shorter events, 0.4 us)
Async XLA Ops:
  0.9 1.7 %collective-permute-start = (bf16[4,1,128,128]{3,2,1,0:T(8,128)(2,1)S(1)}, bf16[4,1,128,128]{3,2,1,0:T(8,128)(2,1)S(1)}, u32[]{:S(2)}, u32[]{:S(2)}) collective-permute-start(bf16[4,1,128,128]{3,2,1,0:T(8,128)(2,1)S(1)} %constant_dynamic-slice_fusion.1), channel_id=1, source_target_pairs={{0,1},{1,0},{2,3},{3,2},{4,5},{5,4},{6,7},{7,6},{8,9},{9,8},{10,11... | collective-permute-start | bytes 393224 | tf_op jit(solution)/shard_map/input_conv_and_recurrence/ppermute | solution.py:13
  2.6 0.6 %copy-start.1 = (bf16[4,1,128,128]{3,2,1,0:T(8,128)(2,1)}, bf16[4,1,128,128]{3,2,1,0:T(8,128)(2,1)S(1)}, u32[]{:S(2)}) copy-start(bf16[4,1,128,128]{3,2,1,0:T(8,128)(2,1)S(1)} %collective-permute-done.top_ref.bottom_ref) | copy-start | bytes 393220
  8.6 22.5 %copy-start.3 = (f32[1,128]{1,0:T(1,128)S(1)}, f32[1,128]{1,0:T(1,128)}, u32[]{:S(2)}) copy-start(f32[1,128]{1,0:T(1,128)} %get-tuple-element.11) | copy-start | bytes 1540
  8.6 11.6 %collective-permute-start.1 = (bf16[1040,128]{1,0:T(8,128)(2,1)}, bf16[1040,128]{1,0:T(8,128)(2,1)S(1)}, u32[]{:S(2)}, u32[]{:S(2)}) collective-permute-start(bf16[1040,128]{1,0:T(8,128)(2,1)} %get-tuple-element.10), channel_id=1, source_target_pairs={{0,2},{2,4},{4,6},{6,8},{8,10},{10,12},{12,14},{14,16},{16,18},{18... | collective-permute-start | bytes 798728 | tf_op jit(solution)/shard_map/carry_across_blocks/ppermute | solution.py:197
  21.5 9.5 %collective-permute-start.2 = (bf16[1040,128]{1,0:T(8,128)(2,1)S(1)}, bf16[1040,128]{1,0:T(8,128)(2,1)S(1)}, u32[]{:S(2)}, u32[]{:S(2)}) collective-permute-start(bf16[1040,128]{1,0:T(8,128)(2,1)S(1)} %pad_maximum_fusion), channel_id=1, source_target_pairs={{0,4},{2,6},{4,8},{6,10},{8,12},{10,14},{12,16},{14,18},{16,20},{1... | collective-permute-start | bytes 798728 | tf_op jit(solution)/shard_map/carry_across_blocks/ppermute | solution.py:197
  31.3 7.7 %collective-permute-start.3 = (bf16[1040,128]{1,0:T(8,128)(2,1)S(1)}, bf16[1040,128]{1,0:T(8,128)(2,1)S(1)}, u32[]{:S(2)}, u32[]{:S(2)}) collective-permute-start(bf16[1040,128]{1,0:T(8,128)(2,1)S(1)} %pad_maximum_fusion.1), channel_id=1, source_target_pairs={{0,8},{2,10},{4,12},{6,14},{8,16},{10,18},{12,20},{14,22},{16,24},... | collective-permute-start | bytes 798728 | tf_op jit(solution)/shard_map/carry_across_blocks/ppermute | solution.py:197
  39.2 16.0 %collective-permute-start.4 = (bf16[1040,128]{1,0:T(8,128)(2,1)S(1)}, bf16[1040,128]{1,0:T(8,128)(2,1)S(1)}, u32[]{:S(2)}, u32[]{:S(2)}) collective-permute-start(bf16[1040,128]{1,0:T(8,128)(2,1)S(1)} %pad_maximum_fusion.2), channel_id=1, source_target_pairs={{0,16},{2,18},{4,20},{6,22},{8,24},{10,26},{12,28},{14,30},{1,17},... | collective-permute-start | bytes 798728 | tf_op jit(solution)/shard_map/carry_across_blocks/ppermute | solution.py:197
  40.5 14.9 %copy-start.4 = (f32[4,128]{1,0:T(4,128)S(1)}, f32[4,128]{1,0:T(4,128)}, u32[]{:S(2)}) copy-start(f32[4,128]{1,0:T(4,128)} %get-tuple-element.9.cum_ref) | copy-start | bytes 6148
  55.3 2.4 %copy-start = (f32[8,128,128]{2,1,0:T(8,128)}, f32[8,128,128]{2,1,0:T(8,128)S(1)}, u32[]{:S(2)}) copy-start(f32[8,128,128]{2,1,0:T(8,128)S(1)} %fusion.incoming_ref) | copy-start | bytes 1572868
  55.5 2.3 %collective-permute-start.5 = (bf16[4,1,128,128]{3,2,1,0:T(8,128)(2,1)S(1)}, bf16[4,1,128,128]{3,2,1,0:T(8,128)(2,1)S(1)}, u32[]{:S(2)}, u32[]{:S(2)}) collective-permute-start(bf16[4,1,128,128]{3,2,1,0:T(8,128)(2,1)S(1)} %fusion.3), channel_id=1, source_target_pairs={{0,1},{1,0},{2,3},{3,2},{4,5},{5,4},{6,7},{7,6},{8,9},{9,8},{10,11... | collective-permute-start | bytes 393224 | tf_op jit(solution)/shard_map/output_conv/ppermute | solution.py:13
  57.8 0.6 %copy-start.2 = (bf16[4,1,128,128]{3,2,1,0:T(8,128)(2,1)}, bf16[4,1,128,128]{3,2,1,0:T(8,128)(2,1)S(1)}, u32[]{:S(2)}) copy-start(bf16[4,1,128,128]{3,2,1,0:T(8,128)(2,1)S(1)} %collective-permute-done.5.top_ref.bottom_ref) | copy-start | bytes 393220

commit v10 on v8

--- a/solution.py
+++ b/solution.py
@@ -176,23 +176,18 @@
     return jnp.pad(parts, ((0, rows - 3), (0, 0)))
 
 
-def incoming_state(power, state, first_payload, axis):
+def incoming_state(power, first_payload, axis):
     n = lax.axis_size(axis)
-    rows, width, channels = state.shape
-    cells = rows * width
-    win_p, win_s = power, state
+    rows = first_payload.shape[0]
+    cells = rows - 16
+    win_p = power
     acc_p, acc_s = None, None
     payload = first_payload
     shift = 1
     while shift < n:
         pairs = [(i, i + shift) for i in range(n - shift)]
-        if payload is None:
-            payload = jnp.concatenate(
-                [win_s.astype(jnp.bfloat16).reshape(cells, channels), split3(win_p, 16)], axis=0
-            )
         got = lax.ppermute(payload, axis, pairs)
-        payload = None
-        got_s = got[:cells].astype(jnp.float32).reshape(rows, width, channels)
+        got_s = got[:cells].astype(jnp.float32)
         got_p = jnp.sum(got[cells : cells + 3].astype(jnp.float32), axis=0)
         if acc_s is None:
             acc_p, acc_s = got_p, got_s
@@ -200,11 +195,12 @@
             acc_s = acc_p * got_s + acc_s
             acc_p = got_p * acc_p
         if 2 * shift < n:
-            win_s = win_p * got_s + win_s
+            win_s = win_p * got_s + payload[:cells].astype(jnp.float32)
             win_p = got_p * win_p
+            payload = jnp.concatenate([win_s.astype(jnp.bfloat16), split3(win_p, 16)], axis=0)
         shift *= 2
     if acc_s is None:
-        return jnp.zeros_like(state)
+        return jnp.zeros((cells, first_payload.shape[1]), jnp.float32)
     return acc_s
 
 
@@ -212,7 +208,7 @@
     with jax.named_scope("input_conv_and_recurrence"):
         local, cumulative, first_payload = input_stage(frames, conv_in, decay)
     with jax.named_scope("carry_across_blocks"):
-        incoming = incoming_state(cumulative[-1], local[-1], first_payload, "tm")
+        incoming = incoming_state(cumulative[-1], first_payload, "tm").reshape(local.shape[1:])
     with jax.named_scope("output_conv"):
         return output_stage(local, cumulative, incoming, frames, conv_out, skip)
 

time: 63.6 us -> 64.5 us (1.014)
  waiting for transfers between devices: 36.4 us -> 37.6 us
  local copies, waits for them, and re-layouts: 4.41 us -> 3.32 us
  other arithmetic: 1.55 us -> 2.35 us
    ppermute x4, waiting for transfers between devices: 34.4 us -> 35.6 us  [incoming_state(): got = lax.ppermute(payload, axis, pairs)]
    slice x2 -> x0, local copies, waits for them, and re-layouts: 1.1 us -> none  [the longest x1 1.08 us: shards(): incoming = incoming_state(cumulative[-1], local[-1], first_payload, 'tm')]
    convert_element_type x6 -> x3, other arithmetic: 0.49 us -> 1.22 us  [incoming_state(): win_s.astype(jnp.bfloat16)]
  transfers between devices with their start and end apart: 6 -> 6, of which waited for: 6 -> 6; matrix products, arithmetic and copies ran while one was open for 4% -> 2% of each run, Pallas kernels for 0% -> 0%
where the time goes in v10:
time: 64.5 us; the launch traced here: 64 us
  waiting for transfers between devices  37.6 us (58%)
  Pallas kernels  10.7 us (17%)
  starting transfers between devices  9.95 us (15%)
  local copies, waits for them, and re-layouts  3.32 us (5%)
  other arithmetic  2.35 us (4%)
    ppermute x4, waiting for transfers between devices, incoming_state(): got = lax.ppermute(payload, axis, pairs)  35.6 us
    ppermute x4, starting transfers between devices, incoming_state(): got = lax.ppermute(payload, axis, pairs)  7.94 us
    pallas_call x1, Pallas kernels, output_stage(): pl.pallas_call(output_kernel, grid=(count,), in_specs=[pl.BlockSpec((coun...  5.49 us
    pallas_call x1, Pallas kernels, input_stage(): pl.pallas_call(input_kernel, grid=(count,), in_specs=[pl.BlockSpec((count...  5.2 us
    ppermute x2, starting transfers between devices, halo_rows(): lax.ppermute(lax.dynamic_slice_in_dim(x, row, 1, axis=dim), axis, [(0, 1)...  2.01 us
    ppermute x2, waiting for transfers between devices, halo_rows(): lax.ppermute(lax.dynamic_slice_in_dim(x, row, 1, axis=dim), axis, [(0, 1)...  1.97 us
    unnamed x8, local copies, waits for them, and re-layouts  1.31 us
  transfers between devices with their start and end apart: 6, of which 6 were waited for; matrix products, arithmetic and copies ran while one was open for 2% of the time, Pallas kernels for 0%

profile of v10, /device:TPU:25, one launch (start us, length us, event | category | flops | bytes accessed | tf_op | source)
XLA Modules:
  0.0 64.0 jit_solution(10643773261510674259)
XLA Ops:
  0.0 0.9 %constant_dynamic-slice_fusion.1 = bf16[4,1,128,128]{3,2,1,0:T(8,128)(2,1)S(1)} fusion(bf16[4,8,128,128]{3,2,1,0:T(8,128)(2,1)} %frame_ref.3, s32[]{:T(128)S(6)} %select_n.6), kind=kLoop, calls=%fused_computation.45 | loop fusion | bytes 262148 | tf_op jit(solution)/shard_map/input_conv_and_recurrence/dynamic_slice | solution.py:13
  0.9 0.7 %collective-permute-start = (bf16[4,1,128,128]{3,2,1,0:T(8,128)(2,1)S(1)}, bf16[4,1,128,128]{3,2,1,0:T(8,128)(2,1)S(1)}, u32[]{:S(2)}, u32[]{:S(2)}) collective-permute-start(bf16[4,1,128,128]{3,2,1,0:T(8,128)(2,1)S(1)} %constant_dynamic-slice_fusion.1), channel_id=1, source_target_pairs={{0,1},{1,0},{2,3},{3,2},{4,5},{5,4},{6,7},{7,6},{8,9},{9,8},{10,11... | collective-permute-start | bytes 393224 | tf_op jit(solution)/shard_map/input_conv_and_recurrence/ppermute | solution.py:13
  1.7 1.0 %collective-permute-done.top_ref.bottom_ref = bf16[4,1,128,128]{3,2,1,0:T(8,128)(2,1)S(1)} collective-permute-done((bf16[4,1,128,128]{3,2,1,0:T(8,128)(2,1)S(1)}, bf16[4,1,128,128]{3,2,1,0:T(8,128)(2,1)S(1)}, u32[]{:S(2)}, u32[]{:S(2)}) %collective-permute-start) | collective-permute-done | bytes 131104 | tf_op jit(solution)/shard_map/input_conv_and_recurrence/ppermute | solution.py:13
  2.6 0.0 copy-start.1
  2.6 0.6 %copy-done.1 = bf16[4,1,128,128]{3,2,1,0:T(8,128)(2,1)} copy-done((bf16[4,1,128,128]{3,2,1,0:T(8,128)(2,1)}, bf16[4,1,128,128]{3,2,1,0:T(8,128)(2,1)S(1)}, u32[]{:S(2)}) %copy-start.1) | copy-done | bytes 131096
  3.3 5.2 %input_conv_and_recurrence.1 = (f32[4,8,128,128]{3,2,1,0:T(8,128)}, f32[4,128]{1,0:T(4,128)}, bf16[1040,128]{1,0:T(8,128)(2,1)}) custom-call(f32[4,128]{1,0:T(4,128)} %decay_ref.1, bf16[4,1,128,128]{3,2,1,0:T(8,128)(2,1)} %copy-done.1, bf16[4,8,128,128]{3,2,1,0:T(8,128)(2,1)} %frame_ref.3, bf16[4,1,128,128]{3,2,1,0:T(8,128)(2,1)} %copy-done.1, ...), custom_call_target="tpu_custom_call" | custom-call | tf_op jit(solution)/shard_map/input_conv_and_recurrence/pallas_call | solution.py:114
  8.5 3.1 %collective-permute-start.1 = (bf16[1040,128]{1,0:T(8,128)(2,1)}, bf16[1040,128]{1,0:T(8,128)(2,1)S(1)}, u32[]{:S(2)}, u32[]{:S(2)}) collective-permute-start(bf16[1040,128]{1,0:T(8,128)(2,1)} %get-tuple-element.9), channel_id=1, source_target_pairs={{0,2},{2,4},{4,6},{6,8},{8,10},{10,12},{12,14},{14,16},{16,18},{18... | collective-permute-start | bytes 798728 | tf_op jit(solution)/shard_map/carry_across_blocks/ppermute | solution.py:189
  11.6 8.4 %collective-permute-done.1 = bf16[1040,128]{1,0:T(8,128)(2,1)S(1)} collective-permute-done((bf16[1040,128]{1,0:T(8,128)(2,1)}, bf16[1040,128]{1,0:T(8,128)(2,1)S(1)}, u32[]{:S(2)}, u32[]{:S(2)}) %collective-permute-start.1) | collective-permute-done | bytes 266272 | tf_op jit(solution)/shard_map/carry_across_blocks/ppermute | solution.py:189
  20.0 0.7 %reduce-precision_convert_fusion.5 = (bf16[1,128]{1,0:T(2,128)(2,1)S(1)}, f32[1,128]{1,0:T(1,128)S(1)}, f32[128]{0:T(128)S(1)}) fusion(f32[4,128]{1,0:T(4,128)} %get-tuple-element.8.cum_ref, f32[128]{0:T(128)S(1)} %convert_reduce_fusion.2), kind=kLoop, calls=%fused_computation.57 | loop fusion | flops 384 | bytes 2304 | tf_op jit(solution)/shard_map/convert.6
  20.7 1.0 %fusion.1 = bf16[1024,128]{1,0:T(8,128)(2,1)S(1)} fusion(bf16[1040,128]{1,0:T(8,128)(2,1)} %get-tuple-element.9, f32[128]{0:T(128)S(1)} %get-tuple-element.21, bf16[1040,128]{1,0:T(8,128)(2,1)S(1)} %collective-permute-done.1), kind=kLoop, calls=%fused_computation.7 | loop fusion | flops 655360 | bytes 786944 | tf_op jit(solution)/shard_map/carry_across_blocks/convert_element_type | solution.py:200
  21.8 2.2 %collective-permute-start.2 = (bf16[1040,128]{1,0:T(8,128)(2,1)S(1)}, bf16[1040,128]{1,0:T(8,128)(2,1)S(1)}, u32[]{:S(2)}, u32[]{:S(2)}) collective-permute-start(bf16[1040,128]{1,0:T(8,128)(2,1)S(1)} %pad_maximum_fusion), channel_id=1, source_target_pairs={{0,4},{2,6},{4,8},{6,10},{8,12},{10,14},{12,16},{14,18},{16,20},{1... | collective-permute-start | bytes 798728 | tf_op jit(solution)/shard_map/carry_across_blocks/ppermute | solution.py:189
  24.1 7.2 %collective-permute-done.2 = bf16[1040,128]{1,0:T(8,128)(2,1)S(1)} collective-permute-done((bf16[1040,128]{1,0:T(8,128)(2,1)S(1)}, bf16[1040,128]{1,0:T(8,128)(2,1)S(1)}, u32[]{:S(2)}, u32[]{:S(2)}) %collective-permute-start.2) | collective-permute-done | bytes 266272 | tf_op jit(solution)/shard_map/carry_across_blocks/ppermute | solution.py:189
  31.3 0.1 fusion.5
  31.5 1.3 %collective-permute-start.3 = (bf16[1040,128]{1,0:T(8,128)(2,1)S(1)}, bf16[1040,128]{1,0:T(8,128)(2,1)S(1)}, u32[]{:S(2)}, u32[]{:S(2)}) collective-permute-start(bf16[1040,128]{1,0:T(8,128)(2,1)S(1)} %pad_maximum_fusion.1), channel_id=1, source_target_pairs={{0,8},{2,10},{4,12},{6,14},{8,16},{10,18},{12,20},{14,22},{16,24},... | collective-permute-start | bytes 798728 | tf_op jit(solution)/shard_map/carry_across_blocks/ppermute | solution.py:189
  32.8 6.4 %collective-permute-done.3 = bf16[1040,128]{1,0:T(8,128)(2,1)S(1)} collective-permute-done((bf16[1040,128]{1,0:T(8,128)(2,1)S(1)}, bf16[1040,128]{1,0:T(8,128)(2,1)S(1)}, u32[]{:S(2)}, u32[]{:S(2)}) %collective-permute-start.3) | collective-permute-done | bytes 266272 | tf_op jit(solution)/shard_map/carry_across_blocks/ppermute | solution.py:189
  39.2 0.1 fusion.7
  39.3 0.0 copy-start.3
  39.3 1.3 %collective-permute-start.4 = (bf16[1040,128]{1,0:T(8,128)(2,1)S(1)}, bf16[1040,128]{1,0:T(8,128)(2,1)S(1)}, u32[]{:S(2)}, u32[]{:S(2)}) collective-permute-start(bf16[1040,128]{1,0:T(8,128)(2,1)S(1)} %pad_maximum_fusion.2), channel_id=1, source_target_pairs={{0,16},{2,18},{4,20},{6,22},{8,24},{10,26},{12,28},{14,30},{1,17},... | collective-permute-start | bytes 798728 | tf_op jit(solution)/shard_map/carry_across_blocks/ppermute | solution.py:189
  40.6 1.1 %fusion.30 = (f32[4,1,128,128]{3,2,1,0:T(8,128)S(1)}, f32[4,1,128,128]{3,2,1,0:T(8,128)S(1)}) fusion(f32[4,8,128,128]{3,2,1,0:T(8,128)} %get-tuple-element.10.local_ref), kind=kLoop, calls=%fused_computation.66 | loop fusion | bytes 1048576 | tf_op jit(solution)/shard_map/output_conv/slice | solution.py:145
  41.7 13.6 %collective-permute-done.4 = bf16[1040,128]{1,0:T(8,128)(2,1)S(1)} collective-permute-done((bf16[1040,128]{1,0:T(8,128)(2,1)S(1)}, bf16[1040,128]{1,0:T(8,128)(2,1)S(1)}, u32[]{:S(2)}, u32[]{:S(2)}) %collective-permute-start.4) | collective-permute-done | bytes 266272 | tf_op jit(solution)/shard_map/carry_across_blocks/ppermute | solution.py:189
  55.3 0.2 fusion.3
  55.5 0.0 copy-start
  55.6 0.0 copy-done.3
  55.6 0.1 fusion.10
  55.6 1.3 %collective-permute-start.5 = (bf16[4,1,128,128]{3,2,1,0:T(8,128)(2,1)S(1)}, bf16[4,1,128,128]{3,2,1,0:T(8,128)(2,1)S(1)}, u32[]{:S(2)}, u32[]{:S(2)}) collective-permute-start(bf16[4,1,128,128]{3,2,1,0:T(8,128)(2,1)S(1)} %fusion.10), channel_id=1, source_target_pairs={{0,1},{1,0},{2,3},{3,2},{4,5},{5,4},{6,7},{7,6},{8,9},{9,8},{10,11... | collective-permute-start | bytes 393224 | tf_op jit(solution)/shard_map/output_conv/ppermute | solution.py:13
  56.9 1.0 %collective-permute-done.5.top_ref.bottom_ref = bf16[4,1,128,128]{3,2,1,0:T(8,128)(2,1)S(1)} collective-permute-done((bf16[4,1,128,128]{3,2,1,0:T(8,128)(2,1)S(1)}, bf16[4,1,128,128]{3,2,1,0:T(8,128)(2,1)S(1)}, u32[]{:S(2)}, u32[]{:S(2)}) %collective-permute-start.5) | collective-permute-done | bytes 131104 | tf_op jit(solution)/shard_map/output_conv/ppermute | solution.py:13
  57.9 0.0 copy-start.2
  57.9 0.0 copy-done
  57.9 0.6 %copy-done.2 = bf16[4,1,128,128]{3,2,1,0:T(8,128)(2,1)} copy-done((bf16[4,1,128,128]{3,2,1,0:T(8,128)(2,1)}, bf16[4,1,128,128]{3,2,1,0:T(8,128)(2,1)S(1)}, u32[]{:S(2)}) %copy-start.2) | copy-done | bytes 131096
  58.5 5.5 %output_conv.1 = bf16[4,8,128,128]{3,2,1,0:T(8,128)(2,1)} custom-call(f32[4,128]{1,0:T(4,128)} %get-tuple-element.8.cum_ref, f32[1,128]{1,0:T(1,128)} %bitcast.29, f32[8,128,128]{2,1,0:T(8,128)} %bitcast.26, bf16[4,1,128,128]{3,2,1,0:T(8,128)(2,1)} %copy-done.2, f32[4,8,128,128]{3,2,1,0:T(8,128)} %get-tuple-element.10.local_ref, ...), custom_call_target="tpu_custom_call" | custom-call | tf_op jit(solution)/shard_map/output_conv/pallas_call | solution.py:151
  (17 shorter events, 0.2 us)
Async XLA Ops:
  0.9 1.7 %collective-permute-start = (bf16[4,1,128,128]{3,2,1,0:T(8,128)(2,1)S(1)}, bf16[4,1,128,128]{3,2,1,0:T(8,128)(2,1)S(1)}, u32[]{:S(2)}, u32[]{:S(2)}) collective-permute-start(bf16[4,1,128,128]{3,2,1,0:T(8,128)(2,1)S(1)} %constant_dynamic-slice_fusion.1), channel_id=1, source_target_pairs={{0,1},{1,0},{2,3},{3,2},{4,5},{5,4},{6,7},{7,6},{8,9},{9,8},{10,11... | collective-permute-start | bytes 393224 | tf_op jit(solution)/shard_map/input_conv_and_recurrence/ppermute | solution.py:13
  2.6 0.7 %copy-start.1 = (bf16[4,1,128,128]{3,2,1,0:T(8,128)(2,1)}, bf16[4,1,128,128]{3,2,1,0:T(8,128)(2,1)S(1)}, u32[]{:S(2)}) copy-start(bf16[4,1,128,128]{3,2,1,0:T(8,128)(2,1)S(1)} %collective-permute-done.top_ref.bottom_ref) | copy-start | bytes 393220
  8.5 11.5 %collective-permute-start.1 = (bf16[1040,128]{1,0:T(8,128)(2,1)}, bf16[1040,128]{1,0:T(8,128)(2,1)S(1)}, u32[]{:S(2)}, u32[]{:S(2)}) collective-permute-start(bf16[1040,128]{1,0:T(8,128)(2,1)} %get-tuple-element.9), channel_id=1, source_target_pairs={{0,2},{2,4},{4,6},{6,8},{8,10},{10,12},{12,14},{14,16},{16,18},{18... | collective-permute-start | bytes 798728 | tf_op jit(solution)/shard_map/carry_across_blocks/ppermute | solution.py:189
  21.8 9.5 %collective-permute-start.2 = (bf16[1040,128]{1,0:T(8,128)(2,1)S(1)}, bf16[1040,128]{1,0:T(8,128)(2,1)S(1)}, u32[]{:S(2)}, u32[]{:S(2)}) collective-permute-start(bf16[1040,128]{1,0:T(8,128)(2,1)S(1)} %pad_maximum_fusion), channel_id=1, source_target_pairs={{0,4},{2,6},{4,8},{6,10},{8,12},{10,14},{12,16},{14,18},{16,20},{1... | collective-permute-start | bytes 798728 | tf_op jit(solution)/shard_map/carry_across_blocks/ppermute | solution.py:189
  31.5 7.7 %collective-permute-start.3 = (bf16[1040,128]{1,0:T(8,128)(2,1)S(1)}, bf16[1040,128]{1,0:T(8,128)(2,1)S(1)}, u32[]{:S(2)}, u32[]{:S(2)}) collective-permute-start(bf16[1040,128]{1,0:T(8,128)(2,1)S(1)} %pad_maximum_fusion.1), channel_id=1, source_target_pairs={{0,8},{2,10},{4,12},{6,14},{8,16},{10,18},{12,20},{14,22},{16,24},... | collective-permute-start | bytes 798728 | tf_op jit(solution)/shard_map/carry_across_blocks/ppermute | solution.py:189
  39.3 16.3 %copy-start.3 = (f32[4,128]{1,0:T(4,128)S(1)}, f32[4,128]{1,0:T(4,128)}, u32[]{:S(2)}) copy-start(f32[4,128]{1,0:T(4,128)} %get-tuple-element.8.cum_ref) | copy-start | bytes 6148
  39.3 16.0 %collective-permute-start.4 = (bf16[1040,128]{1,0:T(8,128)(2,1)S(1)}, bf16[1040,128]{1,0:T(8,128)(2,1)S(1)}, u32[]{:S(2)}, u32[]{:S(2)}) collective-permute-start(bf16[1040,128]{1,0:T(8,128)(2,1)S(1)} %pad_maximum_fusion.2), channel_id=1, source_target_pairs={{0,16},{2,18},{4,20},{6,22},{8,24},{10,26},{12,28},{14,30},{1,17},... | collective-permute-start | bytes 798728 | tf_op jit(solution)/shard_map/carry_across_blocks/ppermute | solution.py:189
  55.5 2.4 %copy-start = (f32[1024,128]{1,0:T(8,128)}, f32[1024,128]{1,0:T(8,128)S(1)}, u32[]{:S(2)}) copy-start(f32[1024,128]{1,0:T(8,128)S(1)} %fusion.3) | copy-start | bytes 1572868
  55.6 2.3 %collective-permute-start.5 = (bf16[4,1,128,128]{3,2,1,0:T(8,128)(2,1)S(1)}, bf16[4,1,128,128]{3,2,1,0:T(8,128)(2,1)S(1)}, u32[]{:S(2)}, u32[]{:S(2)}) collective-permute-start(bf16[4,1,128,128]{3,2,1,0:T(8,128)(2,1)S(1)} %fusion.10), channel_id=1, source_target_pairs={{0,1},{1,0},{2,3},{3,2},{4,5},{5,4},{6,7},{7,6},{8,9},{9,8},{10,11... | collective-permute-start | bytes 393224 | tf_op jit(solution)/shard_map/output_conv/ppermute | solution.py:13
  57.9 0.7 %copy-start.2 = (bf16[4,1,128,128]{3,2,1,0:T(8,128)(2,1)}, bf16[4,1,128,128]{3,2,1,0:T(8,128)(2,1)S(1)}, u32[]{:S(2)}) copy-start(bf16[4,1,128,128]{3,2,1,0:T(8,128)(2,1)S(1)} %collective-permute-done.5.top_ref.bottom_ref) | copy-start | bytes 393220

commit v11 on v8

--- a/solution.py
+++ b/solution.py
@@ -178,34 +178,35 @@
 
 def incoming_state(power, state, first_payload, axis):
     n = lax.axis_size(axis)
+    me = lax.axis_index(axis)
     rows, width, channels = state.shape
     cells = rows * width
-    win_p, win_s = power, state
+    tot_p, tot_s = power, state.reshape(cells, channels)
     acc_p, acc_s = None, None
     payload = first_payload
-    shift = 1
-    while shift < n:
-        pairs = [(i, i + shift) for i in range(n - shift)]
+    bit = 1
+    while bit < n:
+        pairs = [(i, i ^ bit) for i in range(n)]
         if payload is None:
-            payload = jnp.concatenate(
-                [win_s.astype(jnp.bfloat16).reshape(cells, channels), split3(win_p, 16)], axis=0
-            )
+            payload = jnp.concatenate([tot_s.astype(jnp.bfloat16), split3(tot_p, 16)], axis=0)
         got = lax.ppermute(payload, axis, pairs)
         payload = None
-        got_s = got[:cells].astype(jnp.float32).reshape(rows, width, channels)
+        got_s = got[:cells].astype(jnp.float32)
         got_p = jnp.sum(got[cells : cells + 3].astype(jnp.float32), axis=0)
+        earlier = (me & bit) != 0
         if acc_s is None:
-            acc_p, acc_s = got_p, got_s
+            acc_p = jnp.where(earlier, got_p, jnp.ones_like(got_p))
+            acc_s = jnp.where(earlier, got_s, jnp.zeros_like(got_s))
         else:
-            acc_s = acc_p * got_s + acc_s
-            acc_p = got_p * acc_p
-        if 2 * shift < n:
-            win_s = win_p * got_s + win_s
-            win_p = got_p * win_p
-        shift *= 2
+            acc_s = jnp.where(earlier, acc_p * got_s + acc_s, acc_s)
+            acc_p = jnp.where(earlier, got_p * acc_p, acc_p)
+        if 2 * bit < n:
+            tot_s = jnp.where(earlier, tot_p * got_s + tot_s, got_p * tot_s + got_s)
+            tot_p = got_p * tot_p
+        bit *= 2
     if acc_s is None:
         return jnp.zeros_like(state)
-    return acc_s
+    return acc_s.reshape(rows, width, channels)
 
 
 def shards(frames, conv_in, decay, conv_out, skip):

time: 63.6 us -> 55.9 us (0.88)
  the two profiles are of different devices: /device:TPU:25 before, /device:TPU:0 now
where the time goes in v11:
time: 55.9 us; the launch traced here: 55.5 us
  waiting for transfers between devices  29.3 us (52%)
  Pallas kernels  10.7 us (19%)
  starting transfers between devices  9.1 us (16%)
  local copies, waits for them, and re-layouts  4.39 us (8%)
  other arithmetic  1.89 us (3%)
    ppermute x4, waiting for transfers between devices, incoming_state(): got = lax.ppermute(payload, axis, pairs)  27 us
    ppermute x4, starting transfers between devices, incoming_state(): got = lax.ppermute(payload, axis, pairs)  8.51 us
    pallas_call x1, Pallas kernels, output_stage(): pl.pallas_call(output_kernel, grid=(count,), in_specs=[pl.BlockSpec((coun...  5.49 us
    pallas_call x1, Pallas kernels, input_stage(): pl.pallas_call(input_kernel, grid=(count,), in_specs=[pl.BlockSpec((count...  5.2 us
    ppermute x2, waiting for transfers between devices, halo_rows(): lax.ppermute(lax.dynamic_slice_in_dim(x, row, 1, axis=dim), axis, [(0, 1)...  2.32 us
    unnamed x8, local copies, waits for them, and re-layouts  1.31 us
  transfers between devices with their start and end apart: 6, of which 6 were waited for; matrix products, arithmetic and copies ran while one was open for 4% of the time, Pallas kernels for 0%

profile of v11, /device:TPU:0, one launch (start us, length us, event | category | flops | bytes accessed | tf_op | source)
XLA Modules:
  0.0 55.5 jit_solution(794412780509674803)
XLA Ops:
  0.0 0.9 %constant_dynamic-slice_fusion.1 = bf16[4,1,128,128]{3,2,1,0:T(8,128)(2,1)S(1)} fusion(bf16[4,8,128,128]{3,2,1,0:T(8,128)(2,1)} %frame_ref.3, s32[]{:T(128)S(6)} %select_n.85), kind=kLoop, calls=%fused_computation.52 | loop fusion | bytes 262148 | tf_op jit(solution)/shard_map/input_conv_and_recurrence/dynamic_slice | solution.py:13
  0.9 0.5 collective-permute-start
  1.4 1.0 %collective-permute-done.top_ref.bottom_ref = bf16[4,1,128,128]{3,2,1,0:T(8,128)(2,1)S(1)} collective-permute-done((bf16[4,1,128,128]{3,2,1,0:T(8,128)(2,1)S(1)}, bf16[4,1,128,128]{3,2,1,0:T(8,128)(2,1)S(1)}, u32[]{:S(2)}, u32[]{:S(2)}) %collective-permute-start) | collective-permute-done | bytes 131104 | tf_op jit(solution)/shard_map/input_conv_and_recurrence/ppermute | solution.py:13
  2.4 0.0 copy-start.1
  2.4 0.6 %copy-done.1 = bf16[4,1,128,128]{3,2,1,0:T(8,128)(2,1)} copy-done((bf16[4,1,128,128]{3,2,1,0:T(8,128)(2,1)}, bf16[4,1,128,128]{3,2,1,0:T(8,128)(2,1)S(1)}, u32[]{:S(2)}) %copy-start.1) | copy-done | bytes 131096
  3.1 5.2 %input_conv_and_recurrence.1 = (f32[4,8,128,128]{3,2,1,0:T(8,128)}, f32[4,128]{1,0:T(4,128)}, bf16[1040,128]{1,0:T(8,128)(2,1)}) custom-call(f32[4,128]{1,0:T(4,128)} %decay_ref.1, bf16[4,1,128,128]{3,2,1,0:T(8,128)(2,1)} %copy-done.1, bf16[4,8,128,128]{3,2,1,0:T(8,128)(2,1)} %frame_ref.3, bf16[4,1,128,128]{3,2,1,0:T(8,128)(2,1)} %copy-done.1, ...), custom_call_target="tpu_custom_call" | custom-call | tf_op jit(solution)/shard_map/input_conv_and_recurrence/pallas_call | solution.py:114
  8.3 2.8 %collective-permute-start.1 = (bf16[1040,128]{1,0:T(8,128)(2,1)}, bf16[1040,128]{1,0:T(8,128)(2,1)S(1)}, u32[]{:S(2)}, u32[]{:S(2)}) collective-permute-start(bf16[1040,128]{1,0:T(8,128)(2,1)} %get-tuple-element.9), channel_id=1, source_target_pairs={{0,2},{2,0},{4,6},{6,4},{8,10},{10,8},{12,14},{14,12},{16,18},{18,... | collective-permute-start | bytes 798728 | tf_op jit(solution)/shard_map/carry_across_blocks/ppermute | solution.py:192
  11.1 1.1 %slice.44 = f32[1,8,128,128]{3,2,1,0:T(8,128)S(1)} slice(f32[4,8,128,128]{3,2,1,0:T(8,128)} %get-tuple-element.10.local_ref), slice={[3:4], [0:8], [0:128], [0:128]} | slice | bytes 1048576 | tf_op jit(solution)/shard_map/carry_across_blocks/slice | solution.py:216
  12.2 5.8 %collective-permute-done.1 = bf16[1040,128]{1,0:T(8,128)(2,1)S(1)} collective-permute-done((bf16[1040,128]{1,0:T(8,128)(2,1)}, bf16[1040,128]{1,0:T(8,128)(2,1)S(1)}, u32[]{:S(2)}, u32[]{:S(2)}) %collective-permute-start.1) | collective-permute-done | bytes 266272 | tf_op jit(solution)/shard_map/carry_across_blocks/ppermute | solution.py:192
  18.1 0.7 %reduce-precision_convert_fusion.5 = (bf16[1,128]{1,0:T(2,128)(2,1)S(1)}, f32[1,128]{1,0:T(1,128)S(1)}, f32[128]{0:T(128)S(1)}) fusion(f32[4,128]{1,0:T(4,128)} %get-tuple-element.8.cum_ref, f32[128]{0:T(128)S(1)} %convert_reduce_fusion.2), kind=kLoop, calls=%fused_computation.67 | loop fusion | flops 384 | bytes 2304 | tf_op jit(solution)/shard_map/convert.6
  18.8 0.1 fusion.29
  18.9 1.8 %collective-permute-start.2 = (bf16[1040,128]{1,0:T(8,128)(2,1)S(1)}, bf16[1040,128]{1,0:T(8,128)(2,1)S(1)}, u32[]{:S(2)}, u32[]{:S(2)}) collective-permute-start(bf16[1040,128]{1,0:T(8,128)(2,1)S(1)} %pad_maximum_fusion), channel_id=1, source_target_pairs={{0,4},{2,6},{4,0},{6,2},{8,12},{10,14},{12,8},{14,10},{16,20},{18,... | collective-permute-start | bytes 798728 | tf_op jit(solution)/shard_map/carry_across_blocks/ppermute | solution.py:192
  20.8 6.2 %collective-permute-done.2 = bf16[1040,128]{1,0:T(8,128)(2,1)S(1)} collective-permute-done((bf16[1040,128]{1,0:T(8,128)(2,1)S(1)}, bf16[1040,128]{1,0:T(8,128)(2,1)S(1)}, u32[]{:S(2)}, u32[]{:S(2)}) %collective-permute-start.2) | collective-permute-done | bytes 266272 | tf_op jit(solution)/shard_map/carry_across_blocks/ppermute | solution.py:192
  27.0 0.2 fusion.10
  27.2 1.6 %collective-permute-start.3 = (bf16[1040,128]{1,0:T(8,128)(2,1)S(1)}, bf16[1040,128]{1,0:T(8,128)(2,1)S(1)}, u32[]{:S(2)}, u32[]{:S(2)}) collective-permute-start(bf16[1040,128]{1,0:T(8,128)(2,1)S(1)} %pad_maximum_fusion.1), channel_id=1, source_target_pairs={{0,8},{2,10},{4,12},{6,14},{8,0},{10,2},{12,4},{14,6},{16,24},{18,... | collective-permute-start | bytes 798728 | tf_op jit(solution)/shard_map/carry_across_blocks/ppermute | solution.py:192
  28.8 5.5 %collective-permute-done.3 = bf16[1040,128]{1,0:T(8,128)(2,1)S(1)} collective-permute-done((bf16[1040,128]{1,0:T(8,128)(2,1)S(1)}, bf16[1040,128]{1,0:T(8,128)(2,1)S(1)}, u32[]{:S(2)}, u32[]{:S(2)}) %collective-permute-start.3) | collective-permute-done | bytes 266272 | tf_op jit(solution)/shard_map/carry_across_blocks/ppermute | solution.py:192
  34.4 0.3 fusion.6
  34.7 0.0 copy-start.3
  34.8 2.2 %collective-permute-start.4 = (bf16[1040,128]{1,0:T(8,128)(2,1)S(1)}, bf16[1040,128]{1,0:T(8,128)(2,1)S(1)}, u32[]{:S(2)}, u32[]{:S(2)}) collective-permute-start(bf16[1040,128]{1,0:T(8,128)(2,1)S(1)} %pad_maximum_fusion.2), channel_id=1, source_target_pairs={{0,16},{2,18},{4,20},{6,22},{8,24},{10,26},{12,28},{14,30},{16,0},... | collective-permute-start | bytes 798728 | tf_op jit(solution)/shard_map/carry_across_blocks/ppermute | solution.py:192
  37.0 1.1 %fusion.30 = (f32[4,1,128,128]{3,2,1,0:T(8,128)S(1)}, f32[4,1,128,128]{3,2,1,0:T(8,128)S(1)}) fusion(f32[4,8,128,128]{3,2,1,0:T(8,128)} %get-tuple-element.10.local_ref), kind=kLoop, calls=%fused_computation.76 | loop fusion | bytes 1048576 | tf_op jit(solution)/shard_map/output_conv/slice | solution.py:145
  38.1 9.4 %collective-permute-done.4 = bf16[1040,128]{1,0:T(8,128)(2,1)S(1)} collective-permute-done((bf16[1040,128]{1,0:T(8,128)(2,1)S(1)}, bf16[1040,128]{1,0:T(8,128)(2,1)S(1)}, u32[]{:S(2)}, u32[]{:S(2)}) %collective-permute-start.4) | collective-permute-done | bytes 266272 | tf_op jit(solution)/shard_map/carry_across_blocks/ppermute | solution.py:192
  47.5 0.2 add_select_fusion
  47.8 0.0 copy-start
  47.9 0.0 copy-done.3
  47.9 0.1 fusion.9
  47.9 0.1 collective-permute-start.5
  48.0 1.3 %collective-permute-done.5.top_ref.bottom_ref = bf16[4,1,128,128]{3,2,1,0:T(8,128)(2,1)S(1)} collective-permute-done((bf16[4,1,128,128]{3,2,1,0:T(8,128)(2,1)S(1)}, bf16[4,1,128,128]{3,2,1,0:T(8,128)(2,1)S(1)}, u32[]{:S(2)}, u32[]{:S(2)}) %collective-permute-start.5) | collective-permute-done | bytes 131104 | tf_op jit(solution)/shard_map/output_conv/ppermute | solution.py:13
  49.4 0.0 copy-start.2
  49.4 0.0 copy-done
  49.4 0.6 %copy-done.2 = bf16[4,1,128,128]{3,2,1,0:T(8,128)(2,1)} copy-done((bf16[4,1,128,128]{3,2,1,0:T(8,128)(2,1)}, bf16[4,1,128,128]{3,2,1,0:T(8,128)(2,1)S(1)}, u32[]{:S(2)}) %copy-start.2) | copy-done | bytes 131096
  50.0 5.5 %output_conv.1 = bf16[4,8,128,128]{3,2,1,0:T(8,128)(2,1)} custom-call(f32[4,128]{1,0:T(4,128)} %get-tuple-element.8.cum_ref, f32[1,128]{1,0:T(1,128)} %bitcast.41, f32[8,128,128]{2,1,0:T(8,128)} %bitcast.37, bf16[4,1,128,128]{3,2,1,0:T(8,128)(2,1)} %copy-done.2, f32[4,8,128,128]{3,2,1,0:T(8,128)} %get-tuple-element.10.local_ref, ...), custom_call_target="tpu_custom_call" | custom-call | tf_op jit(solution)/shard_map/output_conv/pallas_call | solution.py:151
  (17 shorter events, 0.2 us)
Async XLA Ops:
  0.9 1.5 %collective-permute-start = (bf16[4,1,128,128]{3,2,1,0:T(8,128)(2,1)S(1)}, bf16[4,1,128,128]{3,2,1,0:T(8,128)(2,1)S(1)}, u32[]{:S(2)}, u32[]{:S(2)}) collective-permute-start(bf16[4,1,128,128]{3,2,1,0:T(8,128)(2,1)S(1)} %constant_dynamic-slice_fusion.1), channel_id=1, source_target_pairs={{0,1},{1,0},{2,3},{3,2},{4,5},{5,4},{6,7},{7,6},{8,9},{9,8},{10,11... | collective-permute-start | bytes 393224 | tf_op jit(solution)/shard_map/input_conv_and_recurrence/ppermute | solution.py:13
  2.4 0.7 %copy-start.1 = (bf16[4,1,128,128]{3,2,1,0:T(8,128)(2,1)}, bf16[4,1,128,128]{3,2,1,0:T(8,128)(2,1)S(1)}, u32[]{:S(2)}) copy-start(bf16[4,1,128,128]{3,2,1,0:T(8,128)(2,1)S(1)} %collective-permute-done.top_ref.bottom_ref) | copy-start | bytes 393220
  8.3 9.8 %collective-permute-start.1 = (bf16[1040,128]{1,0:T(8,128)(2,1)}, bf16[1040,128]{1,0:T(8,128)(2,1)S(1)}, u32[]{:S(2)}, u32[]{:S(2)}) collective-permute-start(bf16[1040,128]{1,0:T(8,128)(2,1)} %get-tuple-element.9), channel_id=1, source_target_pairs={{0,2},{2,0},{4,6},{6,4},{8,10},{10,8},{12,14},{14,12},{16,18},{18,... | collective-permute-start | bytes 798728 | tf_op jit(solution)/shard_map/carry_across_blocks/ppermute | solution.py:192
  18.9 8.0 %collective-permute-start.2 = (bf16[1040,128]{1,0:T(8,128)(2,1)S(1)}, bf16[1040,128]{1,0:T(8,128)(2,1)S(1)}, u32[]{:S(2)}, u32[]{:S(2)}) collective-permute-start(bf16[1040,128]{1,0:T(8,128)(2,1)S(1)} %pad_maximum_fusion), channel_id=1, source_target_pairs={{0,4},{2,6},{4,0},{6,2},{8,12},{10,14},{12,8},{14,10},{16,20},{18,... | collective-permute-start | bytes 798728 | tf_op jit(solution)/shard_map/carry_across_blocks/ppermute | solution.py:192
  27.2 7.1 %collective-permute-start.3 = (bf16[1040,128]{1,0:T(8,128)(2,1)S(1)}, bf16[1040,128]{1,0:T(8,128)(2,1)S(1)}, u32[]{:S(2)}, u32[]{:S(2)}) collective-permute-start(bf16[1040,128]{1,0:T(8,128)(2,1)S(1)} %pad_maximum_fusion.1), channel_id=1, source_target_pairs={{0,8},{2,10},{4,12},{6,14},{8,0},{10,2},{12,4},{14,6},{16,24},{18,... | collective-permute-start | bytes 798728 | tf_op jit(solution)/shard_map/carry_across_blocks/ppermute | solution.py:192
  34.7 13.1 %copy-start.3 = (f32[4,128]{1,0:T(4,128)S(1)}, f32[4,128]{1,0:T(4,128)}, u32[]{:S(2)}) copy-start(f32[4,128]{1,0:T(4,128)} %get-tuple-element.8.cum_ref) | copy-start | bytes 6148
  34.8 12.8 %collective-permute-start.4 = (bf16[1040,128]{1,0:T(8,128)(2,1)S(1)}, bf16[1040,128]{1,0:T(8,128)(2,1)S(1)}, u32[]{:S(2)}, u32[]{:S(2)}) collective-permute-start(bf16[1040,128]{1,0:T(8,128)(2,1)S(1)} %pad_maximum_fusion.2), channel_id=1, source_target_pairs={{0,16},{2,18},{4,20},{6,22},{8,24},{10,26},{12,28},{14,30},{16,0},... | collective-permute-start | bytes 798728 | tf_op jit(solution)/shard_map/carry_across_blocks/ppermute | solution.py:192
  47.8 1.6 %copy-start = (f32[1024,128]{1,0:T(8,128)}, f32[1024,128]{1,0:T(8,128)S(1)}, u32[]{:S(2)}) copy-start(f32[1024,128]{1,0:T(8,128)S(1)} %add_select_fusion) | copy-start | bytes 1572868
  47.9 1.4 %collective-permute-start.5 = (bf16[4,1,128,128]{3,2,1,0:T(8,128)(2,1)S(1)}, bf16[4,1,128,128]{3,2,1,0:T(8,128)(2,1)S(1)}, u32[]{:S(2)}, u32[]{:S(2)}) collective-permute-start(bf16[4,1,128,128]{3,2,1,0:T(8,128)(2,1)S(1)} %fusion.9), channel_id=1, source_target_pairs={{0,1},{1,0},{2,3},{3,2},{4,5},{5,4},{6,7},{7,6},{8,9},{9,8},{10,11... | collective-permute-start | bytes 393224 | tf_op jit(solution)/shard_map/output_conv/ppermute | solution.py:13
  49.4 0.7 %copy-start.2 = (bf16[4,1,128,128]{3,2,1,0:T(8,128)(2,1)}, bf16[4,1,128,128]{3,2,1,0:T(8,128)(2,1)S(1)}, u32[]{:S(2)}) copy-start(bf16[4,1,128,128]{3,2,1,0:T(8,128)(2,1)S(1)} %collective-permute-done.5.top_ref.bottom_ref) | copy-start | bytes 393220

commit v12 on v11

--- a/solution.py
+++ b/solution.py
@@ -186,6 +186,23 @@
     payload = first_payload
     bit = 1
     while bit < n:
+        earlier = (me & bit) != 0
+        if 2 * bit == n and n >= 4 and acc_s is not None:
+            quarter, half = n // 4, cells // 2
+            offset = ((me // quarter) % 2) * half
+            piece = lax.dynamic_slice_in_dim(tot_s.astype(jnp.bfloat16), offset, half, axis=0)
+            got_a = lax.ppermute(piece, axis, [(i, i + 2 * quarter) for i in range(2 * quarter)])
+            swap = [(i, i + quarter) for i in range(2 * quarter, 3 * quarter)]
+            swap += [(j, i) for i, j in swap]
+            got_b = lax.ppermute(got_a, axis, swap)
+            third = (me // quarter) == 2
+            lower_total = jnp.where(
+                third,
+                jnp.concatenate([got_a, got_b], axis=0),
+                jnp.concatenate([got_b, got_a], axis=0),
+            ).astype(jnp.float32)
+            acc_s = jnp.where(earlier, acc_p * lower_total + acc_s, acc_s)
+            break
         pairs = [(i, i ^ bit) for i in range(n)]
         if payload is None:
             payload = jnp.concatenate([tot_s.astype(jnp.bfloat16), split3(tot_p, 16)], axis=0)
@@ -193,7 +210,6 @@
         payload = None
         got_s = got[:cells].astype(jnp.float32)
         got_p = jnp.sum(got[cells : cells + 3].astype(jnp.float32), axis=0)
-        earlier = (me & bit) != 0
         if acc_s is None:
             acc_p = jnp.where(earlier, got_p, jnp.ones_like(got_p))
             acc_s = jnp.where(earlier, got_s, jnp.zeros_like(got_s))

time: 55.9 us -> 57.2 us (1.023)
  the two profiles are of different devices: /device:TPU:0 before, /device:TPU:25 now
where the time goes in v12:
time: 57.2 us; the launch traced here: 56.8 us
  waiting for transfers between devices  27.9 us (49%)
  starting transfers between devices  12.1 us (21%)
  Pallas kernels  10.7 us (19%)
  local copies, waits for them, and re-layouts  4.39 us (8%)
  other arithmetic  1.63 us (3%)
    ppermute x3, waiting for transfers between devices, incoming_state(): got = lax.ppermute(payload, axis, pairs)  16.6 us
    ppermute x2, starting transfers between devices, halo_rows(): lax.ppermute(lax.dynamic_slice_in_dim(x, row, 1, axis=dim), axis, [(0, 1)...  6.14 us
    ppermute x1, waiting for transfers between devices, incoming_state(): lax.ppermute(piece, axis, [(i, i + 2 * quarter) for i in range(2 * quarte...  5.52 us
    pallas_call x1, Pallas kernels, output_stage(): pl.pallas_call(output_kernel, grid=(count,), in_specs=[pl.BlockSpec((coun...  5.48 us
    pallas_call x1, Pallas kernels, input_stage(): pl.pallas_call(input_kernel, grid=(count,), in_specs=[pl.BlockSpec((count...  5.21 us
    ppermute x1, waiting for transfers between devices, incoming_state(): got_b = lax.ppermute(got_a, axis, swap)  3.77 us
    ppermute x3, starting transfers between devices, incoming_state(): got = lax.ppermute(payload, axis, pairs)  2.75 us
    ppermute x2, waiting for transfers between devices, halo_rows(): lax.ppermute(lax.dynamic_slice_in_dim(x, row, 1, axis=dim), axis, [(0, 1)...  1.97 us
  transfers between devices with their start and end apart: 7, of which 7 were waited for; matrix products, arithmetic and copies ran while one was open for 4% of the time, Pallas kernels for 0%

profile of v12, /device:TPU:25, one launch (start us, length us, event | category | flops | bytes accessed | tf_op | source)
XLA Modules:
  0.0 56.8 jit_solution(9572886084803611441)
XLA Ops:
  0.0 0.9 %constant_dynamic-slice_fusion.1 = bf16[4,1,128,128]{3,2,1,0:T(8,128)(2,1)S(1)} fusion(bf16[4,8,128,128]{3,2,1,0:T(8,128)(2,1)} %frame_ref.3, s32[]{:T(128)S(6)} %select_n.108), kind=kLoop, calls=%fused_computation.43 | loop fusion | bytes 262148 | tf_op jit(solution)/shard_map/input_conv_and_recurrence/dynamic_slice | solution.py:13
  0.9 0.7 %collective-permute-start = (bf16[4,1,128,128]{3,2,1,0:T(8,128)(2,1)S(1)}, bf16[4,1,128,128]{3,2,1,0:T(8,128)(2,1)S(1)}, u32[]{:S(2)}, u32[]{:S(2)}) collective-permute-start(bf16[4,1,128,128]{3,2,1,0:T(8,128)(2,1)S(1)} %constant_dynamic-slice_fusion.1), channel_id=1, source_target_pairs={{0,1},{1,0},{2,3},{3,2},{4,5},{5,4},{6,7},{7,6},{8,9},{9,8},{10,11... | collective-permute-start | bytes 393224 | tf_op jit(solution)/shard_map/input_conv_and_recurrence/ppermute | solution.py:13
  1.7 1.0 %collective-permute-done.top_ref.bottom_ref = bf16[4,1,128,128]{3,2,1,0:T(8,128)(2,1)S(1)} collective-permute-done((bf16[4,1,128,128]{3,2,1,0:T(8,128)(2,1)S(1)}, bf16[4,1,128,128]{3,2,1,0:T(8,128)(2,1)S(1)}, u32[]{:S(2)}, u32[]{:S(2)}) %collective-permute-start) | collective-permute-done | bytes 131104 | tf_op jit(solution)/shard_map/input_conv_and_recurrence/ppermute | solution.py:13
  2.6 0.0 copy-start.1
  2.6 0.6 %copy-done.1 = bf16[4,1,128,128]{3,2,1,0:T(8,128)(2,1)} copy-done((bf16[4,1,128,128]{3,2,1,0:T(8,128)(2,1)}, bf16[4,1,128,128]{3,2,1,0:T(8,128)(2,1)S(1)}, u32[]{:S(2)}) %copy-start.1) | copy-done | bytes 131096
  3.3 5.2 %input_conv_and_recurrence.1 = (f32[4,8,128,128]{3,2,1,0:T(8,128)}, f32[4,128]{1,0:T(4,128)}, bf16[1040,128]{1,0:T(8,128)(2,1)}) custom-call(f32[4,128]{1,0:T(4,128)} %decay_ref.1, bf16[4,1,128,128]{3,2,1,0:T(8,128)(2,1)} %copy-done.1, bf16[4,8,128,128]{3,2,1,0:T(8,128)(2,1)} %frame_ref.3, bf16[4,1,128,128]{3,2,1,0:T(8,128)(2,1)} %copy-done.1, ...), custom_call_target="tpu_custom_call" | custom-call | tf_op jit(solution)/shard_map/input_conv_and_recurrence/pallas_call | solution.py:114
  8.5 1.2 %collective-permute-start.1 = (bf16[1040,128]{1,0:T(8,128)(2,1)}, bf16[1040,128]{1,0:T(8,128)(2,1)S(1)}, u32[]{:S(2)}, u32[]{:S(2)}) collective-permute-start(bf16[1040,128]{1,0:T(8,128)(2,1)} %get-tuple-element.9), channel_id=1, source_target_pairs={{0,2},{2,0},{4,6},{6,4},{8,10},{10,8},{12,14},{14,12},{16,18},{18,... | collective-permute-start | bytes 798728 | tf_op jit(solution)/shard_map/carry_across_blocks/ppermute | solution.py:209
  9.7 1.1 %slice.41 = f32[1,8,128,128]{3,2,1,0:T(8,128)S(1)} slice(f32[4,8,128,128]{3,2,1,0:T(8,128)} %get-tuple-element.10.local_ref), slice={[3:4], [0:8], [0:128], [0:128]} | slice | bytes 1048576 | tf_op jit(solution)/shard_map/carry_across_blocks/slice | solution.py:232
  10.8 5.5 %collective-permute-done.1 = bf16[1040,128]{1,0:T(8,128)(2,1)S(1)} collective-permute-done((bf16[1040,128]{1,0:T(8,128)(2,1)}, bf16[1040,128]{1,0:T(8,128)(2,1)S(1)}, u32[]{:S(2)}, u32[]{:S(2)}) %collective-permute-start.1) | collective-permute-done | bytes 266272 | tf_op jit(solution)/shard_map/carry_across_blocks/ppermute | solution.py:209
  16.4 0.6 %reduce-precision_convert_fusion.3 = (bf16[1,128]{1,0:T(2,128)(2,1)S(1)}, f32[1,128]{1,0:T(1,128)S(1)}, f32[128]{0:T(128)S(1)}) fusion(f32[4,128]{1,0:T(4,128)} %get-tuple-element.8.cum_ref, f32[128]{0:T(128)S(1)} %convert_reduce_fusion.2), kind=kLoop, calls=%fused_computation.54 | loop fusion | flops 384 | bytes 2304 | tf_op jit(solution)/shard_map/convert.3
  17.0 0.1 fusion.7
  17.2 1.3 %collective-permute-start.2 = (bf16[1040,128]{1,0:T(8,128)(2,1)S(1)}, bf16[1040,128]{1,0:T(8,128)(2,1)S(1)}, u32[]{:S(2)}, u32[]{:S(2)}) collective-permute-start(bf16[1040,128]{1,0:T(8,128)(2,1)S(1)} %pad_maximum_fusion), channel_id=1, source_target_pairs={{0,4},{2,6},{4,0},{6,2},{8,12},{10,14},{12,8},{14,10},{16,20},{18,... | collective-permute-start | bytes 798728 | tf_op jit(solution)/shard_map/carry_across_blocks/ppermute | solution.py:209
  18.5 5.5 %collective-permute-done.2 = bf16[1040,128]{1,0:T(8,128)(2,1)S(1)} collective-permute-done((bf16[1040,128]{1,0:T(8,128)(2,1)S(1)}, bf16[1040,128]{1,0:T(8,128)(2,1)S(1)}, u32[]{:S(2)}, u32[]{:S(2)}) %collective-permute-start.2) | collective-permute-done | bytes 266272 | tf_op jit(solution)/shard_map/carry_across_blocks/ppermute | solution.py:209
  24.0 0.2 fusion.20
  24.3 0.2 collective-permute-start.3
  24.5 5.6 %collective-permute-done.3 = bf16[1040,128]{1,0:T(8,128)(2,1)S(1)} collective-permute-done((bf16[1040,128]{1,0:T(8,128)(2,1)S(1)}, bf16[1040,128]{1,0:T(8,128)(2,1)S(1)}, u32[]{:S(2)}, u32[]{:S(2)}) %collective-permute-start.3) | collective-permute-done | bytes 266272 | tf_op jit(solution)/shard_map/carry_across_blocks/ppermute | solution.py:209
  30.2 0.0 copy-start.3
  30.2 0.1 select_convert_fusion
  30.2 1.3 %collective-permute-start.4 = (bf16[512,128]{1,0:T(8,128)(2,1)S(1)}, bf16[512,128]{1,0:T(8,128)(2,1)S(1)}, u32[]{:S(2)}, u32[]{:S(2)}) collective-permute-start(bf16[512,128]{1,0:T(8,128)(2,1)S(1)} %select_convert_fusion), channel_id=1, source_target_pairs={{0,16},{2,18},{4,20},{6,22},{8,24},{10,26},{12,28},{14,30},{1,17},... | collective-permute-start | bytes 393224 | tf_op jit(solution)/shard_map/carry_across_blocks/ppermute | solution.py:194
  31.5 1.1 %fusion.22 = (f32[4,1,128,128]{3,2,1,0:T(8,128)S(1)}, f32[4,1,128,128]{3,2,1,0:T(8,128)S(1)}) fusion(f32[4,8,128,128]{3,2,1,0:T(8,128)} %get-tuple-element.10.local_ref), kind=kLoop, calls=%fused_computation.61 | loop fusion | bytes 1048576 | tf_op jit(solution)/shard_map/output_conv/slice | solution.py:145
  32.6 5.5 %collective-permute-done.4 = bf16[512,128]{1,0:T(8,128)(2,1)S(1)} collective-permute-done((bf16[512,128]{1,0:T(8,128)(2,1)S(1)}, bf16[512,128]{1,0:T(8,128)(2,1)S(1)}, u32[]{:S(2)}, u32[]{:S(2)}) %collective-permute-start.4) | collective-permute-done | bytes 131104 | tf_op jit(solution)/shard_map/carry_across_blocks/ppermute | solution.py:194
  38.1 1.9 %collective-permute-start.5 = (bf16[512,128]{1,0:T(8,128)(2,1)S(1)}, bf16[512,128]{1,0:T(8,128)(2,1)S(1)}, u32[]{:S(2)}, u32[]{:S(2)}) collective-permute-start(bf16[512,128]{1,0:T(8,128)(2,1)S(1)} %collective-permute-done.4), channel_id=1, source_target_pairs={{16,24},{18,26},{20,28},{22,30},{24,16},{26,18},{28,20},{30,22},{1... | collective-permute-start | bytes 393224 | tf_op jit(solution)/shard_map/carry_across_blocks/ppermute | solution.py:197
  40.1 3.8 %collective-permute-done.5 = bf16[512,128]{1,0:T(8,128)(2,1)S(1)} collective-permute-done((bf16[512,128]{1,0:T(8,128)(2,1)S(1)}, bf16[512,128]{1,0:T(8,128)(2,1)S(1)}, u32[]{:S(2)}, u32[]{:S(2)}) %collective-permute-start.5) | collective-permute-done | bytes 131104 | tf_op jit(solution)/shard_map/carry_across_blocks/ppermute | solution.py:197
  43.8 0.3 add_select_fusion
  44.1 0.0 copy-start
  44.2 0.0 copy-done.3
  44.2 0.1 fusion.6
  44.3 5.4 %collective-permute-start.6 = (bf16[4,1,128,128]{3,2,1,0:T(8,128)(2,1)S(1)}, bf16[4,1,128,128]{3,2,1,0:T(8,128)(2,1)S(1)}, u32[]{:S(2)}, u32[]{:S(2)}) collective-permute-start(bf16[4,1,128,128]{3,2,1,0:T(8,128)(2,1)S(1)} %fusion.6), channel_id=1, source_target_pairs={{0,1},{1,0},{2,3},{3,2},{4,5},{5,4},{6,7},{7,6},{8,9},{9,8},{10,11... | collective-permute-start | bytes 393224 | tf_op jit(solution)/shard_map/output_conv/ppermute | solution.py:13
  49.7 1.0 %collective-permute-done.6.top_ref.bottom_ref = bf16[4,1,128,128]{3,2,1,0:T(8,128)(2,1)S(1)} collective-permute-done((bf16[4,1,128,128]{3,2,1,0:T(8,128)(2,1)S(1)}, bf16[4,1,128,128]{3,2,1,0:T(8,128)(2,1)S(1)}, u32[]{:S(2)}, u32[]{:S(2)}) %collective-permute-start.6) | collective-permute-done | bytes 131104 | tf_op jit(solution)/shard_map/output_conv/ppermute | solution.py:13
  50.7 0.0 copy-start.2
  50.7 0.0 copy-done
  50.7 0.6 %copy-done.2 = bf16[4,1,128,128]{3,2,1,0:T(8,128)(2,1)} copy-done((bf16[4,1,128,128]{3,2,1,0:T(8,128)(2,1)}, bf16[4,1,128,128]{3,2,1,0:T(8,128)(2,1)S(1)}, u32[]{:S(2)}) %copy-start.2) | copy-done | bytes 131096
  51.3 5.5 %output_conv.1 = bf16[4,8,128,128]{3,2,1,0:T(8,128)(2,1)} custom-call(f32[4,128]{1,0:T(4,128)} %get-tuple-element.8.cum_ref, f32[1,128]{1,0:T(1,128)} %bitcast.31, f32[8,128,128]{2,1,0:T(8,128)} %bitcast.28, bf16[4,1,128,128]{3,2,1,0:T(8,128)(2,1)} %copy-done.2, f32[4,8,128,128]{3,2,1,0:T(8,128)} %get-tuple-element.10.local_ref, ...), custom_call_target="tpu_custom_call" | custom-call | tf_op jit(solution)/shard_map/output_conv/pallas_call | solution.py:151
  (15 shorter events, 0.2 us)
Async XLA Ops:
  0.9 1.7 %collective-permute-start = (bf16[4,1,128,128]{3,2,1,0:T(8,128)(2,1)S(1)}, bf16[4,1,128,128]{3,2,1,0:T(8,128)(2,1)S(1)}, u32[]{:S(2)}, u32[]{:S(2)}) collective-permute-start(bf16[4,1,128,128]{3,2,1,0:T(8,128)(2,1)S(1)} %constant_dynamic-slice_fusion.1), channel_id=1, source_target_pairs={{0,1},{1,0},{2,3},{3,2},{4,5},{5,4},{6,7},{7,6},{8,9},{9,8},{10,11... | collective-permute-start | bytes 393224 | tf_op jit(solution)/shard_map/input_conv_and_recurrence/ppermute | solution.py:13
  2.6 0.7 %copy-start.1 = (bf16[4,1,128,128]{3,2,1,0:T(8,128)(2,1)}, bf16[4,1,128,128]{3,2,1,0:T(8,128)(2,1)S(1)}, u32[]{:S(2)}) copy-start(bf16[4,1,128,128]{3,2,1,0:T(8,128)(2,1)S(1)} %collective-permute-done.top_ref.bottom_ref) | copy-start | bytes 393220
  8.5 7.8 %collective-permute-start.1 = (bf16[1040,128]{1,0:T(8,128)(2,1)}, bf16[1040,128]{1,0:T(8,128)(2,1)S(1)}, u32[]{:S(2)}, u32[]{:S(2)}) collective-permute-start(bf16[1040,128]{1,0:T(8,128)(2,1)} %get-tuple-element.9), channel_id=1, source_target_pairs={{0,2},{2,0},{4,6},{6,4},{8,10},{10,8},{12,14},{14,12},{16,18},{18,... | collective-permute-start | bytes 798728 | tf_op jit(solution)/shard_map/carry_across_blocks/ppermute | solution.py:209
  17.2 6.8 %collective-permute-start.2 = (bf16[1040,128]{1,0:T(8,128)(2,1)S(1)}, bf16[1040,128]{1,0:T(8,128)(2,1)S(1)}, u32[]{:S(2)}, u32[]{:S(2)}) collective-permute-start(bf16[1040,128]{1,0:T(8,128)(2,1)S(1)} %pad_maximum_fusion), channel_id=1, source_target_pairs={{0,4},{2,6},{4,0},{6,2},{8,12},{10,14},{12,8},{14,10},{16,20},{18,... | collective-permute-start | bytes 798728 | tf_op jit(solution)/shard_map/carry_across_blocks/ppermute | solution.py:209
  24.3 5.8 %collective-permute-start.3 = (bf16[1040,128]{1,0:T(8,128)(2,1)S(1)}, bf16[1040,128]{1,0:T(8,128)(2,1)S(1)}, u32[]{:S(2)}, u32[]{:S(2)}) collective-permute-start(bf16[1040,128]{1,0:T(8,128)(2,1)S(1)} %pad_maximum_fusion.1), channel_id=1, source_target_pairs={{0,8},{2,10},{4,12},{6,14},{8,0},{10,2},{12,4},{14,6},{16,24},{18,... | collective-permute-start | bytes 798728 | tf_op jit(solution)/shard_map/carry_across_blocks/ppermute | solution.py:209
  30.2 14.1 %copy-start.3 = (f32[4,128]{1,0:T(4,128)S(1)}, f32[4,128]{1,0:T(4,128)}, u32[]{:S(2)}) copy-start(f32[4,128]{1,0:T(4,128)} %get-tuple-element.8.cum_ref) | copy-start | bytes 6148
  30.2 7.9 %collective-permute-start.4 = (bf16[512,128]{1,0:T(8,128)(2,1)S(1)}, bf16[512,128]{1,0:T(8,128)(2,1)S(1)}, u32[]{:S(2)}, u32[]{:S(2)}) collective-permute-start(bf16[512,128]{1,0:T(8,128)(2,1)S(1)} %select_convert_fusion), channel_id=1, source_target_pairs={{0,16},{2,18},{4,20},{6,22},{8,24},{10,26},{12,28},{14,30},{1,17},... | collective-permute-start | bytes 393224 | tf_op jit(solution)/shard_map/carry_across_blocks/ppermute | solution.py:194
  38.1 5.7 %collective-permute-start.5 = (bf16[512,128]{1,0:T(8,128)(2,1)S(1)}, bf16[512,128]{1,0:T(8,128)(2,1)S(1)}, u32[]{:S(2)}, u32[]{:S(2)}) collective-permute-start(bf16[512,128]{1,0:T(8,128)(2,1)S(1)} %collective-permute-done.4), channel_id=1, source_target_pairs={{16,24},{18,26},{20,28},{22,30},{24,16},{26,18},{28,20},{30,22},{1... | collective-permute-start | bytes 393224 | tf_op jit(solution)/shard_map/carry_across_blocks/ppermute | solution.py:197
  44.1 6.5 %copy-start = (f32[1024,128]{1,0:T(8,128)}, f32[1024,128]{1,0:T(8,128)S(1)}, u32[]{:S(2)}) copy-start(f32[1024,128]{1,0:T(8,128)S(1)} %add_select_fusion) | copy-start | bytes 1572868
  44.3 6.4 %collective-permute-start.6 = (bf16[4,1,128,128]{3,2,1,0:T(8,128)(2,1)S(1)}, bf16[4,1,128,128]{3,2,1,0:T(8,128)(2,1)S(1)}, u32[]{:S(2)}, u32[]{:S(2)}) collective-permute-start(bf16[4,1,128,128]{3,2,1,0:T(8,128)(2,1)S(1)} %fusion.6), channel_id=1, source_target_pairs={{0,1},{1,0},{2,3},{3,2},{4,5},{5,4},{6,7},{7,6},{8,9},{9,8},{10,11... | collective-permute-start | bytes 393224 | tf_op jit(solution)/shard_map/output_conv/ppermute | solution.py:13
  50.7 0.7 %copy-start.2 = (bf16[4,1,128,128]{3,2,1,0:T(8,128)(2,1)}, bf16[4,1,128,128]{3,2,1,0:T(8,128)(2,1)S(1)}, u32[]{:S(2)}) copy-start(bf16[4,1,128,128]{3,2,1,0:T(8,128)(2,1)S(1)} %collective-permute-done.6.top_ref.bottom_ref) | copy-start | bytes 393220

commit v13 on v11

--- a/solution.py
+++ b/solution.py
@@ -187,6 +187,8 @@
     bit = 1
     while bit < n:
         pairs = [(i, i ^ bit) for i in range(n)]
+        if 2 * bit == n:
+            pairs = [(i, i + bit) for i in range(bit)]
         if payload is None:
             payload = jnp.concatenate([tot_s.astype(jnp.bfloat16), split3(tot_p, 16)], axis=0)
         got = lax.ppermute(payload, axis, pairs)

time: 55.9 us -> 55.7 us (level)
  the two profiles are of different devices: /device:TPU:0 before, /device:TPU:25 now
where the time goes in v13:
time: 55.7 us; the launch traced here: 55.3 us
  waiting for transfers between devices  32.2 us (58%)
  Pallas kernels  10.7 us (19%)
  starting transfers between devices  6.05 us (11%)
  local copies, waits for them, and re-layouts  4.39 us (8%)
  other arithmetic  1.89 us (3%)
    ppermute x4, waiting for transfers between devices, incoming_state(): got = lax.ppermute(payload, axis, pairs)  30.2 us
    pallas_call x1, Pallas kernels, output_stage(): pl.pallas_call(output_kernel, grid=(count,), in_specs=[pl.BlockSpec((coun...  5.49 us
    pallas_call x1, Pallas kernels, input_stage(): pl.pallas_call(input_kernel, grid=(count,), in_specs=[pl.BlockSpec((count...  5.2 us
    ppermute x4, starting transfers between devices, incoming_state(): got = lax.ppermute(payload, axis, pairs)  4.04 us
    ppermute x2, starting transfers between devices, halo_rows(): lax.ppermute(lax.dynamic_slice_in_dim(x, row, 1, axis=dim), axis, [(0, 1)...  2.01 us
    ppermute x2, waiting for transfers between devices, halo_rows(): lax.ppermute(lax.dynamic_slice_in_dim(x, row, 1, axis=dim), axis, [(0, 1)...  1.97 us
    unnamed x8, local copies, waits for them, and re-layouts  1.31 us
  transfers between devices with their start and end apart: 6, of which 6 were waited for; matrix products, arithmetic and copies ran while one was open for 4% of the time, Pallas kernels for 0%

profile of v13, /device:TPU:25, one launch (start us, length us, event | category | flops | bytes accessed | tf_op | source)
XLA Modules:
  0.0 55.3 jit_solution(7647842118294049031)
XLA Ops:
  0.0 0.9 %constant_dynamic-slice_fusion.1 = bf16[4,1,128,128]{3,2,1,0:T(8,128)(2,1)S(1)} fusion(bf16[4,8,128,128]{3,2,1,0:T(8,128)(2,1)} %frame_ref.3, s32[]{:T(128)S(6)} %select_n.85), kind=kLoop, calls=%fused_computation.52 | loop fusion | bytes 262148 | tf_op jit(solution)/shard_map/input_conv_and_recurrence/dynamic_slice | solution.py:13
  0.9 0.7 %collective-permute-start = (bf16[4,1,128,128]{3,2,1,0:T(8,128)(2,1)S(1)}, bf16[4,1,128,128]{3,2,1,0:T(8,128)(2,1)S(1)}, u32[]{:S(2)}, u32[]{:S(2)}) collective-permute-start(bf16[4,1,128,128]{3,2,1,0:T(8,128)(2,1)S(1)} %constant_dynamic-slice_fusion.1), channel_id=1, source_target_pairs={{0,1},{1,0},{2,3},{3,2},{4,5},{5,4},{6,7},{7,6},{8,9},{9,8},{10,11... | collective-permute-start | bytes 393224 | tf_op jit(solution)/shard_map/input_conv_and_recurrence/ppermute | solution.py:13
  1.7 1.0 %collective-permute-done.top_ref.bottom_ref = bf16[4,1,128,128]{3,2,1,0:T(8,128)(2,1)S(1)} collective-permute-done((bf16[4,1,128,128]{3,2,1,0:T(8,128)(2,1)S(1)}, bf16[4,1,128,128]{3,2,1,0:T(8,128)(2,1)S(1)}, u32[]{:S(2)}, u32[]{:S(2)}) %collective-permute-start) | collective-permute-done | bytes 131104 | tf_op jit(solution)/shard_map/input_conv_and_recurrence/ppermute | solution.py:13
  2.6 0.0 copy-start.1
  2.6 0.6 %copy-done.1 = bf16[4,1,128,128]{3,2,1,0:T(8,128)(2,1)} copy-done((bf16[4,1,128,128]{3,2,1,0:T(8,128)(2,1)}, bf16[4,1,128,128]{3,2,1,0:T(8,128)(2,1)S(1)}, u32[]{:S(2)}) %copy-start.1) | copy-done | bytes 131096
  3.3 5.2 %input_conv_and_recurrence.1 = (f32[4,8,128,128]{3,2,1,0:T(8,128)}, f32[4,128]{1,0:T(4,128)}, bf16[1040,128]{1,0:T(8,128)(2,1)}) custom-call(f32[4,128]{1,0:T(4,128)} %decay_ref.1, bf16[4,1,128,128]{3,2,1,0:T(8,128)(2,1)} %copy-done.1, bf16[4,8,128,128]{3,2,1,0:T(8,128)(2,1)} %frame_ref.3, bf16[4,1,128,128]{3,2,1,0:T(8,128)(2,1)} %copy-done.1, ...), custom_call_target="tpu_custom_call" | custom-call | tf_op jit(solution)/shard_map/input_conv_and_recurrence/pallas_call | solution.py:114
  8.5 1.2 %collective-permute-start.1 = (bf16[1040,128]{1,0:T(8,128)(2,1)}, bf16[1040,128]{1,0:T(8,128)(2,1)S(1)}, u32[]{:S(2)}, u32[]{:S(2)}) collective-permute-start(bf16[1040,128]{1,0:T(8,128)(2,1)} %get-tuple-element.9), channel_id=1, source_target_pairs={{0,2},{2,0},{4,6},{6,4},{8,10},{10,8},{12,14},{14,12},{16,18},{18,... | collective-permute-start | bytes 798728 | tf_op jit(solution)/shard_map/carry_across_blocks/ppermute | solution.py:194
  9.7 1.1 %slice.44 = f32[1,8,128,128]{3,2,1,0:T(8,128)S(1)} slice(f32[4,8,128,128]{3,2,1,0:T(8,128)} %get-tuple-element.10.local_ref), slice={[3:4], [0:8], [0:128], [0:128]} | slice | bytes 1048576 | tf_op jit(solution)/shard_map/carry_across_blocks/slice | solution.py:218
  10.8 5.5 %collective-permute-done.1 = bf16[1040,128]{1,0:T(8,128)(2,1)S(1)} collective-permute-done((bf16[1040,128]{1,0:T(8,128)(2,1)}, bf16[1040,128]{1,0:T(8,128)(2,1)S(1)}, u32[]{:S(2)}, u32[]{:S(2)}) %collective-permute-start.1) | collective-permute-done | bytes 266272 | tf_op jit(solution)/shard_map/carry_across_blocks/ppermute | solution.py:194
  16.4 0.7 %reduce-precision_convert_fusion.5 = (bf16[1,128]{1,0:T(2,128)(2,1)S(1)}, f32[1,128]{1,0:T(1,128)S(1)}, f32[128]{0:T(128)S(1)}) fusion(f32[4,128]{1,0:T(4,128)} %get-tuple-element.8.cum_ref, f32[128]{0:T(128)S(1)} %convert_reduce_fusion.2), kind=kLoop, calls=%fused_computation.67 | loop fusion | flops 384 | bytes 2304 | tf_op jit(solution)/shard_map/convert.6
  17.0 0.1 fusion.29
  17.2 1.3 %collective-permute-start.2 = (bf16[1040,128]{1,0:T(8,128)(2,1)S(1)}, bf16[1040,128]{1,0:T(8,128)(2,1)S(1)}, u32[]{:S(2)}, u32[]{:S(2)}) collective-permute-start(bf16[1040,128]{1,0:T(8,128)(2,1)S(1)} %pad_maximum_fusion), channel_id=1, source_target_pairs={{0,4},{2,6},{4,0},{6,2},{8,12},{10,14},{12,8},{14,10},{16,20},{18,... | collective-permute-start | bytes 798728 | tf_op jit(solution)/shard_map/carry_across_blocks/ppermute | solution.py:194
  18.5 5.5 %collective-permute-done.2 = bf16[1040,128]{1,0:T(8,128)(2,1)S(1)} collective-permute-done((bf16[1040,128]{1,0:T(8,128)(2,1)S(1)}, bf16[1040,128]{1,0:T(8,128)(2,1)S(1)}, u32[]{:S(2)}, u32[]{:S(2)}) %collective-permute-start.2) | collective-permute-done | bytes 266272 | tf_op jit(solution)/shard_map/carry_across_blocks/ppermute | solution.py:194
  24.0 0.2 fusion.10
  24.3 0.2 collective-permute-start.3
  24.5 5.6 %collective-permute-done.3 = bf16[1040,128]{1,0:T(8,128)(2,1)S(1)} collective-permute-done((bf16[1040,128]{1,0:T(8,128)(2,1)S(1)}, bf16[1040,128]{1,0:T(8,128)(2,1)S(1)}, u32[]{:S(2)}, u32[]{:S(2)}) %collective-permute-start.3) | collective-permute-done | bytes 266272 | tf_op jit(solution)/shard_map/carry_across_blocks/ppermute | solution.py:194
  30.2 0.3 fusion.6
  30.5 0.0 copy-start.3
  30.5 1.3 %collective-permute-start.4 = (bf16[1040,128]{1,0:T(8,128)(2,1)S(1)}, bf16[1040,128]{1,0:T(8,128)(2,1)S(1)}, u32[]{:S(2)}, u32[]{:S(2)}) collective-permute-start(bf16[1040,128]{1,0:T(8,128)(2,1)S(1)} %pad_maximum_fusion.2), channel_id=1, source_target_pairs={{0,16},{2,18},{4,20},{6,22},{8,24},{10,26},{12,28},{14,30},{1,17},... | collective-permute-start | bytes 798728 | tf_op jit(solution)/shard_map/carry_across_blocks/ppermute | solution.py:194
  31.8 1.1 %fusion.30 = (f32[4,1,128,128]{3,2,1,0:T(8,128)S(1)}, f32[4,1,128,128]{3,2,1,0:T(8,128)S(1)}) fusion(f32[4,8,128,128]{3,2,1,0:T(8,128)} %get-tuple-element.10.local_ref), kind=kLoop, calls=%fused_computation.76 | loop fusion | bytes 1048576 | tf_op jit(solution)/shard_map/output_conv/slice | solution.py:145
  32.9 13.6 %collective-permute-done.4 = bf16[1040,128]{1,0:T(8,128)(2,1)S(1)} collective-permute-done((bf16[1040,128]{1,0:T(8,128)(2,1)S(1)}, bf16[1040,128]{1,0:T(8,128)(2,1)S(1)}, u32[]{:S(2)}, u32[]{:S(2)}) %collective-permute-start.4) | collective-permute-done | bytes 266272 | tf_op jit(solution)/shard_map/carry_across_blocks/ppermute | solution.py:194
  46.5 0.2 add_select_fusion
  46.8 0.0 copy-start
  46.9 0.0 copy-done.3
  46.9 0.1 fusion.9
  46.9 1.3 %collective-permute-start.5 = (bf16[4,1,128,128]{3,2,1,0:T(8,128)(2,1)S(1)}, bf16[4,1,128,128]{3,2,1,0:T(8,128)(2,1)S(1)}, u32[]{:S(2)}, u32[]{:S(2)}) collective-permute-start(bf16[4,1,128,128]{3,2,1,0:T(8,128)(2,1)S(1)} %fusion.9), channel_id=1, source_target_pairs={{0,1},{1,0},{2,3},{3,2},{4,5},{5,4},{6,7},{7,6},{8,9},{9,8},{10,11... | collective-permute-start | bytes 393224 | tf_op jit(solution)/shard_map/output_conv/ppermute | solution.py:13
  48.2 1.0 %collective-permute-done.5.top_ref.bottom_ref = bf16[4,1,128,128]{3,2,1,0:T(8,128)(2,1)S(1)} collective-permute-done((bf16[4,1,128,128]{3,2,1,0:T(8,128)(2,1)S(1)}, bf16[4,1,128,128]{3,2,1,0:T(8,128)(2,1)S(1)}, u32[]{:S(2)}, u32[]{:S(2)}) %collective-permute-start.5) | collective-permute-done | bytes 131104 | tf_op jit(solution)/shard_map/output_conv/ppermute | solution.py:13
  49.2 0.0 copy-start.2
  49.2 0.0 copy-done
  49.2 0.6 %copy-done.2 = bf16[4,1,128,128]{3,2,1,0:T(8,128)(2,1)} copy-done((bf16[4,1,128,128]{3,2,1,0:T(8,128)(2,1)}, bf16[4,1,128,128]{3,2,1,0:T(8,128)(2,1)S(1)}, u32[]{:S(2)}) %copy-start.2) | copy-done | bytes 131096
  49.8 5.5 %output_conv.1 = bf16[4,8,128,128]{3,2,1,0:T(8,128)(2,1)} custom-call(f32[4,128]{1,0:T(4,128)} %get-tuple-element.8.cum_ref, f32[1,128]{1,0:T(1,128)} %bitcast.41, f32[8,128,128]{2,1,0:T(8,128)} %bitcast.37, bf16[4,1,128,128]{3,2,1,0:T(8,128)(2,1)} %copy-done.2, f32[4,8,128,128]{3,2,1,0:T(8,128)} %get-tuple-element.10.local_ref, ...), custom_call_target="tpu_custom_call" | custom-call | tf_op jit(solution)/shard_map/output_conv/pallas_call | solution.py:151
  (17 shorter events, 0.2 us)
Async XLA Ops:
  0.9 1.7 %collective-permute-start = (bf16[4,1,128,128]{3,2,1,0:T(8,128)(2,1)S(1)}, bf16[4,1,128,128]{3,2,1,0:T(8,128)(2,1)S(1)}, u32[]{:S(2)}, u32[]{:S(2)}) collective-permute-start(bf16[4,1,128,128]{3,2,1,0:T(8,128)(2,1)S(1)} %constant_dynamic-slice_fusion.1), channel_id=1, source_target_pairs={{0,1},{1,0},{2,3},{3,2},{4,5},{5,4},{6,7},{7,6},{8,9},{9,8},{10,11... | collective-permute-start | bytes 393224 | tf_op jit(solution)/shard_map/input_conv_and_recurrence/ppermute | solution.py:13
  2.6 0.7 %copy-start.1 = (bf16[4,1,128,128]{3,2,1,0:T(8,128)(2,1)}, bf16[4,1,128,128]{3,2,1,0:T(8,128)(2,1)S(1)}, u32[]{:S(2)}) copy-start(bf16[4,1,128,128]{3,2,1,0:T(8,128)(2,1)S(1)} %collective-permute-done.top_ref.bottom_ref) | copy-start | bytes 393220
  8.5 7.8 %collective-permute-start.1 = (bf16[1040,128]{1,0:T(8,128)(2,1)}, bf16[1040,128]{1,0:T(8,128)(2,1)S(1)}, u32[]{:S(2)}, u32[]{:S(2)}) collective-permute-start(bf16[1040,128]{1,0:T(8,128)(2,1)} %get-tuple-element.9), channel_id=1, source_target_pairs={{0,2},{2,0},{4,6},{6,4},{8,10},{10,8},{12,14},{14,12},{16,18},{18,... | collective-permute-start | bytes 798728 | tf_op jit(solution)/shard_map/carry_across_blocks/ppermute | solution.py:194
  17.2 6.8 %collective-permute-start.2 = (bf16[1040,128]{1,0:T(8,128)(2,1)S(1)}, bf16[1040,128]{1,0:T(8,128)(2,1)S(1)}, u32[]{:S(2)}, u32[]{:S(2)}) collective-permute-start(bf16[1040,128]{1,0:T(8,128)(2,1)S(1)} %pad_maximum_fusion), channel_id=1, source_target_pairs={{0,4},{2,6},{4,0},{6,2},{8,12},{10,14},{12,8},{14,10},{16,20},{18,... | collective-permute-start | bytes 798728 | tf_op jit(solution)/shard_map/carry_across_blocks/ppermute | solution.py:194
  24.3 5.8 %collective-permute-start.3 = (bf16[1040,128]{1,0:T(8,128)(2,1)S(1)}, bf16[1040,128]{1,0:T(8,128)(2,1)S(1)}, u32[]{:S(2)}, u32[]{:S(2)}) collective-permute-start(bf16[1040,128]{1,0:T(8,128)(2,1)S(1)} %pad_maximum_fusion.1), channel_id=1, source_target_pairs={{0,8},{2,10},{4,12},{6,14},{8,0},{10,2},{12,4},{14,6},{16,24},{18,... | collective-permute-start | bytes 798728 | tf_op jit(solution)/shard_map/carry_across_blocks/ppermute | solution.py:194
  30.5 16.3 %copy-start.3 = (f32[4,128]{1,0:T(4,128)S(1)}, f32[4,128]{1,0:T(4,128)}, u32[]{:S(2)}) copy-start(f32[4,128]{1,0:T(4,128)} %get-tuple-element.8.cum_ref) | copy-start | bytes 6148
  30.5 16.0 %collective-permute-start.4 = (bf16[1040,128]{1,0:T(8,128)(2,1)S(1)}, bf16[1040,128]{1,0:T(8,128)(2,1)S(1)}, u32[]{:S(2)}, u32[]{:S(2)}) collective-permute-start(bf16[1040,128]{1,0:T(8,128)(2,1)S(1)} %pad_maximum_fusion.2), channel_id=1, source_target_pairs={{0,16},{2,18},{4,20},{6,22},{8,24},{10,26},{12,28},{14,30},{1,17},... | collective-permute-start | bytes 798728 | tf_op jit(solution)/shard_map/carry_across_blocks/ppermute | solution.py:194
  46.8 2.4 %copy-start = (f32[1024,128]{1,0:T(8,128)}, f32[1024,128]{1,0:T(8,128)S(1)}, u32[]{:S(2)}) copy-start(f32[1024,128]{1,0:T(8,128)S(1)} %add_select_fusion) | copy-start | bytes 1572868
  46.9 2.3 %collective-permute-start.5 = (bf16[4,1,128,128]{3,2,1,0:T(8,128)(2,1)S(1)}, bf16[4,1,128,128]{3,2,1,0:T(8,128)(2,1)S(1)}, u32[]{:S(2)}, u32[]{:S(2)}) collective-permute-start(bf16[4,1,128,128]{3,2,1,0:T(8,128)(2,1)S(1)} %fusion.9), channel_id=1, source_target_pairs={{0,1},{1,0},{2,3},{3,2},{4,5},{5,4},{6,7},{7,6},{8,9},{9,8},{10,11... | collective-permute-start | bytes 393224 | tf_op jit(solution)/shard_map/output_conv/ppermute | solution.py:13
  49.2 0.7 %copy-start.2 = (bf16[4,1,128,128]{3,2,1,0:T(8,128)(2,1)}, bf16[4,1,128,128]{3,2,1,0:T(8,128)(2,1)S(1)}, u32[]{:S(2)}) copy-start(bf16[4,1,128,128]{3,2,1,0:T(8,128)(2,1)S(1)} %collective-permute-done.5.top_ref.bottom_ref) | copy-start | bytes 393220

commit v14 on v11

--- a/solution.py
+++ b/solution.py
@@ -210,10 +210,14 @@
 
 
 def shards(frames, conv_in, decay, conv_out, skip):
+    with jax.named_scope("block_decay_product"):
+        block_power = decay[0]
+        for frame_index in range(1, decay.shape[0]):
+            block_power = block_power * decay[frame_index]
     with jax.named_scope("input_conv_and_recurrence"):
         local, cumulative, first_payload = input_stage(frames, conv_in, decay)
     with jax.named_scope("carry_across_blocks"):
-        incoming = incoming_state(cumulative[-1], local[-1], first_payload, "tm")
+        incoming = incoming_state(block_power, local[-1], first_payload, "tm")
     with jax.named_scope("output_conv"):
         return output_stage(local, cumulative, incoming, frames, conv_out, skip)
 

time: 55.9 us -> 55.2 us (0.987)
  other arithmetic: 1.89 us -> 1.23 us
    another operation x5, other arithmetic: 0.71 us -> 0.05 us
    unnamed x8 -> x10, local copies, waits for them, and re-layouts: 1.31 us -> 1.31 us
where the time goes in v14:
time: 55.2 us; the launch traced here: 54.9 us
  waiting for transfers between devices  29.3 us (53%)
  Pallas kernels  10.7 us (19%)
  starting transfers between devices  9.1 us (16%)
  local copies, waits for them, and re-layouts  4.4 us (8%)
  other arithmetic  1.23 us (2%)
    ppermute x4, waiting for transfers between devices, incoming_state(): got = lax.ppermute(payload, axis, pairs)  27 us
    ppermute x4, starting transfers between devices, incoming_state(): got = lax.ppermute(payload, axis, pairs)  8.51 us
    pallas_call x1, Pallas kernels, output_stage(): pl.pallas_call(output_kernel, grid=(count,), in_specs=[pl.BlockSpec((coun...  5.48 us
    pallas_call x1, Pallas kernels, input_stage(): pl.pallas_call(input_kernel, grid=(count,), in_specs=[pl.BlockSpec((count...  5.2 us
    ppermute x2, waiting for transfers between devices, halo_rows(): lax.ppermute(lax.dynamic_slice_in_dim(x, row, 1, axis=dim), axis, [(0, 1)...  2.32 us
    unnamed x10, local copies, waits for them, and re-layouts  1.31 us
  transfers between devices with their start and end apart: 6, of which 6 were waited for; matrix products, arithmetic and copies ran while one was open for 4% of the time, Pallas kernels for 0%

profile of v14, /device:TPU:0, one launch (start us, length us, event | category | flops | bytes accessed | tf_op | source)
XLA Modules:
  0.0 54.9 jit_solution(14289385057021092289)
XLA Ops:
  0.0 0.0 copy-start.4
  0.0 0.9 %constant_dynamic-slice_fusion.1 = bf16[4,1,128,128]{3,2,1,0:T(8,128)(2,1)S(1)} fusion(bf16[4,8,128,128]{3,2,1,0:T(8,128)(2,1)} %frame_ref.3, s32[]{:T(128)S(6)} %select_n.85), kind=kLoop, calls=%fused_computation.52 | loop fusion | bytes 262148 | tf_op jit(solution)/shard_map/input_conv_and_recurrence/dynamic_slice | solution.py:13
  0.9 0.5 collective-permute-start
  1.5 1.0 %collective-permute-done.top_ref.bottom_ref = bf16[4,1,128,128]{3,2,1,0:T(8,128)(2,1)S(1)} collective-permute-done((bf16[4,1,128,128]{3,2,1,0:T(8,128)(2,1)S(1)}, bf16[4,1,128,128]{3,2,1,0:T(8,128)(2,1)S(1)}, u32[]{:S(2)}, u32[]{:S(2)}) %collective-permute-start) | collective-permute-done | bytes 131104 | tf_op jit(solution)/shard_map/input_conv_and_recurrence/ppermute | solution.py:13
  2.4 0.0 copy-start.1
  2.4 0.6 %copy-done.1 = bf16[4,1,128,128]{3,2,1,0:T(8,128)(2,1)} copy-done((bf16[4,1,128,128]{3,2,1,0:T(8,128)(2,1)}, bf16[4,1,128,128]{3,2,1,0:T(8,128)(2,1)S(1)}, u32[]{:S(2)}) %copy-start.1) | copy-done | bytes 131096
  3.1 5.2 %input_conv_and_recurrence.1 = (f32[4,8,128,128]{3,2,1,0:T(8,128)}, f32[4,128]{1,0:T(4,128)}, bf16[1040,128]{1,0:T(8,128)(2,1)}) custom-call(f32[4,128]{1,0:T(4,128)} %decay_ref.1, bf16[4,1,128,128]{3,2,1,0:T(8,128)(2,1)} %copy-done.1, bf16[4,8,128,128]{3,2,1,0:T(8,128)(2,1)} %frame_ref.3, bf16[4,1,128,128]{3,2,1,0:T(8,128)(2,1)} %copy-done.1, ...), custom_call_target="tpu_custom_call" | custom-call | tf_op jit(solution)/shard_map/input_conv_and_recurrence/pallas_call | solution.py:114
  8.3 2.8 %collective-permute-start.1 = (bf16[1040,128]{1,0:T(8,128)(2,1)}, bf16[1040,128]{1,0:T(8,128)(2,1)S(1)}, u32[]{:S(2)}, u32[]{:S(2)}) collective-permute-start(bf16[1040,128]{1,0:T(8,128)(2,1)} %get-tuple-element.9), channel_id=1, source_target_pairs={{0,2},{2,0},{4,6},{6,4},{8,10},{10,8},{12,14},{14,12},{16,18},{18,... | collective-permute-start | bytes 798728 | tf_op jit(solution)/shard_map/carry_across_blocks/ppermute | solution.py:192
  11.1 1.1 %slice.56 = f32[1,8,128,128]{3,2,1,0:T(8,128)S(1)} slice(f32[4,8,128,128]{3,2,1,0:T(8,128)} %get-tuple-element.10.local_ref), slice={[3:4], [0:8], [0:128], [0:128]} | slice | bytes 1048576 | tf_op jit(solution)/shard_map/carry_across_blocks/slice | solution.py:220
  12.2 5.8 %collective-permute-done.1 = bf16[1040,128]{1,0:T(8,128)(2,1)S(1)} collective-permute-done((bf16[1040,128]{1,0:T(8,128)(2,1)}, bf16[1040,128]{1,0:T(8,128)(2,1)S(1)}, u32[]{:S(2)}, u32[]{:S(2)}) %collective-permute-start.1) | collective-permute-done | bytes 266272 | tf_op jit(solution)/shard_map/carry_across_blocks/ppermute | solution.py:192
  18.1 0.0 copy-done.4
  18.1 0.1 fusion.29
  18.3 1.8 %collective-permute-start.2 = (bf16[1040,128]{1,0:T(8,128)(2,1)S(1)}, bf16[1040,128]{1,0:T(8,128)(2,1)S(1)}, u32[]{:S(2)}, u32[]{:S(2)}) collective-permute-start(bf16[1040,128]{1,0:T(8,128)(2,1)S(1)} %pad_maximum_fusion), channel_id=1, source_target_pairs={{0,4},{2,6},{4,0},{6,2},{8,12},{10,14},{12,8},{14,10},{16,20},{18,... | collective-permute-start | bytes 798728 | tf_op jit(solution)/shard_map/carry_across_blocks/ppermute | solution.py:192
  20.1 6.2 %collective-permute-done.2 = bf16[1040,128]{1,0:T(8,128)(2,1)S(1)} collective-permute-done((bf16[1040,128]{1,0:T(8,128)(2,1)S(1)}, bf16[1040,128]{1,0:T(8,128)(2,1)S(1)}, u32[]{:S(2)}, u32[]{:S(2)}) %collective-permute-start.2) | collective-permute-done | bytes 266272 | tf_op jit(solution)/shard_map/carry_across_blocks/ppermute | solution.py:192
  26.3 0.2 fusion.10
  26.6 1.6 %collective-permute-start.3 = (bf16[1040,128]{1,0:T(8,128)(2,1)S(1)}, bf16[1040,128]{1,0:T(8,128)(2,1)S(1)}, u32[]{:S(2)}, u32[]{:S(2)}) collective-permute-start(bf16[1040,128]{1,0:T(8,128)(2,1)S(1)} %pad_maximum_fusion.1), channel_id=1, source_target_pairs={{0,8},{2,10},{4,12},{6,14},{8,0},{10,2},{12,4},{14,6},{16,24},{18,... | collective-permute-start | bytes 798728 | tf_op jit(solution)/shard_map/carry_across_blocks/ppermute | solution.py:192
  28.2 5.5 %collective-permute-done.3 = bf16[1040,128]{1,0:T(8,128)(2,1)S(1)} collective-permute-done((bf16[1040,128]{1,0:T(8,128)(2,1)S(1)}, bf16[1040,128]{1,0:T(8,128)(2,1)S(1)}, u32[]{:S(2)}, u32[]{:S(2)}) %collective-permute-start.3) | collective-permute-done | bytes 266272 | tf_op jit(solution)/shard_map/carry_across_blocks/ppermute | solution.py:192
  33.8 0.3 fusion.6
  34.1 0.0 copy-start.3
  34.1 2.2 %collective-permute-start.4 = (bf16[1040,128]{1,0:T(8,128)(2,1)S(1)}, bf16[1040,128]{1,0:T(8,128)(2,1)S(1)}, u32[]{:S(2)}, u32[]{:S(2)}) collective-permute-start(bf16[1040,128]{1,0:T(8,128)(2,1)S(1)} %pad_maximum_fusion.2), channel_id=1, source_target_pairs={{0,16},{2,18},{4,20},{6,22},{8,24},{10,26},{12,28},{14,30},{16,0},... | collective-permute-start | bytes 798728 | tf_op jit(solution)/shard_map/carry_across_blocks/ppermute | solution.py:192
  36.4 1.1 %fusion.30 = (f32[4,1,128,128]{3,2,1,0:T(8,128)S(1)}, f32[4,1,128,128]{3,2,1,0:T(8,128)S(1)}) fusion(f32[4,8,128,128]{3,2,1,0:T(8,128)} %get-tuple-element.10.local_ref), kind=kLoop, calls=%fused_computation.76 | loop fusion | bytes 1048576 | tf_op jit(solution)/shard_map/output_conv/slice | solution.py:145
  37.5 9.4 %collective-permute-done.4 = bf16[1040,128]{1,0:T(8,128)(2,1)S(1)} collective-permute-done((bf16[1040,128]{1,0:T(8,128)(2,1)S(1)}, bf16[1040,128]{1,0:T(8,128)(2,1)S(1)}, u32[]{:S(2)}, u32[]{:S(2)}) %collective-permute-start.4) | collective-permute-done | bytes 266272 | tf_op jit(solution)/shard_map/carry_across_blocks/ppermute | solution.py:192
  46.9 0.2 add_select_fusion
  47.2 0.0 copy-start
  47.2 0.0 copy-done.3
  47.2 0.1 fusion.9
  47.3 0.1 collective-permute-start.5
  47.4 1.3 %collective-permute-done.5.top_ref.bottom_ref = bf16[4,1,128,128]{3,2,1,0:T(8,128)(2,1)S(1)} collective-permute-done((bf16[4,1,128,128]{3,2,1,0:T(8,128)(2,1)S(1)}, bf16[4,1,128,128]{3,2,1,0:T(8,128)(2,1)S(1)}, u32[]{:S(2)}, u32[]{:S(2)}) %collective-permute-start.5) | collective-permute-done | bytes 131104 | tf_op jit(solution)/shard_map/output_conv/ppermute | solution.py:13
  48.7 0.0 copy-start.2
  48.7 0.0 copy-done
  48.7 0.6 %copy-done.2 = bf16[4,1,128,128]{3,2,1,0:T(8,128)(2,1)} copy-done((bf16[4,1,128,128]{3,2,1,0:T(8,128)(2,1)}, bf16[4,1,128,128]{3,2,1,0:T(8,128)(2,1)S(1)}, u32[]{:S(2)}) %copy-start.2) | copy-done | bytes 131096
  49.4 5.5 %output_conv.1 = bf16[4,8,128,128]{3,2,1,0:T(8,128)(2,1)} custom-call(f32[4,128]{1,0:T(4,128)} %get-tuple-element.8.cum_ref, f32[1,128]{1,0:T(1,128)} %bitcast.43, f32[8,128,128]{2,1,0:T(8,128)} %bitcast.36, bf16[4,1,128,128]{3,2,1,0:T(8,128)(2,1)} %copy-done.2, f32[4,8,128,128]{3,2,1,0:T(8,128)} %get-tuple-element.10.local_ref, ...), custom_call_target="tpu_custom_call" | custom-call | tf_op jit(solution)/shard_map/output_conv/pallas_call | solution.py:151
  (18 shorter events, 0.2 us)
Async XLA Ops:
  0.0 18.1 %copy-start.4 = (f32[4,128]{1,0:T(4,128)S(1)}, f32[4,128]{1,0:T(4,128)}, u32[]{:S(2)}) copy-start(f32[4,128]{1,0:T(4,128)} %decay_ref.1) | copy-start | bytes 6148
  0.9 1.5 %collective-permute-start = (bf16[4,1,128,128]{3,2,1,0:T(8,128)(2,1)S(1)}, bf16[4,1,128,128]{3,2,1,0:T(8,128)(2,1)S(1)}, u32[]{:S(2)}, u32[]{:S(2)}) collective-permute-start(bf16[4,1,128,128]{3,2,1,0:T(8,128)(2,1)S(1)} %constant_dynamic-slice_fusion.1), channel_id=1, source_target_pairs={{0,1},{1,0},{2,3},{3,2},{4,5},{5,4},{6,7},{7,6},{8,9},{9,8},{10,11... | collective-permute-start | bytes 393224 | tf_op jit(solution)/shard_map/input_conv_and_recurrence/ppermute | solution.py:13
  2.4 0.7 %copy-start.1 = (bf16[4,1,128,128]{3,2,1,0:T(8,128)(2,1)}, bf16[4,1,128,128]{3,2,1,0:T(8,128)(2,1)S(1)}, u32[]{:S(2)}) copy-start(bf16[4,1,128,128]{3,2,1,0:T(8,128)(2,1)S(1)} %collective-permute-done.top_ref.bottom_ref) | copy-start | bytes 393220
  8.3 9.8 %collective-permute-start.1 = (bf16[1040,128]{1,0:T(8,128)(2,1)}, bf16[1040,128]{1,0:T(8,128)(2,1)S(1)}, u32[]{:S(2)}, u32[]{:S(2)}) collective-permute-start(bf16[1040,128]{1,0:T(8,128)(2,1)} %get-tuple-element.9), channel_id=1, source_target_pairs={{0,2},{2,0},{4,6},{6,4},{8,10},{10,8},{12,14},{14,12},{16,18},{18,... | collective-permute-start | bytes 798728 | tf_op jit(solution)/shard_map/carry_across_blocks/ppermute | solution.py:192
  18.3 8.0 %collective-permute-start.2 = (bf16[1040,128]{1,0:T(8,128)(2,1)S(1)}, bf16[1040,128]{1,0:T(8,128)(2,1)S(1)}, u32[]{:S(2)}, u32[]{:S(2)}) collective-permute-start(bf16[1040,128]{1,0:T(8,128)(2,1)S(1)} %pad_maximum_fusion), channel_id=1, source_target_pairs={{0,4},{2,6},{4,0},{6,2},{8,12},{10,14},{12,8},{14,10},{16,20},{18,... | collective-permute-start | bytes 798728 | tf_op jit(solution)/shard_map/carry_across_blocks/ppermute | solution.py:192
  26.6 7.1 %collective-permute-start.3 = (bf16[1040,128]{1,0:T(8,128)(2,1)S(1)}, bf16[1040,128]{1,0:T(8,128)(2,1)S(1)}, u32[]{:S(2)}, u32[]{:S(2)}) collective-permute-start(bf16[1040,128]{1,0:T(8,128)(2,1)S(1)} %pad_maximum_fusion.1), channel_id=1, source_target_pairs={{0,8},{2,10},{4,12},{6,14},{8,0},{10,2},{12,4},{14,6},{16,24},{18,... | collective-permute-start | bytes 798728 | tf_op jit(solution)/shard_map/carry_across_blocks/ppermute | solution.py:192
  34.1 13.1 %copy-start.3 = (f32[4,128]{1,0:T(4,128)S(1)}, f32[4,128]{1,0:T(4,128)}, u32[]{:S(2)}) copy-start(f32[4,128]{1,0:T(4,128)} %get-tuple-element.8.cum_ref) | copy-start | bytes 6148
  34.1 12.8 %collective-permute-start.4 = (bf16[1040,128]{1,0:T(8,128)(2,1)S(1)}, bf16[1040,128]{1,0:T(8,128)(2,1)S(1)}, u32[]{:S(2)}, u32[]{:S(2)}) collective-permute-start(bf16[1040,128]{1,0:T(8,128)(2,1)S(1)} %pad_maximum_fusion.2), channel_id=1, source_target_pairs={{0,16},{2,18},{4,20},{6,22},{8,24},{10,26},{12,28},{14,30},{16,0},... | collective-permute-start | bytes 798728 | tf_op jit(solution)/shard_map/carry_across_blocks/ppermute | solution.py:192
  47.2 1.6 %copy-start = (f32[1024,128]{1,0:T(8,128)}, f32[1024,128]{1,0:T(8,128)S(1)}, u32[]{:S(2)}) copy-start(f32[1024,128]{1,0:T(8,128)S(1)} %add_select_fusion) | copy-start | bytes 1572868
  47.3 1.4 %collective-permute-start.5 = (bf16[4,1,128,128]{3,2,1,0:T(8,128)(2,1)S(1)}, bf16[4,1,128,128]{3,2,1,0:T(8,128)(2,1)S(1)}, u32[]{:S(2)}, u32[]{:S(2)}) collective-permute-start(bf16[4,1,128,128]{3,2,1,0:T(8,128)(2,1)S(1)} %fusion.9), channel_id=1, source_target_pairs={{0,1},{1,0},{2,3},{3,2},{4,5},{5,4},{6,7},{7,6},{8,9},{9,8},{10,11... | collective-permute-start | bytes 393224 | tf_op jit(solution)/shard_map/output_conv/ppermute | solution.py:13
  48.7 0.7 %copy-start.2 = (bf16[4,1,128,128]{3,2,1,0:T(8,128)(2,1)}, bf16[4,1,128,128]{3,2,1,0:T(8,128)(2,1)S(1)}, u32[]{:S(2)}) copy-start(bf16[4,1,128,128]{3,2,1,0:T(8,128)(2,1)S(1)} %collective-permute-done.5.top_ref.bottom_ref) | copy-start | bytes 393220

commit v15 on v14

--- a/solution.py
+++ b/solution.py
@@ -4,6 +4,8 @@
 from jax.experimental import pallas as pl
 from jax.experimental.pallas import tpu as pltpu
 from jax.sharding import PartitionSpec as P
+
+PER_STEP = 2
 
 
 def halo_rows(x, axis, dim):
@@ -70,15 +72,20 @@
         state_ref[...] = jnp.zeros_like(state_ref)
         power_ref[...] = jnp.ones_like(power_ref)
 
-    x = padded_band(top_ref[f], frame_ref[0], bottom_ref[f], "rows")
-    drive = conv_taps(x, w_ref)
-    rate = decay_ref[pl.ds(f, 1), :]
-    state = rate * state_ref[...] + drive
-    power = rate * power_ref[...]
+    per = frame_ref.shape[0]
+    state = state_ref[...]
+    power = power_ref[...]
+    for j in range(per):
+        g = f * per + j
+        x = padded_band(top_ref[g], frame_ref[j], bottom_ref[g], "rows")
+        drive = conv_taps(x, w_ref)
+        rate = decay_ref[pl.ds(g, 1), :]
+        state = rate * state + drive
+        power = rate * power
+        out_ref[j] = state.reshape(band, width, m)
+        cum_ref[pl.ds(g, 1), :] = power
     state_ref[...] = state
     power_ref[...] = power
-    out_ref[0] = state.reshape(band, width, m)
-    cum_ref[pl.ds(f, 1), :] = power
 
     @pl.when(f == pl.num_programs(0) - 1)
     def _():
@@ -97,12 +104,15 @@
 ):
     f = pl.program_id(0)
     band, width, m = out_ref.shape[1:]
-    inner = (local_ref[0] + cum_ref[pl.ds(f, 1), :] * incoming_ref[...]).astype(jnp.bfloat16)
-    x = padded_band(top_ref[f], inner, bottom_ref[f], "rows")
-    total = conv_taps(x, w_ref)
-    frame = frame_ref[0].reshape(band * width, m).astype(jnp.float32)
-    total = total + skip_ref[...] * frame
-    out_ref[0] = total.astype(jnp.bfloat16).reshape(band, width, m)
+    per = frame_ref.shape[0]
+    for j in range(per):
+        g = f * per + j
+        inner = (local_ref[j] + cum_ref[pl.ds(g, 1), :] * incoming_ref[...]).astype(jnp.bfloat16)
+        x = padded_band(top_ref[g], inner, bottom_ref[g], "rows")
+        total = conv_taps(x, w_ref)
+        frame = frame_ref[j].reshape(band * width, m).astype(jnp.float32)
+        total = total + skip_ref[...] * frame
+        out_ref[j] = total.astype(jnp.bfloat16).reshape(band, width, m)
 
 
 def input_stage(frames, conv_in, decay):
@@ -113,16 +123,16 @@
     payload_rows = band * width + 16
     return pl.pallas_call(
         input_kernel,
-        grid=(count,),
+        grid=(count // PER_STEP,),
         in_specs=[
             pl.BlockSpec((count, state_width), lambda f: (0, 0)),
             halo,
-            pl.BlockSpec((1, band, width, channels), lambda f: (f, 0, 0, 0)),
+            pl.BlockSpec((PER_STEP, band, width, channels), lambda f: (f, 0, 0, 0)),
             halo,
             pl.BlockSpec((3, 3, channels, state_width), lambda f: (0, 0, 0, 0)),
         ],
         out_specs=[
-            pl.BlockSpec((1, band, width, state_width), lambda f: (f, 0, 0, 0)),
+            pl.BlockSpec((PER_STEP, band, width, state_width), lambda f: (f, 0, 0, 0)),
             pl.BlockSpec((count, state_width), lambda f: (0, 0)),
             pl.BlockSpec((payload_rows, state_width), lambda f: (0, 0)),
         ],
@@ -150,18 +160,18 @@
     halo = pl.BlockSpec(memory_space=pltpu.VMEM)
     return pl.pallas_call(
         output_kernel,
-        grid=(count,),
+        grid=(count // PER_STEP,),
         in_specs=[
             pl.BlockSpec((count, state_width), lambda f: (0, 0)),
             pl.BlockSpec((1, channels), lambda f: (0, 0)),
             pl.BlockSpec((band, width, state_width), lambda f: (0, 0, 0)),
             halo,
-            pl.BlockSpec((1, band, width, state_width), lambda f: (f, 0, 0, 0)),
-            halo,
-            pl.BlockSpec((1, band, width, channels), lambda f: (f, 0, 0, 0)),
+            pl.BlockSpec((PER_STEP, band, width, state_width), lambda f: (f, 0, 0, 0)),
+            halo,
+            pl.BlockSpec((PER_STEP, band, width, channels), lambda f: (f, 0, 0, 0)),
             pl.BlockSpec((3, 3, state_width, channels), lambda f: (0, 0, 0, 0)),
         ],
-        out_specs=pl.BlockSpec((1, band, width, channels), lambda f: (f, 0, 0, 0)),
+        out_specs=pl.BlockSpec((PER_STEP, band, width, channels), lambda f: (f, 0, 0, 0)),
         out_shape=jax.ShapeDtypeStruct((count, band, width, channels), jnp.bfloat16),
         compiler_params=pltpu.CompilerParams(dimension_semantics=("arbitrary",)),
     )(cumulative, skip.reshape(1, channels), incoming, top, local, bottom, frames, conv_out)

time: 55.2 us -> 54.2 us (0.982)
  Pallas kernels: 10.7 us -> 9.77 us
    pallas_call x2, Pallas kernels: 10.7 us -> 9.77 us  [the longest x1 5.1 us: output_stage(): pl.pallas_call(output_kernel, grid=(count // PER_STEP,), in_specs=[pl.Blo...]
where the time goes in v15:
time: 54.2 us; the launch traced here: 54 us
  waiting for transfers between devices  29.3 us (54%)
  Pallas kernels  9.77 us (18%)
  starting transfers between devices  9.1 us (17%)
  local copies, waits for them, and re-layouts  4.4 us (8%)
  other arithmetic  1.23 us (2%)
    ppermute x4, waiting for transfers between devices, incoming_state(): got = lax.ppermute(payload, axis, pairs)  27 us
    ppermute x4, starting transfers between devices, incoming_state(): got = lax.ppermute(payload, axis, pairs)  8.51 us
    pallas_call x1, Pallas kernels, output_stage(): pl.pallas_call(output_kernel, grid=(count // PER_STEP,), in_specs=[pl.Blo...  5.1 us
    pallas_call x1, Pallas kernels, input_stage(): pl.pallas_call(input_kernel, grid=(count // PER_STEP,), in_specs=[pl.Bloc...  4.67 us
    ppermute x2, waiting for transfers between devices, halo_rows(): lax.ppermute(lax.dynamic_slice_in_dim(x, row, 1, axis=dim), axis, [(0, 1)...  2.32 us
    unnamed x10, local copies, waits for them, and re-layouts  1.31 us
  transfers between devices with their start and end apart: 6, of which 6 were waited for; matrix products, arithmetic and copies ran while one was open for 4% of the time, Pallas kernels for 0%

profile of v15, /device:TPU:0, one launch (start us, length us, event | category | flops | bytes accessed | tf_op | source)
XLA Modules:
  0.0 54.0 jit_solution(4476383167389564326)
XLA Ops:
  0.0 0.0 copy-start.4
  0.0 0.9 %constant_dynamic-slice_fusion.1 = bf16[4,1,128,128]{3,2,1,0:T(8,128)(2,1)S(1)} fusion(bf16[4,8,128,128]{3,2,1,0:T(8,128)(2,1)} %frame_ref.3, s32[]{:T(128)S(6)} %select_n.85), kind=kLoop, calls=%fused_computation.52 | loop fusion | bytes 262148 | tf_op jit(solution)/shard_map/input_conv_and_recurrence/dynamic_slice | solution.py:15
  0.9 0.5 collective-permute-start
  1.5 1.0 %collective-permute-done.top_ref.bottom_ref = bf16[4,1,128,128]{3,2,1,0:T(8,128)(2,1)S(1)} collective-permute-done((bf16[4,1,128,128]{3,2,1,0:T(8,128)(2,1)S(1)}, bf16[4,1,128,128]{3,2,1,0:T(8,128)(2,1)S(1)}, u32[]{:S(2)}, u32[]{:S(2)}) %collective-permute-start) | collective-permute-done | bytes 131104 | tf_op jit(solution)/shard_map/input_conv_and_recurrence/ppermute | solution.py:15
  2.4 0.0 copy-start.1
  2.4 0.6 %copy-done.1 = bf16[4,1,128,128]{3,2,1,0:T(8,128)(2,1)} copy-done((bf16[4,1,128,128]{3,2,1,0:T(8,128)(2,1)}, bf16[4,1,128,128]{3,2,1,0:T(8,128)(2,1)S(1)}, u32[]{:S(2)}) %copy-start.1) | copy-done | bytes 131096
  3.1 4.7 %input_conv_and_recurrence.1 = (f32[4,8,128,128]{3,2,1,0:T(8,128)}, f32[4,128]{1,0:T(4,128)}, bf16[1040,128]{1,0:T(8,128)(2,1)}) custom-call(f32[4,128]{1,0:T(4,128)} %decay_ref.1, bf16[4,1,128,128]{3,2,1,0:T(8,128)(2,1)} %copy-done.1, bf16[4,8,128,128]{3,2,1,0:T(8,128)(2,1)} %frame_ref.3, bf16[4,1,128,128]{3,2,1,0:T(8,128)(2,1)} %copy-done.1, ...), custom_call_target="tpu_custom_call" | custom-call | tf_op jit(solution)/shard_map/input_conv_and_recurrence/pallas_call | solution.py:124
  7.8 2.8 %collective-permute-start.1 = (bf16[1040,128]{1,0:T(8,128)(2,1)}, bf16[1040,128]{1,0:T(8,128)(2,1)S(1)}, u32[]{:S(2)}, u32[]{:S(2)}) collective-permute-start(bf16[1040,128]{1,0:T(8,128)(2,1)} %get-tuple-element.9), channel_id=1, source_target_pairs={{0,2},{2,0},{4,6},{6,4},{8,10},{10,8},{12,14},{14,12},{16,18},{18,... | collective-permute-start | bytes 798728 | tf_op jit(solution)/shard_map/carry_across_blocks/ppermute | solution.py:202
  10.6 1.1 %slice.56 = f32[1,8,128,128]{3,2,1,0:T(8,128)S(1)} slice(f32[4,8,128,128]{3,2,1,0:T(8,128)} %get-tuple-element.10.local_ref), slice={[3:4], [0:8], [0:128], [0:128]} | slice | bytes 1048576 | tf_op jit(solution)/shard_map/carry_across_blocks/slice | solution.py:230
  11.7 5.8 %collective-permute-done.1 = bf16[1040,128]{1,0:T(8,128)(2,1)S(1)} collective-permute-done((bf16[1040,128]{1,0:T(8,128)(2,1)}, bf16[1040,128]{1,0:T(8,128)(2,1)S(1)}, u32[]{:S(2)}, u32[]{:S(2)}) %collective-permute-start.1) | collective-permute-done | bytes 266272 | tf_op jit(solution)/shard_map/carry_across_blocks/ppermute | solution.py:202
  17.5 0.0 copy-done.4
  17.6 0.1 fusion.29
  17.8 1.8 %collective-permute-start.2 = (bf16[1040,128]{1,0:T(8,128)(2,1)S(1)}, bf16[1040,128]{1,0:T(8,128)(2,1)S(1)}, u32[]{:S(2)}, u32[]{:S(2)}) collective-permute-start(bf16[1040,128]{1,0:T(8,128)(2,1)S(1)} %pad_maximum_fusion), channel_id=1, source_target_pairs={{0,4},{2,6},{4,0},{6,2},{8,12},{10,14},{12,8},{14,10},{16,20},{18,... | collective-permute-start | bytes 798728 | tf_op jit(solution)/shard_map/carry_across_blocks/ppermute | solution.py:202
  19.6 6.2 %collective-permute-done.2 = bf16[1040,128]{1,0:T(8,128)(2,1)S(1)} collective-permute-done((bf16[1040,128]{1,0:T(8,128)(2,1)S(1)}, bf16[1040,128]{1,0:T(8,128)(2,1)S(1)}, u32[]{:S(2)}, u32[]{:S(2)}) %collective-permute-start.2) | collective-permute-done | bytes 266272 | tf_op jit(solution)/shard_map/carry_across_blocks/ppermute | solution.py:202
  25.8 0.2 fusion.10
  26.1 1.6 %collective-permute-start.3 = (bf16[1040,128]{1,0:T(8,128)(2,1)S(1)}, bf16[1040,128]{1,0:T(8,128)(2,1)S(1)}, u32[]{:S(2)}, u32[]{:S(2)}) collective-permute-start(bf16[1040,128]{1,0:T(8,128)(2,1)S(1)} %pad_maximum_fusion.1), channel_id=1, source_target_pairs={{0,8},{2,10},{4,12},{6,14},{8,0},{10,2},{12,4},{14,6},{16,24},{18,... | collective-permute-start | bytes 798728 | tf_op jit(solution)/shard_map/carry_across_blocks/ppermute | solution.py:202
  27.6 5.5 %collective-permute-done.3 = bf16[1040,128]{1,0:T(8,128)(2,1)S(1)} collective-permute-done((bf16[1040,128]{1,0:T(8,128)(2,1)S(1)}, bf16[1040,128]{1,0:T(8,128)(2,1)S(1)}, u32[]{:S(2)}, u32[]{:S(2)}) %collective-permute-start.3) | collective-permute-done | bytes 266272 | tf_op jit(solution)/shard_map/carry_across_blocks/ppermute | solution.py:202
  33.2 0.3 fusion.6
  33.6 0.0 copy-start.3
  33.6 2.2 %collective-permute-start.4 = (bf16[1040,128]{1,0:T(8,128)(2,1)S(1)}, bf16[1040,128]{1,0:T(8,128)(2,1)S(1)}, u32[]{:S(2)}, u32[]{:S(2)}) collective-permute-start(bf16[1040,128]{1,0:T(8,128)(2,1)S(1)} %pad_maximum_fusion.2), channel_id=1, source_target_pairs={{0,16},{2,18},{4,20},{6,22},{8,24},{10,26},{12,28},{14,30},{16,0},... | collective-permute-start | bytes 798728 | tf_op jit(solution)/shard_map/carry_across_blocks/ppermute | solution.py:202
  35.8 1.1 %fusion.30 = (f32[4,1,128,128]{3,2,1,0:T(8,128)S(1)}, f32[4,1,128,128]{3,2,1,0:T(8,128)S(1)}) fusion(f32[4,8,128,128]{3,2,1,0:T(8,128)} %get-tuple-element.10.local_ref), kind=kLoop, calls=%fused_computation.76 | loop fusion | bytes 1048576 | tf_op jit(solution)/shard_map/output_conv/slice | solution.py:155
  36.9 9.4 %collective-permute-done.4 = bf16[1040,128]{1,0:T(8,128)(2,1)S(1)} collective-permute-done((bf16[1040,128]{1,0:T(8,128)(2,1)S(1)}, bf16[1040,128]{1,0:T(8,128)(2,1)S(1)}, u32[]{:S(2)}, u32[]{:S(2)}) %collective-permute-start.4) | collective-permute-done | bytes 266272 | tf_op jit(solution)/shard_map/carry_across_blocks/ppermute | solution.py:202
  46.4 0.2 add_select_fusion
  46.6 0.0 copy-start
  46.7 0.0 copy-done.3
  46.7 0.1 fusion.9
  46.8 0.1 collective-permute-start.5
  46.9 1.3 %collective-permute-done.5.top_ref.bottom_ref = bf16[4,1,128,128]{3,2,1,0:T(8,128)(2,1)S(1)} collective-permute-done((bf16[4,1,128,128]{3,2,1,0:T(8,128)(2,1)S(1)}, bf16[4,1,128,128]{3,2,1,0:T(8,128)(2,1)S(1)}, u32[]{:S(2)}, u32[]{:S(2)}) %collective-permute-start.5) | collective-permute-done | bytes 131104 | tf_op jit(solution)/shard_map/output_conv/ppermute | solution.py:15
  48.2 0.0 copy-start.2
  48.2 0.0 copy-done
  48.2 0.6 %copy-done.2 = bf16[4,1,128,128]{3,2,1,0:T(8,128)(2,1)} copy-done((bf16[4,1,128,128]{3,2,1,0:T(8,128)(2,1)}, bf16[4,1,128,128]{3,2,1,0:T(8,128)(2,1)S(1)}, u32[]{:S(2)}) %copy-start.2) | copy-done | bytes 131096
  48.9 5.1 %output_conv.1 = bf16[4,8,128,128]{3,2,1,0:T(8,128)(2,1)} custom-call(f32[4,128]{1,0:T(4,128)} %get-tuple-element.8.cum_ref, f32[1,128]{1,0:T(1,128)} %bitcast.43, f32[8,128,128]{2,1,0:T(8,128)} %bitcast.36, bf16[4,1,128,128]{3,2,1,0:T(8,128)(2,1)} %copy-done.2, f32[4,8,128,128]{3,2,1,0:T(8,128)} %get-tuple-element.10.local_ref, ...), custom_call_target="tpu_custom_call" | custom-call | tf_op jit(solution)/shard_map/output_conv/pallas_call | solution.py:161
  (18 shorter events, 0.2 us)
Async XLA Ops:
  0.0 17.5 %copy-start.4 = (f32[4,128]{1,0:T(4,128)S(1)}, f32[4,128]{1,0:T(4,128)}, u32[]{:S(2)}) copy-start(f32[4,128]{1,0:T(4,128)} %decay_ref.1) | copy-start | bytes 6148
  0.9 1.5 %collective-permute-start = (bf16[4,1,128,128]{3,2,1,0:T(8,128)(2,1)S(1)}, bf16[4,1,128,128]{3,2,1,0:T(8,128)(2,1)S(1)}, u32[]{:S(2)}, u32[]{:S(2)}) collective-permute-start(bf16[4,1,128,128]{3,2,1,0:T(8,128)(2,1)S(1)} %constant_dynamic-slice_fusion.1), channel_id=1, source_target_pairs={{0,1},{1,0},{2,3},{3,2},{4,5},{5,4},{6,7},{7,6},{8,9},{9,8},{10,11... | collective-permute-start | bytes 393224 | tf_op jit(solution)/shard_map/input_conv_and_recurrence/ppermute | solution.py:15
  2.4 0.7 %copy-start.1 = (bf16[4,1,128,128]{3,2,1,0:T(8,128)(2,1)}, bf16[4,1,128,128]{3,2,1,0:T(8,128)(2,1)S(1)}, u32[]{:S(2)}) copy-start(bf16[4,1,128,128]{3,2,1,0:T(8,128)(2,1)S(1)} %collective-permute-done.top_ref.bottom_ref) | copy-start | bytes 393220
  7.8 9.8 %collective-permute-start.1 = (bf16[1040,128]{1,0:T(8,128)(2,1)}, bf16[1040,128]{1,0:T(8,128)(2,1)S(1)}, u32[]{:S(2)}, u32[]{:S(2)}) collective-permute-start(bf16[1040,128]{1,0:T(8,128)(2,1)} %get-tuple-element.9), channel_id=1, source_target_pairs={{0,2},{2,0},{4,6},{6,4},{8,10},{10,8},{12,14},{14,12},{16,18},{18,... | collective-permute-start | bytes 798728 | tf_op jit(solution)/shard_map/carry_across_blocks/ppermute | solution.py:202
  17.8 8.0 %collective-permute-start.2 = (bf16[1040,128]{1,0:T(8,128)(2,1)S(1)}, bf16[1040,128]{1,0:T(8,128)(2,1)S(1)}, u32[]{:S(2)}, u32[]{:S(2)}) collective-permute-start(bf16[1040,128]{1,0:T(8,128)(2,1)S(1)} %pad_maximum_fusion), channel_id=1, source_target_pairs={{0,4},{2,6},{4,0},{6,2},{8,12},{10,14},{12,8},{14,10},{16,20},{18,... | collective-permute-start | bytes 798728 | tf_op jit(solution)/shard_map/carry_across_blocks/ppermute | solution.py:202
  26.1 7.1 %collective-permute-start.3 = (bf16[1040,128]{1,0:T(8,128)(2,1)S(1)}, bf16[1040,128]{1,0:T(8,128)(2,1)S(1)}, u32[]{:S(2)}, u32[]{:S(2)}) collective-permute-start(bf16[1040,128]{1,0:T(8,128)(2,1)S(1)} %pad_maximum_fusion.1), channel_id=1, source_target_pairs={{0,8},{2,10},{4,12},{6,14},{8,0},{10,2},{12,4},{14,6},{16,24},{18,... | collective-permute-start | bytes 798728 | tf_op jit(solution)/shard_map/carry_across_blocks/ppermute | solution.py:202
  33.6 13.1 %copy-start.3 = (f32[4,128]{1,0:T(4,128)S(1)}, f32[4,128]{1,0:T(4,128)}, u32[]{:S(2)}) copy-start(f32[4,128]{1,0:T(4,128)} %get-tuple-element.8.cum_ref) | copy-start | bytes 6148
  33.6 12.8 %collective-permute-start.4 = (bf16[1040,128]{1,0:T(8,128)(2,1)S(1)}, bf16[1040,128]{1,0:T(8,128)(2,1)S(1)}, u32[]{:S(2)}, u32[]{:S(2)}) collective-permute-start(bf16[1040,128]{1,0:T(8,128)(2,1)S(1)} %pad_maximum_fusion.2), channel_id=1, source_target_pairs={{0,16},{2,18},{4,20},{6,22},{8,24},{10,26},{12,28},{14,30},{16,0},... | collective-permute-start | bytes 798728 | tf_op jit(solution)/shard_map/carry_across_blocks/ppermute | solution.py:202
  46.6 1.6 %copy-start = (f32[1024,128]{1,0:T(8,128)}, f32[1024,128]{1,0:T(8,128)S(1)}, u32[]{:S(2)}) copy-start(f32[1024,128]{1,0:T(8,128)S(1)} %add_select_fusion) | copy-start | bytes 1572868
  46.8 1.4 %collective-permute-start.5 = (bf16[4,1,128,128]{3,2,1,0:T(8,128)(2,1)S(1)}, bf16[4,1,128,128]{3,2,1,0:T(8,128)(2,1)S(1)}, u32[]{:S(2)}, u32[]{:S(2)}) collective-permute-start(bf16[4,1,128,128]{3,2,1,0:T(8,128)(2,1)S(1)} %fusion.9), channel_id=1, source_target_pairs={{0,1},{1,0},{2,3},{3,2},{4,5},{5,4},{6,7},{7,6},{8,9},{9,8},{10,11... | collective-permute-start | bytes 393224 | tf_op jit(solution)/shard_map/output_conv/ppermute | solution.py:15
  48.2 0.7 %copy-start.2 = (bf16[4,1,128,128]{3,2,1,0:T(8,128)(2,1)}, bf16[4,1,128,128]{3,2,1,0:T(8,128)(2,1)S(1)}, u32[]{:S(2)}) copy-start(bf16[4,1,128,128]{3,2,1,0:T(8,128)(2,1)S(1)} %collective-permute-done.5.top_ref.bottom_ref) | copy-start | bytes 393220

commit v16 on v15

--- a/solution.py
+++ b/solution.py
@@ -99,20 +99,63 @@
         )
 
 
-def output_kernel(
-    cum_ref, skip_ref, incoming_ref, top_ref, local_ref, bottom_ref, frame_ref, w_ref, out_ref
-):
+def output_kernel(cum_ref, skip_ref, incoming_ref, local_ref, frame_ref, w_ref, out_ref, rim_ref):
     f = pl.program_id(0)
     band, width, m = out_ref.shape[1:]
     per = frame_ref.shape[0]
     for j in range(per):
         g = f * per + j
         inner = (local_ref[j] + cum_ref[pl.ds(g, 1), :] * incoming_ref[...]).astype(jnp.bfloat16)
-        x = padded_band(top_ref[g], inner, bottom_ref[g], "rows")
-        total = conv_taps(x, w_ref)
+        zero = jnp.zeros((1, width, inner.shape[2]), jnp.bfloat16)
+        total = conv_taps(jnp.concatenate([zero, inner, zero], axis=0), w_ref)
         frame = frame_ref[j].reshape(band * width, m).astype(jnp.float32)
         total = total + skip_ref[...] * frame
         out_ref[j] = total.astype(jnp.bfloat16).reshape(band, width, m)
+        rim_ref[j, 0] = total[:width]
+        rim_ref[j, 1] = total[(band - 1) * width :]
+
+
+def halo_effect(rows_2d, w_ref, a, width):
+    m = w_ref.shape[3]
+    taps = jnp.concatenate([w_ref[a, b] for b in range(3)], axis=1)
+    acc = jnp.dot(rows_2d, taps, preferred_element_type=jnp.float32)
+    n = acc.shape[0]
+    column = lax.broadcasted_iota(jnp.int32, (n, m), 0) % width
+    from_left = pltpu.roll(acc[:, :m], 1, 0)
+    from_right = pltpu.roll(acc[:, 2 * m :], n - 1, 0)
+    total = acc[:, m : 2 * m]
+    total = total + jnp.where(column == 0, 0.0, from_left)
+    return total + jnp.where(column == width - 1, 0.0, from_right)
+
+
+def output_edge_kernel(rim_ref, top_ref, bottom_ref, w_ref, body_ref, out_ref, upper_buf, lower_buf, sems):
+    del body_ref
+    count, _, width, m = rim_ref.shape
+    band = out_ref.shape[1]
+    k = top_ref.shape[3]
+    above = top_ref[...].reshape(count * width, k)
+    below = bottom_ref[...].reshape(count * width, k)
+    up = halo_effect(above, w_ref, 0, width)
+    down = halo_effect(below, w_ref, 2, width)
+    if lax.axis_size("rows") == 2:
+        position = lax.axis_index("rows")
+        up = jnp.where(position == 1, up, 0.0)
+        down = jnp.where(position == 0, down, 0.0)
+    rim = rim_ref[...]
+    upper_buf[...] = (rim[:, 0].reshape(count * width, m) + up).astype(jnp.bfloat16).reshape(
+        count, 1, width, m
+    )
+    lower_buf[...] = (rim[:, 1].reshape(count * width, m) + down).astype(jnp.bfloat16).reshape(
+        count, 1, width, m
+    )
+    copies = [
+        pltpu.make_async_copy(upper_buf, out_ref.at[:, pl.ds(0, 1)], sems.at[0]),
+        pltpu.make_async_copy(lower_buf, out_ref.at[:, pl.ds(band - 1, 1)], sems.at[1]),
+    ]
+    for copy in copies:
+        copy.start()
+    for copy in copies:
+        copy.wait()
 
 
 def input_stage(frames, conv_in, decay):
@@ -157,24 +200,40 @@
         [incoming[None, :1], incoming[None, -1:]], axis=1
     )
     top, bottom = halo_rows(edges.astype(jnp.bfloat16), "rows", 1)
-    halo = pl.BlockSpec(memory_space=pltpu.VMEM)
-    return pl.pallas_call(
+    body, rim = pl.pallas_call(
         output_kernel,
         grid=(count // PER_STEP,),
         in_specs=[
             pl.BlockSpec((count, state_width), lambda f: (0, 0)),
             pl.BlockSpec((1, channels), lambda f: (0, 0)),
             pl.BlockSpec((band, width, state_width), lambda f: (0, 0, 0)),
-            halo,
             pl.BlockSpec((PER_STEP, band, width, state_width), lambda f: (f, 0, 0, 0)),
-            halo,
             pl.BlockSpec((PER_STEP, band, width, channels), lambda f: (f, 0, 0, 0)),
             pl.BlockSpec((3, 3, state_width, channels), lambda f: (0, 0, 0, 0)),
         ],
-        out_specs=pl.BlockSpec((PER_STEP, band, width, channels), lambda f: (f, 0, 0, 0)),
+        out_specs=[
+            pl.BlockSpec((PER_STEP, band, width, channels), lambda f: (f, 0, 0, 0)),
+            pl.BlockSpec((PER_STEP, 2, width, channels), lambda f: (f, 0, 0, 0)),
+        ],
+        out_shape=[
+            jax.ShapeDtypeStruct((count, band, width, channels), jnp.bfloat16),
+            jax.ShapeDtypeStruct((count, 2, width, channels), jnp.float32),
+        ],
+        compiler_params=pltpu.CompilerParams(dimension_semantics=("arbitrary",)),
+    )(cumulative, skip.reshape(1, channels), incoming, local, frames, conv_out)
+    vmem = pl.BlockSpec(memory_space=pltpu.VMEM)
+    return pl.pallas_call(
+        output_edge_kernel,
+        in_specs=[vmem, vmem, vmem, vmem, pl.BlockSpec(memory_space=pl.ANY)],
+        out_specs=pl.BlockSpec(memory_space=pl.ANY),
         out_shape=jax.ShapeDtypeStruct((count, band, width, channels), jnp.bfloat16),
-        compiler_params=pltpu.CompilerParams(dimension_semantics=("arbitrary",)),
-    )(cumulative, skip.reshape(1, channels), incoming, top, local, bottom, frames, conv_out)
+        scratch_shapes=[
+            pltpu.VMEM((count, 1, width, channels), jnp.bfloat16),
+            pltpu.VMEM((count, 1, width, channels), jnp.bfloat16),
+            pltpu.SemaphoreType.DMA((2,)),
+        ],
+        input_output_aliases={4: 0},
+    )(rim, top, bottom, conv_out, body)
 
 
 def split3(p, rows):

time: 54.2 us -> 55.4 us (1.022)
  Pallas kernels: 9.77 us -> 11.7 us
  waiting for transfers between devices: 29.3 us -> 28 us
  local copies, waits for them, and re-layouts: 4.4 us -> 4.97 us
    pallas_call x0 -> x1, Pallas kernels: none -> 2.26 us  [output_stage(): pl.pallas_call(output_edge_kernel, in_specs=[vmem, vmem, vmem, vmem, pl.B...]
    ppermute x2, waiting for transfers between devices: 2.32 us -> 0.99 us  [halo_rows(): lax.ppermute(lax.dynamic_slice_in_dim(x, row, 1, axis=dim), axis, [(0, 1)...]
    unnamed x10, local copies, waits for them, and re-layouts: 1.31 us -> 1.87 us
  transfers between devices with their start and end apart: 6 -> 6, of which waited for: 6 -> 5; matrix products, arithmetic and copies ran while one was open for 4% -> 4% of each run, Pallas kernels for 0% -> 9%
where the time goes in v16:
time: 55.4 us; the launch traced here: 55.1 us
  waiting for transfers between devices  28 us (51%)
  Pallas kernels  11.7 us (21%)
  starting transfers between devices  9.1 us (16%)
  local copies, waits for them, and re-layouts  4.97 us (9%)
  other arithmetic  1.23 us (2%)
    ppermute x4, waiting for transfers between devices, incoming_state(): got = lax.ppermute(payload, axis, pairs)  27 us
    ppermute x4, starting transfers between devices, incoming_state(): got = lax.ppermute(payload, axis, pairs)  8.51 us
    pallas_call x1, Pallas kernels, output_stage(): pl.pallas_call(output_kernel, grid=(count // PER_STEP,), in_specs=[pl.Blo...  4.79 us
    pallas_call x1, Pallas kernels, input_stage(): pl.pallas_call(input_kernel, grid=(count // PER_STEP,), in_specs=[pl.Bloc...  4.64 us
    pallas_call x1, Pallas kernels, output_stage(): pl.pallas_call(output_edge_kernel, in_specs=[vmem, vmem, vmem, vmem, pl.B...  2.26 us
    unnamed x10, local copies, waits for them, and re-layouts  1.87 us
  transfers between devices with their start and end apart: 6, of which 5 were waited for; matrix products, arithmetic and copies ran while one was open for 4% of the time, Pallas kernels for 9%

profile of v16, /device:TPU:0, one launch (start us, length us, event | category | flops | bytes accessed | tf_op | source)
XLA Modules:
  0.0 55.1 jit_solution(11194879924122251592)
XLA Ops:
  0.0 0.0 copy-start.4
  0.0 0.9 %constant_dynamic-slice_fusion.1 = bf16[4,1,128,128]{3,2,1,0:T(8,128)(2,1)S(1)} fusion(bf16[4,8,128,128]{3,2,1,0:T(8,128)(2,1)} %frame_ref.3, s32[]{:T(128)S(6)} %select_n.85), kind=kLoop, calls=%fused_computation.52 | loop fusion | bytes 262148 | tf_op jit(solution)/shard_map/input_conv_and_recurrence/dynamic_slice | solution.py:15
  0.9 0.5 collective-permute-start
  1.5 1.0 %collective-permute-done.top_ref.bottom_ref = bf16[4,1,128,128]{3,2,1,0:T(8,128)(2,1)S(1)} collective-permute-done((bf16[4,1,128,128]{3,2,1,0:T(8,128)(2,1)S(1)}, bf16[4,1,128,128]{3,2,1,0:T(8,128)(2,1)S(1)}, u32[]{:S(2)}, u32[]{:S(2)}) %collective-permute-start) | collective-permute-done | bytes 131104 | tf_op jit(solution)/shard_map/input_conv_and_recurrence/ppermute | solution.py:15
  2.4 0.0 copy-start.2
  2.4 0.6 %copy-done.2 = bf16[4,1,128,128]{3,2,1,0:T(8,128)(2,1)} copy-done((bf16[4,1,128,128]{3,2,1,0:T(8,128)(2,1)}, bf16[4,1,128,128]{3,2,1,0:T(8,128)(2,1)S(1)}, u32[]{:S(2)}) %copy-start.2) | copy-done | bytes 131096
  3.1 4.6 %input_conv_and_recurrence.1 = (f32[4,8,128,128]{3,2,1,0:T(8,128)}, f32[4,128]{1,0:T(4,128)}, bf16[1040,128]{1,0:T(8,128)(2,1)}) custom-call(f32[4,128]{1,0:T(4,128)} %decay_ref.1, bf16[4,1,128,128]{3,2,1,0:T(8,128)(2,1)} %copy-done.2, bf16[4,8,128,128]{3,2,1,0:T(8,128)(2,1)} %frame_ref.3, bf16[4,1,128,128]{3,2,1,0:T(8,128)(2,1)} %copy-done.2, ...), custom_call_target="tpu_custom_call" | custom-call | tf_op jit(solution)/shard_map/input_conv_and_recurrence/pallas_call | solution.py:167
  7.7 2.8 %collective-permute-start.1 = (bf16[1040,128]{1,0:T(8,128)(2,1)}, bf16[1040,128]{1,0:T(8,128)(2,1)S(1)}, u32[]{:S(2)}, u32[]{:S(2)}) collective-permute-start(bf16[1040,128]{1,0:T(8,128)(2,1)} %get-tuple-element.11), channel_id=1, source_target_pairs={{0,2},{2,0},{4,6},{6,4},{8,10},{10,8},{12,14},{14,12},{16,18},{18,... | collective-permute-start | bytes 798728 | tf_op jit(solution)/shard_map/carry_across_blocks/ppermute | solution.py:261
  10.6 1.1 %slice.56 = f32[1,8,128,128]{3,2,1,0:T(8,128)S(1)} slice(f32[4,8,128,128]{3,2,1,0:T(8,128)} %get-tuple-element.12.local_ref), slice={[3:4], [0:8], [0:128], [0:128]} | slice | bytes 1048576 | tf_op jit(solution)/shard_map/carry_across_blocks/slice | solution.py:289
  11.6 5.8 %collective-permute-done.1 = bf16[1040,128]{1,0:T(8,128)(2,1)S(1)} collective-permute-done((bf16[1040,128]{1,0:T(8,128)(2,1)}, bf16[1040,128]{1,0:T(8,128)(2,1)S(1)}, u32[]{:S(2)}, u32[]{:S(2)}) %collective-permute-start.1) | collective-permute-done | bytes 266272 | tf_op jit(solution)/shard_map/carry_across_blocks/ppermute | solution.py:261
  17.5 0.0 copy-done.4
  17.5 0.1 fusion.29
  17.7 1.8 %collective-permute-start.2 = (bf16[1040,128]{1,0:T(8,128)(2,1)S(1)}, bf16[1040,128]{1,0:T(8,128)(2,1)S(1)}, u32[]{:S(2)}, u32[]{:S(2)}) collective-permute-start(bf16[1040,128]{1,0:T(8,128)(2,1)S(1)} %pad_maximum_fusion), channel_id=1, source_target_pairs={{0,4},{2,6},{4,0},{6,2},{8,12},{10,14},{12,8},{14,10},{16,20},{18,... | collective-permute-start | bytes 798728 | tf_op jit(solution)/shard_map/carry_across_blocks/ppermute | solution.py:261
  19.5 6.2 %collective-permute-done.2 = bf16[1040,128]{1,0:T(8,128)(2,1)S(1)} collective-permute-done((bf16[1040,128]{1,0:T(8,128)(2,1)S(1)}, bf16[1040,128]{1,0:T(8,128)(2,1)S(1)}, u32[]{:S(2)}, u32[]{:S(2)}) %collective-permute-start.2) | collective-permute-done | bytes 266272 | tf_op jit(solution)/shard_map/carry_across_blocks/ppermute | solution.py:261
  25.8 0.2 fusion.10
  26.0 1.6 %collective-permute-start.3 = (bf16[1040,128]{1,0:T(8,128)(2,1)S(1)}, bf16[1040,128]{1,0:T(8,128)(2,1)S(1)}, u32[]{:S(2)}, u32[]{:S(2)}) collective-permute-start(bf16[1040,128]{1,0:T(8,128)(2,1)S(1)} %pad_maximum_fusion.1), channel_id=1, source_target_pairs={{0,8},{2,10},{4,12},{6,14},{8,0},{10,2},{12,4},{14,6},{16,24},{18,... | collective-permute-start | bytes 798728 | tf_op jit(solution)/shard_map/carry_across_blocks/ppermute | solution.py:261
  27.6 5.5 %collective-permute-done.3 = bf16[1040,128]{1,0:T(8,128)(2,1)S(1)} collective-permute-done((bf16[1040,128]{1,0:T(8,128)(2,1)S(1)}, bf16[1040,128]{1,0:T(8,128)(2,1)S(1)}, u32[]{:S(2)}, u32[]{:S(2)}) %collective-permute-start.3) | collective-permute-done | bytes 266272 | tf_op jit(solution)/shard_map/carry_across_blocks/ppermute | solution.py:261
  33.2 0.3 fusion.6
  33.5 0.0 copy-start.3
  33.6 2.2 %collective-permute-start.4 = (bf16[1040,128]{1,0:T(8,128)(2,1)S(1)}, bf16[1040,128]{1,0:T(8,128)(2,1)S(1)}, u32[]{:S(2)}, u32[]{:S(2)}) collective-permute-start(bf16[1040,128]{1,0:T(8,128)(2,1)S(1)} %pad_maximum_fusion.2), channel_id=1, source_target_pairs={{0,16},{2,18},{4,20},{6,22},{8,24},{10,26},{12,28},{14,30},{16,0},... | collective-permute-start | bytes 798728 | tf_op jit(solution)/shard_map/carry_across_blocks/ppermute | solution.py:261
  35.8 1.1 %fusion.30 = (f32[4,1,128,128]{3,2,1,0:T(8,128)S(1)}, f32[4,1,128,128]{3,2,1,0:T(8,128)S(1)}) fusion(f32[4,8,128,128]{3,2,1,0:T(8,128)} %get-tuple-element.12.local_ref), kind=kLoop, calls=%fused_computation.76 | loop fusion | bytes 1048576 | tf_op jit(solution)/shard_map/output_conv/slice | solution.py:198
  36.9 9.4 %collective-permute-done.4 = bf16[1040,128]{1,0:T(8,128)(2,1)S(1)} collective-permute-done((bf16[1040,128]{1,0:T(8,128)(2,1)S(1)}, bf16[1040,128]{1,0:T(8,128)(2,1)S(1)}, u32[]{:S(2)}, u32[]{:S(2)}) %collective-permute-start.4) | collective-permute-done | bytes 266272 | tf_op jit(solution)/shard_map/carry_across_blocks/ppermute | solution.py:261
  46.3 0.2 add_select_fusion
  46.6 0.0 copy-start
  46.7 0.0 copy-done.3
  46.7 0.1 fusion.9
  46.7 0.1 collective-permute-start.5
  46.8 0.6 %copy-done = f32[1024,128]{1,0:T(8,128)} copy-done((f32[1024,128]{1,0:T(8,128)}, f32[1024,128]{1,0:T(8,128)S(1)}, u32[]{:S(2)}) %copy-start) | copy-done | bytes 524312
  47.4 4.8 %output_conv.2 = (bf16[4,8,128,128]{3,2,1,0:T(8,128)(2,1)}, f32[4,2,128,128]{3,2,1,0:T(8,128)}) custom-call(f32[4,128]{1,0:T(4,128)} %get-tuple-element.10.cum_ref, f32[1,128]{1,0:T(1,128)} %bitcast.43, f32[8,128,128]{2,1,0:T(8,128)} %bitcast.36, f32[4,8,128,128]{3,2,1,0:T(8,128)} %get-tuple-element.12.local_ref, bf16[4,8,128,128]{3,2,1,0:T(8,128)(2,1)} %frame_ref.3, ...), custom_call_target="tpu_custom_call" | custom-call | tf_op jit(solution)/shard_map/output_conv/pallas_call | solution.py:203
  52.2 0.0 collective-permute-done.5.top_ref.bottom_ref
  52.2 0.0 copy-start.1
  52.2 0.6 %copy-done.1 = bf16[4,1,128,128]{3,2,1,0:T(8,128)(2,1)} copy-done((bf16[4,1,128,128]{3,2,1,0:T(8,128)(2,1)}, bf16[4,1,128,128]{3,2,1,0:T(8,128)(2,1)S(1)}, u32[]{:S(2)}) %copy-start.1) | copy-done | bytes 131096
  52.8 2.3 %output_conv.3 = bf16[4,8,128,128]{3,2,1,0:T(8,128)(2,1)} custom-call(f32[4,2,128,128]{3,2,1,0:T(8,128)} %get-tuple-element.13.rim_ref, bf16[4,1,128,128]{3,2,1,0:T(8,128)(2,1)} %copy-done.1, bf16[4,1,128,128]{3,2,1,0:T(8,128)(2,1)} %copy-done.1, bf16[3,3,128,128]{3,2,1,0:T(8,128)(2,1)} %w_ref.5, ...), custom_call_target="tpu_custom_call", output_to_operand_aliasing={{}: (4, {})} | custom-call | tf_op jit(solution)/shard_map/output_conv/pallas_call | solution.py:225
  (18 shorter events, 0.2 us)
Async XLA Ops:
  0.0 17.5 %copy-start.4 = (f32[4,128]{1,0:T(4,128)S(1)}, f32[4,128]{1,0:T(4,128)}, u32[]{:S(2)}) copy-start(f32[4,128]{1,0:T(4,128)} %decay_ref.1) | copy-start | bytes 6148
  0.9 1.5 %collective-permute-start = (bf16[4,1,128,128]{3,2,1,0:T(8,128)(2,1)S(1)}, bf16[4,1,128,128]{3,2,1,0:T(8,128)(2,1)S(1)}, u32[]{:S(2)}, u32[]{:S(2)}) collective-permute-start(bf16[4,1,128,128]{3,2,1,0:T(8,128)(2,1)S(1)} %constant_dynamic-slice_fusion.1), channel_id=1, source_target_pairs={{0,1},{1,0},{2,3},{3,2},{4,5},{5,4},{6,7},{7,6},{8,9},{9,8},{10,11... | collective-permute-start | bytes 393224 | tf_op jit(solution)/shard_map/input_conv_and_recurrence/ppermute | solution.py:15
  2.4 0.6 %copy-start.2 = (bf16[4,1,128,128]{3,2,1,0:T(8,128)(2,1)}, bf16[4,1,128,128]{3,2,1,0:T(8,128)(2,1)S(1)}, u32[]{:S(2)}) copy-start(bf16[4,1,128,128]{3,2,1,0:T(8,128)(2,1)S(1)} %collective-permute-done.top_ref.bottom_ref) | copy-start | bytes 393220
  7.7 9.8 %collective-permute-start.1 = (bf16[1040,128]{1,0:T(8,128)(2,1)}, bf16[1040,128]{1,0:T(8,128)(2,1)S(1)}, u32[]{:S(2)}, u32[]{:S(2)}) collective-permute-start(bf16[1040,128]{1,0:T(8,128)(2,1)} %get-tuple-element.11), channel_id=1, source_target_pairs={{0,2},{2,0},{4,6},{6,4},{8,10},{10,8},{12,14},{14,12},{16,18},{18,... | collective-permute-start | bytes 798728 | tf_op jit(solution)/shard_map/carry_across_blocks/ppermute | solution.py:261
  17.7 8.0 %collective-permute-start.2 = (bf16[1040,128]{1,0:T(8,128)(2,1)S(1)}, bf16[1040,128]{1,0:T(8,128)(2,1)S(1)}, u32[]{:S(2)}, u32[]{:S(2)}) collective-permute-start(bf16[1040,128]{1,0:T(8,128)(2,1)S(1)} %pad_maximum_fusion), channel_id=1, source_target_pairs={{0,4},{2,6},{4,0},{6,2},{8,12},{10,14},{12,8},{14,10},{16,20},{18,... | collective-permute-start | bytes 798728 | tf_op jit(solution)/shard_map/carry_across_blocks/ppermute | solution.py:261
  26.0 7.1 %collective-permute-start.3 = (bf16[1040,128]{1,0:T(8,128)(2,1)S(1)}, bf16[1040,128]{1,0:T(8,128)(2,1)S(1)}, u32[]{:S(2)}, u32[]{:S(2)}) collective-permute-start(bf16[1040,128]{1,0:T(8,128)(2,1)S(1)} %pad_maximum_fusion.1), channel_id=1, source_target_pairs={{0,8},{2,10},{4,12},{6,14},{8,0},{10,2},{12,4},{14,6},{16,24},{18,... | collective-permute-start | bytes 798728 | tf_op jit(solution)/shard_map/carry_across_blocks/ppermute | solution.py:261
  33.5 13.1 %copy-start.3 = (f32[4,128]{1,0:T(4,128)S(1)}, f32[4,128]{1,0:T(4,128)}, u32[]{:S(2)}) copy-start(f32[4,128]{1,0:T(4,128)} %get-tuple-element.10.cum_ref) | copy-start | bytes 6148
  33.6 12.8 %collective-permute-start.4 = (bf16[1040,128]{1,0:T(8,128)(2,1)S(1)}, bf16[1040,128]{1,0:T(8,128)(2,1)S(1)}, u32[]{:S(2)}, u32[]{:S(2)}) collective-permute-start(bf16[1040,128]{1,0:T(8,128)(2,1)S(1)} %pad_maximum_fusion.2), channel_id=1, source_target_pairs={{0,16},{2,18},{4,20},{6,22},{8,24},{10,26},{12,28},{14,30},{16,0},... | collective-permute-start | bytes 798728 | tf_op jit(solution)/shard_map/carry_across_blocks/ppermute | solution.py:261
  46.6 0.8 %copy-start = (f32[1024,128]{1,0:T(8,128)}, f32[1024,128]{1,0:T(8,128)S(1)}, u32[]{:S(2)}) copy-start(f32[1024,128]{1,0:T(8,128)S(1)} %add_select_fusion) | copy-start | bytes 1572868
  46.7 5.4 %collective-permute-start.5 = (bf16[4,1,128,128]{3,2,1,0:T(8,128)(2,1)S(1)}, bf16[4,1,128,128]{3,2,1,0:T(8,128)(2,1)S(1)}, u32[]{:S(2)}, u32[]{:S(2)}) collective-permute-start(bf16[4,1,128,128]{3,2,1,0:T(8,128)(2,1)S(1)} %fusion.9), channel_id=1, source_target_pairs={{0,1},{1,0},{2,3},{3,2},{4,5},{5,4},{6,7},{7,6},{8,9},{9,8},{10,11... | collective-permute-start | bytes 393224 | tf_op jit(solution)/shard_map/output_conv/ppermute | solution.py:15
  52.2 0.7 %copy-start.1 = (bf16[4,1,128,128]{3,2,1,0:T(8,128)(2,1)}, bf16[4,1,128,128]{3,2,1,0:T(8,128)(2,1)S(1)}, u32[]{:S(2)}) copy-start(bf16[4,1,128,128]{3,2,1,0:T(8,128)(2,1)S(1)} %collective-permute-done.5.top_ref.bottom_ref) | copy-start | bytes 393220

commit v17 on v15

--- a/solution.py
+++ b/solution.py
@@ -1,3 +1,5 @@
+import functools
+
 import jax
 import jax.numpy as jnp
 from jax import lax
@@ -100,9 +102,29 @@
 
 
 def output_kernel(
-    cum_ref, skip_ref, incoming_ref, top_ref, local_ref, bottom_ref, frame_ref, w_ref, out_ref
+    last_bit,
+    cum_ref,
+    skip_ref,
+    scale_ref,
+    got_ref,
+    base_ref,
+    top_ref,
+    local_ref,
+    bottom_ref,
+    frame_ref,
+    w_ref,
+    out_ref,
+    incoming_ref,
 ):
     f = pl.program_id(0)
+
+    @pl.when(f == 0)
+    def _():
+        earlier = (lax.axis_index("tm") & last_bit) != 0
+        base = base_ref[...]
+        update = scale_ref[...] * got_ref[...].astype(jnp.float32) + base
+        incoming_ref[...] = jnp.where(earlier, update, base)
+
     band, width, m = out_ref.shape[1:]
     per = frame_ref.shape[0]
     for j in range(per):
@@ -149,22 +171,33 @@
     )(decay, top, frames, bottom, conv_in)
 
 
-def output_stage(local, cumulative, incoming, frames, conv_out, skip):
+def output_stage(local, cumulative, pieces, frames, conv_out, skip):
     count, band, width, state_width = local.shape
     channels = conv_out.shape[3]
+    scale, got_rows, base, last_bit = pieces
+    earlier = (lax.axis_index("tm") & last_bit) != 0
+
+    def rows_of(x):
+        return jnp.concatenate([x[:1], x[-1:]], axis=0)
+
+    base_rows = rows_of(base)
+    incoming_rows = jnp.where(
+        earlier, scale * rows_of(got_rows).astype(jnp.float32) + base_rows, base_rows
+    )
     edges = jnp.concatenate([local[:, :1], local[:, -1:]], axis=1)
-    edges = edges + cumulative[:, None, None, :] * jnp.concatenate(
-        [incoming[None, :1], incoming[None, -1:]], axis=1
-    )
+    edges = edges + cumulative[:, None, None, :] * incoming_rows[None]
     top, bottom = halo_rows(edges.astype(jnp.bfloat16), "rows", 1)
     halo = pl.BlockSpec(memory_space=pltpu.VMEM)
+    whole_state = pl.BlockSpec((band, width, state_width), lambda f: (0, 0, 0))
     return pl.pallas_call(
-        output_kernel,
+        functools.partial(output_kernel, last_bit),
         grid=(count // PER_STEP,),
         in_specs=[
             pl.BlockSpec((count, state_width), lambda f: (0, 0)),
             pl.BlockSpec((1, channels), lambda f: (0, 0)),
-            pl.BlockSpec((band, width, state_width), lambda f: (0, 0, 0)),
+            pl.BlockSpec((1, state_width), lambda f: (0, 0)),
+            whole_state,
+            whole_state,
             halo,
             pl.BlockSpec((PER_STEP, band, width, state_width), lambda f: (f, 0, 0, 0)),
             halo,
@@ -173,8 +206,9 @@
         ],
         out_specs=pl.BlockSpec((PER_STEP, band, width, channels), lambda f: (f, 0, 0, 0)),
         out_shape=jax.ShapeDtypeStruct((count, band, width, channels), jnp.bfloat16),
+        scratch_shapes=[pltpu.VMEM((band, width, state_width), jnp.float32)],
         compiler_params=pltpu.CompilerParams(dimension_semantics=("arbitrary",)),
-    )(cumulative, skip.reshape(1, channels), incoming, top, local, bottom, frames, conv_out)
+    )(cumulative, skip.reshape(1, channels), scale, got_rows, base, top, local, bottom, frames, conv_out)
 
 
 def split3(p, rows):
@@ -192,8 +226,10 @@
     rows, width, channels = state.shape
     cells = rows * width
     tot_p, tot_s = power, state.reshape(cells, channels)
-    acc_p, acc_s = None, None
+    acc_p = jnp.ones_like(power)
+    acc_s = jnp.zeros((cells, channels), jnp.float32)
     payload = first_payload
+    last = (acc_p, jnp.zeros((cells, channels), jnp.bfloat16), acc_s, 0)
     bit = 1
     while bit < n:
         pairs = [(i, i ^ bit) for i in range(n)]
@@ -201,22 +237,21 @@
             payload = jnp.concatenate([tot_s.astype(jnp.bfloat16), split3(tot_p, 16)], axis=0)
         got = lax.ppermute(payload, axis, pairs)
         payload = None
+        if 2 * bit >= n:
+            last = (acc_p, got[:cells], acc_s, bit)
+            break
         got_s = got[:cells].astype(jnp.float32)
         got_p = jnp.sum(got[cells : cells + 3].astype(jnp.float32), axis=0)
         earlier = (me & bit) != 0
-        if acc_s is None:
-            acc_p = jnp.where(earlier, got_p, jnp.ones_like(got_p))
-            acc_s = jnp.where(earlier, got_s, jnp.zeros_like(got_s))
-        else:
-            acc_s = jnp.where(earlier, acc_p * got_s + acc_s, acc_s)
-            acc_p = jnp.where(earlier, got_p * acc_p, acc_p)
+        acc_s = jnp.where(earlier, acc_p * got_s + acc_s, acc_s)
+        acc_p = jnp.where(earlier, got_p * acc_p, acc_p)
         if 2 * bit < n:
             tot_s = jnp.where(earlier, tot_p * got_s + tot_s, got_p * tot_s + got_s)
             tot_p = got_p * tot_p
         bit *= 2
-    if acc_s is None:
-        return jnp.zeros_like(state)
-    return acc_s.reshape(rows, width, channels)
+    scale, got_rows, base, last_bit = last
+    shape = (rows, width, channels)
+    return scale.reshape(1, channels), got_rows.reshape(shape), base.reshape(shape), last_bit
 
 
 def shards(frames, conv_in, decay, conv_out, skip):
@@ -227,9 +262,9 @@
     with jax.named_scope("input_conv_and_recurrence"):
         local, cumulative, first_payload = input_stage(frames, conv_in, decay)
     with jax.named_scope("carry_across_blocks"):
-        incoming = incoming_state(block_power, local[-1], first_payload, "tm")
+        pieces = incoming_state(block_power, local[-1], first_payload, "tm")
     with jax.named_scope("output_conv"):
-        return output_stage(local, cumulative, incoming, frames, conv_out, skip)
+        return output_stage(local, cumulative, pieces, frames, conv_out, skip)
 
 
 def solution(mesh):

time: 54.2 us -> 54.7 us (level)
  local copies, waits for them, and re-layouts: 4.4 us -> 5.13 us
  waiting for transfers between devices: 29.3 us -> 28.6 us
    ppermute x2, waiting for transfers between devices: 2.32 us -> 1.59 us  [halo_rows(): lax.ppermute(lax.dynamic_slice_in_dim(x, row, 1, axis=dim), axis, [(0, 1)...]
    slice x1 -> x2, local copies, waits for them, and re-layouts: 1.08 us -> 1.8 us  [the longest x1 1.08 us: shards(): pieces = incoming_state(block_power, local[-1], first_payload, 'tm')]
  transfers between devices with their start and end apart: 6 -> 6, of which waited for: 6 -> 6; matrix products, arithmetic and copies ran while one was open for 4% -> 5% of each run, Pallas kernels for 0% -> 0%
where the time goes in v17:
time: 54.7 us; the launch traced here: 54.4 us
  waiting for transfers between devices  28.6 us (52%)
  Pallas kernels  9.89 us (18%)
  starting transfers between devices  9.1 us (17%)
  local copies, waits for them, and re-layouts  5.13 us (9%)
  other arithmetic  1.61 us (3%)
    ppermute x4, waiting for transfers between devices, incoming_state(): got = lax.ppermute(payload, axis, pairs)  27 us
    ppermute x4, starting transfers between devices, incoming_state(): got = lax.ppermute(payload, axis, pairs)  8.51 us
    pallas_call x1, Pallas kernels, output_stage(): pl.pallas_call(functools.partial(output_kernel, last_bit), grid=(count //...  5.26 us
    pallas_call x1, Pallas kernels, input_stage(): pl.pallas_call(input_kernel, grid=(count // PER_STEP,), in_specs=[pl.Bloc...  4.63 us
    ppermute x2, waiting for transfers between devices, halo_rows(): lax.ppermute(lax.dynamic_slice_in_dim(x, row, 1, axis=dim), axis, [(0, 1)...  1.59 us
    unnamed x10, local copies, waits for them, and re-layouts  1.3 us
  transfers between devices with their start and end apart: 6, of which 6 were waited for; matrix products, arithmetic and copies ran while one was open for 5% of the time, Pallas kernels for 0%

profile of v17, /device:TPU:0, one launch (start us, length us, event | category | flops | bytes accessed | tf_op | source)
XLA Modules:
  0.0 54.4 jit_solution(11350597964604479460)
XLA Ops:
  0.0 0.0 copy-start.4
  0.0 0.9 %constant_dynamic-slice_fusion.1 = bf16[4,1,128,128]{3,2,1,0:T(8,128)(2,1)S(1)} fusion(bf16[4,8,128,128]{3,2,1,0:T(8,128)(2,1)} %frame_ref.3, s32[]{:T(128)S(6)} %select_n.124), kind=kLoop, calls=%fused_computation.53 | loop fusion | bytes 262148 | tf_op jit(solution)/shard_map/input_conv_and_recurrence/dynamic_slice | solution.py:17
  0.9 0.5 collective-permute-start
  1.5 1.0 %collective-permute-done.top_ref.bottom_ref = bf16[4,1,128,128]{3,2,1,0:T(8,128)(2,1)S(1)} collective-permute-done((bf16[4,1,128,128]{3,2,1,0:T(8,128)(2,1)S(1)}, bf16[4,1,128,128]{3,2,1,0:T(8,128)(2,1)S(1)}, u32[]{:S(2)}, u32[]{:S(2)}) %collective-permute-start) | collective-permute-done | bytes 131104 | tf_op jit(solution)/shard_map/input_conv_and_recurrence/ppermute | solution.py:17
  2.4 0.0 copy-start.2
  2.4 0.6 %copy-done.2 = bf16[4,1,128,128]{3,2,1,0:T(8,128)(2,1)} copy-done((bf16[4,1,128,128]{3,2,1,0:T(8,128)(2,1)}, bf16[4,1,128,128]{3,2,1,0:T(8,128)(2,1)S(1)}, u32[]{:S(2)}) %copy-start.2) | copy-done | bytes 131096
  3.1 4.6 %input_conv_and_recurrence.1 = (f32[4,8,128,128]{3,2,1,0:T(8,128)}, f32[4,128]{1,0:T(4,128)}, bf16[1040,128]{1,0:T(8,128)(2,1)}) custom-call(f32[4,128]{1,0:T(4,128)} %decay_ref.1, bf16[4,1,128,128]{3,2,1,0:T(8,128)(2,1)} %copy-done.2, bf16[4,8,128,128]{3,2,1,0:T(8,128)(2,1)} %frame_ref.3, bf16[4,1,128,128]{3,2,1,0:T(8,128)(2,1)} %copy-done.2, ...), custom_call_target="tpu_custom_call" | custom-call | tf_op jit(solution)/shard_map/input_conv_and_recurrence/pallas_call | solution.py:146
  7.7 2.8 %collective-permute-start.1 = (bf16[1040,128]{1,0:T(8,128)(2,1)}, bf16[1040,128]{1,0:T(8,128)(2,1)S(1)}, u32[]{:S(2)}, u32[]{:S(2)}) collective-permute-start(bf16[1040,128]{1,0:T(8,128)(2,1)} %get-tuple-element.9), channel_id=1, source_target_pairs={{0,2},{2,0},{4,6},{6,4},{8,10},{10,8},{12,14},{14,12},{16,18},{18,... | collective-permute-start | bytes 798728 | tf_op jit(solution)/shard_map/carry_across_blocks/ppermute | solution.py:238
  10.6 1.1 %slice.66 = f32[1,8,128,128]{3,2,1,0:T(8,128)S(1)} slice(f32[4,8,128,128]{3,2,1,0:T(8,128)} %get-tuple-element.10.local_ref), slice={[3:4], [0:8], [0:128], [0:128]} | slice | bytes 1048576 | tf_op jit(solution)/shard_map/carry_across_blocks/slice | solution.py:265
  11.6 5.8 %collective-permute-done.1 = bf16[1040,128]{1,0:T(8,128)(2,1)S(1)} collective-permute-done((bf16[1040,128]{1,0:T(8,128)(2,1)}, bf16[1040,128]{1,0:T(8,128)(2,1)S(1)}, u32[]{:S(2)}, u32[]{:S(2)}) %collective-permute-start.1) | collective-permute-done | bytes 266272 | tf_op jit(solution)/shard_map/carry_across_blocks/ppermute | solution.py:238
  17.5 0.0 copy-done.4
  17.5 0.1 fusion.29
  17.7 1.8 %collective-permute-start.2 = (bf16[1040,128]{1,0:T(8,128)(2,1)S(1)}, bf16[1040,128]{1,0:T(8,128)(2,1)S(1)}, u32[]{:S(2)}, u32[]{:S(2)}) collective-permute-start(bf16[1040,128]{1,0:T(8,128)(2,1)S(1)} %pad_maximum_fusion), channel_id=1, source_target_pairs={{0,4},{2,6},{4,0},{6,2},{8,12},{10,14},{12,8},{14,10},{16,20},{18,... | collective-permute-start | bytes 798728 | tf_op jit(solution)/shard_map/carry_across_blocks/ppermute | solution.py:238
  19.5 6.2 %collective-permute-done.2 = bf16[1040,128]{1,0:T(8,128)(2,1)S(1)} collective-permute-done((bf16[1040,128]{1,0:T(8,128)(2,1)S(1)}, bf16[1040,128]{1,0:T(8,128)(2,1)S(1)}, u32[]{:S(2)}, u32[]{:S(2)}) %collective-permute-start.2) | collective-permute-done | bytes 266272 | tf_op jit(solution)/shard_map/carry_across_blocks/ppermute | solution.py:238
  25.8 0.2 fusion.10
  26.0 1.6 %collective-permute-start.3 = (bf16[1040,128]{1,0:T(8,128)(2,1)S(1)}, bf16[1040,128]{1,0:T(8,128)(2,1)S(1)}, u32[]{:S(2)}, u32[]{:S(2)}) collective-permute-start(bf16[1040,128]{1,0:T(8,128)(2,1)S(1)} %pad_maximum_fusion.1), channel_id=1, source_target_pairs={{0,8},{2,10},{4,12},{6,14},{8,0},{10,2},{12,4},{14,6},{16,24},{18,... | collective-permute-start | bytes 798728 | tf_op jit(solution)/shard_map/carry_across_blocks/ppermute | solution.py:238
  27.6 5.5 %collective-permute-done.3 = bf16[1040,128]{1,0:T(8,128)(2,1)S(1)} collective-permute-done((bf16[1040,128]{1,0:T(8,128)(2,1)S(1)}, bf16[1040,128]{1,0:T(8,128)(2,1)S(1)}, u32[]{:S(2)}, u32[]{:S(2)}) %collective-permute-start.3) | collective-permute-done | bytes 266272 | tf_op jit(solution)/shard_map/carry_across_blocks/ppermute | solution.py:238
  33.2 0.5 reduce-precision_convert_fusion.1
  33.7 0.0 copy-start.3
  33.7 0.5 add_select_fusion
  34.2 0.0 copy-start
  34.2 2.2 %collective-permute-start.4 = (bf16[1040,128]{1,0:T(8,128)(2,1)S(1)}, bf16[1040,128]{1,0:T(8,128)(2,1)S(1)}, u32[]{:S(2)}, u32[]{:S(2)}) collective-permute-start(bf16[1040,128]{1,0:T(8,128)(2,1)S(1)} %pad_maximum_fusion.2), channel_id=1, source_target_pairs={{0,16},{2,18},{4,20},{6,22},{8,24},{10,26},{12,28},{14,30},{16,0},... | collective-permute-start | bytes 798728 | tf_op jit(solution)/shard_map/carry_across_blocks/ppermute | solution.py:238
  36.4 1.1 %fusion.30 = (f32[4,1,128,128]{3,2,1,0:T(8,128)S(1)}, f32[4,1,128,128]{3,2,1,0:T(8,128)S(1)}) fusion(f32[4,8,128,128]{3,2,1,0:T(8,128)} %get-tuple-element.10.local_ref), kind=kLoop, calls=%fused_computation.80 | loop fusion | bytes 1048576 | tf_op jit(solution)/shard_map/output_conv/slice | solution.py:187
  37.5 9.4 %collective-permute-done.4 = bf16[1040,128]{1,0:T(8,128)(2,1)S(1)} collective-permute-done((bf16[1040,128]{1,0:T(8,128)(2,1)S(1)}, bf16[1040,128]{1,0:T(8,128)(2,1)S(1)}, u32[]{:S(2)}, u32[]{:S(2)}) %collective-permute-start.4) | collective-permute-done | bytes 266272 | tf_op jit(solution)/shard_map/carry_across_blocks/ppermute | solution.py:238
  47.0 0.0 copy-done.3
  47.0 0.1 fusion.9
  47.1 0.1 collective-permute-start.5
  47.2 0.7 %slice.84 = bf16[1024,128]{1,0:T(8,128)(2,1)} slice(bf16[1040,128]{1,0:T(8,128)(2,1)S(1)} %collective-permute-done.4), slice={[0:1024], [0:128]} | slice | bytes 524288 | tf_op jit(solution)/shard_map/carry_across_blocks/slice | solution.py:241
  47.9 0.6 %collective-permute-done.5.top_ref.bottom_ref = bf16[4,1,128,128]{3,2,1,0:T(8,128)(2,1)S(1)} collective-permute-done((bf16[4,1,128,128]{3,2,1,0:T(8,128)(2,1)S(1)}, bf16[4,1,128,128]{3,2,1,0:T(8,128)(2,1)S(1)}, u32[]{:S(2)}, u32[]{:S(2)}) %collective-permute-start.5) | collective-permute-done | bytes 131104 | tf_op jit(solution)/shard_map/output_conv/ppermute | solution.py:17
  48.5 0.0 copy-start.1
  48.5 0.0 copy-done
  48.5 0.6 %copy-done.1 = bf16[4,1,128,128]{3,2,1,0:T(8,128)(2,1)} copy-done((bf16[4,1,128,128]{3,2,1,0:T(8,128)(2,1)}, bf16[4,1,128,128]{3,2,1,0:T(8,128)(2,1)S(1)}, u32[]{:S(2)}) %copy-start.1) | copy-done | bytes 131096
  49.2 5.3 %output_conv.1 = bf16[4,8,128,128]{3,2,1,0:T(8,128)(2,1)} custom-call(f32[4,128]{1,0:T(4,128)} %get-tuple-element.8.cum_ref, f32[1,128]{1,0:T(1,128)} %bitcast.50, f32[1,128]{1,0:T(1,128)} %get-tuple-element.30.scale_ref, bf16[8,128,128]{2,1,0:T(8,128)(2,1)} %bitcast.43, f32[8,128,128]{2,1,0:T(8,128)} %bitcast.42, bf16[4,1,128,128]{3,2,1,0:T(8,128)(2,1)} %copy-done.1, ...), custom_call_target="tpu_custom_call" | custom-call | tf_op jit(solution)/shard_map/output_conv/pallas_call | solution.py:192
  (18 shorter events, 0.2 us)
Async XLA Ops:
  0.0 17.5 %copy-start.4 = (f32[4,128]{1,0:T(4,128)S(1)}, f32[4,128]{1,0:T(4,128)}, u32[]{:S(2)}) copy-start(f32[4,128]{1,0:T(4,128)} %decay_ref.1) | copy-start | bytes 6148
  0.9 1.5 %collective-permute-start = (bf16[4,1,128,128]{3,2,1,0:T(8,128)(2,1)S(1)}, bf16[4,1,128,128]{3,2,1,0:T(8,128)(2,1)S(1)}, u32[]{:S(2)}, u32[]{:S(2)}) collective-permute-start(bf16[4,1,128,128]{3,2,1,0:T(8,128)(2,1)S(1)} %constant_dynamic-slice_fusion.1), channel_id=1, source_target_pairs={{0,1},{1,0},{2,3},{3,2},{4,5},{5,4},{6,7},{7,6},{8,9},{9,8},{10,11... | collective-permute-start | bytes 393224 | tf_op jit(solution)/shard_map/input_conv_and_recurrence/ppermute | solution.py:17
  2.4 0.6 %copy-start.2 = (bf16[4,1,128,128]{3,2,1,0:T(8,128)(2,1)}, bf16[4,1,128,128]{3,2,1,0:T(8,128)(2,1)S(1)}, u32[]{:S(2)}) copy-start(bf16[4,1,128,128]{3,2,1,0:T(8,128)(2,1)S(1)} %collective-permute-done.top_ref.bottom_ref) | copy-start | bytes 393220
  7.7 9.8 %collective-permute-start.1 = (bf16[1040,128]{1,0:T(8,128)(2,1)}, bf16[1040,128]{1,0:T(8,128)(2,1)S(1)}, u32[]{:S(2)}, u32[]{:S(2)}) collective-permute-start(bf16[1040,128]{1,0:T(8,128)(2,1)} %get-tuple-element.9), channel_id=1, source_target_pairs={{0,2},{2,0},{4,6},{6,4},{8,10},{10,8},{12,14},{14,12},{16,18},{18,... | collective-permute-start | bytes 798728 | tf_op jit(solution)/shard_map/carry_across_blocks/ppermute | solution.py:238
  17.7 8.0 %collective-permute-start.2 = (bf16[1040,128]{1,0:T(8,128)(2,1)S(1)}, bf16[1040,128]{1,0:T(8,128)(2,1)S(1)}, u32[]{:S(2)}, u32[]{:S(2)}) collective-permute-start(bf16[1040,128]{1,0:T(8,128)(2,1)S(1)} %pad_maximum_fusion), channel_id=1, source_target_pairs={{0,4},{2,6},{4,0},{6,2},{8,12},{10,14},{12,8},{14,10},{16,20},{18,... | collective-permute-start | bytes 798728 | tf_op jit(solution)/shard_map/carry_across_blocks/ppermute | solution.py:238
  26.0 7.1 %collective-permute-start.3 = (bf16[1040,128]{1,0:T(8,128)(2,1)S(1)}, bf16[1040,128]{1,0:T(8,128)(2,1)S(1)}, u32[]{:S(2)}, u32[]{:S(2)}) collective-permute-start(bf16[1040,128]{1,0:T(8,128)(2,1)S(1)} %pad_maximum_fusion.1), channel_id=1, source_target_pairs={{0,8},{2,10},{4,12},{6,14},{8,0},{10,2},{12,4},{14,6},{16,24},{18,... | collective-permute-start | bytes 798728 | tf_op jit(solution)/shard_map/carry_across_blocks/ppermute | solution.py:238
  33.7 13.3 %copy-start.3 = (f32[4,128]{1,0:T(4,128)S(1)}, f32[4,128]{1,0:T(4,128)}, u32[]{:S(2)}) copy-start(f32[4,128]{1,0:T(4,128)} %get-tuple-element.8.cum_ref) | copy-start | bytes 6148
  34.2 14.4 %copy-start = (f32[1024,128]{1,0:T(8,128)}, f32[1024,128]{1,0:T(8,128)S(1)}, u32[]{:S(2)}) copy-start(f32[1024,128]{1,0:T(8,128)S(1)} %get-tuple-element.21) | copy-start | bytes 1572868
  34.2 12.8 %collective-permute-start.4 = (bf16[1040,128]{1,0:T(8,128)(2,1)S(1)}, bf16[1040,128]{1,0:T(8,128)(2,1)S(1)}, u32[]{:S(2)}, u32[]{:S(2)}) collective-permute-start(bf16[1040,128]{1,0:T(8,128)(2,1)S(1)} %pad_maximum_fusion.2), channel_id=1, source_target_pairs={{0,16},{2,18},{4,20},{6,22},{8,24},{10,26},{12,28},{14,30},{16,0},... | collective-permute-start | bytes 798728 | tf_op jit(solution)/shard_map/carry_across_blocks/ppermute | solution.py:238
  47.1 1.4 %collective-permute-start.5 = (bf16[4,1,128,128]{3,2,1,0:T(8,128)(2,1)S(1)}, bf16[4,1,128,128]{3,2,1,0:T(8,128)(2,1)S(1)}, u32[]{:S(2)}, u32[]{:S(2)}) collective-permute-start(bf16[4,1,128,128]{3,2,1,0:T(8,128)(2,1)S(1)} %fusion.9), channel_id=1, source_target_pairs={{0,1},{1,0},{2,3},{3,2},{4,5},{5,4},{6,7},{7,6},{8,9},{9,8},{10,11... | collective-permute-start | bytes 393224 | tf_op jit(solution)/shard_map/output_conv/ppermute | solution.py:17
  48.5 0.6 %copy-start.1 = (bf16[4,1,128,128]{3,2,1,0:T(8,128)(2,1)}, bf16[4,1,128,128]{3,2,1,0:T(8,128)(2,1)S(1)}, u32[]{:S(2)}) copy-start(bf16[4,1,128,128]{3,2,1,0:T(8,128)(2,1)S(1)} %collective-permute-done.5.top_ref.bottom_ref) | copy-start | bytes 393220

commit v18 on v15

--- a/solution.py
+++ b/solution.py
@@ -5,6 +5,7 @@
 from jax.experimental.pallas import tpu as pltpu
 from jax.sharding import PartitionSpec as P
 
+IN_STEP = 4
 PER_STEP = 2
 
 
@@ -123,16 +124,16 @@
     payload_rows = band * width + 16
     return pl.pallas_call(
         input_kernel,
-        grid=(count // PER_STEP,),
+        grid=(count // IN_STEP,),
         in_specs=[
             pl.BlockSpec((count, state_width), lambda f: (0, 0)),
             halo,
-            pl.BlockSpec((PER_STEP, band, width, channels), lambda f: (f, 0, 0, 0)),
+            pl.BlockSpec((IN_STEP, band, width, channels), lambda f: (f, 0, 0, 0)),
             halo,
             pl.BlockSpec((3, 3, channels, state_width), lambda f: (0, 0, 0, 0)),
         ],
         out_specs=[
-            pl.BlockSpec((PER_STEP, band, width, state_width), lambda f: (f, 0, 0, 0)),
+            pl.BlockSpec((IN_STEP, band, width, state_width), lambda f: (f, 0, 0, 0)),
             pl.BlockSpec((count, state_width), lambda f: (0, 0)),
             pl.BlockSpec((payload_rows, state_width), lambda f: (0, 0)),
         ],

time: 54.2 us -> 54.4 us (level)
  no operation moved by 1% of the time
where the time goes in v18:
time: 54.4 us; the launch traced here: 54.2 us
  waiting for transfers between devices  29.3 us (54%)
  Pallas kernels  10 us (18%)
  starting transfers between devices  9.1 us (17%)
  local copies, waits for them, and re-layouts  4.4 us (8%)
  other arithmetic  1.23 us (2%)
    ppermute x4, waiting for transfers between devices, incoming_state(): got = lax.ppermute(payload, axis, pairs)  27 us
    ppermute x4, starting transfers between devices, incoming_state(): got = lax.ppermute(payload, axis, pairs)  8.51 us
    pallas_call x1, Pallas kernels, output_stage(): pl.pallas_call(output_kernel, grid=(count // PER_STEP,), in_specs=[pl.Blo...  5.12 us
    pallas_call x1, Pallas kernels, input_stage(): pl.pallas_call(input_kernel, grid=(count // IN_STEP,), in_specs=[pl.Block...  4.91 us
    ppermute x2, waiting for transfers between devices, halo_rows(): lax.ppermute(lax.dynamic_slice_in_dim(x, row, 1, axis=dim), axis, [(0, 1)...  2.32 us
    unnamed x10, local copies, waits for them, and re-layouts  1.31 us
  transfers between devices with their start and end apart: 6, of which 6 were waited for; matrix products, arithmetic and copies ran while one was open for 4% of the time, Pallas kernels for 0%

profile of v18, /device:TPU:0, one launch (start us, length us, event | category | flops | bytes accessed | tf_op | source)
XLA Modules:
  0.0 54.2 jit_solution(18167126512119127670)
XLA Ops:
  0.0 0.0 copy-start.4
  0.0 0.9 %constant_dynamic-slice_fusion.1 = bf16[4,1,128,128]{3,2,1,0:T(8,128)(2,1)S(1)} fusion(bf16[4,8,128,128]{3,2,1,0:T(8,128)(2,1)} %frame_ref.3, s32[]{:T(128)S(6)} %select_n.85), kind=kLoop, calls=%fused_computation.52 | loop fusion | bytes 262148 | tf_op jit(solution)/shard_map/input_conv_and_recurrence/dynamic_slice | solution.py:16
  0.9 0.5 collective-permute-start
  1.5 1.0 %collective-permute-done.top_ref.bottom_ref = bf16[4,1,128,128]{3,2,1,0:T(8,128)(2,1)S(1)} collective-permute-done((bf16[4,1,128,128]{3,2,1,0:T(8,128)(2,1)S(1)}, bf16[4,1,128,128]{3,2,1,0:T(8,128)(2,1)S(1)}, u32[]{:S(2)}, u32[]{:S(2)}) %collective-permute-start) | collective-permute-done | bytes 131104 | tf_op jit(solution)/shard_map/input_conv_and_recurrence/ppermute | solution.py:16
  2.4 0.0 copy-start.1
  2.4 0.6 %copy-done.1 = bf16[4,1,128,128]{3,2,1,0:T(8,128)(2,1)} copy-done((bf16[4,1,128,128]{3,2,1,0:T(8,128)(2,1)}, bf16[4,1,128,128]{3,2,1,0:T(8,128)(2,1)S(1)}, u32[]{:S(2)}) %copy-start.1) | copy-done | bytes 131096
  3.1 4.9 %input_conv_and_recurrence.1 = (f32[4,8,128,128]{3,2,1,0:T(8,128)}, f32[4,128]{1,0:T(4,128)}, bf16[1040,128]{1,0:T(8,128)(2,1)}) custom-call(f32[4,128]{1,0:T(4,128)} %decay_ref.1, bf16[4,1,128,128]{3,2,1,0:T(8,128)(2,1)} %copy-done.1, bf16[4,8,128,128]{3,2,1,0:T(8,128)(2,1)} %frame_ref.3, bf16[4,1,128,128]{3,2,1,0:T(8,128)(2,1)} %copy-done.1, ...), custom_call_target="tpu_custom_call" | custom-call | tf_op jit(solution)/shard_map/input_conv_and_recurrence/pallas_call | solution.py:125
  8.0 2.8 %collective-permute-start.1 = (bf16[1040,128]{1,0:T(8,128)(2,1)}, bf16[1040,128]{1,0:T(8,128)(2,1)S(1)}, u32[]{:S(2)}, u32[]{:S(2)}) collective-permute-start(bf16[1040,128]{1,0:T(8,128)(2,1)} %get-tuple-element.9), channel_id=1, source_target_pairs={{0,2},{2,0},{4,6},{6,4},{8,10},{10,8},{12,14},{14,12},{16,18},{18,... | collective-permute-start | bytes 798728 | tf_op jit(solution)/shard_map/carry_across_blocks/ppermute | solution.py:203
  10.8 1.1 %slice.56 = f32[1,8,128,128]{3,2,1,0:T(8,128)S(1)} slice(f32[4,8,128,128]{3,2,1,0:T(8,128)} %get-tuple-element.10.local_ref), slice={[3:4], [0:8], [0:128], [0:128]} | slice | bytes 1048576 | tf_op jit(solution)/shard_map/carry_across_blocks/slice | solution.py:231
  11.9 5.8 %collective-permute-done.1 = bf16[1040,128]{1,0:T(8,128)(2,1)S(1)} collective-permute-done((bf16[1040,128]{1,0:T(8,128)(2,1)}, bf16[1040,128]{1,0:T(8,128)(2,1)S(1)}, u32[]{:S(2)}, u32[]{:S(2)}) %collective-permute-start.1) | collective-permute-done | bytes 266272 | tf_op jit(solution)/shard_map/carry_across_blocks/ppermute | solution.py:203
  17.8 0.0 copy-done.4
  17.8 0.1 fusion.29
  18.0 1.8 %collective-permute-start.2 = (bf16[1040,128]{1,0:T(8,128)(2,1)S(1)}, bf16[1040,128]{1,0:T(8,128)(2,1)S(1)}, u32[]{:S(2)}, u32[]{:S(2)}) collective-permute-start(bf16[1040,128]{1,0:T(8,128)(2,1)S(1)} %pad_maximum_fusion), channel_id=1, source_target_pairs={{0,4},{2,6},{4,0},{6,2},{8,12},{10,14},{12,8},{14,10},{16,20},{18,... | collective-permute-start | bytes 798728 | tf_op jit(solution)/shard_map/carry_across_blocks/ppermute | solution.py:203
  19.8 6.2 %collective-permute-done.2 = bf16[1040,128]{1,0:T(8,128)(2,1)S(1)} collective-permute-done((bf16[1040,128]{1,0:T(8,128)(2,1)S(1)}, bf16[1040,128]{1,0:T(8,128)(2,1)S(1)}, u32[]{:S(2)}, u32[]{:S(2)}) %collective-permute-start.2) | collective-permute-done | bytes 266272 | tf_op jit(solution)/shard_map/carry_across_blocks/ppermute | solution.py:203
  26.0 0.2 fusion.10
  26.3 1.6 %collective-permute-start.3 = (bf16[1040,128]{1,0:T(8,128)(2,1)S(1)}, bf16[1040,128]{1,0:T(8,128)(2,1)S(1)}, u32[]{:S(2)}, u32[]{:S(2)}) collective-permute-start(bf16[1040,128]{1,0:T(8,128)(2,1)S(1)} %pad_maximum_fusion.1), channel_id=1, source_target_pairs={{0,8},{2,10},{4,12},{6,14},{8,0},{10,2},{12,4},{14,6},{16,24},{18,... | collective-permute-start | bytes 798728 | tf_op jit(solution)/shard_map/carry_across_blocks/ppermute | solution.py:203
  27.9 5.5 %collective-permute-done.3 = bf16[1040,128]{1,0:T(8,128)(2,1)S(1)} collective-permute-done((bf16[1040,128]{1,0:T(8,128)(2,1)S(1)}, bf16[1040,128]{1,0:T(8,128)(2,1)S(1)}, u32[]{:S(2)}, u32[]{:S(2)}) %collective-permute-start.3) | collective-permute-done | bytes 266272 | tf_op jit(solution)/shard_map/carry_across_blocks/ppermute | solution.py:203
  33.5 0.3 fusion.6
  33.8 0.0 copy-start.3
  33.8 2.2 %collective-permute-start.4 = (bf16[1040,128]{1,0:T(8,128)(2,1)S(1)}, bf16[1040,128]{1,0:T(8,128)(2,1)S(1)}, u32[]{:S(2)}, u32[]{:S(2)}) collective-permute-start(bf16[1040,128]{1,0:T(8,128)(2,1)S(1)} %pad_maximum_fusion.2), channel_id=1, source_target_pairs={{0,16},{2,18},{4,20},{6,22},{8,24},{10,26},{12,28},{14,30},{16,0},... | collective-permute-start | bytes 798728 | tf_op jit(solution)/shard_map/carry_across_blocks/ppermute | solution.py:203
  36.1 1.1 %fusion.30 = (f32[4,1,128,128]{3,2,1,0:T(8,128)S(1)}, f32[4,1,128,128]{3,2,1,0:T(8,128)S(1)}) fusion(f32[4,8,128,128]{3,2,1,0:T(8,128)} %get-tuple-element.10.local_ref), kind=kLoop, calls=%fused_computation.76 | loop fusion | bytes 1048576 | tf_op jit(solution)/shard_map/output_conv/slice | solution.py:156
  37.2 9.4 %collective-permute-done.4 = bf16[1040,128]{1,0:T(8,128)(2,1)S(1)} collective-permute-done((bf16[1040,128]{1,0:T(8,128)(2,1)S(1)}, bf16[1040,128]{1,0:T(8,128)(2,1)S(1)}, u32[]{:S(2)}, u32[]{:S(2)}) %collective-permute-start.4) | collective-permute-done | bytes 266272 | tf_op jit(solution)/shard_map/carry_across_blocks/ppermute | solution.py:203
  46.6 0.2 add_select_fusion
  46.9 0.0 copy-start
  46.9 0.0 copy-done.3
  46.9 0.1 fusion.9
  47.0 0.1 collective-permute-start.5
  47.1 1.3 %collective-permute-done.5.top_ref.bottom_ref = bf16[4,1,128,128]{3,2,1,0:T(8,128)(2,1)S(1)} collective-permute-done((bf16[4,1,128,128]{3,2,1,0:T(8,128)(2,1)S(1)}, bf16[4,1,128,128]{3,2,1,0:T(8,128)(2,1)S(1)}, u32[]{:S(2)}, u32[]{:S(2)}) %collective-permute-start.5) | collective-permute-done | bytes 131104 | tf_op jit(solution)/shard_map/output_conv/ppermute | solution.py:16
  48.4 0.0 copy-start.2
  48.4 0.0 copy-done
  48.4 0.6 %copy-done.2 = bf16[4,1,128,128]{3,2,1,0:T(8,128)(2,1)} copy-done((bf16[4,1,128,128]{3,2,1,0:T(8,128)(2,1)}, bf16[4,1,128,128]{3,2,1,0:T(8,128)(2,1)S(1)}, u32[]{:S(2)}) %copy-start.2) | copy-done | bytes 131096
  49.1 5.1 %output_conv.1 = bf16[4,8,128,128]{3,2,1,0:T(8,128)(2,1)} custom-call(f32[4,128]{1,0:T(4,128)} %get-tuple-element.8.cum_ref, f32[1,128]{1,0:T(1,128)} %bitcast.43, f32[8,128,128]{2,1,0:T(8,128)} %bitcast.36, bf16[4,1,128,128]{3,2,1,0:T(8,128)(2,1)} %copy-done.2, f32[4,8,128,128]{3,2,1,0:T(8,128)} %get-tuple-element.10.local_ref, ...), custom_call_target="tpu_custom_call" | custom-call | tf_op jit(solution)/shard_map/output_conv/pallas_call | solution.py:162
  (18 shorter events, 0.2 us)
Async XLA Ops:
  0.0 17.8 %copy-start.4 = (f32[4,128]{1,0:T(4,128)S(1)}, f32[4,128]{1,0:T(4,128)}, u32[]{:S(2)}) copy-start(f32[4,128]{1,0:T(4,128)} %decay_ref.1) | copy-start | bytes 6148
  0.9 1.5 %collective-permute-start = (bf16[4,1,128,128]{3,2,1,0:T(8,128)(2,1)S(1)}, bf16[4,1,128,128]{3,2,1,0:T(8,128)(2,1)S(1)}, u32[]{:S(2)}, u32[]{:S(2)}) collective-permute-start(bf16[4,1,128,128]{3,2,1,0:T(8,128)(2,1)S(1)} %constant_dynamic-slice_fusion.1), channel_id=1, source_target_pairs={{0,1},{1,0},{2,3},{3,2},{4,5},{5,4},{6,7},{7,6},{8,9},{9,8},{10,11... | collective-permute-start | bytes 393224 | tf_op jit(solution)/shard_map/input_conv_and_recurrence/ppermute | solution.py:16
  2.4 0.7 %copy-start.1 = (bf16[4,1,128,128]{3,2,1,0:T(8,128)(2,1)}, bf16[4,1,128,128]{3,2,1,0:T(8,128)(2,1)S(1)}, u32[]{:S(2)}) copy-start(bf16[4,1,128,128]{3,2,1,0:T(8,128)(2,1)S(1)} %collective-permute-done.top_ref.bottom_ref) | copy-start | bytes 393220
  8.0 9.8 %collective-permute-start.1 = (bf16[1040,128]{1,0:T(8,128)(2,1)}, bf16[1040,128]{1,0:T(8,128)(2,1)S(1)}, u32[]{:S(2)}, u32[]{:S(2)}) collective-permute-start(bf16[1040,128]{1,0:T(8,128)(2,1)} %get-tuple-element.9), channel_id=1, source_target_pairs={{0,2},{2,0},{4,6},{6,4},{8,10},{10,8},{12,14},{14,12},{16,18},{18,... | collective-permute-start | bytes 798728 | tf_op jit(solution)/shard_map/carry_across_blocks/ppermute | solution.py:203
  18.0 8.0 %collective-permute-start.2 = (bf16[1040,128]{1,0:T(8,128)(2,1)S(1)}, bf16[1040,128]{1,0:T(8,128)(2,1)S(1)}, u32[]{:S(2)}, u32[]{:S(2)}) collective-permute-start(bf16[1040,128]{1,0:T(8,128)(2,1)S(1)} %pad_maximum_fusion), channel_id=1, source_target_pairs={{0,4},{2,6},{4,0},{6,2},{8,12},{10,14},{12,8},{14,10},{16,20},{18,... | collective-permute-start | bytes 798728 | tf_op jit(solution)/shard_map/carry_across_blocks/ppermute | solution.py:203
  26.3 7.1 %collective-permute-start.3 = (bf16[1040,128]{1,0:T(8,128)(2,1)S(1)}, bf16[1040,128]{1,0:T(8,128)(2,1)S(1)}, u32[]{:S(2)}, u32[]{:S(2)}) collective-permute-start(bf16[1040,128]{1,0:T(8,128)(2,1)S(1)} %pad_maximum_fusion.1), channel_id=1, source_target_pairs={{0,8},{2,10},{4,12},{6,14},{8,0},{10,2},{12,4},{14,6},{16,24},{18,... | collective-permute-start | bytes 798728 | tf_op jit(solution)/shard_map/carry_across_blocks/ppermute | solution.py:203
  33.8 13.1 %copy-start.3 = (f32[4,128]{1,0:T(4,128)S(1)}, f32[4,128]{1,0:T(4,128)}, u32[]{:S(2)}) copy-start(f32[4,128]{1,0:T(4,128)} %get-tuple-element.8.cum_ref) | copy-start | bytes 6148
  33.8 12.8 %collective-permute-start.4 = (bf16[1040,128]{1,0:T(8,128)(2,1)S(1)}, bf16[1040,128]{1,0:T(8,128)(2,1)S(1)}, u32[]{:S(2)}, u32[]{:S(2)}) collective-permute-start(bf16[1040,128]{1,0:T(8,128)(2,1)S(1)} %pad_maximum_fusion.2), channel_id=1, source_target_pairs={{0,16},{2,18},{4,20},{6,22},{8,24},{10,26},{12,28},{14,30},{16,0},... | collective-permute-start | bytes 798728 | tf_op jit(solution)/shard_map/carry_across_blocks/ppermute | solution.py:203
  46.9 1.6 %copy-start = (f32[1024,128]{1,0:T(8,128)}, f32[1024,128]{1,0:T(8,128)S(1)}, u32[]{:S(2)}) copy-start(f32[1024,128]{1,0:T(8,128)S(1)} %add_select_fusion) | copy-start | bytes 1572868
  47.0 1.4 %collective-permute-start.5 = (bf16[4,1,128,128]{3,2,1,0:T(8,128)(2,1)S(1)}, bf16[4,1,128,128]{3,2,1,0:T(8,128)(2,1)S(1)}, u32[]{:S(2)}, u32[]{:S(2)}) collective-permute-start(bf16[4,1,128,128]{3,2,1,0:T(8,128)(2,1)S(1)} %fusion.9), channel_id=1, source_target_pairs={{0,1},{1,0},{2,3},{3,2},{4,5},{5,4},{6,7},{7,6},{8,9},{9,8},{10,11... | collective-permute-start | bytes 393224 | tf_op jit(solution)/shard_map/output_conv/ppermute | solution.py:16
  48.4 0.7 %copy-start.2 = (bf16[4,1,128,128]{3,2,1,0:T(8,128)(2,1)}, bf16[4,1,128,128]{3,2,1,0:T(8,128)(2,1)S(1)}, u32[]{:S(2)}) copy-start(bf16[4,1,128,128]{3,2,1,0:T(8,128)(2,1)S(1)} %collective-permute-done.5.top_ref.bottom_ref) | copy-start | bytes 393220
